TPU v7x, 32 devices: a whole 2x2x4 slice. The times are simulated.
32 devices in a mesh: dp: 2 (over core), row: 4 (over y, x), col: 4 (over z).
Axes of the slice: x: 2, y: 2, z: 4, core: 2. Of those that a mesh axis runs over, the one named last changes fastest.
Arguments:
- hidden_in: bfloat16 [2, 8, 1024, 2048], P(None, ('dp', 'col'), None, 'row'), may hold values from -60 to 60
- segment_ids: int32 [2, 8, 1024], P(None, ('dp', 'row')), may hold values from 0 to 3, never falling along the last dimension, each value on 1 to 800 neighbouring positions
- w_query: bfloat16 [2048, 2048], P('row', 'col'), may hold values from -0.5 to 0.5
- w_key: bfloat16 [2048, 512], P('row', 'col'), may hold values from -0.5 to 0.5
- w_value: bfloat16 [2048, 512], P('row', 'col'), may hold values from -0.125 to 0.125
- w_out: bfloat16 [2048, 2048], P('col', 'row'), may hold values from -3 to 3
- w_gate: bfloat16 [2048, 8192], P('row', 'col'), may hold values from -0.125 to 0.125
- w_up: bfloat16 [2048, 8192], P('row', 'col'), may hold values from -0.125 to 0.125
- w_down: bfloat16 [8192, 2048], P('col', 'row'), may hold values from -0.375 to 0.375
- gain_attn: float32 [2048], P('row'), may hold values from 0.1 to 1.9
- gain_ffn: float32 [2048], P('row'), may hold values from 0.1 to 1.9
- cotangent: bfloat16 [2, 8, 1024, 2048], P(None, ('dp', 'col'), None, 'row'), may hold values from -6 to 6
Outputs:
- block_out: bfloat16 [2, 8, 1024, 2048], P(None, ('dp', 'col'), None, 'row')
- grad_input: float32 [2, 8, 1024, 2048], P(None, ('dp', 'col'), None, 'row')
- grad_query: float32 [2048, 2048], P('row', 'col')
- grad_key: float32 [2048, 512], P('row', 'col')
- grad_value: float32 [2048, 512], P('row', 'col')
- grad_out: float32 [2048, 2048], P('col', 'row')
- gate_weight_gradient: float32 [2048, 8192], P('row', 'col')
- grad_up: float32 [2048, 8192], P('row', 'col')
- grad_down: float32 [8192, 2048], P('col', 'row')
- grad_gain_attn: float32 [2048], P('row')
- grad_gain_ffn: float32 [2048], P('row')
Inputs may be any that keep to these rules, and one draw needn't show every extreme that they name: `segment_ids`: segment numbers never fall along a sequence; each of the 4 documents of a sequence has 1 to 800 tokens, one of them exactly 800.
All inputs are finite; a program needn't handle non-finite values.
Results may differ from a plain program's by a relative error of at most 0.014.
The roundings to bfloat16 on the way count: a program that leaves them out, or rounds other values in their place, can miss the bound.
Values may be sent and summed in bfloat16 or wider, within the bound.
No kernel may reach another device: no remote copies, remote signals or barrier semaphores. Data moves between devices by JAX's collectives and lax.ppermute only.
A program may use at most 576 MiB of HBM per device.

v0:
```python
from functools import partial
import math

import jax
import jax.numpy as jnp
from jax import lax
from jax.sharding import PartitionSpec as P

D = 2048
HD = 64


EPSILON = 1e-05
RESIDUAL_SCALE = 0.22
SCORE_SCALE = 0.015625
ROPE_BASE = 10000000.0
MASKED_SCORE = -1e30


def spread_cols(operand):
    return lax.all_gather(operand, "col", axis=0, tiled=True)


def gather_rows(operand):
    return lax.all_gather(operand, "row", axis=0, tiled=True)


def scatter_rows(operand):
    return lax.psum_scatter(operand, "row", scatter_dimension=0, tiled=True)


def scatter_cols(operand):
    return lax.psum_scatter(operand, "col", scatter_dimension=0, tiled=True)


def feature_total(operand):
    return lax.psum(operand, "row")


def project(left_operand_half, right_operand_half):
    return jnp.einsum(
        "tgf,fm->tgm", left_operand_half, right_operand_half, preferred_element_type=jnp.float32
    )


def project_back(left_operand_half, right_operand_half):
    return jnp.einsum(
        "kqx,px->kqp", left_operand_half, right_operand_half, preferred_element_type=jnp.float32
    )


def outer_sum(left_operand_half, right_operand_half):
    return jnp.einsum(
        "ruf,ruy->fy", left_operand_half, right_operand_half, preferred_element_type=jnp.float32
    )


def positions(segment_row):
    places = jnp.arange(segment_row.shape[0], dtype=jnp.int32)
    starts = jnp.concatenate([jnp.ones((1,), jnp.bool_), segment_row[1:] != segment_row[:-1]])
    first_place = lax.cummax(jnp.where(starts, places, jnp.zeros_like(places)), axis=0)
    return places - first_place


def rotary(segment_row):
    half_dim = HD // 2
    frequency = jnp.exp(jnp.arange(half_dim, dtype=jnp.float32) * (-2.0 * math.log(ROPE_BASE) / HD))
    angles = positions(segment_row).astype(jnp.float32)[:, None] * frequency[None, :]
    return (jnp.cos(angles)[:, None, :], jnp.sin(angles)[:, None, :])


def rotate(head_rows, cosine, sine_part):
    half_dim = head_rows.shape[-1] // 2
    first_half = head_rows[..., :half_dim]
    second_half = head_rows[..., half_dim:]
    return jnp.concatenate(
        [
            first_half * cosine - second_half * sine_part,
            second_half * cosine + first_half * sine_part,
        ],
        axis=-1,
    )


def masked_scores(query_rot, key_rot, segment_row):
    places = jnp.arange(segment_row.shape[0])
    allowed = (segment_row[:, None] == segment_row[None, :]) & (places[:, None] >= places[None, :])
    raw_scores = (
        jnp.einsum("qkgd,pkd->kgqp", query_rot, key_rot, preferred_element_type=jnp.float32)
        * SCORE_SCALE
    )
    return jnp.where(allowed, raw_scores, MASKED_SCORE)


def attend_forward(pieces, heads_q, heads_k):
    qkv_row, segment_row = pieces
    seq_len = segment_row.shape[0]
    width_q = heads_q * HD
    width_k = heads_k * HD
    cosine, sine_part = rotary(segment_row)
    query_rot = rotate(
        qkv_row[:, :width_q].reshape(seq_len, heads_q, HD), cosine, sine_part
    ).astype(jnp.bfloat16)
    query_rot = query_rot.reshape(seq_len, heads_k, heads_q // heads_k, HD)
    key_rot = rotate(
        qkv_row[:, width_q : width_q + width_k].reshape(seq_len, heads_k, HD), cosine, sine_part
    ).astype(jnp.bfloat16)
    value_low = qkv_row[:, width_q + width_k :].reshape(seq_len, heads_k, HD).astype(jnp.bfloat16)
    attention_scores = masked_scores(query_rot, key_rot, segment_row)
    row_peak = jnp.max(attention_scores, axis=-1, keepdims=True)
    log_total = row_peak + jnp.log(
        jnp.sum(jnp.exp(attention_scores - row_peak), axis=-1, keepdims=True)
    )
    attn_probs = jnp.exp(attention_scores - log_total).astype(jnp.bfloat16)
    mixed = jnp.einsum("kgqp,pkd->qkgd", attn_probs, value_low, preferred_element_type=jnp.float32)
    return (
        mixed.reshape(seq_len, width_q).astype(jnp.bfloat16),
        log_total,
        query_rot,
        key_rot,
        value_low,
    )


def attend_backward(pieces):
    grad_mixed, query_rot, key_rot, value_low, log_total, segment_row = pieces
    seq_len, heads_k, group_count, head_dim = query_rot.shape
    grad_grouped = grad_mixed.reshape(seq_len, heads_k, group_count, head_dim)
    attn_probs = jnp.exp(masked_scores(query_rot, key_rot, segment_row) - log_total)
    grad_probs = jnp.einsum(
        "qkgd,pkd->kgqp", grad_grouped, value_low, preferred_element_type=jnp.float32
    )
    grad_value = jnp.einsum(
        "kgqp,qkgd->pkd",
        attn_probs.astype(jnp.bfloat16),
        grad_grouped,
        preferred_element_type=jnp.float32,
    )
    grad_scores = (
        attn_probs * (grad_probs - jnp.sum(attn_probs * grad_probs, axis=-1, keepdims=True))
    ).astype(jnp.bfloat16)
    grad_query = (
        jnp.einsum("kgqp,pkd->qkgd", grad_scores, key_rot, preferred_element_type=jnp.float32)
        * SCORE_SCALE
    )
    grad_key = (
        jnp.einsum("kgqp,qkgd->pkd", grad_scores, query_rot, preferred_element_type=jnp.float32)
        * SCORE_SCALE
    )
    cosine, sine_part = rotary(segment_row)
    grad_query = rotate(
        grad_query.reshape(seq_len, heads_k * group_count, head_dim), cosine, -sine_part
    )
    grad_key = rotate(grad_key, cosine, -sine_part)
    joined = jnp.concatenate(
        [
            grad_query.reshape(seq_len, -1),
            grad_key.reshape(seq_len, -1),
            grad_value.reshape(seq_len, -1),
        ],
        axis=-1,
    )
    return joined.astype(jnp.bfloat16)


def add_up(old_set, new_set):
    if old_set is None:
        return new_set
    return tuple((old_part + new_part for old_part, new_part in zip(old_set, new_set)))


def shards(
    hidden_in,
    segment_ids,
    w_query,
    w_key,
    w_value,
    w_out,
    w_gate,
    w_up,
    w_down,
    gain_attn,
    gain_ffn,
    cotangent,
):
    batches = hidden_in.shape[0]
    heads_q = w_query.shape[1] // HD
    heads_k = w_key.shape[1] // HD
    query_cols = w_query.shape[1]
    key_end = query_cols + w_key.shape[1]
    ffn_cols = w_gate.shape[1]
    w_qkv = jnp.concatenate([w_query, w_key, w_value], axis=1)
    w_pair = jnp.concatenate([w_gate, w_up], axis=1)
    forward_fn = partial(attend_forward, heads_q=heads_q, heads_k=heads_k)
    grad_totals = None
    gain_attn_total = jnp.zeros(gain_attn.shape, jnp.float32)
    gain_ffn_total = jnp.zeros(gain_ffn.shape, jnp.float32)
    outs_list = []
    inputs_grad = []
    for batch_index in range(batches):
        rows_f = hidden_in[batch_index].astype(jnp.float32)
        segment_here = segment_ids[batch_index]
        inv_attn = lax.rsqrt(feature_total(jnp.sum(rows_f * rows_f, axis=-1)) / D + EPSILON)[
            ..., None
        ]
        norm_attn = rows_f * inv_attn
        normed_attn = (norm_attn * gain_attn).astype(jnp.bfloat16)
        spread_attn = spread_cols(normed_attn)
        qkv_here = scatter_rows(project(spread_attn, w_qkv))
        mixed, log_total, query_rot, key_rot, value_low = lax.map(
            forward_fn, (qkv_here, segment_here)
        )
        gathered_mixed = gather_rows(mixed)
        attn_branch = scatter_cols(project(gathered_mixed, w_out))
        resid_mid = rows_f + RESIDUAL_SCALE * attn_branch
        inv_ffn = lax.rsqrt(feature_total(jnp.sum(resid_mid * resid_mid, axis=-1)) / D + EPSILON)[
            ..., None
        ]
        norm_ffn = resid_mid * inv_ffn
        normed_ffn = (norm_ffn * gain_ffn).astype(jnp.bfloat16)
        spread_ffn = spread_cols(normed_ffn)
        pair_here = scatter_rows(project(spread_ffn, w_pair))
        gate_rows = pair_here[..., :ffn_cols]
        up_projection_rows = pair_here[..., ffn_cols:]
        sigmoid_gate = jax.nn.sigmoid(gate_rows)
        act_low = (gate_rows * sigmoid_gate * up_projection_rows).astype(jnp.bfloat16)
        gathered_act = gather_rows(act_low)
        ffn_branch = scatter_cols(project(gathered_act, w_down))
        outs_list.append((resid_mid + RESIDUAL_SCALE * ffn_branch).astype(jnp.bfloat16))
        grad_rows = cotangent[batch_index].astype(jnp.float32)
        grad_ffn = (RESIDUAL_SCALE * grad_rows).astype(jnp.bfloat16)
        spread_grad_ffn = spread_cols(grad_ffn)
        fresh_down = outer_sum(gathered_act, spread_grad_ffn)
        grad_act = scatter_rows(project_back(spread_grad_ffn, w_down))
        grad_gate_rows = (
            grad_act * up_projection_rows * sigmoid_gate * (1.0 + gate_rows * (1.0 - sigmoid_gate))
        )
        grad_up_rows = grad_act * gate_rows * sigmoid_gate
        paired_gradient = jnp.concatenate([grad_gate_rows, grad_up_rows], axis=-1).astype(
            jnp.bfloat16
        )
        spread_grad_pair = gather_rows(paired_gradient)
        fresh_pair = outer_sum(spread_ffn, spread_grad_pair)
        grad_normed_ffn = scatter_cols(project_back(spread_grad_pair, w_pair))
        scaled_ffn = grad_normed_ffn * gain_ffn
        gain_ffn_total = gain_ffn_total + jnp.sum(grad_normed_ffn * norm_ffn, axis=(0, 1))
        inner_ffn = feature_total(jnp.sum(scaled_ffn * norm_ffn, axis=-1))[..., None] / D
        grad_mid = grad_rows + inv_ffn * (scaled_ffn - norm_ffn * inner_ffn)
        grad_attn = (RESIDUAL_SCALE * grad_mid).astype(jnp.bfloat16)
        spread_grad_attn = spread_cols(grad_attn)
        fresh_out = outer_sum(gathered_mixed, spread_grad_attn)
        grad_mixed = scatter_rows(project_back(spread_grad_attn, w_out)).astype(jnp.bfloat16)
        grad_qkv = lax.map(
            attend_backward, (grad_mixed, query_rot, key_rot, value_low, log_total, segment_here)
        )
        spread_grad_qkv = gather_rows(grad_qkv)
        new_query_key_value = outer_sum(spread_attn, spread_grad_qkv)
        grad_normed_attn = scatter_cols(project_back(spread_grad_qkv, w_qkv))
        scaled_attn = grad_normed_attn * gain_attn
        gain_attn_total = gain_attn_total + jnp.sum(grad_normed_attn * norm_attn, axis=(0, 1))
        inner_attn = feature_total(jnp.sum(scaled_attn * norm_attn, axis=-1))[..., None] / D
        inputs_grad.append(grad_mid + inv_attn * (scaled_attn - norm_attn * inner_attn))
        fresh_grads = (new_query_key_value, fresh_out, fresh_pair, fresh_down)
        grad_totals = add_up(grad_totals, fresh_grads)
    qkv_part, out_part, pair_part, down_part = grad_totals
    grad_totals = lax.psum((qkv_part, out_part, pair_part, down_part), "dp")
    total_qkv, total_out, total_pair, total_down = grad_totals
    gain_attn_total, gain_ffn_total = lax.psum((gain_attn_total, gain_ffn_total), ("dp", "col"))
    return (
        jnp.stack(outs_list),
        jnp.stack(inputs_grad),
        total_qkv[:, :query_cols],
        total_qkv[:, query_cols:key_end],
        total_qkv[:, key_end:],
        total_out,
        total_pair[:, :ffn_cols],
        total_pair[:, ffn_cols:],
        total_down,
        gain_attn_total,
        gain_ffn_total,
    )


def solution(mesh):
    return jax.shard_map(
        shards,
        mesh=mesh,
        in_specs=(
            P(None, ("dp", "col"), None, "row"),
            P(None, ("dp", "row"), None),
            P("row", "col"),
            P("row", "col"),
            P("row", "col"),
            P("col", "row"),
            P("row", "col"),
            P("row", "col"),
            P("col", "row"),
            P("row"),
            P("row"),
            P(None, ("dp", "col"), None, "row"),
        ),
        out_specs=(
            P(None, ("dp", "col"), None, "row"),
            P(None, ("dp", "col"), None, "row"),
            P("row", "col"),
            P("row", "col"),
            P("row", "col"),
            P("col", "row"),
            P("row", "col"),
            P("row", "col"),
            P("col", "row"),
            P("row"),
            P("row"),
        ),
        check_vma=False,
    )
```

profile of v0, /device:TPU:0, one launch (start us, length us, event | category | flops | bytes accessed | tf_op | source)
XLA Modules:
  0.0 6477.2 jit_solution(8374444182642608279)
XLA Ops:
  9.5 11.5 all-reduce.12
  25.9 79.5 %all-gather.17.cloned.1.call-done = bf16[4,1024,512]{2,1,0:T(8,128)(2,1)} async-done(((bf16[1,1024,512]{2,1,0:T(8,128)(2,1)}), bf16[4,1024,512]{2,1,0:T(8,128)(2,1)}) %all-gather.17.cloned.1.call-update) | async-done | bytes 4194320 | tf_op jit(solution)/shard_map/all_gather | solution.py:21
  105.3 10.9 fusion.106
  116.3 70.5 %all-gather.25.cloned.1.call-done = bf16[4,1024,512]{2,1,0:T(8,128)(2,1)} async-done(((bf16[1,1024,512]{2,1,0:T(8,128)(2,1)}), bf16[4,1024,512]{2,1,0:T(8,128)(2,1)}) %all-gather.25.cloned.1.call-update) | async-done | bytes 4194320 | tf_op jit(solution)/shard_map/all_gather | solution.py:21
  186.7 10.8 fusion.105
  202.9 106.0 %reduce-scatter.43.cloned.1.call-done = f32[1,1024,768]{2,1,0:T(8,128)} async-done(((f32[4,1024,768]{2,1,0:T(8,128)}), f32[1,1024,768]{2,1,0:T(8,128)}) %reduce-scatter.43.cloned.1.call-update) | async-done | bytes 3145744
  317.1 14.2 fusion.110
  331.3 14.0 exponential_reduce_fusion.1
  345.3 14.5 fusion.52
  363.0 69.6 %reduce-scatter.45.cloned.1.call-done = f32[1,1024,768]{2,1,0:T(8,128)} async-done(((f32[4,1024,768]{2,1,0:T(8,128)}), f32[1,1024,768]{2,1,0:T(8,128)}) %reduce-scatter.45.cloned.1.call-update) | async-done | bytes 3145744
  440.7 13.6 fusion.111
  454.4 13.7 exponential_reduce_fusion
  468.1 14.4 fusion.55
  495.3 47.0 all-gather.27.cloned.1.call-done
  554.2 135.0 %reduce-scatter.27.cloned.1.call-done = f32[1,1024,512]{2,1,0:T(8,128)} async-done(((f32[4,1024,512]{2,1,0:T(8,128)}), f32[1,1024,512]{2,1,0:T(8,128)}) %reduce-scatter.27.cloned.1.call-update) | async-done | bytes 2097168 | tf_op jit(solution)/shard_map/reduce_scatter | solution.py:33
  689.3 147.6 %reduce-scatter.31.cloned.1.call-done = f32[1,1024,512]{2,1,0:T(8,128)} async-done(((f32[4,1024,512]{2,1,0:T(8,128)}), f32[1,1024,512]{2,1,0:T(8,128)}) %reduce-scatter.31.cloned.1.call-update) | async-done | bytes 2097168 | tf_op jit(solution)/shard_map/reduce_scatter | solution.py:33
  855.1 65.4 %all-gather.33.cloned.1.call-done = bf16[4,1024,512]{2,1,0:T(8,128)(2,1)} async-done(((bf16[1,1024,512]{2,1,0:T(8,128)(2,1)}), bf16[4,1024,512]{2,1,0:T(8,128)(2,1)}) %all-gather.33.cloned.1.call-update) | async-done | bytes 4194320 | tf_op jit(solution)/shard_map/all_gather | solution.py:21
  920.4 18.2 fusion.46
  938.8 62.9 all-gather.21.cloned.1.call-done
  1001.7 31.9 fusion.102
  1034.9 257.0 %reduce-scatter.47.cloned.1.call-done = f32[1,1024,2048]{2,1,0:T(8,128)} async-done(((f32[4,1024,2048]{2,1,0:T(8,128)}), f32[1,1024,2048]{2,1,0:T(8,128)}) %reduce-scatter.47.cloned.1.call-update) | async-done | bytes 8388624
  1291.8 1120.2 %all-reduce.18.cloned.1.call-done = f32[4,1024,4096]{2,1,0:T(8,128)} async-done(((f32[4,1024,4096]{2,1,0:T(8,128)}), f32[4,1024,4096]{2,1,0:T(8,128)}) %all-reduce.18.cloned.1.call-update) | async-done | bytes 67108880
  2412.0 14.4 multiply_convert_fusion.3
  2434.4 298.6 %all-gather.35.cloned.1.call-done = bf16[4,1024,4096]{2,1,0:T(8,128)(2,1)} async-done(((bf16[1,1024,4096]{2,1,0:T(8,128)(2,1)}), bf16[4,1024,4096]{2,1,0:T(8,128)(2,1)}) %all-gather.35.cloned.1.call-update) | async-done | bytes 33554448 | tf_op jit(solution)/shard_map/all_gather | solution.py:25
  2733.0 25.2 fusion.100
  2758.9 144.1 %reduce-scatter.35.cloned.1.call-done = f32[1,1024,512]{2,1,0:T(8,128)} async-done(((f32[4,1024,512]{2,1,0:T(8,128)}), f32[1,1024,512]{2,1,0:T(8,128)}) %reduce-scatter.35.cloned.1.call-update) | async-done | bytes 2097168 | tf_op jit(solution)/shard_map/reduce_scatter | solution.py:33
  2908.4 78.0 %all-gather.41.cloned.1.call-done = bf16[4,1024,512]{2,1,0:T(8,128)(2,1)} async-done(((bf16[1,1024,512]{2,1,0:T(8,128)(2,1)}), bf16[4,1024,512]{2,1,0:T(8,128)(2,1)}) %all-gather.41.cloned.1.call-update) | async-done | bytes 4194320 | tf_op jit(solution)/shard_map/all_gather | solution.py:21
  2986.4 18.2 fusion.44
  3004.7 62.9 all-gather.29.cloned.1.call-done
  3067.6 31.9 fusion.101
  3100.0 257.6 %reduce-scatter.51.cloned.1.call-done = f32[1,1024,2048]{2,1,0:T(8,128)} async-done(((f32[4,1024,2048]{2,1,0:T(8,128)}), f32[1,1024,2048]{2,1,0:T(8,128)}) %reduce-scatter.51.cloned.1.call-update) | async-done | bytes 8388624
  3357.6 1120.2 %all-reduce.20.cloned.1.call-done = f32[4,1024,4096]{2,1,0:T(8,128)} async-done(((f32[4,1024,4096]{2,1,0:T(8,128)}), f32[4,1024,4096]{2,1,0:T(8,128)}) %all-reduce.20.cloned.1.call-update) | async-done | bytes 67108880
  4477.8 14.4 multiply_convert_fusion.1
  4500.8 298.0 %all-gather.43.cloned.1.call-done = bf16[4,1024,4096]{2,1,0:T(8,128)(2,1)} async-done(((bf16[1,1024,4096]{2,1,0:T(8,128)(2,1)}), bf16[4,1024,4096]{2,1,0:T(8,128)(2,1)}) %all-gather.43.cloned.1.call-update) | async-done | bytes 33554448 | tf_op jit(solution)/shard_map/all_gather | solution.py:25
  4798.7 26.0 fusion.99
  4824.9 133.4 %all-gather.31.cloned.1.call-done = bf16[4,1024,2048]{2,1,0:T(8,128)(2,1)} async-done(((bf16[1,1024,2048]{2,1,0:T(8,128)(2,1)}), bf16[4,1024,2048]{2,1,0:T(8,128)(2,1)}) %all-gather.31.cloned.1.call-update) | async-done | bytes 16777232 | tf_op jit(solution)/shard_map/all_gather | solution.py:25
  4958.3 14.5 fusion.48
  4972.9 132.5 %reduce-scatter.39.cloned.1.call-done = f32[1,1024,512]{2,1,0:T(8,128)} async-done(((f32[4,1024,512]{2,1,0:T(8,128)}), f32[1,1024,512]{2,1,0:T(8,128)}) %reduce-scatter.39.cloned.1.call-update) | async-done | bytes 2097168 | tf_op jit(solution)/shard_map/reduce_scatter | solution.py:33
  5108.7 10.0 all-reduce.10
  5118.8 134.2 %reduce-scatter.33.cloned.1.call-done = f32[1,1024,512]{2,1,0:T(8,128)} async-done(((f32[4,1024,512]{2,1,0:T(8,128)}), f32[1,1024,512]{2,1,0:T(8,128)}) %reduce-scatter.33.cloned.1.call-update) | async-done | bytes 2097168 | tf_op jit(solution)/shard_map/reduce_scatter | solution.py:33
  5261.2 80.1 %all-gather.37.cloned.1.call-done = bf16[4,1024,512]{2,1,0:T(8,128)(2,1)} async-done(((bf16[1,1024,512]{2,1,0:T(8,128)(2,1)}), bf16[4,1024,512]{2,1,0:T(8,128)(2,1)}) %all-gather.37.cloned.1.call-update) | async-done | bytes 4194320 | tf_op jit(solution)/shard_map/all_gather | solution.py:21
  5349.2 73.4 %all-gather.45.cloned.1.call-done = bf16[4,1024,512]{2,1,0:T(8,128)(2,1)} async-done(((bf16[1,1024,512]{2,1,0:T(8,128)(2,1)}), bf16[4,1024,512]{2,1,0:T(8,128)(2,1)}) %all-gather.45.cloned.1.call-update) | async-done | bytes 4194320 | tf_op jit(solution)/shard_map/all_gather | solution.py:21
  5431.0 149.8 %all-gather.23.cloned.1.call-done = bf16[4,1024,2048]{2,1,0:T(8,128)(2,1)} async-done(((bf16[1,1024,2048]{2,1,0:T(8,128)(2,1)}), bf16[4,1024,2048]{2,1,0:T(8,128)(2,1)}) %all-gather.23.cloned.1.call-update) | async-done | bytes 16777232 | tf_op jit(solution)/shard_map/all_gather | solution.py:25
  5580.8 14.9 fusion.114
  5595.7 74.3 %reduce-scatter.49.cloned.1.call-done = f32[1,1024,512]{2,1,0:T(8,128)} async-done(((f32[4,1024,512]{2,1,0:T(8,128)}), f32[1,1024,512]{2,1,0:T(8,128)}) %reduce-scatter.49.cloned.1.call-update) | async-done | bytes 2097168
  5671.8 21.9 fusion.3
  5693.8 30.4 fusion.5
  5724.2 12.3 fusion.62
  5749.2 13.7 fusion.72
  5770.2 22.4 fusion
  5792.6 28.9 fusion.2
  5821.5 12.1 fusion.61
  5845.8 13.3 fusion.69
  5864.4 24.7 fusion.113
  5889.1 13.8 bitcast_add_fusion.1
  5902.9 28.3 bitcast_add_fusion
  5968.0 10.9 fusion.104
  5978.9 15.2 fusion.50
  5994.8 18.7 all-reduce.22.cloned.1.call-done
  6025.6 136.0 %reduce-scatter.41.cloned.1.call-done = f32[1,1024,512]{2,1,0:T(8,128)} async-done(((f32[4,1024,512]{2,1,0:T(8,128)}), f32[1,1024,512]{2,1,0:T(8,128)}) %reduce-scatter.41.cloned.1.call-update) | async-done | bytes 2097168 | tf_op jit(solution)/shard_map/reduce_scatter | solution.py:33
  6161.7 147.6 %reduce-scatter.37.cloned.1.call-done = f32[1,1024,512]{2,1,0:T(8,128)} async-done(((f32[4,1024,512]{2,1,0:T(8,128)}), f32[1,1024,512]{2,1,0:T(8,128)}) %reduce-scatter.37.cloned.1.call-update) | async-done | bytes 2097168 | tf_op jit(solution)/shard_map/reduce_scatter | solution.py:33
  6312.8 10.0 all-reduce.9
  6322.8 18.2 all-reduce.8
  6346.1 111.3 %reduce-scatter.29.cloned.1.call-done = f32[1,1024,512]{2,1,0:T(8,128)} async-done(((f32[4,1024,512]{2,1,0:T(8,128)}), f32[1,1024,512]{2,1,0:T(8,128)}) %reduce-scatter.29.cloned.1.call-update) | async-done | bytes 2097168 | tf_op jit(solution)/shard_map/reduce_scatter | solution.py:33
  (287 shorter events, 236.9 us)
Async XLA Ops:
  7.2 913.3 %copy-start = (bf16[2048,512]{1,0:T(8,128)(2,1)S(1)}, bf16[2048,512]{1,0:T(8,128)(2,1)}, u32[]{:S(2)}) copy-start(bf16[2048,512]{1,0:T(8,128)(2,1)} %param.20) | copy-start | bytes 6291460
  7.2 98.1 %copy-start.58 = (bf16[512,128]{1,0:T(8,128)(2,1)S(1)}, bf16[512,128]{1,0:T(8,128)(2,1)}, u32[]{:S(2)}) copy-start(bf16[512,128]{1,0:T(8,128)(2,1)} %param.16) | copy-start | bytes 393220
  7.2 98.1 %copy-start.60 = (bf16[512,128]{1,0:T(8,128)(2,1)S(1)}, bf16[512,128]{1,0:T(8,128)(2,1)}, u32[]{:S(2)}) copy-start(bf16[512,128]{1,0:T(8,128)(2,1)} %param.15) | copy-start | bytes 393220
  7.2 98.1 %copy-start.56 = (bf16[512,512]{1,0:T(8,128)(2,1)S(1)}, bf16[512,512]{1,0:T(8,128)(2,1)}, u32[]{:S(2)}) copy-start(bf16[512,512]{1,0:T(8,128)(2,1)} %param.14) | copy-start | bytes 1572868
  7.2 98.1 %all-gather.17.cloned.1.call-start = ((), (), s32[]{:S(2)}) async-start(), calls=%async_computation.14 | async-start | bytes 5242880 | tf_op jit(solution)/shard_map/all_gather | solution.py:21
  25.1 161.7 %all-gather.25.cloned.1.call-start = ((), (), s32[]{:S(2)}) async-start(), calls=%async_computation.20 | async-start | bytes 5242880 | tf_op jit(solution)/shard_map/all_gather | solution.py:21
  25.8 283.1 %reduce-scatter.43.cloned.1.call-start = ((), (), s32[]{:S(2)}) async-start(), calls=%async_computation.40 | async-start | bytes 15728640
  116.2 316.3 %reduce-scatter.45.cloned.1.call-start = ((), (), s32[]{:S(2)}) async-start(), calls=%async_computation.41 | async-start | bytes 15728640
  197.6 289.8 %all-gather.19.cloned.1.call-start = ((), (), s32[]{:S(2)}) async-start(), calls=%async_computation.15 | async-start | bytes 5242880 | tf_op jit(solution)/shard_map/all_gather | solution.py:25
  201.4 115.3 %copy-start.10 = (f32[1024,32]{0,1:T(8,128)}, f32[1024,32]{0,1:T(8,128)S(1)}, u32[]{:S(2)}) copy-start(f32[1024,32]{0,1:T(8,128)S(1)} %get-tuple-element.180) | copy-start | bytes 393220
  201.4 239.0 %copy-start.8 = (f32[1024,32]{0,1:T(8,128)}, f32[1024,32]{0,1:T(8,128)S(1)}, u32[]{:S(2)}) copy-start(f32[1024,32]{0,1:T(8,128)S(1)} %get-tuple-element.186) | copy-start | bytes 393220
  313.6 31.8 copy-start.14
  361.2 181.1 %all-gather.27.cloned.1.call-start = ((), (), s32[]{:S(2)}) async-start(), calls=%async_computation.21 | async-start | bytes 5242880 | tf_op jit(solution)/shard_map/all_gather | solution.py:25
  437.2 30.9 copy-start.12
  468.1 19.3 copy-start.3
  484.8 204.5 %reduce-scatter.27.cloned.1.call-start = ((), (), s32[]{:S(2)}) async-start(), calls=%async_computation.16 | async-start | bytes 10485760 | tf_op jit(solution)/shard_map/reduce_scatter | solution.py:33
  495.3 341.6 %reduce-scatter.31.cloned.1.call-start = ((), (), s32[]{:S(2)}) async-start(), calls=%async_computation.22 | async-start | bytes 10485760 | tf_op jit(solution)/shard_map/reduce_scatter | solution.py:33
  550.1 370.3 %all-gather.33.cloned.1.call-start = ((), (), s32[]{:S(2)}) async-start(), calls=%async_computation.26 | async-start | bytes 5242880 | tf_op jit(solution)/shard_map/all_gather | solution.py:21
  554.2 298.0 %copy-start.39 = (f32[512]{0:T(512)S(1)}, f32[512]{0:T(512)}, u32[]{:S(2)}) copy-start(f32[512]{0:T(512)} %param.22) | copy-start | bytes 6148
  554.2 447.5 %all-gather.21.cloned.1.call-start = ((), (), s32[]{:S(2)}) async-start(), calls=%async_computation.17 | async-start | bytes 5242880 | tf_op jit(solution)/shard_map/all_gather | solution.py:21
  852.2 2050.8 %copy-start.33 = (f32[1,1024]{1,0:T(1,128)}, f32[1,1024]{1,0:T(1,128)S(1)}, u32[]{:S(2)}) copy-start(f32[1,1024]{1,0:T(1,128)S(1)} %add_rsqrt_fusion.2) | copy-start | bytes 12292
  855.0 436.8 %reduce-scatter.47.cloned.1.call-start = ((), (), s32[]{:S(2)}) async-start(), calls=%async_computation.42 | async-start | bytes 41943040
  938.7 1473.3 %all-reduce.18.cloned.1.call-start = ((), (), s32[]{:S(2)}) async-start(), calls=%async_computation.38 | async-start | bytes 134217728
  1033.6 1699.3 %all-gather.35.cloned.1.call-start = ((), (), s32[]{:S(2)}) async-start(), calls=%async_computation.27 | async-start | bytes 41943040 | tf_op jit(solution)/shard_map/all_gather | solution.py:25
  2434.4 468.6 %reduce-scatter.35.cloned.1.call-start = ((), (), s32[]{:S(2)}) async-start(), calls=%async_computation.28 | async-start | bytes 10485760 | tf_op jit(solution)/shard_map/reduce_scatter | solution.py:33
  2758.2 228.1 %all-gather.41.cloned.1.call-start = ((), (), s32[]{:S(2)}) async-start(), calls=%async_computation.32 | async-start | bytes 5242880 | tf_op jit(solution)/shard_map/all_gather | solution.py:21
  2758.8 308.8 %all-gather.29.cloned.1.call-start = ((), (), s32[]{:S(2)}) async-start(), calls=%async_computation.23 | async-start | bytes 5242880 | tf_op jit(solution)/shard_map/all_gather | solution.py:21
  2758.9 149.2 %copy-start.36 = (f32[1,1024]{1,0:T(1,128)}, f32[1,1024]{1,0:T(1,128)S(1)}, u32[]{:S(2)}) copy-start(f32[1,1024]{1,0:T(1,128)S(1)} %add_rsqrt_fusion) | copy-start | bytes 12292
  2908.1 449.5 %reduce-scatter.51.cloned.1.call-start = ((), (), s32[]{:S(2)}) async-start(), calls=%async_computation.44 | async-start | bytes 41943040
  3004.6 1473.2 %all-reduce.20.cloned.1.call-start = ((), (), s32[]{:S(2)}) async-start(), calls=%async_computation.39 | async-start | bytes 134217728
  3099.6 1699.2 %all-gather.43.cloned.1.call-start = ((), (), s32[]{:S(2)}) async-start(), calls=%async_computation.33 | async-start | bytes 41943040 | tf_op jit(solution)/shard_map/all_gather | solution.py:25
  4500.1 458.2 %all-gather.31.cloned.1.call-start = ((), (), s32[]{:S(2)}) async-start(), calls=%async_computation.24 | async-start | bytes 20971520 | tf_op jit(solution)/shard_map/all_gather | solution.py:25
  4500.7 604.6 %reduce-scatter.39.cloned.1.call-start = ((), (), s32[]{:S(2)}) async-start(), calls=%async_computation.34 | async-start | bytes 10485760 | tf_op jit(solution)/shard_map/reduce_scatter | solution.py:33
  4824.7 428.2 %reduce-scatter.33.cloned.1.call-start = ((), (), s32[]{:S(2)}) async-start(), calls=%async_computation.25 | async-start | bytes 10485760 | tf_op jit(solution)/shard_map/reduce_scatter | solution.py:33
  4972.8 132.6 %copy-start.37 = (f32[1,1024]{1,0:T(1,128)S(1)}, f32[1,1024]{1,0:T(1,128)}, u32[]{:S(2)}) copy-start(f32[1,1024]{1,0:T(1,128)} %copy-done.36) | copy-start | bytes 12292
  4972.8 132.6 %copy-start.40 = (f32[512]{0:T(512)S(1)}, f32[512]{0:T(512)}, u32[]{:S(2)}) copy-start(f32[512]{0:T(512)} %param.22) | copy-start | bytes 6148
  4972.8 135.9 %copy-start.52 = (f32[1024]{0:T(1024)S(1)}, f32[1024]{0:T(1024)}, u32[]{:S(2)}) copy-start(f32[1024]{0:T(1024)} %get-tuple-element.86) | copy-start | bytes 12292
  4972.8 280.1 %copy-start.34 = (f32[1,1024]{1,0:T(1,128)S(1)}, f32[1,1024]{1,0:T(1,128)}, u32[]{:S(2)}) copy-start(f32[1,1024]{1,0:T(1,128)} %copy-done.33) | copy-start | bytes 12292
  4972.8 368.5 %all-gather.37.cloned.1.call-start = ((), (), s32[]{:S(2)}) async-start(), calls=%async_computation.29 | async-start | bytes 5242880 | tf_op jit(solution)/shard_map/all_gather | solution.py:21
  5118.7 134.2 %copy-start.49 = (f32[1,1024]{1,0:T(1,128)}, f32[1,1024]{1,0:T(1,128)S(1)}, u32[]{:S(2)}) copy-start(f32[1,1024]{1,0:T(1,128)S(1)} %broadcast_multiply_fusion.1) | copy-start | bytes 12292
  5118.8 134.2 %copy-start.47 = (f32[1,1024]{1,0:T(1,128)}, f32[1,1024]{1,0:T(1,128)S(1)}, u32[]{:S(2)}) copy-start(f32[1,1024]{1,0:T(1,128)S(1)} %broadcast_multiply_fusion.3) | copy-start | bytes 12292
  5259.8 81.5 %copy-start.4 = (bf16[512,512]{1,0:T(8,128)(2,1)S(1)}, bf16[512,512]{1,0:T(8,128)(2,1)}, u32[]{:S(2)}) copy-start(bf16[512,512]{1,0:T(8,128)(2,1)} %param.17) | copy-start | bytes 1572868
  5259.8 162.8 %all-gather.45.cloned.1.call-start = ((), (), s32[]{:S(2)}) async-start(), calls=%async_computation.35 | async-start | bytes 5242880 | tf_op jit(solution)/shard_map/all_gather | solution.py:21
  5260.4 320.4 %all-gather.23.cloned.1.call-start = ((), (), s32[]{:S(2)}) async-start(), calls=%async_computation.18 | async-start | bytes 20971520 | tf_op jit(solution)/shard_map/all_gather | solution.py:25
  5261.1 408.9 %reduce-scatter.49.cloned.1.call-start = ((), (), s32[]{:S(2)}) async-start(), calls=%async_computation.43 | async-start | bytes 10485760
  5349.1 419.1 %reduce-scatter.53.cloned.1.call-start = ((), (), s32[]{:S(2)}) async-start(), calls=%async_computation.45 | async-start | bytes 10485760
  5430.7 241.1 %copy-start.15 = (bf16[1024,128]{0,1:T(8,128)(2,1)S(1)}, bf16[1024,128]{0,1:T(8,128)(2,1)}, u32[]{:S(2)}) copy-start(bf16[1024,128]{0,1:T(8,128)(2,1)} %copy-done.14) | copy-start | bytes 786436
  5430.7 241.1 %copy-start.19 = (f32[1,8,1024]{2,1,0:T(8,128)S(1)}, f32[1,8,1024]{2,1,0:T(8,128)}, u32[]{:S(2)}) copy-start(f32[1,8,1024]{2,1,0:T(8,128)} %copy-done.18) | copy-start | bytes 98308
  5430.7 509.8 %all-gather.39.cloned.1.call-start = ((), (), s32[]{:S(2)}) async-start(), calls=%async_computation.30 | async-start | bytes 7864320 | tf_op jit(solution)/shard_map/all_gather | solution.py:25
  5768.1 181.1 %all-gather.47.cloned.1.call-start = ((), (), s32[]{:S(2)}) async-start(), calls=%async_computation.36 | async-start | bytes 7864320 | tf_op jit(solution)/shard_map/all_gather | solution.py:25
  5864.3 149.2 %all-reduce.22.cloned.1.call-start = ((), (), s32[]{:S(2)}) async-start(), calls=%async_computation.46 | async-start | bytes 30408704 | tf_op jit(solution)/shard_map/psum | solution.py:266
  5864.4 24.7 copy-start.55
  5864.4 24.7 copy-start.63
  5958.3 203.4 %reduce-scatter.41.cloned.1.call-start = ((), (), s32[]{:S(2)}) async-start(), calls=%async_computation.37 | async-start | bytes 10485760 | tf_op jit(solution)/shard_map/reduce_scatter | solution.py:33
  5967.9 341.3 %reduce-scatter.37.cloned.1.call-start = ((), (), s32[]{:S(2)}) async-start(), calls=%async_computation.31 | async-start | bytes 10485760 | tf_op jit(solution)/shard_map/reduce_scatter | solution.py:33
  5978.9 478.5 %reduce-scatter.29.cloned.1.call-start = ((), (), s32[]{:S(2)}) async-start(), calls=%async_computation.19 | async-start | bytes 10485760 | tf_op jit(solution)/shard_map/reduce_scatter | solution.py:33
  6017.6 291.7 %copy-start.44 = (f32[1,1024]{1,0:T(1,128)S(1)}, f32[1,1024]{1,0:T(1,128)}, u32[]{:S(2)}) copy-start(f32[1,1024]{1,0:T(1,128)} %copy-done.43) | copy-start | bytes 12292
  6017.6 291.7 %copy-start.46 = (f32[1,1024]{1,0:T(1,128)S(1)}, f32[1,1024]{1,0:T(1,128)}, u32[]{:S(2)}) copy-start(f32[1,1024]{1,0:T(1,128)} %copy-done.45) | copy-start | bytes 12292
  6017.6 291.7 %copy-start.51 = (f32[512]{0:T(512)S(1)}, f32[512]{0:T(512)}, u32[]{:S(2)}) copy-start(f32[512]{0:T(512)} %param.21) | copy-start | bytes 6148
  6025.6 315.4 %copy-start.38 = (f32[1,1024]{1,0:T(1,128)S(1)}, f32[1,1024]{1,0:T(1,128)}, u32[]{:S(2)}) copy-start(f32[1,1024]{1,0:T(1,128)} %copy-done.36) | copy-start | bytes 12292
  6025.6 315.4 %copy-start.41 = (f32[512]{0:T(512)S(1)}, f32[512]{0:T(512)}, u32[]{:S(2)}) copy-start(f32[512]{0:T(512)} %param.22) | copy-start | bytes 6148
  6025.6 315.5 %copy-start.50 = (f32[1,1024]{1,0:T(1,128)S(1)}, f32[1,1024]{1,0:T(1,128)}, u32[]{:S(2)}) copy-start(f32[1,1024]{1,0:T(1,128)} %copy-done.49) | copy-start | bytes 12292
  6341.1 116.3 %copy-start.35 = (f32[1,1024]{1,0:T(1,128)S(1)}, f32[1,1024]{1,0:T(1,128)}, u32[]{:S(2)}) copy-start(f32[1,1024]{1,0:T(1,128)} %copy-done.33) | copy-start | bytes 12292
  6341.1 116.3 %copy-start.48 = (f32[1,1024]{1,0:T(1,128)S(1)}, f32[1,1024]{1,0:T(1,128)}, u32[]{:S(2)}) copy-start(f32[1,1024]{1,0:T(1,128)} %copy-done.47) | copy-start | bytes 12292
  (33 other events, 242.1 us)
Sparse Core Ops, SparseCore 0:
  25.2 80.0 all-gather.16
  107.5 79.2 all-gather.24
  189.8 119.0 reduce-scatter.42
  311.9 120.6 reduce-scatter.44
  434.8 52.5 all-gather.18
  489.7 52.5 all-gather.26
  544.6 144.6 reduce-scatter.26
  691.6 145.2 reduce-scatter.30
  839.1 81.3 all-gather.32
  922.4 79.2 all-gather.20
  1004.8 287.0 reduce-scatter.46
  1295.2 1116.8 all-reduce.17
  2434.5 298.4 all-gather.34
  2758.3 144.6 reduce-scatter.34
  2905.0 81.3 all-gather.40
  2988.4 79.2 all-gather.28
  3070.5 287.0 reduce-scatter.50
  3360.9 1116.8 all-reduce.19
  4500.2 298.4 all-gather.42
  4801.0 157.2 all-gather.30
  4960.7 144.6 reduce-scatter.38
  5107.7 145.2 reduce-scatter.32
  5259.9 81.3 all-gather.36
  5343.3 79.2 all-gather.44
  5424.9 155.7 all-gather.22
  5583.7 86.3 reduce-scatter.48
  5672.9 86.3 reduce-scatter.52
  5768.3 70.0 all-gather.38
  5864.4 69.7 all-gather.46
  5958.4 55.0 all-reduce.21
  6015.9 145.7 reduce-scatter.40
  6164.0 145.2 reduce-scatter.36
  6311.5 145.8 reduce-scatter.28
where the time goes:
time: 6480 us
  waiting for transfers between devices  5620 us (87%)
  matrix products  533 us (8%)
  other arithmetic  200 us (3%)
    unnamed x41, waiting for transfers between devices  3010 us
    reduce_scatter x8, waiting for transfers between devices, scatter_cols(): return lax.psum_scatter(operand, 'col', scatter_dimension=0, tiled=True)  1090 us
    all_gather x8, waiting for transfers between devices, gather_rows(): return lax.all_gather(operand, 'row', axis=0, tiled=True)  929 us
    all_gather x8, waiting for transfers between devices, spread_cols(): return lax.all_gather(operand, 'col', axis=0, tiled=True)  573 us
    dot_general x8, matrix products, project(): jnp.einsum('tgf,fm->tgm', left_operand_half, right_operand_half, preferre...  131 us
  transfers between devices with their start and end apart: 33, of which 30 were waited for; matrix products, arithmetic and copies ran while one was open for 10% of the time, Pallas kernels for 0%

commit v1 on v0

v1 whole, which is shorter than its diff:
```python
import math

import jax
import jax.numpy as jnp
from jax import lax
from jax.sharding import PartitionSpec as P

HD = 64

EPSILON = 1e-05
RESIDUAL_SCALE = 0.22
SCORE_SCALE = 0.015625
ROPE_BASE = 10000000.0
MASKED_SCORE = -1e30


def positions(segment_rows):
    seq_len = segment_rows.shape[-1]
    places = jnp.arange(seq_len, dtype=jnp.int32)
    starts = jnp.concatenate(
        [
            jnp.ones(segment_rows.shape[:-1] + (1,), jnp.bool_),
            segment_rows[..., 1:] != segment_rows[..., :-1],
        ],
        axis=-1,
    )
    first_place = lax.cummax(
        jnp.where(starts, places, jnp.zeros_like(places)), axis=segment_rows.ndim - 1
    )
    return places - first_place


def rotary(place_rows):
    half_dim = HD // 2
    frequency = jnp.exp(jnp.arange(half_dim, dtype=jnp.float32) * (-2.0 * math.log(ROPE_BASE) / HD))
    angles = place_rows.astype(jnp.float32)[..., None] * frequency
    return (jnp.cos(angles)[..., None, :], jnp.sin(angles)[..., None, :])


def rotate(head_rows, cosine, sine_part):
    half_dim = head_rows.shape[-1] // 2
    first_half = head_rows[..., :half_dim]
    second_half = head_rows[..., half_dim:]
    return jnp.concatenate(
        [
            first_half * cosine - second_half * sine_part,
            second_half * cosine + first_half * sine_part,
        ],
        axis=-1,
    )


def masked_scores(query_rot, key_rot, query_segment, key_segment, query_place):
    key_place = jnp.arange(key_segment.shape[0])
    allowed = (query_segment[:, None] == key_segment[None, :]) & (
        query_place[:, None] >= key_place[None, :]
    )
    raw_scores = (
        jnp.einsum("qkgd,pkd->kgqp", query_rot, key_rot, preferred_element_type=jnp.float32)
        * SCORE_SCALE
    )
    return jnp.where(allowed, raw_scores, MASKED_SCORE)


def attend_forward(pieces):
    query_rot, key_all, value_all, query_segment, key_segment, query_place = pieces
    chunk, heads_k, group_count, head_dim = query_rot.shape
    attention_scores = masked_scores(query_rot, key_all, query_segment, key_segment, query_place)
    row_peak = jnp.max(attention_scores, axis=-1, keepdims=True)
    log_total = row_peak + jnp.log(
        jnp.sum(jnp.exp(attention_scores - row_peak), axis=-1, keepdims=True)
    )
    attn_probs = jnp.exp(attention_scores - log_total).astype(jnp.bfloat16)
    mixed = jnp.einsum("kgqp,pkd->qkgd", attn_probs, value_all, preferred_element_type=jnp.float32)
    return mixed.reshape(chunk, -1).astype(jnp.bfloat16), log_total


def attend_backward(pieces):
    grad_mixed, query_rot, key_all, value_all, log_total, query_segment, key_segment, query_place = pieces
    chunk, heads_k, group_count, head_dim = query_rot.shape
    grad_grouped = grad_mixed.reshape(chunk, heads_k, group_count, head_dim)
    attn_probs = jnp.exp(
        masked_scores(query_rot, key_all, query_segment, key_segment, query_place) - log_total
    )
    grad_probs = jnp.einsum(
        "qkgd,pkd->kgqp", grad_grouped, value_all, preferred_element_type=jnp.float32
    )
    grad_value = jnp.einsum(
        "kgqp,qkgd->pkd",
        attn_probs.astype(jnp.bfloat16),
        grad_grouped,
        preferred_element_type=jnp.float32,
    )
    grad_scores = (
        attn_probs * (grad_probs - jnp.sum(attn_probs * grad_probs, axis=-1, keepdims=True))
    ).astype(jnp.bfloat16)
    grad_query = (
        jnp.einsum("kgqp,pkd->qkgd", grad_scores, key_all, preferred_element_type=jnp.float32)
        * SCORE_SCALE
    )
    grad_key = (
        jnp.einsum("kgqp,qkgd->pkd", grad_scores, query_rot, preferred_element_type=jnp.float32)
        * SCORE_SCALE
    )
    return grad_query, jnp.concatenate([grad_key, grad_value], axis=-1)


def make_shards(n_dp, n_row, n_col):
    def gather_features(block, axis):
        half = block.shape[axis] // n_dp
        mine = lax.dynamic_slice_in_dim(block, lax.axis_index("dp") * half, half, axis=axis)
        gathered = lax.all_gather(mine, "row", axis=axis)
        gathered = lax.all_gather(gathered, "dp", axis=axis)
        gathered = jnp.swapaxes(gathered, axis, axis + 1)
        shape = list(block.shape)
        shape[axis] = block.shape[axis] * n_row
        return gathered.reshape(shape)

    def reduce_features(partial, axis):
        half = partial.shape[axis] // (n_row * n_dp)
        shape = list(partial.shape)
        shape[axis : axis + 1] = [n_row, n_dp, half]
        split = jnp.swapaxes(partial.reshape(shape), axis, axis + 1)
        split = lax.psum_scatter(split, "dp", scatter_dimension=axis)
        split = lax.psum_scatter(split, "row", scatter_dimension=axis)
        return lax.all_gather(split, "dp", axis=axis, tiled=True)

    def to_tokens(rows):
        batches, local, seq_len, width = rows.shape
        rows = rows.reshape(batches, local, n_row, seq_len // n_row, width)
        rows = lax.all_to_all(rows, "row", 2, 3)
        return rows.reshape(batches, local, seq_len // n_row, n_row * width)

    def to_features(rows):
        batches, local, chunk, width = rows.shape
        rows = rows.reshape(batches, local, chunk, n_row, width // n_row)
        rows = lax.all_to_all(rows, "row", 3, 2)
        return rows.reshape(batches, local, n_row * chunk, width // n_row)

    def shards(
        hidden_in,
        segment_ids,
        w_query,
        w_key,
        w_value,
        w_out,
        w_gate,
        w_up,
        w_down,
        gain_attn,
        gain_ffn,
        cotangent,
    ):
        batches, local, seq_len, width_r = hidden_in.shape
        chunk = seq_len // n_row
        row_index = lax.axis_index("row")
        query_cols = w_query.shape[1]
        key_cols = w_key.shape[1]
        heads_q = query_cols // HD
        heads_k = key_cols // HD
        group_count = heads_q // heads_k
        ffn_cols = w_gate.shape[1]

        w_qkv = gather_features(jnp.concatenate([w_query, w_key, w_value], axis=1), 0)
        w_pair = gather_features(jnp.concatenate([w_gate, w_up], axis=1), 0)
        w_out_all = gather_features(w_out, 1)
        w_down_all = gather_features(w_down, 1)
        gain_attn_all = lax.all_gather(gain_attn, "row", tiled=True)
        gain_ffn_all = lax.all_gather(gain_ffn, "row", tiled=True)

        segments = lax.all_gather(segment_ids, "row", axis=1, tiled=True)
        places = positions(segments)
        query_segments = lax.dynamic_slice_in_dim(segments, row_index * chunk, chunk, axis=2)
        query_places_seq = lax.dynamic_slice_in_dim(places, row_index * chunk, chunk, axis=2)
        query_index = row_index * chunk + jnp.arange(chunk)
        seq_all = segments.shape[1]

        hidden_t = to_tokens(hidden_in)
        cotangent_t = to_tokens(cotangent)

        grad_qkv_w = None
        grad_out_w = None
        grad_pair_w = None
        grad_down_w = None
        gain_attn_total = jnp.zeros(gain_attn_all.shape, jnp.float32)
        gain_ffn_total = jnp.zeros(gain_ffn_all.shape, jnp.float32)
        outs_list = []
        inputs_grad = []
        for batch_index in range(batches):
            rows_f = hidden_t[batch_index].astype(jnp.float32)
            inv_attn = lax.rsqrt(jnp.mean(rows_f * rows_f, axis=-1, keepdims=True) + EPSILON)
            norm_attn = rows_f * inv_attn
            normed_attn = (norm_attn * gain_attn_all).astype(jnp.bfloat16)
            spread_attn = lax.all_gather(normed_attn, "col", axis=0, tiled=True)
            qkv = jnp.einsum(
                "std,dm->stm", spread_attn, w_qkv, preferred_element_type=jnp.float32
            )
            cosine, sine_part = rotary(query_places_seq[batch_index])
            query_rot = rotate(
                qkv[..., :query_cols].reshape(seq_all, chunk, heads_q, HD), cosine, sine_part
            ).astype(jnp.bfloat16)
            key_rot = rotate(
                qkv[..., query_cols : query_cols + key_cols].reshape(seq_all, chunk, heads_k, HD),
                cosine,
                sine_part,
            ).astype(jnp.bfloat16)
            value_low = (
                qkv[..., query_cols + key_cols :]
                .reshape(seq_all, chunk, heads_k, HD)
                .astype(jnp.bfloat16)
            )
            key_value = lax.all_gather(
                jnp.concatenate([key_rot, value_low], axis=-1), "row", axis=1, tiled=True
            )
            key_all = key_value[..., :HD]
            value_all = key_value[..., HD:]
            query_grouped = query_rot.reshape(seq_all, chunk, heads_k, group_count, HD)
            query_place = jnp.broadcast_to(query_index, (seq_all, chunk))
            mixed, log_total = lax.map(
                attend_forward,
                (
                    query_grouped,
                    key_all,
                    value_all,
                    query_segments[batch_index],
                    segments[batch_index],
                    query_place,
                ),
            )
            attn_part = jnp.einsum(
                "stm,md->std", mixed, w_out_all, preferred_element_type=jnp.float32
            )
            attn_branch = lax.psum_scatter(attn_part, "col", scatter_dimension=0, tiled=True)
            resid_mid = rows_f + RESIDUAL_SCALE * attn_branch
            inv_ffn = lax.rsqrt(jnp.mean(resid_mid * resid_mid, axis=-1, keepdims=True) + EPSILON)
            norm_ffn = resid_mid * inv_ffn
            normed_ffn = (norm_ffn * gain_ffn_all).astype(jnp.bfloat16)
            spread_ffn = lax.all_gather(normed_ffn, "col", axis=0, tiled=True)
            pair = jnp.einsum(
                "std,df->stf", spread_ffn, w_pair, preferred_element_type=jnp.float32
            )
            gate_rows = pair[..., :ffn_cols]
            up_rows = pair[..., ffn_cols:]
            sigmoid_gate = jax.nn.sigmoid(gate_rows)
            act_low = (gate_rows * sigmoid_gate * up_rows).astype(jnp.bfloat16)
            ffn_part = jnp.einsum(
                "stf,fd->std", act_low, w_down_all, preferred_element_type=jnp.float32
            )
            ffn_branch = lax.psum_scatter(ffn_part, "col", scatter_dimension=0, tiled=True)
            outs_list.append((resid_mid + RESIDUAL_SCALE * ffn_branch).astype(jnp.bfloat16))

            grad_rows = cotangent_t[batch_index].astype(jnp.float32)
            grad_ffn = (RESIDUAL_SCALE * grad_rows).astype(jnp.bfloat16)
            spread_grad_ffn = lax.all_gather(grad_ffn, "col", axis=0, tiled=True)
            fresh_down = jnp.einsum(
                "stf,std->fd", act_low, spread_grad_ffn, preferred_element_type=jnp.float32
            )
            grad_act = jnp.einsum(
                "std,fd->stf", spread_grad_ffn, w_down_all, preferred_element_type=jnp.float32
            )
            grad_gate_rows = (
                grad_act * up_rows * sigmoid_gate * (1.0 + gate_rows * (1.0 - sigmoid_gate))
            )
            grad_up_rows = grad_act * gate_rows * sigmoid_gate
            paired_gradient = jnp.concatenate([grad_gate_rows, grad_up_rows], axis=-1).astype(
                jnp.bfloat16
            )
            fresh_pair = jnp.einsum(
                "std,stf->df", spread_ffn, paired_gradient, preferred_element_type=jnp.float32
            )
            grad_normed_part = jnp.einsum(
                "stf,df->std", paired_gradient, w_pair, preferred_element_type=jnp.float32
            )
            grad_normed_ffn = lax.psum_scatter(
                grad_normed_part, "col", scatter_dimension=0, tiled=True
            )
            scaled_ffn = grad_normed_ffn * gain_ffn_all
            gain_ffn_total = gain_ffn_total + jnp.sum(grad_normed_ffn * norm_ffn, axis=(0, 1))
            inner_ffn = jnp.mean(scaled_ffn * norm_ffn, axis=-1, keepdims=True)
            grad_mid = grad_rows + inv_ffn * (scaled_ffn - norm_ffn * inner_ffn)
            grad_attn = (RESIDUAL_SCALE * grad_mid).astype(jnp.bfloat16)
            spread_grad_attn = lax.all_gather(grad_attn, "col", axis=0, tiled=True)
            fresh_out = jnp.einsum(
                "stm,std->md", mixed, spread_grad_attn, preferred_element_type=jnp.float32
            )
            grad_mixed = jnp.einsum(
                "std,md->stm", spread_grad_attn, w_out_all, preferred_element_type=jnp.float32
            ).astype(jnp.bfloat16)
            grad_query_rot, grad_kv_part = lax.map(
                attend_backward,
                (
                    grad_mixed,
                    query_grouped,
                    key_all,
                    value_all,
                    log_total,
                    query_segments[batch_index],
                    segments[batch_index],
                    query_place,
                ),
            )
            grad_kv = lax.psum_scatter(grad_kv_part, "row", scatter_dimension=1, tiled=True)
            grad_query = rotate(
                grad_query_rot.reshape(seq_all, chunk, heads_q, HD), cosine, -sine_part
            )
            grad_key = rotate(grad_kv[..., :HD], cosine, -sine_part)
            grad_qkv = jnp.concatenate(
                [
                    grad_query.reshape(seq_all, chunk, -1),
                    grad_key.reshape(seq_all, chunk, -1),
                    grad_kv[..., HD:].reshape(seq_all, chunk, -1),
                ],
                axis=-1,
            ).astype(jnp.bfloat16)
            fresh_qkv = jnp.einsum(
                "std,stm->dm", spread_attn, grad_qkv, preferred_element_type=jnp.float32
            )
            grad_normed_attn_part = jnp.einsum(
                "stm,dm->std", grad_qkv, w_qkv, preferred_element_type=jnp.float32
            )
            grad_normed_attn = lax.psum_scatter(
                grad_normed_attn_part, "col", scatter_dimension=0, tiled=True
            )
            scaled_attn = grad_normed_attn * gain_attn_all
            gain_attn_total = gain_attn_total + jnp.sum(grad_normed_attn * norm_attn, axis=(0, 1))
            inner_attn = jnp.mean(scaled_attn * norm_attn, axis=-1, keepdims=True)
            inputs_grad.append(grad_mid + inv_attn * (scaled_attn - norm_attn * inner_attn))
            if grad_qkv_w is None:
                grad_qkv_w, grad_out_w = fresh_qkv, fresh_out
                grad_pair_w, grad_down_w = fresh_pair, fresh_down
            else:
                grad_qkv_w = grad_qkv_w + fresh_qkv
                grad_out_w = grad_out_w + fresh_out
                grad_pair_w = grad_pair_w + fresh_pair
                grad_down_w = grad_down_w + fresh_down

        total_pair = reduce_features(grad_pair_w, 0)
        total_down = reduce_features(grad_down_w, 1)
        total_qkv = reduce_features(grad_qkv_w, 0)
        total_out = reduce_features(grad_out_w, 1)
        gain_totals = lax.psum(
            jnp.stack([gain_attn_total, gain_ffn_total]), ("dp", "row", "col")
        )
        gain_totals = lax.dynamic_slice_in_dim(gain_totals, row_index * width_r, width_r, axis=1)
        key_end = query_cols + key_cols
        return (
            to_features(jnp.stack(outs_list)),
            to_features(jnp.stack(inputs_grad)),
            total_qkv[:, :query_cols],
            total_qkv[:, query_cols:key_end],
            total_qkv[:, key_end:],
            total_out,
            total_pair[:, :ffn_cols],
            total_pair[:, ffn_cols:],
            total_down,
            gain_totals[0],
            gain_totals[1],
        )

    return shards


def solution(mesh):
    activation = P(None, ("dp", "col"), None, "row")
    return jax.shard_map(
        make_shards(mesh.shape["dp"], mesh.shape["row"], mesh.shape["col"]),
        mesh=mesh,
        in_specs=(
            activation,
            P(None, ("dp", "row"), None),
            P("row", "col"),
            P("row", "col"),
            P("row", "col"),
            P("col", "row"),
            P("row", "col"),
            P("row", "col"),
            P("col", "row"),
            P("row"),
            P("row"),
            activation,
        ),
        out_specs=(
            activation,
            activation,
            P("row", "col"),
            P("row", "col"),
            P("row", "col"),
            P("col", "row"),
            P("row", "col"),
            P("row", "col"),
            P("col", "row"),
            P("row"),
            P("row"),
        ),
        check_vma=False,
    )
```

time: 6480 us -> 3340 us (0.52)
  waiting for transfers between devices: 5620 us -> 2260 us
  local copies, waits for them, and re-layouts: 48 us -> 265 us
  blocking collectives: 59.7 us -> 155 us
  other arithmetic: 200 us -> 116 us
    unnamed x41 -> x44, waiting for transfers between devices: 3010 us -> 327 us
    all_gather x16 -> x22, waiting for transfers between devices: 1500 us -> 728 us  [the longest x2 163 us: shards(): spread_grad_attn = lax.all_gather(grad_attn, 'col', axis=0, tiled=True)]
    reduce_scatter x8 -> x14, waiting for transfers between devices: 1090 us -> 1200 us  [the longest x2 290 us: shards(): lax.psum_scatter(ffn_part, 'col', scatter_dimension=0, tiled=True)]
    reshape x0 -> x15, local copies, waits for them, and re-layouts: none -> 74.4 us  [the longest x5 55.1 us: reduce_features(): split = jnp.swapaxes(partial.reshape(shape), axis, axis + 1)]
    dot_general x30 -> x48, matrix products: 454 us -> 423 us  [the longest x2 59.6 us: shards(): jnp.einsum('std,stf->df', spread_ffn, paired_gradient, preferred_element_...]
  transfers between devices with their start and end apart: 33 -> 43, of which waited for: 30 -> 28; matrix products, arithmetic and copies ran while one was open for 10% -> 15% of each run, Pallas kernels for 0% -> 0%
where the time goes in v1:
time: 3340 us; the launch traced here: 3330 us
  waiting for transfers between devices  2260 us (68%)
  matrix products  500 us (15%)
  local copies, waits for them, and re-layouts  265 us (8%)
  blocking collectives  155 us (5%)
  other arithmetic  116 us (3%)
    unnamed x44, waiting for transfers between devices  327 us
    reduce_scatter x2, waiting for transfers between devices, shards(): lax.psum_scatter(ffn_part, 'col', scatter_dimension=0, tiled=True)  290 us
    reduce_scatter x2, waiting for transfers between devices, shards(): lax.psum_scatter(attn_part, 'col', scatter_dimension=0, tiled=True)  283 us
    reduce_scatter x2, waiting for transfers between devices, shards(): lax.psum_scatter(grad_normed_attn_part, 'col', scatter_dimension=0, tiled...  267 us
    reduce_scatter x2, waiting for transfers between devices, shards(): lax.psum_scatter(grad_normed_part, 'col', scatter_dimension=0, tiled=True)  257 us
    all_gather x2, waiting for transfers between devices, shards(): spread_grad_attn = lax.all_gather(grad_attn, 'col', axis=0, tiled=True)  163 us
    all_gather x2, waiting for transfers between devices, shards(): spread_attn = lax.all_gather(normed_attn, 'col', axis=0, tiled=True)  145 us
    all_gather x4, waiting for transfers between devices, gather_features(): gathered = lax.all_gather(mine, 'row', axis=axis)  131 us
  transfers between devices with their start and end apart: 43, of which 28 were waited for; matrix products, arithmetic and copies ran while one was open for 15% of the time, Pallas kernels for 0%

profile of v1, /device:TPU:0, one launch (start us, length us, event | category | flops | bytes accessed | tf_op | source)
XLA Modules:
  0.0 3326.0 jit_solution(8025774637371553679)
XLA Ops:
  11.1 32.9 all-gather.57.cloned.1.call-done
  51.6 32.6 all-gather.12
  100.2 7.6 all_gather.105
  119.1 63.8 %all-gather.37.cloned.1.call-done = bf16[4,256,2048]{2,1,0:T(8,128)(2,1)} async-done(((bf16[1,256,2048]{2,1,0:T(8,128)(2,1)}), bf16[4,256,2048]{2,1,0:T(8,128)(2,1)}) %all-gather.37.cloned.1.call-update) | async-done | bytes 4194320 | tf_op jit(solution)/shard_map/all_gather | solution.py:194
  212.3 20.2 all-gather.39.cloned.1.call-done
  236.3 28.7 while.48
  265.1 8.4 fusion.132
  273.5 14.0 all-gather.69.cloned.1.call-done
  293.8 83.7 %all-gather.65.cloned.1.call-done = bf16[1024,4096]{1,0:T(8,128)(2,1)} async-done(((bf16[256,4096]{1,0:T(8,128)(2,1)}), bf16[1024,4096]{1,0:T(8,128)(2,1)}) %all-gather.65.cloned.1.call-update) | async-done | bytes 8388624 | tf_op jit(solution)/shard_map/all_gather | solution.py:112
  378.1 8.5 all-gather.13
  386.6 137.8 %reduce-scatter.27.cloned.1.call-done = f32[1,256,2048]{2,1,0:T(8,128)} async-done(((f32[4,256,2048]{2,1,0:T(8,128)}), f32[1,256,2048]{2,1,0:T(8,128)}) %reduce-scatter.27.cloned.1.call-update) | async-done | bytes 2097168 | tf_op jit(solution)/shard_map/reduce_scatter | solution.py:233
  529.3 28.4 all_to_all.60
  566.8 16.7 copy.236
  583.5 14.7 reshape.769
  598.2 14.0 copy.233
  612.2 51.4 %all-gather.41.cloned.1.call-done = bf16[4,256,2048]{2,1,0:T(8,128)(2,1)} async-done(((bf16[1,256,2048]{2,1,0:T(8,128)(2,1)}), bf16[4,256,2048]{2,1,0:T(8,128)(2,1)}) %all-gather.41.cloned.1.call-update) | async-done | bytes 4194320 | tf_op jit(solution)/shard_map/all_gather | solution.py:238
  663.7 23.5 fusion.133
  687.2 57.9 %all-gather.49.cloned.1.call-done = bf16[4,256,2048]{2,1,0:T(8,128)(2,1)} async-done(((bf16[1,256,2048]{2,1,0:T(8,128)(2,1)}), bf16[4,256,2048]{2,1,0:T(8,128)(2,1)}) %all-gather.49.cloned.1.call-update) | async-done | bytes 4194320 | tf_op jit(solution)/shard_map/all_gather | solution.py:254
  745.1 21.9 multiply_convert_fusion.3
  767.0 24.4 fusion.106
  791.5 14.6 fusion.134
  806.1 128.6 %reduce-scatter.35.cloned.1.call-done = f32[1,256,2048]{2,1,0:T(8,128)} async-done(((f32[4,256,2048]{2,1,0:T(8,128)}), f32[1,256,2048]{2,1,0:T(8,128)}) %reduce-scatter.35.cloned.1.call-update) | async-done | bytes 2097168 | tf_op jit(solution)/shard_map/reduce_scatter | solution.py:274
  937.4 144.7 %reduce-scatter.29.cloned.1.call-done = f32[1,256,2048]{2,1,0:T(8,128)} async-done(((f32[4,256,2048]{2,1,0:T(8,128)}), f32[1,256,2048]{2,1,0:T(8,128)}) %reduce-scatter.29.cloned.1.call-update) | async-done | bytes 2097168 | tf_op jit(solution)/shard_map/reduce_scatter | solution.py:249
  1087.7 81.5 %all-gather.51.cloned.1.call-done = bf16[4,256,2048]{2,1,0:T(8,128)(2,1)} async-done(((bf16[1,256,2048]{2,1,0:T(8,128)(2,1)}), bf16[4,256,2048]{2,1,0:T(8,128)(2,1)}) %all-gather.51.cloned.1.call-update) | async-done | bytes 4194320 | tf_op jit(solution)/shard_map/all_gather | solution.py:282
  1169.2 6.2 convolution_convert_fusion.1
  1179.5 91.7 %while.50 = (s32[]{:T(128)}, f32[4,256,2,4,64]{1,4,3,2,0:T(8,128)}, f32[4,1024,2,128]{1,3,2,0:T(8,128)}, bf16[4,1024,2,64]{1,3,2,0:T(8,128)(2,1)S(1)}, s32[4,256...) while((s32[]{:T(128)}, f32[4,256,2,4,64]{1,4,3,2,0:T(8,128)}, ...), condition=%wide.region_22.23_spmd, body=%wide.region_20.22_spmd.sunk | while | flops 1374943232 | bytes 95761592 | solution.py:289
  1274.7 47.8 %reduce-scatter.37.cloned.1.call-done = f32[4,256,2,128]{1,3,2,0:T(8,128)} async-done(((f32[4,1024,2,128]{1,3,2,0:T(8,128)}), f32[4,256,2,128]{1,3,2,0:T(8,128)}) %reduce-scatter.37.cloned.1.call-update) | async-done | bytes 1048592 | tf_op jit(solution)/shard_map/reduce_scatter | solution.py:302
  1325.2 7.6 fusion.110
  1341.1 136.5 %reduce-scatter.39.cloned.1.call-done = f32[1,256,2048]{2,1,0:T(8,128)} async-done(((f32[4,256,2048]{2,1,0:T(8,128)}), f32[1,256,2048]{2,1,0:T(8,128)}) %reduce-scatter.39.cloned.1.call-update) | async-done | bytes 2097168 | tf_op jit(solution)/shard_map/reduce_scatter | solution.py:321
  1484.5 81.4 %all-gather.43.cloned.1.call-done = bf16[4,256,2048]{2,1,0:T(8,128)(2,1)} async-done(((bf16[1,256,2048]{2,1,0:T(8,128)(2,1)}), bf16[4,256,2048]{2,1,0:T(8,128)(2,1)}) %all-gather.43.cloned.1.call-update) | async-done | bytes 4194320 | tf_op jit(solution)/shard_map/all_gather | solution.py:194
  1580.9 27.9 all-gather.45.cloned.1.call-done
  1612.6 28.7 while.49
  1641.4 8.0 fusion.136
  1649.4 144.7 %reduce-scatter.31.cloned.1.call-done = f32[1,256,2048]{2,1,0:T(8,128)} async-done(((f32[4,256,2048]{2,1,0:T(8,128)}), f32[1,256,2048]{2,1,0:T(8,128)}) %reduce-scatter.31.cloned.1.call-update) | async-done | bytes 2097168 | tf_op jit(solution)/shard_map/reduce_scatter | solution.py:233
  1805.6 74.6 %all-gather.47.cloned.1.call-done = bf16[4,256,2048]{2,1,0:T(8,128)(2,1)} async-done(((bf16[1,256,2048]{2,1,0:T(8,128)(2,1)}), bf16[4,256,2048]{2,1,0:T(8,128)(2,1)}) %all-gather.47.cloned.1.call-update) | async-done | bytes 4194320 | tf_op jit(solution)/shard_map/all_gather | solution.py:238
  1880.2 23.9 fusion.137
  1904.1 56.9 %all-gather.53.cloned.1.call-done = bf16[4,256,2048]{2,1,0:T(8,128)(2,1)} async-done(((bf16[1,256,2048]{2,1,0:T(8,128)(2,1)}), bf16[4,256,2048]{2,1,0:T(8,128)(2,1)}) %all-gather.53.cloned.1.call-update) | async-done | bytes 4194320 | tf_op jit(solution)/shard_map/all_gather | solution.py:254
  1961.0 21.9 multiply_convert_fusion.1
  1982.9 24.2 fusion.104
  2007.3 14.6 fusion.138
  2022.0 128.4 %reduce-scatter.41.cloned.1.call-done = f32[1,256,2048]{2,1,0:T(8,128)} async-done(((f32[4,256,2048]{2,1,0:T(8,128)}), f32[1,256,2048]{2,1,0:T(8,128)}) %reduce-scatter.41.cloned.1.call-update) | async-done | bytes 2097168 | tf_op jit(solution)/shard_map/reduce_scatter | solution.py:274
  2153.1 144.9 %reduce-scatter.33.cloned.1.call-done = f32[1,256,2048]{2,1,0:T(8,128)} async-done(((f32[4,256,2048]{2,1,0:T(8,128)}), f32[1,256,2048]{2,1,0:T(8,128)}) %reduce-scatter.33.cloned.1.call-update) | async-done | bytes 2097168 | tf_op jit(solution)/shard_map/reduce_scatter | solution.py:249
  2303.7 81.5 %all-gather.55.cloned.1.call-done = bf16[4,256,2048]{2,1,0:T(8,128)(2,1)} async-done(((bf16[1,256,2048]{2,1,0:T(8,128)(2,1)}), bf16[4,256,2048]{2,1,0:T(8,128)(2,1)}) %all-gather.55.cloned.1.call-update) | async-done | bytes 4194320 | tf_op jit(solution)/shard_map/all_gather | solution.py:282
  2385.2 6.2 convolution_convert_fusion
  2395.5 83.1 %while.51 = (s32[]{:T(128)}, f32[4,256,2,4,64]{1,4,3,2,0:T(8,128)}, f32[4,1024,2,128]{1,3,2,0:T(8,128)}, bf16[4,1024,2,64]{1,3,2,0:T(8,128)(2,1)S(1)}, s32[4,256...) while((s32[]{:T(128)}, f32[4,256,2,4,64]{1,4,3,2,0:T(8,128)}, ...), condition=%wide.region_30.31_spmd, body=%wide.region_28.30_spmd.sunk | while | flops 1374943232 | bytes 95761592 | solution.py:289
  2489.0 6.7 reshape.731
  2502.6 8.4 fusion.109
  2513.5 16.3 reduce-scatter.43.cloned.1.call-done
  2532.4 7.9 bitcast_add_fusion.2
  2544.1 16.8 fusion.140
  2560.9 17.2 bitcast_add_fusion.1
  2578.1 16.5 copy.268
  2594.9 26.9 fusion.105
  2621.8 32.7 bitcast_add_fusion
  2654.5 22.9 copy.314
  2679.5 41.5 %reduce-scatter.51.cloned.1.call-done = f32[1,4,256,4096]{3,2,1,0:T(8,128)} async-done(((f32[2,4,256,4096]{3,2,1,0:T(8,128)}), f32[1,4,256,4096]{3,2,1,0:T(8,128)}) %reduce-scatter.51.cloned.1.call-update) | async-done | bytes 16777232 | tf_op jit(solution)/shard_map/reduce_scatter | solution.py:124
  2721.0 7.6 fusion.108
  2728.7 31.7 reduce-scatter.57.cloned.1.call-done
  2760.5 46.7 %reduce-scatter.55.cloned.1.call-done = f32[1,256,768]{2,1,0:T(8,128)} async-done(((f32[4,256,768]{2,1,0:T(8,128)}), f32[1,256,768]{2,1,0:T(8,128)}) %reduce-scatter.55.cloned.1.call-update) | async-done | bytes 786448
  2807.3 89.3 %reduce-scatter.61.cloned.1.call-done = f32[2048,1,256]{2,0,1:T(8,128)} async-done(((f32[2048,4,256]{2,0,1:T(8,128)}), f32[2048,1,256]{2,0,1:T(8,128)}) %reduce-scatter.61.cloned.1.call-update) | async-done | bytes 2097168
  2897.0 156.5 %reduce-scatter.59.cloned.1.call-done = f32[1,256,4096]{2,1,0:T(8,128)} async-done(((f32[4,256,4096]{2,1,0:T(8,128)}), f32[1,256,4096]{2,1,0:T(8,128)}) %reduce-scatter.59.cloned.1.call-update) | async-done | bytes 4194320
  3070.1 130.2 %reduce-scatter.45.cloned.1.call-done = f32[1,256,2048]{2,1,0:T(8,128)} async-done(((f32[4,256,2048]{2,1,0:T(8,128)}), f32[1,256,2048]{2,1,0:T(8,128)}) %reduce-scatter.45.cloned.1.call-update) | async-done | bytes 2097168 | tf_op jit(solution)/shard_map/reduce_scatter | solution.py:321
  3220.3 77.9 %psum.7 = f32[2,2048]{1,0:T(2,128)S(1)} all-reduce(f32[2,2048]{1,0:T(2,128)S(1)} %pad_maximum_fusion.22), channel_id=1, replica_groups=mesh['dp'=2,'row'=4,'col'=4] {'dp','row','col'}, use_global_device_ids=true, to_apply=%region_46.47 | all-reduce | flops 4096 | bytes 32768 | tf_op jit(solution)/shard_map/psum | solution.py:341
  3307.6 8.1 fusion.125
  (593 shorter events, 477.9 us)
Async XLA Ops:
  7.2 186.7 %copy-start = (bf16[2048,512]{1,0:T(8,128)(2,1)S(1)}, bf16[2048,512]{1,0:T(8,128)(2,1)}, u32[]{:S(2)}) copy-start(bf16[2048,512]{1,0:T(8,128)(2,1)} %param.28) | copy-start | bytes 6291460
  7.2 36.8 %all-gather.57.cloned.1.call-start = ((), (), s32[]{:S(2)}) async-start(), calls=%async_computation.46 | async-start | bytes 1966080 | tf_op jit(solution)/shard_map/all_gather | solution.py:112
  9.2 101.8 %all-gather.61.cloned.1.call-start = ((), (), s32[]{:S(2)}) async-start(), calls=%async_computation.48 | async-start | bytes 1310720 | tf_op jit(solution)/shard_map/all_gather | solution.py:112
  11.1 104.3 %all-gather.59.cloned.1.call-start = ((), (), s32[]{:S(2)}) async-start(), calls=%async_computation.47 | async-start | bytes 4718592 | tf_op jit(solution)/shard_map/all_gather | solution.py:113
  47.1 37.1 %all-to-all-start = ((bf16[2,1,4,256,1,512]{5,3,0,4,1,2:T(8,128)(2,1)}), bf16[2,1,4,256,1,512]{5,3,0,4,1,2:T(8,128)(2,1)}, u32[]{:S(2)}, u32[]{:S(2)}) async-start(bf16[2,1,4,256,1,512]{5,3,0,4,1,2:T(8,128)(2,1)} %copy.221), calls=%async_computation | async-start | bytes 4194304 | tf_op jit(solution)/shard_map/all_to_all | solution.py:131
  51.6 131.4 %all-gather.37.cloned.1.call-start = ((), (), s32[]{:S(2)}) async-start(), calls=%async_computation.22 | async-start | bytes 5242880 | tf_op jit(solution)/shard_map/all_gather | solution.py:194
  100.1 100.2 %all-gather.63.cloned.1.call-start = ((), (), s32[]{:S(2)}) async-start(), calls=%async_computation.49 | async-start | bytes 3145728 | tf_op jit(solution)/shard_map/all_gather | solution.py:113
  113.3 119.2 %all-gather.39.cloned.1.call-start = ((), (), s32[]{:S(2)}) async-start(), calls=%async_computation.23 | async-start | bytes 2621440 | tf_op jit(solution)/shard_map/all_gather | solution.py:212
  115.4 96.5 %copy-start.30 = (f32[4,256,32]{1,2,0:T(8,128)}, f32[4,256,32]{1,2,0:T(8,128)S(1)}, u32[]{:S(2)}) copy-start(f32[4,256,32]{1,2,0:T(8,128)S(1)} %get-tuple-element.518) | copy-start | bytes 393220
  193.8 93.7 %all-gather.69.cloned.1.call-start = ((), (), s32[]{:S(2)}) async-start(), calls=%async_computation.52 | async-start | bytes 5242880 | tf_op jit(solution)/shard_map/all_gather | solution.py:112
  195.4 182.1 %all-gather.65.cloned.1.call-start = ((), (), s32[]{:S(2)}) async-start(), calls=%async_computation.50 | async-start | bytes 10485760 | tf_op jit(solution)/shard_map/all_gather | solution.py:112
  198.7 325.8 %reduce-scatter.27.cloned.1.call-start = ((), (), s32[]{:S(2)}) async-start(), calls=%async_computation.24 | async-start | bytes 10485760 | tf_op jit(solution)/shard_map/reduce_scatter | solution.py:233
  273.5 293.3 %all-gather.71.cloned.1.call-start = ((), (), s32[]{:S(2)}) async-start(), calls=%async_computation.53 | async-start | bytes 12582912 | tf_op jit(solution)/shard_map/all_gather | solution.py:113
  293.7 304.5 %all-gather.67.cloned.1.call-start = ((), (), s32[]{:S(2)}) async-start(), calls=%async_computation.51 | async-start | bytes 25165824 | tf_op jit(solution)/shard_map/all_gather | solution.py:113
  377.5 147.0 %copy-start.2 = (f32[1,256,2048]{2,1,0:T(8,128)S(1)}, f32[1,256,2048]{2,1,0:T(8,128)}, u32[]{:S(2)}) copy-start(f32[1,256,2048]{2,1,0:T(8,128)} %reshape.734) | copy-start | bytes 6291460
  377.5 286.2 %all-gather.41.cloned.1.call-start = ((), (), s32[]{:S(2)}) async-start(), calls=%async_computation.25 | async-start | bytes 5242880 | tf_op jit(solution)/shard_map/all_gather | solution.py:238
  386.6 695.5 %copy-start.44 = (f32[4,1,512]{2,1,0:T(1,128)}, f32[4,1,512]{2,1,0:T(1,128)S(1)}, u32[]{:S(2)}) copy-start(f32[4,1,512]{2,1,0:T(1,128)S(1)} %all-gather.13) | copy-start | bytes 24580
  529.0 216.1 %all-gather.49.cloned.1.call-start = ((), (), s32[]{:S(2)}) async-start(), calls=%async_computation.32 | async-start | bytes 5242880 | tf_op jit(solution)/shard_map/all_gather | solution.py:254
  565.3 18.2 copy-start.17
  566.7 367.9 %reduce-scatter.35.cloned.1.call-start = ((), (), s32[]{:S(2)}) async-start(), calls=%async_computation.33 | async-start | bytes 10485760 | tf_op jit(solution)/shard_map/reduce_scatter | solution.py:274
  791.4 290.7 %reduce-scatter.29.cloned.1.call-start = ((), (), s32[]{:S(2)}) async-start(), calls=%async_computation.26 | async-start | bytes 10485760 | tf_op jit(solution)/shard_map/reduce_scatter | solution.py:249
  806.0 128.6 %copy-start.8 = (f32[1,256,2048]{2,1,0:T(8,128)S(1)}, f32[1,256,2048]{2,1,0:T(8,128)}, u32[]{:S(2)}) copy-start(f32[1,256,2048]{2,1,0:T(8,128)} %copy-done.7) | copy-start | bytes 6291460
  806.1 363.1 %all-gather.51.cloned.1.call-start = ((), (), s32[]{:S(2)}) async-start(), calls=%async_computation.34 | async-start | bytes 5242880 | tf_op jit(solution)/shard_map/all_gather | solution.py:282
  1087.7 234.8 %reduce-scatter.37.cloned.1.call-start = ((), (), s32[]{:S(2)}) async-start(), calls=%async_computation.35 | async-start | bytes 5242880 | tf_op jit(solution)/shard_map/reduce_scatter | solution.py:302
  1271.2 206.4 %reduce-scatter.39.cloned.1.call-start = ((), (), s32[]{:S(2)}) async-start(), calls=%async_computation.36 | async-start | bytes 10485760 | tf_op jit(solution)/shard_map/reduce_scatter | solution.py:321
  1274.7 58.1 %copy-start.39 = (bf16[4,256,512]{2,1,0:T(8,128)(2,1)}, bf16[4,256,512]{2,1,0:T(8,128)(2,1)S(1)}, u32[]{:S(2)}) copy-start(bf16[4,256,512]{2,1,0:T(8,128)(2,1)S(1)} %copy.248) | copy-start | bytes 3145732
  1332.9 233.1 %all-gather.43.cloned.1.call-start = ((), (), s32[]{:S(2)}) async-start(), calls=%async_computation.27 | async-start | bytes 5242880 | tf_op jit(solution)/shard_map/all_gather | solution.py:194
  1332.9 144.7 %copy-start.3 = (f32[1,256,2048]{2,1,0:T(8,128)S(1)}, f32[1,256,2048]{2,1,0:T(8,128)}, u32[]{:S(2)}) copy-start(f32[1,256,2048]{2,1,0:T(8,128)} %reshape.734) | copy-start | bytes 6291460
  1332.9 144.7 %copy-start.47 = (f32[4,1,512]{2,1,0:T(1,128)S(1)}, f32[4,1,512]{2,1,0:T(1,128)}, u32[]{:S(2)}) copy-start(f32[4,1,512]{2,1,0:T(1,128)} %copy-done.46) | copy-start | bytes 24580
  1332.9 144.7 %copy-start.64 = (f32[256]{0:T(256)S(1)}, f32[256]{0:T(256)}, u32[]{:S(2)}) copy-start(f32[256]{0:T(256)} %copy-done.63) | copy-start | bytes 3076
  1341.1 143.4 %copy-start.65 = (f32[256]{0:T(256)}, f32[256]{0:T(256)S(1)}, u32[]{:S(2)}) copy-start(f32[256]{0:T(256)S(1)} %add_rsqrt_fusion.1) | copy-start | bytes 3076
  1484.5 89.7 %copy-start.28 = (f32[4,256,32]{1,2,0:T(8,128)S(1)}, f32[4,256,32]{1,2,0:T(8,128)}, u32[]{:S(2)}) copy-start(f32[4,256,32]{1,2,0:T(8,128)} %get-tuple-element.523) | copy-start | bytes 393220
  1484.5 89.7 %copy-start.37 = (f32[4,256,32]{1,2,0:T(8,128)S(1)}, f32[4,256,32]{1,2,0:T(8,128)}, u32[]{:S(2)}) copy-start(f32[4,256,32]{1,2,0:T(8,128)} %get-tuple-element.522) | copy-start | bytes 393220
  1484.5 124.3 %all-gather.45.cloned.1.call-start = ((), (), s32[]{:S(2)}) async-start(), calls=%async_computation.28 | async-start | bytes 2621440 | tf_op jit(solution)/shard_map/all_gather | solution.py:212
  1575.1 219.0 %reduce-scatter.31.cloned.1.call-start = ((), (), s32[]{:S(2)}) async-start(), calls=%async_computation.29 | async-start | bytes 10485760 | tf_op jit(solution)/shard_map/reduce_scatter | solution.py:233
  1649.4 144.8 %copy-start.5 = (f32[1,256,2048]{2,1,0:T(8,128)S(1)}, f32[1,256,2048]{2,1,0:T(8,128)}, u32[]{:S(2)}) copy-start(f32[1,256,2048]{2,1,0:T(8,128)} %reshape.735) | copy-start | bytes 6291460
  1649.4 148.1 %copy-start.45 = (f32[4,1,512]{2,1,0:T(1,128)S(1)}, f32[4,1,512]{2,1,0:T(1,128)}, u32[]{:S(2)}) copy-start(f32[4,1,512]{2,1,0:T(1,128)} %copy-done.44) | copy-start | bytes 24580
  1649.4 230.8 %all-gather.47.cloned.1.call-start = ((), (), s32[]{:S(2)}) async-start(), calls=%async_computation.30 | async-start | bytes 5242880 | tf_op jit(solution)/shard_map/all_gather | solution.py:238
  1798.7 162.3 %all-gather.53.cloned.1.call-start = ((), (), s32[]{:S(2)}) async-start(), calls=%async_computation.37 | async-start | bytes 5242880 | tf_op jit(solution)/shard_map/all_gather | solution.py:254
  1804.1 100.0 %copy-start.18 = (f32[1,256,2048]{2,1,0:T(8,128)}, f32[1,256,2048]{2,1,0:T(8,128)S(1)}, u32[]{:S(2)}) copy-start(f32[1,256,2048]{2,1,0:T(8,128)S(1)} %reshape.737) | copy-start | bytes 6291460
  1805.5 344.8 %reduce-scatter.41.cloned.1.call-start = ((), (), s32[]{:S(2)}) async-start(), calls=%async_computation.38 | async-start | bytes 10485760 | tf_op jit(solution)/shard_map/reduce_scatter | solution.py:274
  2007.1 290.9 %reduce-scatter.33.cloned.1.call-start = ((), (), s32[]{:S(2)}) async-start(), calls=%async_computation.31 | async-start | bytes 10485760 | tf_op jit(solution)/shard_map/reduce_scatter | solution.py:249
  2021.9 128.5 %copy-start.10 = (f32[1,256,2048]{2,1,0:T(8,128)S(1)}, f32[1,256,2048]{2,1,0:T(8,128)}, u32[]{:S(2)}) copy-start(f32[1,256,2048]{2,1,0:T(8,128)} %copy-done.9) | copy-start | bytes 6291460
  2021.9 363.3 %all-gather.55.cloned.1.call-start = ((), (), s32[]{:S(2)}) async-start(), calls=%async_computation.39 | async-start | bytes 5242880 | tf_op jit(solution)/shard_map/all_gather | solution.py:282
  2303.7 226.2 %reduce-scatter.43.cloned.1.call-start = ((), (), s32[]{:S(2)}) async-start(), calls=%async_computation.40 | async-start | bytes 5242880 | tf_op jit(solution)/shard_map/reduce_scatter | solution.py:302
  2478.6 198.9 %reduce-scatter.49.cloned.1.call-start = ((), (), s32[]{:S(2)}) async-start(), calls=%async_computation.43 | async-start | bytes 6291456 | tf_op jit(solution)/shard_map/reduce_scatter | solution.py:124
  2501.3 176.9 %reduce-scatter.47.cloned.1.call-start = ((), (), s32[]{:S(2)}) async-start(), calls=%async_computation.42 | async-start | bytes 9437184 | tf_op jit(solution)/shard_map/reduce_scatter | solution.py:124
  2543.9 134.9 %reduce-scatter.53.cloned.1.call-start = ((), (), s32[]{:S(2)}) async-start(), calls=%async_computation.45 | async-start | bytes 25165824 | tf_op jit(solution)/shard_map/reduce_scatter | solution.py:124
  2594.7 126.3 %reduce-scatter.51.cloned.1.call-start = ((), (), s32[]{:S(2)}) async-start(), calls=%async_computation.44 | async-start | bytes 50331648 | tf_op jit(solution)/shard_map/reduce_scatter | solution.py:124
  2677.4 83.0 %reduce-scatter.57.cloned.1.call-start = ((), (), s32[]{:S(2)}) async-start(), calls=%async_computation.59 | async-start | bytes 2621440
  2678.1 129.1 %reduce-scatter.55.cloned.1.call-start = ((), (), s32[]{:S(2)}) async-start(), calls=%async_computation.58 | async-start | bytes 3932160
  2678.7 217.9 %reduce-scatter.61.cloned.1.call-start = ((), (), s32[]{:S(2)}) async-start(), calls=%async_computation.61 | async-start | bytes 10485760
  2679.5 374.0 %reduce-scatter.59.cloned.1.call-start = ((), (), s32[]{:S(2)}) async-start(), calls=%async_computation.60 | async-start | bytes 20971520
  2721.0 479.3 %reduce-scatter.45.cloned.1.call-start = ((), (), s32[]{:S(2)}) async-start(), calls=%async_computation.41 | async-start | bytes 10485760 | tf_op jit(solution)/shard_map/reduce_scatter | solution.py:321
  2728.6 324.8 %copy-start.24 = (bf16[1,256,2048]{2,1,0:T(8,128)(2,1)S(1)}, bf16[1,256,2048]{2,1,0:T(8,128)(2,1)}, u32[]{:S(2)}) copy-start(bf16[1,256,2048]{2,1,0:T(8,128)(2,1)} %get-tuple-element.486) | copy-start | bytes 3145732
  2728.7 491.6 %all-gather.75.cloned.1.call-start = ((), (), s32[]{:S(2)}) async-start(), calls=%async_computation.55 | async-start | bytes 1572864 | tf_op jit(solution)/shard_map/all_gather | solution.py:126
  2760.5 543.0 %all-gather.73.cloned.1.call-start = ((), (), s32[]{:S(2)}) async-start(), calls=%async_computation.54 | async-start | bytes 2359296 | tf_op jit(solution)/shard_map/all_gather | solution.py:126
  2807.3 500.4 %all-gather.79.cloned.1.call-start = ((), (), s32[]{:S(2)}) async-start(), calls=%async_computation.57 | async-start | bytes 6291456 | tf_op jit(solution)/shard_map/all_gather | solution.py:126
  2896.7 411.0 %all-gather.77.cloned.1.call-start = ((), (), s32[]{:S(2)}) async-start(), calls=%async_computation.56 | async-start | bytes 12582912 | tf_op jit(solution)/shard_map/all_gather | solution.py:126
  3058.2 154.0 %all-to-all-start.1 = ((bf16[2,1,1,256,4,512]{5,3,2,1,0,4:T(8,128)(2,1)}), bf16[2,1,1,256,4,512]{5,3,2,1,0,4:T(8,128)(2,1)}, u32[]{:S(2)}, u32[]{:S(2)}) async-start(bf16[2,1,1,256,4,512]{5,3,2,1,0,4:T(8,128)(2,1)} %pad_maximum_fusion.7), calls=%async_computation.5 | async-start | bytes 4194304 | tf_op jit(solution)/shard_map/all_to_all | solution.py:137
  3062.7 137.6 %copy-start.6 = (f32[1,256,2048]{2,1,0:T(8,128)S(1)}, f32[1,256,2048]{2,1,0:T(8,128)}, u32[]{:S(2)}) copy-start(f32[1,256,2048]{2,1,0:T(8,128)} %reshape.735) | copy-start | bytes 6291460
  3062.7 137.6 %copy-start.48 = (f32[4,1,512]{2,1,0:T(1,128)S(1)}, f32[4,1,512]{2,1,0:T(1,128)}, u32[]{:S(2)}) copy-start(f32[4,1,512]{2,1,0:T(1,128)} %copy-done.46) | copy-start | bytes 24580
  3062.7 137.6 %copy-start.66 = (f32[256]{0:T(256)S(1)}, f32[256]{0:T(256)}, u32[]{:S(2)}) copy-start(f32[256]{0:T(256)} %copy-done.65) | copy-start | bytes 3076
  3212.2 86.7 %all-to-all-start.3 = ((f32[2,1,1,256,4,512]{5,3,2,1,0,4:T(8,128)}), f32[2,1,1,256,4,512]{5,3,2,1,0,4:T(8,128)}, u32[]{:S(2)}, u32[]{:S(2)}) async-start(f32[2,1,1,256,4,512]{5,3,2,1,0,4:T(8,128)} %pad_maximum_fusion.6), calls=%async_computation.13 | async-start | bytes 8388608 | tf_op jit(solution)/shard_map/all_to_all | solution.py:137
  (68 other events, 339.6 us)
Sparse Core Ops, SparseCore 0:
  10.4 33.5 all-gather.56
  46.4 38.8 all-gather.60
  86.8 12.1 all-gather.58
  101.0 81.9 all-gather.36
  184.9 9.0 all-gather.62
  196.3 36.2 all-gather.38
  234.9 52.5 all-gather.68
  289.9 87.4 all-gather.64
  379.8 144.6 reduce-scatter.26
  526.4 20.4 all-gather.70
  548.5 31.2 all-gather.66
  581.7 81.9 all-gather.40
  665.8 79.2 all-gather.48
  791.5 143.0 reduce-scatter.34
  936.9 145.2 reduce-scatter.28
  1087.8 81.3 all-gather.50
  1271.4 51.0 reduce-scatter.36
  1333.0 144.6 reduce-scatter.38
  1484.6 81.3 all-gather.42
  1575.2 33.5 all-gather.44
  1649.5 144.6 reduce-scatter.30
  1798.8 81.3 all-gather.46
  1881.8 79.2 all-gather.52
  2007.2 143.0 reduce-scatter.40
  2152.7 145.2 reduce-scatter.32
  2303.8 81.3 all-gather.54
  2478.7 51.0 reduce-scatter.42
  2532.1 12.0 reduce-scatter.48
  2546.5 15.3 reduce-scatter.46
  2594.8 25.7 reduce-scatter.52
  2677.5 43.3 reduce-scatter.50
  2723.9 36.4 reduce-scatter.56
  2763.3 43.9 reduce-scatter.54
  2810.3 86.2 reduce-scatter.60
  2899.7 153.7 reduce-scatter.58
  3055.7 144.6 reduce-scatter.44
  3201.7 9.6 all-gather.74
  3212.9 10.9 all-gather.72
  3225.3 14.8 all-gather.78
  3241.8 21.0 all-gather.76

commit v2 on v1

--- a/solution.py
+++ b/solution.py
@@ -103,6 +103,12 @@
         * SCORE_SCALE
     )
     return grad_query, jnp.concatenate([grad_key, grad_value], axis=-1)
+
+
+def scatter_low(partial, axis_name, axis):
+    return lax.psum_scatter(
+        partial.astype(jnp.bfloat16), axis_name, scatter_dimension=axis, tiled=True
+    ).astype(jnp.float32)
 
 
 def make_shards(n_dp, n_row, n_col):
@@ -230,7 +236,7 @@
             attn_part = jnp.einsum(
                 "stm,md->std", mixed, w_out_all, preferred_element_type=jnp.float32
             )
-            attn_branch = lax.psum_scatter(attn_part, "col", scatter_dimension=0, tiled=True)
+            attn_branch = scatter_low(attn_part, "col", 0)
             resid_mid = rows_f + RESIDUAL_SCALE * attn_branch
             inv_ffn = lax.rsqrt(jnp.mean(resid_mid * resid_mid, axis=-1, keepdims=True) + EPSILON)
             norm_ffn = resid_mid * inv_ffn
@@ -246,7 +252,7 @@
             ffn_part = jnp.einsum(
                 "stf,fd->std", act_low, w_down_all, preferred_element_type=jnp.float32
             )
-            ffn_branch = lax.psum_scatter(ffn_part, "col", scatter_dimension=0, tiled=True)
+            ffn_branch = scatter_low(ffn_part, "col", 0)
             outs_list.append((resid_mid + RESIDUAL_SCALE * ffn_branch).astype(jnp.bfloat16))
 
             grad_rows = cotangent_t[batch_index].astype(jnp.float32)
@@ -271,9 +277,7 @@
             grad_normed_part = jnp.einsum(
                 "stf,df->std", paired_gradient, w_pair, preferred_element_type=jnp.float32
             )
-            grad_normed_ffn = lax.psum_scatter(
-                grad_normed_part, "col", scatter_dimension=0, tiled=True
-            )
+            grad_normed_ffn = scatter_low(grad_normed_part, "col", 0)
             scaled_ffn = grad_normed_ffn * gain_ffn_all
             gain_ffn_total = gain_ffn_total + jnp.sum(grad_normed_ffn * norm_ffn, axis=(0, 1))
             inner_ffn = jnp.mean(scaled_ffn * norm_ffn, axis=-1, keepdims=True)
@@ -318,9 +322,7 @@
             grad_normed_attn_part = jnp.einsum(
                 "stm,dm->std", grad_qkv, w_qkv, preferred_element_type=jnp.float32
             )
-            grad_normed_attn = lax.psum_scatter(
-                grad_normed_attn_part, "col", scatter_dimension=0, tiled=True
-            )
+            grad_normed_attn = scatter_low(grad_normed_attn_part, "col", 0)
             scaled_attn = grad_normed_attn * gain_attn_all
             gain_attn_total = gain_attn_total + jnp.sum(grad_normed_attn * norm_attn, axis=(0, 1))
             inner_attn = jnp.mean(scaled_attn * norm_attn, axis=-1, keepdims=True)

time: 3340 us -> 2830 us (0.85)
  waiting for transfers between devices: 2260 us -> 1730 us
    reduce_scatter x8, waiting for transfers between devices: 1100 us -> 584 us  [scatter_low(): lax.psum_scatter(partial.astype(jnp.bfloat16), axis_name, scatter_dimensi...]
  transfers between devices with their start and end apart: 43 -> 43, of which waited for: 28 -> 29; matrix products, arithmetic and copies ran while one was open for 15% -> 18% of each run, Pallas kernels for 0% -> 0%
where the time goes in v2:
time: 2830 us; the launch traced here: 2820 us
  waiting for transfers between devices  1730 us (61%)
  matrix products  510 us (18%)
  local copies, waits for them, and re-layouts  268 us (9%)
  blocking collectives  158 us (6%)
  other arithmetic  118 us (4%)
    reduce_scatter x8, waiting for transfers between devices, scatter_low(): lax.psum_scatter(partial.astype(jnp.bfloat16), axis_name, scatter_dimensi...  584 us
    unnamed x44, waiting for transfers between devices  314 us
    all_gather x2, waiting for transfers between devices, shards(): spread_grad_attn = lax.all_gather(grad_attn, 'col', axis=0, tiled=True)  163 us
    all_gather x2, waiting for transfers between devices, shards(): spread_attn = lax.all_gather(normed_attn, 'col', axis=0, tiled=True)  145 us
    all_gather x4, waiting for transfers between devices, gather_features(): gathered = lax.all_gather(mine, 'row', axis=axis)  132 us
    all_gather x2, waiting for transfers between devices, shards(): spread_ffn = lax.all_gather(normed_ffn, 'col', axis=0, tiled=True)  121 us
    all_gather x2, waiting for transfers between devices, shards(): spread_grad_ffn = lax.all_gather(grad_ffn, 'col', axis=0, tiled=True)  116 us
    psum x1, blocking collectives, shards(): lax.psum(jnp.stack([gain_attn_total, gain_ffn_total]), ('dp', 'row', 'col'))  80.7 us
  transfers between devices with their start and end apart: 43, of which 29 were waited for; matrix products, arithmetic and copies ran while one was open for 18% of the time, Pallas kernels for 0%

profile of v2, /device:TPU:0, one launch (start us, length us, event | category | flops | bytes accessed | tf_op | source)
XLA Modules:
  0.0 2819.3 jit_solution(5169501704167346831)
XLA Ops:
  11.1 32.9 %all-gather.57.cloned.1.call-done = bf16[1024,768]{1,0:T(8,128)(2,1)} async-done(((bf16[256,768]{1,0:T(8,128)(2,1)}), bf16[1024,768]{1,0:T(8,128)(2,1)}) %all-gather.57.cloned.1.call-update) | async-done | bytes 1572880 | tf_op jit(solution)/shard_map/all_gather | solution.py:118
  51.6 32.6 %all-gather.12 = f32[4,1,512]{2,1,0:T(1,128)S(1)} all-gather(f32[1,1,512]{2,1,0:T(1,128)S(1)} %bitcast.645), channel_id=1, replica_groups=mesh['dp'=2,'row'=4,'col'=4] {'row'}, dimensions={0}, use_global_device_ids=true | all-gather | bytes 10240 | tf_op jit(solution)/shard_map/all_gather | solution.py:174
  100.1 7.6 all_gather.105
  119.1 63.9 %all-gather.37.cloned.1.call-done = bf16[4,256,2048]{2,1,0:T(8,128)(2,1)} async-done(((bf16[1,256,2048]{2,1,0:T(8,128)(2,1)}), bf16[4,256,2048]{2,1,0:T(8,128)(2,1)}) %all-gather.37.cloned.1.call-update) | async-done | bytes 4194320 | tf_op jit(solution)/shard_map/all_gather | solution.py:200
  212.6 19.9 all-gather.39.cloned.1.call-done
  236.3 28.7 %while.48 = (s32[]{:T(128)}, bf16[4,256,512]{1,2,0:T(8,128)(2,1)}, f32[4,2,4,256,1]{3,2,1,4,0:T(4,128)S(1)}, bf16[4,1024,2,64]{1,3,2,0:T(8,128)(2,1)}, s32[4,256...) while((s32[]{:T(128)}, bf16[4,256,512]{1,2,0:T(8,128)(2,1)}, ...), condition=%wide.region_6.7_spmd, body=%wide.region_3.6_spmd.sunk | while | flops 560855040 | bytes 27873392 | solution.py:225
  265.0 7.1 convolution_convert_fusion.3
  272.2 15.3 all-gather.69.cloned.1.call-done
  293.8 83.7 %all-gather.65.cloned.1.call-done = bf16[1024,4096]{1,0:T(8,128)(2,1)} async-done(((bf16[256,4096]{1,0:T(8,128)(2,1)}), bf16[1024,4096]{1,0:T(8,128)(2,1)}) %all-gather.65.cloned.1.call-update) | async-done | bytes 8388624 | tf_op jit(solution)/shard_map/all_gather | solution.py:118
  378.1 8.2 all-gather.13
  386.4 70.8 %reduce-scatter.27.cloned.1.call-done = bf16[1,256,2048]{2,1,0:T(8,128)(2,1)} async-done(((bf16[4,256,2048]{2,1,0:T(8,128)(2,1)}), bf16[1,256,2048]{2,1,0:T(8,128)(2,1)}) %reduce-scatter.27.cloned.1.call-update) | async-done | bytes 1048592 | tf_op jit(solution)/shard_map/reduce_scatter | solution.py:109
  463.3 28.5 %all_to_all.60 = bf16[2,1,4,256,1,512]{5,3,0,4,1,2:T(8,128)(2,1)S(1)} all-to-all(bf16[2,1,4,256,1,512]{5,3,0,4,1,2:T(8,128)(2,1)S(1)} %copy.245), channel_id=1, replica_groups=mesh['dp'=2,'row'=4,'col'=4] {'row'}, dimensions={2} | all-to-all | bytes 4194304 | tf_op jit(solution)/shard_map/all_to_all | solution.py:137
  503.2 16.6 copy.236
  519.7 14.6 reshape.769
  534.4 14.1 copy.233
  548.5 47.8 %all-gather.41.cloned.1.call-done = bf16[4,256,2048]{2,1,0:T(8,128)(2,1)} async-done(((bf16[1,256,2048]{2,1,0:T(8,128)(2,1)}), bf16[4,256,2048]{2,1,0:T(8,128)(2,1)}) %all-gather.41.cloned.1.call-update) | async-done | bytes 4194320 | tf_op jit(solution)/shard_map/all_gather | solution.py:244
  596.3 23.5 fusion.156
  619.8 57.9 %all-gather.49.cloned.1.call-done = bf16[4,256,2048]{2,1,0:T(8,128)(2,1)} async-done(((bf16[1,256,2048]{2,1,0:T(8,128)(2,1)}), bf16[4,256,2048]{2,1,0:T(8,128)(2,1)}) %all-gather.49.cloned.1.call-update) | async-done | bytes 4194320 | tf_op jit(solution)/shard_map/all_gather | solution.py:260
  677.7 21.9 multiply_convert_fusion.3
  699.6 24.2 fusion.107
  723.8 75.4 %reduce-scatter.35.cloned.1.call-done = bf16[1,256,2048]{2,1,0:T(8,128)(2,1)} async-done(((bf16[4,256,2048]{2,1,0:T(8,128)(2,1)}), bf16[1,256,2048]{2,1,0:T(8,128)(2,1)}) %reduce-scatter.35.cloned.1.call-update) | async-done | bytes 1048592 | tf_op jit(solution)/shard_map/reduce_scatter | solution.py:109
  804.1 81.3 %all-gather.51.cloned.1.call-done = bf16[4,256,2048]{2,1,0:T(8,128)(2,1)} async-done(((bf16[1,256,2048]{2,1,0:T(8,128)(2,1)}), bf16[4,256,2048]{2,1,0:T(8,128)(2,1)}) %all-gather.51.cloned.1.call-update) | async-done | bytes 4194320 | tf_op jit(solution)/shard_map/all_gather | solution.py:286
  885.5 6.2 convolution_convert_fusion.7
  895.8 97.7 %while.50 = (s32[]{:T(128)}, f32[4,256,2,4,64]{1,4,3,2,0:T(8,128)}, f32[4,1024,2,128]{1,3,2,0:T(8,128)}, bf16[4,1024,2,64]{1,3,2,0:T(8,128)(2,1)}, s32[4,256]{1,...) while((s32[]{:T(128)}, f32[4,256,2,4,64]{1,4,3,2,0:T(8,128)}, ...), condition=%wide.region_22.23_spmd, body=%wide.region_20.22_spmd.sunk | while | flops 1374943232 | bytes 95762104 | solution.py:293
  997.7 47.0 %reduce-scatter.37.cloned.1.call-done = f32[4,256,2,128]{1,3,2,0:T(8,128)} async-done(((f32[4,1024,2,128]{1,3,2,0:T(8,128)}), f32[4,256,2,128]{1,3,2,0:T(8,128)}) %reduce-scatter.37.cloned.1.call-update) | async-done | bytes 1048592 | tf_op jit(solution)/shard_map/reduce_scatter | solution.py:306
  1047.4 7.8 convolution_convert_fusion.5
  1063.2 68.9 %reduce-scatter.39.cloned.1.call-done = bf16[1,256,2048]{2,1,0:T(8,128)(2,1)} async-done(((bf16[4,256,2048]{2,1,0:T(8,128)(2,1)}), bf16[1,256,2048]{2,1,0:T(8,128)(2,1)}) %reduce-scatter.39.cloned.1.call-update) | async-done | bytes 1048592 | tf_op jit(solution)/shard_map/reduce_scatter | solution.py:109
  1136.6 81.3 %all-gather.43.cloned.1.call-done = bf16[4,256,2048]{2,1,0:T(8,128)(2,1)} async-done(((bf16[1,256,2048]{2,1,0:T(8,128)(2,1)}), bf16[4,256,2048]{2,1,0:T(8,128)(2,1)}) %all-gather.43.cloned.1.call-update) | async-done | bytes 4194320 | tf_op jit(solution)/shard_map/all_gather | solution.py:200
  1237.3 25.1 all-gather.45.cloned.1.call-done
  1266.6 32.4 %while.49 = (s32[]{:T(128)}, bf16[4,256,512]{1,2,0:T(8,128)(2,1)}, f32[4,2,4,256,1]{3,2,1,4,0:T(4,128)S(1)}, bf16[4,1024,2,64]{1,3,2,0:T(8,128)(2,1)}, s32[4,256...) while((s32[]{:T(128)}, bf16[4,256,512]{1,2,0:T(8,128)(2,1)}, ...), condition=%wide.region_14.15_spmd, body=%wide.region_11.14_spmd.sunk | while | flops 560855040 | bytes 27873392 | solution.py:225
  1299.1 6.6 convolution_convert_fusion.1
  1305.8 13.8 convolution_convert_fusion.2
  1319.8 62.8 %reduce-scatter.31.cloned.1.call-done = bf16[1,256,2048]{2,1,0:T(8,128)(2,1)} async-done(((bf16[4,256,2048]{2,1,0:T(8,128)(2,1)}), bf16[1,256,2048]{2,1,0:T(8,128)(2,1)}) %reduce-scatter.31.cloned.1.call-update) | async-done | bytes 1048592 | tf_op jit(solution)/shard_map/reduce_scatter | solution.py:109
  1385.0 77.9 %reduce-scatter.29.cloned.1.call-done = bf16[1,256,2048]{2,1,0:T(8,128)(2,1)} async-done(((bf16[4,256,2048]{2,1,0:T(8,128)(2,1)}), bf16[1,256,2048]{2,1,0:T(8,128)(2,1)}) %reduce-scatter.29.cloned.1.call-update) | async-done | bytes 1048592 | tf_op jit(solution)/shard_map/reduce_scatter | solution.py:109
  1476.8 73.0 %all-gather.47.cloned.1.call-done = bf16[4,256,2048]{2,1,0:T(8,128)(2,1)} async-done(((bf16[1,256,2048]{2,1,0:T(8,128)(2,1)}), bf16[4,256,2048]{2,1,0:T(8,128)(2,1)}) %all-gather.47.cloned.1.call-update) | async-done | bytes 4194320 | tf_op jit(solution)/shard_map/all_gather | solution.py:244
  1549.7 23.5 fusion.158
  1573.2 57.9 %all-gather.53.cloned.1.call-done = bf16[4,256,2048]{2,1,0:T(8,128)(2,1)} async-done(((bf16[1,256,2048]{2,1,0:T(8,128)(2,1)}), bf16[4,256,2048]{2,1,0:T(8,128)(2,1)}) %all-gather.53.cloned.1.call-update) | async-done | bytes 4194320 | tf_op jit(solution)/shard_map/all_gather | solution.py:260
  1631.1 21.8 multiply_convert_fusion.1
  1652.9 24.2 fusion.108
  1677.2 75.4 %reduce-scatter.41.cloned.1.call-done = bf16[1,256,2048]{2,1,0:T(8,128)(2,1)} async-done(((bf16[4,256,2048]{2,1,0:T(8,128)(2,1)}), bf16[1,256,2048]{2,1,0:T(8,128)(2,1)}) %reduce-scatter.41.cloned.1.call-update) | async-done | bytes 1048592 | tf_op jit(solution)/shard_map/reduce_scatter | solution.py:109
  1757.5 81.3 %all-gather.55.cloned.1.call-done = bf16[4,256,2048]{2,1,0:T(8,128)(2,1)} async-done(((bf16[1,256,2048]{2,1,0:T(8,128)(2,1)}), bf16[4,256,2048]{2,1,0:T(8,128)(2,1)}) %all-gather.55.cloned.1.call-update) | async-done | bytes 4194320 | tf_op jit(solution)/shard_map/all_gather | solution.py:286
  1849.2 83.0 %while.51 = (s32[]{:T(128)}, f32[4,256,2,4,64]{1,4,3,2,0:T(8,128)}, f32[4,1024,2,128]{1,3,2,0:T(8,128)}, bf16[4,1024,2,64]{1,3,2,0:T(8,128)(2,1)S(1)}, s32[4,256...) while((s32[]{:T(128)}, f32[4,256,2,4,64]{1,4,3,2,0:T(8,128)}, ...), condition=%wide.region_30.31_spmd, body=%wide.region_28.30_spmd.sunk | while | flops 1374943232 | bytes 95761592 | solution.py:293
  1942.5 6.7 reshape.731
  1956.2 8.3 fusion.134
  1967.1 16.4 reduce-scatter.43.cloned.1.call-done
  1986.1 7.9 bitcast_add_fusion.2
  1997.7 16.7 fusion.160
  2014.5 17.2 bitcast_add_fusion.1
  2031.7 16.5 copy.268
  2048.7 26.8 fusion.105
  2075.5 32.7 %bitcast_add_fusion = f32[2048,4096]{1,0:T(8,128)} fusion(f32[2048,4096,1]{1,0,2:T(8,128)} %fusion.105, bf16[4,256,2048]{2,1,0:T(8,128)(2,1)} %all-gather.47.cloned.1.call-done, bf16[4,256,2048]{2,1,0:T(8,128)(2,1)} %get-tuple-element.465, bf16[4,256,2048]{2,1,0:T(8,128)(2,1)} %get-tuple-element.464), kind=kOutput, calls=%fused_computation.142 | convolution fusion | flops 17205035008 | bytes 79691776 | tf_op jit(solution)/shard_map/std,stf->df/dot_general | solution.py:274
  2108.2 22.9 copy.314
  2133.2 41.5 %reduce-scatter.51.cloned.1.call-done = f32[1,4,256,4096]{3,2,1,0:T(8,128)} async-done(((f32[2,4,256,4096]{3,2,1,0:T(8,128)}), f32[1,4,256,4096]{3,2,1,0:T(8,128)}) %reduce-scatter.51.cloned.1.call-update) | async-done | bytes 16777232 | tf_op jit(solution)/shard_map/reduce_scatter | solution.py:130
  2174.7 6.9 convolution_convert_fusion.4
  2181.8 13.8 convolution_convert_fusion
  2195.7 18.4 reduce-scatter.57.cloned.1.call-done
  2214.2 46.9 %reduce-scatter.55.cloned.1.call-done = f32[1,256,768]{2,1,0:T(8,128)} async-done(((f32[4,256,768]{2,1,0:T(8,128)}), f32[1,256,768]{2,1,0:T(8,128)}) %reduce-scatter.55.cloned.1.call-update) | async-done | bytes 786448
  2261.1 89.2 %reduce-scatter.61.cloned.1.call-done = f32[2048,1,256]{2,0,1:T(8,128)} async-done(((f32[2048,4,256]{2,0,1:T(8,128)}), f32[2048,1,256]{2,0,1:T(8,128)}) %reduce-scatter.61.cloned.1.call-update) | async-done | bytes 2097168
  2350.4 156.8 %reduce-scatter.59.cloned.1.call-done = f32[1,256,4096]{2,1,0:T(8,128)} async-done(((f32[4,256,4096]{2,1,0:T(8,128)}), f32[1,256,4096]{2,1,0:T(8,128)}) %reduce-scatter.59.cloned.1.call-update) | async-done | bytes 4194320
  2512.4 74.5 %reduce-scatter.45.cloned.1.call-done = bf16[1,256,2048]{2,1,0:T(8,128)(2,1)} async-done(((bf16[4,256,2048]{2,1,0:T(8,128)(2,1)}), bf16[1,256,2048]{2,1,0:T(8,128)(2,1)}) %reduce-scatter.45.cloned.1.call-update) | async-done | bytes 1048592 | tf_op jit(solution)/shard_map/reduce_scatter | solution.py:109
  2588.8 78.1 %reduce-scatter.33.cloned.1.call-done = bf16[1,256,2048]{2,1,0:T(8,128)(2,1)} async-done(((bf16[4,256,2048]{2,1,0:T(8,128)(2,1)}), bf16[1,256,2048]{2,1,0:T(8,128)(2,1)}) %reduce-scatter.33.cloned.1.call-update) | async-done | bytes 1048592 | tf_op jit(solution)/shard_map/reduce_scatter | solution.py:109
  2696.0 8.6 all-to-all-done.1
  2709.6 80.7 %psum.7 = f32[2,2048]{1,0:T(2,128)S(1)} all-reduce(f32[2,2048]{1,0:T(2,128)S(1)} %pad_maximum_fusion.26), channel_id=1, replica_groups=mesh['dp'=2,'row'=4,'col'=4] {'dp','row','col'}, use_global_device_ids=true, to_apply=%region_46.47 | all-reduce | flops 4096 | bytes 32768 | tf_op jit(solution)/shard_map/psum | solution.py:343
  2801.2 8.1 fusion.149
  (586 shorter events, 504.8 us)
Async XLA Ops:
  7.2 186.7 %copy-start = (bf16[2048,512]{1,0:T(8,128)(2,1)S(1)}, bf16[2048,512]{1,0:T(8,128)(2,1)}, u32[]{:S(2)}) copy-start(bf16[2048,512]{1,0:T(8,128)(2,1)} %param.28) | copy-start | bytes 6291460
  7.2 36.8 %all-gather.57.cloned.1.call-start = ((), (), s32[]{:S(2)}) async-start(), calls=%async_computation.46 | async-start | bytes 1966080 | tf_op jit(solution)/shard_map/all_gather | solution.py:118
  9.2 101.7 %all-gather.61.cloned.1.call-start = ((), (), s32[]{:S(2)}) async-start(), calls=%async_computation.48 | async-start | bytes 1310720 | tf_op jit(solution)/shard_map/all_gather | solution.py:118
  11.1 104.2 %all-gather.59.cloned.1.call-start = ((), (), s32[]{:S(2)}) async-start(), calls=%async_computation.47 | async-start | bytes 4718592 | tf_op jit(solution)/shard_map/all_gather | solution.py:119
  47.1 37.1 %all-to-all-start = ((bf16[2,1,4,256,1,512]{5,3,0,4,1,2:T(8,128)(2,1)}), bf16[2,1,4,256,1,512]{5,3,0,4,1,2:T(8,128)(2,1)}, u32[]{:S(2)}, u32[]{:S(2)}) async-start(bf16[2,1,4,256,1,512]{5,3,0,4,1,2:T(8,128)(2,1)} %copy.221), calls=%async_computation | async-start | bytes 4194304 | tf_op jit(solution)/shard_map/all_to_all | solution.py:137
  51.6 131.4 %all-gather.37.cloned.1.call-start = ((), (), s32[]{:S(2)}) async-start(), calls=%async_computation.22 | async-start | bytes 5242880 | tf_op jit(solution)/shard_map/all_gather | solution.py:200
  100.0 100.5 %all-gather.63.cloned.1.call-start = ((), (), s32[]{:S(2)}) async-start(), calls=%async_computation.49 | async-start | bytes 3145728 | tf_op jit(solution)/shard_map/all_gather | solution.py:119
  113.2 119.3 %all-gather.39.cloned.1.call-start = ((), (), s32[]{:S(2)}) async-start(), calls=%async_computation.23 | async-start | bytes 2621440 | tf_op jit(solution)/shard_map/all_gather | solution.py:218
  115.3 96.9 %copy-start.24 = (f32[4,256,32]{1,2,0:T(8,128)}, f32[4,256,32]{1,2,0:T(8,128)S(1)}, u32[]{:S(2)}) copy-start(f32[4,256,32]{1,2,0:T(8,128)S(1)} %get-tuple-element.512) | copy-start | bytes 393220
  193.8 93.7 %all-gather.69.cloned.1.call-start = ((), (), s32[]{:S(2)}) async-start(), calls=%async_computation.52 | async-start | bytes 5242880 | tf_op jit(solution)/shard_map/all_gather | solution.py:118
  195.4 182.1 %all-gather.65.cloned.1.call-start = ((), (), s32[]{:S(2)}) async-start(), calls=%async_computation.50 | async-start | bytes 10485760 | tf_op jit(solution)/shard_map/all_gather | solution.py:118
  198.7 258.5 %reduce-scatter.27.cloned.1.call-start = ((), (), s32[]{:S(2)}) async-start(), calls=%async_computation.24 | async-start | bytes 5242880 | tf_op jit(solution)/shard_map/reduce_scatter | solution.py:109
  272.1 231.0 %all-gather.71.cloned.1.call-start = ((), (), s32[]{:S(2)}) async-start(), calls=%async_computation.53 | async-start | bytes 12582912 | tf_op jit(solution)/shard_map/all_gather | solution.py:119
  293.7 240.6 %all-gather.67.cloned.1.call-start = ((), (), s32[]{:S(2)}) async-start(), calls=%async_computation.51 | async-start | bytes 25165824 | tf_op jit(solution)/shard_map/all_gather | solution.py:119
  377.5 79.7 %copy-start.2 = (f32[1,256,2048]{2,1,0:T(8,128)S(1)}, f32[1,256,2048]{2,1,0:T(8,128)}, u32[]{:S(2)}) copy-start(f32[1,256,2048]{2,1,0:T(8,128)} %reshape.734) | copy-start | bytes 6291460
  377.5 218.8 %all-gather.41.cloned.1.call-start = ((), (), s32[]{:S(2)}) async-start(), calls=%async_computation.25 | async-start | bytes 5242880 | tf_op jit(solution)/shard_map/all_gather | solution.py:244
  386.4 415.8 %copy-start.36 = (f32[4,1,512]{2,1,0:T(1,128)}, f32[4,1,512]{2,1,0:T(1,128)S(1)}, u32[]{:S(2)}) copy-start(f32[4,1,512]{2,1,0:T(1,128)S(1)} %all-gather.13) | copy-start | bytes 24580
  458.8 343.3 %copy-start.51 = (f32[256]{0:T(256)}, f32[256]{0:T(256)S(1)}, u32[]{:S(2)}) copy-start(f32[256]{0:T(256)S(1)} %add_rsqrt_fusion.2) | copy-start | bytes 3076
  461.4 216.2 %all-gather.49.cloned.1.call-start = ((), (), s32[]{:S(2)}) async-start(), calls=%async_computation.32 | async-start | bytes 5242880 | tf_op jit(solution)/shard_map/all_gather | solution.py:260
  503.1 296.1 %reduce-scatter.35.cloned.1.call-start = ((), (), s32[]{:S(2)}) async-start(), calls=%async_computation.33 | async-start | bytes 5242880 | tf_op jit(solution)/shard_map/reduce_scatter | solution.py:109
  723.8 161.7 %all-gather.51.cloned.1.call-start = ((), (), s32[]{:S(2)}) async-start(), calls=%async_computation.34 | async-start | bytes 5242880 | tf_op jit(solution)/shard_map/all_gather | solution.py:286
  804.1 240.6 %reduce-scatter.37.cloned.1.call-start = ((), (), s32[]{:S(2)}) async-start(), calls=%async_computation.35 | async-start | bytes 5242880 | tf_op jit(solution)/shard_map/reduce_scatter | solution.py:306
  993.5 138.7 %reduce-scatter.39.cloned.1.call-start = ((), (), s32[]{:S(2)}) async-start(), calls=%async_computation.36 | async-start | bytes 5242880 | tf_op jit(solution)/shard_map/reduce_scatter | solution.py:109
  1055.2 162.8 %all-gather.43.cloned.1.call-start = ((), (), s32[]{:S(2)}) async-start(), calls=%async_computation.27 | async-start | bytes 5242880 | tf_op jit(solution)/shard_map/all_gather | solution.py:200
  1063.2 160.9 %copy-start.56 = (f32[256]{0:T(256)}, f32[256]{0:T(256)S(1)}, u32[]{:S(2)}) copy-start(f32[256]{0:T(256)S(1)} %add_rsqrt_fusion.1) | copy-start | bytes 3076
  1136.6 91.3 %copy-start.22 = (f32[4,256,32]{1,2,0:T(8,128)S(1)}, f32[4,256,32]{1,2,0:T(8,128)}, u32[]{:S(2)}) copy-start(f32[4,256,32]{1,2,0:T(8,128)} %get-tuple-element.517) | copy-start | bytes 393220
  1136.6 91.3 %copy-start.30 = (f32[4,256,32]{1,2,0:T(8,128)S(1)}, f32[4,256,32]{1,2,0:T(8,128)}, u32[]{:S(2)}) copy-start(f32[4,256,32]{1,2,0:T(8,128)} %get-tuple-element.516) | copy-start | bytes 393220
  1136.6 125.9 %all-gather.45.cloned.1.call-start = ((), (), s32[]{:S(2)}) async-start(), calls=%async_computation.28 | async-start | bytes 2621440 | tf_op jit(solution)/shard_map/all_gather | solution.py:218
  1228.8 153.9 %reduce-scatter.31.cloned.1.call-start = ((), (), s32[]{:S(2)}) async-start(), calls=%async_computation.29 | async-start | bytes 5242880 | tf_op jit(solution)/shard_map/reduce_scatter | solution.py:109
  1305.7 157.1 %reduce-scatter.29.cloned.1.call-start = ((), (), s32[]{:S(2)}) async-start(), calls=%async_computation.26 | async-start | bytes 5242880 | tf_op jit(solution)/shard_map/reduce_scatter | solution.py:109
  1319.6 143.3 %copy-start.9 = (bf16[1,256,2048]{2,1,0:T(8,128)(2,1)S(1)}, bf16[1,256,2048]{2,1,0:T(8,128)(2,1)}, u32[]{:S(2)}) copy-start(bf16[1,256,2048]{2,1,0:T(8,128)(2,1)} %reduce-scatter.27.cloned.1.call-done) | copy-start | bytes 3145732
  1319.6 143.3 %copy-start.37 = (f32[4,1,512]{2,1,0:T(1,128)S(1)}, f32[4,1,512]{2,1,0:T(1,128)}, u32[]{:S(2)}) copy-start(f32[4,1,512]{2,1,0:T(1,128)} %copy-done.36) | copy-start | bytes 24580
  1319.6 143.3 %copy-start.52 = (f32[256]{0:T(256)S(1)}, f32[256]{0:T(256)}, u32[]{:S(2)}) copy-start(f32[256]{0:T(256)} %copy-done.51) | copy-start | bytes 3076
  1319.6 143.3 %copy-start.63 = (f32[256]{0:T(256)S(1)}, f32[256]{0:T(256)}, u32[]{:S(2)}) copy-start(f32[256]{0:T(256)} %copy-done.62) | copy-start | bytes 3076
  1319.6 230.1 %all-gather.47.cloned.1.call-start = ((), (), s32[]{:S(2)}) async-start(), calls=%async_computation.30 | async-start | bytes 5242880 | tf_op jit(solution)/shard_map/all_gather | solution.py:244
  1385.0 370.6 %copy-start.53 = (f32[256]{0:T(256)}, f32[256]{0:T(256)S(1)}, u32[]{:S(2)}) copy-start(f32[256]{0:T(256)S(1)} %add_rsqrt_fusion) | copy-start | bytes 3076
  1468.3 162.8 %all-gather.53.cloned.1.call-start = ((), (), s32[]{:S(2)}) async-start(), calls=%async_computation.37 | async-start | bytes 5242880 | tf_op jit(solution)/shard_map/all_gather | solution.py:260
  1475.3 97.9 %copy-start.5 = (f32[1,256,2048]{2,1,0:T(8,128)}, f32[1,256,2048]{2,1,0:T(8,128)S(1)}, u32[]{:S(2)}) copy-start(f32[1,256,2048]{2,1,0:T(8,128)S(1)} %reshape.737) | copy-start | bytes 6291460
  1476.7 275.9 %reduce-scatter.41.cloned.1.call-start = ((), (), s32[]{:S(2)}) async-start(), calls=%async_computation.38 | async-start | bytes 5242880 | tf_op jit(solution)/shard_map/reduce_scatter | solution.py:109
  1677.2 161.7 %all-gather.55.cloned.1.call-start = ((), (), s32[]{:S(2)}) async-start(), calls=%async_computation.39 | async-start | bytes 5242880 | tf_op jit(solution)/shard_map/all_gather | solution.py:286
  1757.5 226.0 %reduce-scatter.43.cloned.1.call-start = ((), (), s32[]{:S(2)}) async-start(), calls=%async_computation.40 | async-start | bytes 5242880 | tf_op jit(solution)/shard_map/reduce_scatter | solution.py:306
  1932.3 198.9 %reduce-scatter.49.cloned.1.call-start = ((), (), s32[]{:S(2)}) async-start(), calls=%async_computation.43 | async-start | bytes 6291456 | tf_op jit(solution)/shard_map/reduce_scatter | solution.py:130
  1954.9 177.0 %reduce-scatter.47.cloned.1.call-start = ((), (), s32[]{:S(2)}) async-start(), calls=%async_computation.42 | async-start | bytes 9437184 | tf_op jit(solution)/shard_map/reduce_scatter | solution.py:130
  1997.5 135.1 %reduce-scatter.53.cloned.1.call-start = ((), (), s32[]{:S(2)}) async-start(), calls=%async_computation.45 | async-start | bytes 25165824 | tf_op jit(solution)/shard_map/reduce_scatter | solution.py:130
  2048.2 126.4 %reduce-scatter.51.cloned.1.call-start = ((), (), s32[]{:S(2)}) async-start(), calls=%async_computation.44 | async-start | bytes 50331648 | tf_op jit(solution)/shard_map/reduce_scatter | solution.py:130
  2131.1 83.0 %reduce-scatter.57.cloned.1.call-start = ((), (), s32[]{:S(2)}) async-start(), calls=%async_computation.59 | async-start | bytes 2621440
  2131.8 129.2 %reduce-scatter.55.cloned.1.call-start = ((), (), s32[]{:S(2)}) async-start(), calls=%async_computation.58 | async-start | bytes 3932160
  2132.5 217.8 %reduce-scatter.61.cloned.1.call-start = ((), (), s32[]{:S(2)}) async-start(), calls=%async_computation.61 | async-start | bytes 10485760
  2133.1 374.0 %reduce-scatter.59.cloned.1.call-start = ((), (), s32[]{:S(2)}) async-start(), calls=%async_computation.60 | async-start | bytes 20971520
  2174.6 412.2 %reduce-scatter.45.cloned.1.call-start = ((), (), s32[]{:S(2)}) async-start(), calls=%async_computation.41 | async-start | bytes 5242880 | tf_op jit(solution)/shard_map/reduce_scatter | solution.py:109
  2181.6 485.3 %reduce-scatter.33.cloned.1.call-start = ((), (), s32[]{:S(2)}) async-start(), calls=%async_computation.31 | async-start | bytes 5242880 | tf_op jit(solution)/shard_map/reduce_scatter | solution.py:109
  2195.7 513.9 %all-gather.75.cloned.1.call-start = ((), (), s32[]{:S(2)}) async-start(), calls=%async_computation.55 | async-start | bytes 1572864 | tf_op jit(solution)/shard_map/all_gather | solution.py:132
  2214.1 582.9 %all-gather.73.cloned.1.call-start = ((), (), s32[]{:S(2)}) async-start(), calls=%async_computation.54 | async-start | bytes 2359296 | tf_op jit(solution)/shard_map/all_gather | solution.py:132
  2261.1 540.1 %all-gather.79.cloned.1.call-start = ((), (), s32[]{:S(2)}) async-start(), calls=%async_computation.57 | async-start | bytes 6291456 | tf_op jit(solution)/shard_map/all_gather | solution.py:132
  2350.3 450.8 %all-gather.77.cloned.1.call-start = ((), (), s32[]{:S(2)}) async-start(), calls=%async_computation.56 | async-start | bytes 12582912 | tf_op jit(solution)/shard_map/all_gather | solution.py:132
  2507.1 79.7 %copy-start.4 = (f32[1,256,2048]{2,1,0:T(8,128)S(1)}, f32[1,256,2048]{2,1,0:T(8,128)}, u32[]{:S(2)}) copy-start(f32[1,256,2048]{2,1,0:T(8,128)} %reshape.735) | copy-start | bytes 6291460
  2507.1 79.7 %copy-start.41 = (f32[4,1,512]{2,1,0:T(1,128)S(1)}, f32[4,1,512]{2,1,0:T(1,128)}, u32[]{:S(2)}) copy-start(f32[4,1,512]{2,1,0:T(1,128)} %copy-done.39) | copy-start | bytes 24580
  2507.1 79.7 %copy-start.57 = (f32[256]{0:T(256)S(1)}, f32[256]{0:T(256)}, u32[]{:S(2)}) copy-start(f32[256]{0:T(256)} %copy-done.56) | copy-start | bytes 3076
  2507.2 159.7 %copy-start.11 = (bf16[1,256,2048]{2,1,0:T(8,128)(2,1)S(1)}, bf16[1,256,2048]{2,1,0:T(8,128)(2,1)}, u32[]{:S(2)}) copy-start(bf16[1,256,2048]{2,1,0:T(8,128)(2,1)} %reduce-scatter.31.cloned.1.call-done) | copy-start | bytes 3145732
  2507.2 159.7 %copy-start.38 = (f32[4,1,512]{2,1,0:T(1,128)S(1)}, f32[4,1,512]{2,1,0:T(1,128)}, u32[]{:S(2)}) copy-start(f32[4,1,512]{2,1,0:T(1,128)} %copy-done.36) | copy-start | bytes 24580
  2507.2 159.7 %copy-start.54 = (f32[256]{0:T(256)S(1)}, f32[256]{0:T(256)}, u32[]{:S(2)}) copy-start(f32[256]{0:T(256)} %copy-done.53) | copy-start | bytes 3076
  2507.2 159.7 %copy-start.61 = (f32[256]{0:T(256)S(1)}, f32[256]{0:T(256)}, u32[]{:S(2)}) copy-start(f32[256]{0:T(256)} %copy-done.60) | copy-start | bytes 3076
  2676.2 28.4 %all-to-all-start.1 = ((bf16[2,1,1,256,4,512]{5,3,2,1,0,4:T(8,128)(2,1)}), bf16[2,1,1,256,4,512]{5,3,2,1,0,4:T(8,128)(2,1)S(1)}, u32[]{:S(2)}, u32[]{:S(2)}) async-start(bf16[2,1,1,256,4,512]{5,3,2,1,0,4:T(8,128)(2,1)} %pad_maximum_fusion.11), calls=%async_computation.5 | async-start | bytes 4194304 | tf_op jit(solution)/shard_map/all_to_all | solution.py:143
  2704.6 87.8 %all-to-all-start.3 = ((f32[2,1,1,256,4,512]{5,3,2,1,0,4:T(8,128)}), f32[2,1,1,256,4,512]{5,3,2,1,0,4:T(8,128)}, u32[]{:S(2)}, u32[]{:S(2)}) async-start(f32[2,1,1,256,4,512]{5,3,2,1,0,4:T(8,128)} %pad_maximum_fusion.6), calls=%async_computation.13 | async-start | bytes 8388608 | tf_op jit(solution)/shard_map/all_to_all | solution.py:143
  (65 other events, 708.7 us)
Sparse Core Ops, SparseCore 0:
  10.4 33.5 all-gather.56
  46.4 38.8 all-gather.60
  86.8 12.1 all-gather.58
  101.0 81.8 all-gather.36
  184.9 9.0 all-gather.62
  196.3 36.2 all-gather.38
  234.9 52.5 all-gather.68
  290.0 87.4 all-gather.64
  380.3 76.7 reduce-scatter.26
  459.1 20.3 all-gather.70
  481.1 31.2 all-gather.66
  514.3 81.9 all-gather.40
  598.4 79.2 all-gather.48
  723.9 75.2 reduce-scatter.34
  804.2 81.2 all-gather.50
  993.6 51.0 reduce-scatter.36
  1055.3 76.7 reduce-scatter.38
  1136.7 81.2 all-gather.42
  1228.9 33.5 all-gather.44
  1305.8 76.7 reduce-scatter.30
  1385.5 77.2 reduce-scatter.28
  1468.4 81.2 all-gather.46
  1551.9 79.2 all-gather.52
  1677.3 75.2 reduce-scatter.40
  1757.6 81.2 all-gather.54
  1932.4 51.0 reduce-scatter.42
  1985.6 12.0 reduce-scatter.48
  2000.0 15.3 reduce-scatter.46
  2048.3 25.7 reduce-scatter.52
  2131.2 43.3 reduce-scatter.50
  2177.6 36.4 reduce-scatter.56
  2217.1 43.8 reduce-scatter.54
  2263.9 86.3 reduce-scatter.60
  2353.4 153.7 reduce-scatter.58
  2510.0 76.7 reduce-scatter.44
  2589.5 77.3 reduce-scatter.32
  2668.3 9.5 all-gather.74
  2679.4 10.9 all-gather.72
  2691.8 14.8 all-gather.78
  2708.2 21.0 all-gather.76

commit v3 on v2

--- a/solution.py
+++ b/solution.py
@@ -112,24 +112,34 @@
 
 
 def make_shards(n_dp, n_row, n_col):
-    def gather_features(block, axis):
+    assert n_row == n_col
+    transpose_pairs = [
+        (a * n_col + b, b * n_col + a) for a in range(n_row) for b in range(n_col)
+    ]
+
+    def gather_features(block, axis, axis_name):
+        count = n_row if axis_name == "row" else n_col
         half = block.shape[axis] // n_dp
         mine = lax.dynamic_slice_in_dim(block, lax.axis_index("dp") * half, half, axis=axis)
-        gathered = lax.all_gather(mine, "row", axis=axis)
+        gathered = lax.all_gather(mine, axis_name, axis=axis)
         gathered = lax.all_gather(gathered, "dp", axis=axis)
         gathered = jnp.swapaxes(gathered, axis, axis + 1)
         shape = list(block.shape)
-        shape[axis] = block.shape[axis] * n_row
+        shape[axis] = block.shape[axis] * count
         return gathered.reshape(shape)
 
-    def reduce_features(partial, axis):
-        half = partial.shape[axis] // (n_row * n_dp)
+    def reduce_features(partial, axis, axis_name):
+        count = n_row if axis_name == "row" else n_col
+        half = partial.shape[axis] // (count * n_dp)
         shape = list(partial.shape)
-        shape[axis : axis + 1] = [n_row, n_dp, half]
+        shape[axis : axis + 1] = [count, n_dp, half]
         split = jnp.swapaxes(partial.reshape(shape), axis, axis + 1)
         split = lax.psum_scatter(split, "dp", scatter_dimension=axis)
-        split = lax.psum_scatter(split, "row", scatter_dimension=axis)
+        split = lax.psum_scatter(split, axis_name, scatter_dimension=axis)
         return lax.all_gather(split, "dp", axis=axis, tiled=True)
+
+    def transpose_grid(block):
+        return lax.ppermute(block, ("row", "col"), transpose_pairs)
 
     def to_tokens(rows):
         batches, local, seq_len, width = rows.shape
@@ -160,32 +170,35 @@
         batches, local, seq_len, width_r = hidden_in.shape
         chunk = seq_len // n_row
         row_index = lax.axis_index("row")
+        col_index = lax.axis_index("col")
         query_cols = w_query.shape[1]
         key_cols = w_key.shape[1]
+        key_end = query_cols + key_cols
+        qkv_cols = key_end + w_value.shape[1]
         heads_q = query_cols // HD
         heads_k = key_cols // HD
         group_count = heads_q // heads_k
         ffn_cols = w_gate.shape[1]
 
-        w_qkv = gather_features(jnp.concatenate([w_query, w_key, w_value], axis=1), 0)
-        w_pair = gather_features(jnp.concatenate([w_gate, w_up], axis=1), 0)
-        w_out_all = gather_features(w_out, 1)
-        w_down_all = gather_features(w_down, 1)
+        w_attn = gather_features(
+            transpose_grid(jnp.concatenate([w_query, w_key, w_value, w_out.T], axis=1)), 0, "col"
+        )
+        w_qkv = w_attn[:, :qkv_cols]
+        w_out_heads = w_attn[:, qkv_cols:].T
+        w_pair = gather_features(jnp.concatenate([w_gate, w_up], axis=1), 0, "row")
+        w_down_all = gather_features(w_down, 1, "row")
         gain_attn_all = lax.all_gather(gain_attn, "row", tiled=True)
         gain_ffn_all = lax.all_gather(gain_ffn, "row", tiled=True)
 
         segments = lax.all_gather(segment_ids, "row", axis=1, tiled=True)
+        segments = lax.dynamic_slice_in_dim(segments, col_index * local, local, axis=1)
         places = positions(segments)
-        query_segments = lax.dynamic_slice_in_dim(segments, row_index * chunk, chunk, axis=2)
-        query_places_seq = lax.dynamic_slice_in_dim(places, row_index * chunk, chunk, axis=2)
-        query_index = row_index * chunk + jnp.arange(chunk)
-        seq_all = segments.shape[1]
+        token_place = jnp.broadcast_to(jnp.arange(seq_len), (local, seq_len))
 
         hidden_t = to_tokens(hidden_in)
         cotangent_t = to_tokens(cotangent)
 
-        grad_qkv_w = None
-        grad_out_w = None
+        grad_attn_w = None
         grad_pair_w = None
         grad_down_w = None
         gain_attn_total = jnp.zeros(gain_attn_all.shape, jnp.float32)
@@ -197,46 +210,38 @@
             inv_attn = lax.rsqrt(jnp.mean(rows_f * rows_f, axis=-1, keepdims=True) + EPSILON)
             norm_attn = rows_f * inv_attn
             normed_attn = (norm_attn * gain_attn_all).astype(jnp.bfloat16)
-            spread_attn = lax.all_gather(normed_attn, "col", axis=0, tiled=True)
+            spread_attn = lax.all_gather(normed_attn, "row", axis=1, tiled=True)
             qkv = jnp.einsum(
                 "std,dm->stm", spread_attn, w_qkv, preferred_element_type=jnp.float32
             )
-            cosine, sine_part = rotary(query_places_seq[batch_index])
+            cosine, sine_part = rotary(places[batch_index])
             query_rot = rotate(
-                qkv[..., :query_cols].reshape(seq_all, chunk, heads_q, HD), cosine, sine_part
+                qkv[..., :query_cols].reshape(local, seq_len, heads_q, HD), cosine, sine_part
             ).astype(jnp.bfloat16)
-            key_rot = rotate(
-                qkv[..., query_cols : query_cols + key_cols].reshape(seq_all, chunk, heads_k, HD),
+            key_all = rotate(
+                qkv[..., query_cols:key_end].reshape(local, seq_len, heads_k, HD),
                 cosine,
                 sine_part,
             ).astype(jnp.bfloat16)
-            value_low = (
-                qkv[..., query_cols + key_cols :]
-                .reshape(seq_all, chunk, heads_k, HD)
-                .astype(jnp.bfloat16)
-            )
-            key_value = lax.all_gather(
-                jnp.concatenate([key_rot, value_low], axis=-1), "row", axis=1, tiled=True
-            )
-            key_all = key_value[..., :HD]
-            value_all = key_value[..., HD:]
-            query_grouped = query_rot.reshape(seq_all, chunk, heads_k, group_count, HD)
-            query_place = jnp.broadcast_to(query_index, (seq_all, chunk))
+            value_all = (
+                qkv[..., key_end:].reshape(local, seq_len, heads_k, HD).astype(jnp.bfloat16)
+            )
+            query_grouped = query_rot.reshape(local, seq_len, heads_k, group_count, HD)
             mixed, log_total = lax.map(
                 attend_forward,
                 (
                     query_grouped,
                     key_all,
                     value_all,
-                    query_segments[batch_index],
                     segments[batch_index],
-                    query_place,
+                    segments[batch_index],
+                    token_place,
                 ),
             )
             attn_part = jnp.einsum(
-                "stm,md->std", mixed, w_out_all, preferred_element_type=jnp.float32
-            )
-            attn_branch = scatter_low(attn_part, "col", 0)
+                "stm,md->std", mixed, w_out_heads, preferred_element_type=jnp.float32
+            )
+            attn_branch = scatter_low(attn_part, "row", 1)
             resid_mid = rows_f + RESIDUAL_SCALE * attn_branch
             inv_ffn = lax.rsqrt(jnp.mean(resid_mid * resid_mid, axis=-1, keepdims=True) + EPSILON)
             norm_ffn = resid_mid * inv_ffn
@@ -283,14 +288,14 @@
             inner_ffn = jnp.mean(scaled_ffn * norm_ffn, axis=-1, keepdims=True)
             grad_mid = grad_rows + inv_ffn * (scaled_ffn - norm_ffn * inner_ffn)
             grad_attn = (RESIDUAL_SCALE * grad_mid).astype(jnp.bfloat16)
-            spread_grad_attn = lax.all_gather(grad_attn, "col", axis=0, tiled=True)
+            spread_grad_attn = lax.all_gather(grad_attn, "row", axis=1, tiled=True)
             fresh_out = jnp.einsum(
-                "stm,std->md", mixed, spread_grad_attn, preferred_element_type=jnp.float32
+                "std,stm->dm", spread_grad_attn, mixed, preferred_element_type=jnp.float32
             )
             grad_mixed = jnp.einsum(
-                "std,md->stm", spread_grad_attn, w_out_all, preferred_element_type=jnp.float32
+                "std,md->stm", spread_grad_attn, w_out_heads, preferred_element_type=jnp.float32
             ).astype(jnp.bfloat16)
-            grad_query_rot, grad_kv_part = lax.map(
+            grad_query_rot, grad_kv = lax.map(
                 attend_backward,
                 (
                     grad_mixed,
@@ -298,21 +303,20 @@
                     key_all,
                     value_all,
                     log_total,
-                    query_segments[batch_index],
                     segments[batch_index],
-                    query_place,
+                    segments[batch_index],
+                    token_place,
                 ),
             )
-            grad_kv = lax.psum_scatter(grad_kv_part, "row", scatter_dimension=1, tiled=True)
             grad_query = rotate(
-                grad_query_rot.reshape(seq_all, chunk, heads_q, HD), cosine, -sine_part
+                grad_query_rot.reshape(local, seq_len, heads_q, HD), cosine, -sine_part
             )
             grad_key = rotate(grad_kv[..., :HD], cosine, -sine_part)
             grad_qkv = jnp.concatenate(
                 [
-                    grad_query.reshape(seq_all, chunk, -1),
-                    grad_key.reshape(seq_all, chunk, -1),
-                    grad_kv[..., HD:].reshape(seq_all, chunk, -1),
+                    grad_query.reshape(local, seq_len, -1),
+                    grad_key.reshape(local, seq_len, -1),
+                    grad_kv[..., HD:].reshape(local, seq_len, -1),
                 ],
                 axis=-1,
             ).astype(jnp.bfloat16)
@@ -322,36 +326,34 @@
             grad_normed_attn_part = jnp.einsum(
                 "stm,dm->std", grad_qkv, w_qkv, preferred_element_type=jnp.float32
             )
-            grad_normed_attn = scatter_low(grad_normed_attn_part, "col", 0)
+            grad_normed_attn = scatter_low(grad_normed_attn_part, "row", 1)
             scaled_attn = grad_normed_attn * gain_attn_all
             gain_attn_total = gain_attn_total + jnp.sum(grad_normed_attn * norm_attn, axis=(0, 1))
             inner_attn = jnp.mean(scaled_attn * norm_attn, axis=-1, keepdims=True)
             inputs_grad.append(grad_mid + inv_attn * (scaled_attn - norm_attn * inner_attn))
-            if grad_qkv_w is None:
-                grad_qkv_w, grad_out_w = fresh_qkv, fresh_out
+            fresh_attn = jnp.concatenate([fresh_qkv, fresh_out], axis=1)
+            if grad_attn_w is None:
+                grad_attn_w = fresh_attn
                 grad_pair_w, grad_down_w = fresh_pair, fresh_down
             else:
-                grad_qkv_w = grad_qkv_w + fresh_qkv
-                grad_out_w = grad_out_w + fresh_out
+                grad_attn_w = grad_attn_w + fresh_attn
                 grad_pair_w = grad_pair_w + fresh_pair
                 grad_down_w = grad_down_w + fresh_down
 
-        total_pair = reduce_features(grad_pair_w, 0)
-        total_down = reduce_features(grad_down_w, 1)
-        total_qkv = reduce_features(grad_qkv_w, 0)
-        total_out = reduce_features(grad_out_w, 1)
+        total_pair = reduce_features(grad_pair_w, 0, "row")
+        total_down = reduce_features(grad_down_w, 1, "row")
+        total_attn = transpose_grid(reduce_features(grad_attn_w, 0, "col"))
         gain_totals = lax.psum(
             jnp.stack([gain_attn_total, gain_ffn_total]), ("dp", "row", "col")
         )
         gain_totals = lax.dynamic_slice_in_dim(gain_totals, row_index * width_r, width_r, axis=1)
-        key_end = query_cols + key_cols
         return (
             to_features(jnp.stack(outs_list)),
             to_features(jnp.stack(inputs_grad)),
-            total_qkv[:, :query_cols],
-            total_qkv[:, query_cols:key_end],
-            total_qkv[:, key_end:],
-            total_out,
+            total_attn[:, :query_cols],
+            total_attn[:, query_cols:key_end],
+            total_attn[:, key_end:qkv_cols],
+            total_attn[:, qkv_cols:].T,
             total_pair[:, :ffn_cols],
             total_pair[:, ffn_cols:],
             total_down,

time: 2830 us -> 2660 us (0.940)
  waiting for transfers between devices: 1730 us -> 1470 us
  blocking collectives: 158 us -> 245 us
  local copies, waits for them, and re-layouts: 268 us -> 229 us
  other arithmetic: 118 us -> 155 us
    all_gather x10 -> x7, waiting for transfers between devices: 485 us -> 384 us  [the longest x3 229 us: gather_features(): gathered = lax.all_gather(mine, axis_name, axis=axis)]
    reduce_scatter x8, waiting for transfers between devices: 584 us -> 487 us  [scatter_low(): lax.psum_scatter(partial.astype(jnp.bfloat16), axis_name, scatter_dimensi...]
    psum x1, blocking collectives: 80.7 us -> 173 us  [shards(): lax.psum(jnp.stack([gain_attn_total, gain_ffn_total]), ('dp', 'row', 'col'))]
    unnamed x44 -> x34, waiting for transfers between devices: 314 us -> 248 us
    convert_element_type x8 -> x2, other arithmetic: 18.8 us -> 56.3 us  [attend_backward(): grad_scores = (attn_probs * (grad_probs - jnp.sum(attn_probs * grad_probs...]
    dot_general x16 -> x2, matrix products: 56.6 us -> 27.5 us  [masked_scores(): jnp.einsum('qkgd,pkd->kgqp', query_rot, key_rot, preferred_element_type=j...]
    reduce_scatter x2 -> x1, waiting for transfers between devices: 63.4 us -> 75.2 us  [reduce_features(): split = lax.psum_scatter(split, axis_name, scatter_dimension=axis)]
  transfers between devices with their start and end apart: 43 -> 36, of which waited for: 29 -> 24; matrix products, arithmetic and copies ran while one was open for 18% -> 18% of each run, Pallas kernels for 0% -> 0%
where the time goes in v3:
time: 2660 us; the launch traced here: 2650 us
  waiting for transfers between devices  1470 us (55%)
  matrix products  490 us (18%)
  blocking collectives  245 us (9%)
  local copies, waits for them, and re-layouts  229 us (9%)
  other arithmetic  155 us (6%)
  starting transfers between devices  37.6 us (1%)
    reduce_scatter x8, waiting for transfers between devices, scatter_low(): lax.psum_scatter(partial.astype(jnp.bfloat16), axis_name, scatter_dimensi...  487 us
    unnamed x34, waiting for transfers between devices  248 us
    all_gather x3, waiting for transfers between devices, gather_features(): gathered = lax.all_gather(mine, axis_name, axis=axis)  229 us
    psum x1, blocking collectives, shards(): lax.psum(jnp.stack([gain_attn_total, gain_ffn_total]), ('dp', 'row', 'col'))  173 us
    all_gather x2, waiting for transfers between devices, shards(): spread_ffn = lax.all_gather(normed_ffn, 'col', axis=0, tiled=True)  121 us
    all_gather x2, waiting for transfers between devices, shards(): spread_grad_ffn = lax.all_gather(grad_ffn, 'col', axis=0, tiled=True)  116 us
    all_gather x2, waiting for transfers between devices, shards(): spread_attn = lax.all_gather(normed_attn, 'row', axis=1, tiled=True)  81 us
    reduce_scatter x1, waiting for transfers between devices, reduce_features(): split = lax.psum_scatter(split, axis_name, scatter_dimension=axis)  75.2 us
  transfers between devices with their start and end apart: 36, of which 24 were waited for; matrix products, arithmetic and copies ran while one was open for 18% of the time, Pallas kernels for 0%

profile of v3, /device:TPU:0, one launch (start us, length us, event | category | flops | bytes accessed | tf_op | source)
XLA Modules:
  0.0 2646.9 jit_solution(4187553294367581079)
XLA Ops:
  15.8 144.4 %all-gather.45.cloned.1.call-done = bf16[1024,1280]{0,1:T(8,128)(2,1)} async-done(((bf16[256,1280]{0,1:T(8,128)(2,1)}), bf16[1024,1280]{0,1:T(8,128)(2,1)}) %all-gather.45.cloned.1.call-update) | async-done | bytes 2621456 | tf_op jit(solution)/shard_map/all_gather | solution.py:124
  172.3 28.1 %all-gather.9 = f32[4,1,512]{2,1,0:T(1,128)S(1)} all-gather(f32[1,1,512]{2,1,0:T(1,128)S(1)} %bitcast.435), channel_id=1, replica_groups=mesh['dp'=2,'row'=4,'col'=4] {'row'}, dimensions={0}, use_global_device_ids=true | all-gather | bytes 10240 | tf_op jit(solution)/shard_map/all_gather | solution.py:190
  220.8 7.8 all_gather.78
  238.1 28.9 %all-gather.29.cloned.1.call-done = bf16[1,1024,2048]{2,1,0:T(8,128)(2,1)} async-done(((bf16[1,256,2048]{2,1,0:T(8,128)(2,1)}), bf16[1,1024,2048]{2,1,0:T(8,128)(2,1)}) %all-gather.29.cloned.1.call-update) | async-done | bytes 4194320 | tf_op jit(solution)/shard_map/all_gather | solution.py:213
  273.9 13.9 fusion.125
  287.8 13.4 exponential_reduce_fusion.1
  301.3 13.6 fusion.75
  328.1 83.5 %all-gather.49.cloned.1.call-done = bf16[1024,4096]{1,0:T(8,128)(2,1)} async-done(((bf16[256,4096]{1,0:T(8,128)(2,1)}), bf16[1024,4096]{1,0:T(8,128)(2,1)}) %all-gather.49.cloned.1.call-update) | async-done | bytes 8388624 | tf_op jit(solution)/shard_map/all_gather | solution.py:124
  412.3 8.0 all-gather.10
  420.4 47.3 %reduce-scatter.21.cloned.1.call-done = bf16[1,256,2048]{2,1,0:T(8,128)(2,1)} async-done(((bf16[1,1024,2048]{2,1,0:T(8,128)(2,1)}), bf16[1,256,2048]{2,1,0:T(8,128)(2,1)}) %reduce-scatter.21.cloned.1.call-update) | async-done | bytes 1048592 | tf_op jit(solution)/shard_map/reduce_scatter | solution.py:109
  473.8 28.0 %all_to_all.60 = bf16[2,1,4,256,1,512]{5,3,0,4,1,2:T(8,128)(2,1)S(1)} all-to-all(bf16[2,1,4,256,1,512]{5,3,0,4,1,2:T(8,128)(2,1)S(1)} %copy.201), channel_id=1, replica_groups=mesh['dp'=2,'row'=4,'col'=4] {'row'}, dimensions={2} | all-to-all | bytes 4194304 | tf_op jit(solution)/shard_map/all_to_all | solution.py:147
  513.1 16.8 copy.195
  529.9 14.6 reshape.1151
  544.5 14.1 copy.192
  558.7 47.9 %all-gather.31.cloned.1.call-done = bf16[4,256,2048]{2,1,0:T(8,128)(2,1)} async-done(((bf16[1,256,2048]{2,1,0:T(8,128)(2,1)}), bf16[4,256,2048]{2,1,0:T(8,128)(2,1)}) %all-gather.31.cloned.1.call-update) | async-done | bytes 4194320 | tf_op jit(solution)/shard_map/all_gather | solution.py:249
  606.6 23.4 fusion.127
  630.0 57.8 %all-gather.37.cloned.1.call-done = bf16[4,256,2048]{2,1,0:T(8,128)(2,1)} async-done(((bf16[1,256,2048]{2,1,0:T(8,128)(2,1)}), bf16[4,256,2048]{2,1,0:T(8,128)(2,1)}) %all-gather.37.cloned.1.call-update) | async-done | bytes 4194320 | tf_op jit(solution)/shard_map/all_gather | solution.py:265
  687.8 21.9 multiply_convert_fusion.3
  709.7 24.3 fusion.30
  734.0 75.4 %reduce-scatter.29.cloned.1.call-done = bf16[1,256,2048]{2,1,0:T(8,128)(2,1)} async-done(((bf16[4,256,2048]{2,1,0:T(8,128)(2,1)}), bf16[1,256,2048]{2,1,0:T(8,128)(2,1)}) %reduce-scatter.29.cloned.1.call-update) | async-done | bytes 1048592 | tf_op jit(solution)/shard_map/reduce_scatter | solution.py:109
  814.4 53.2 %all-gather.39.cloned.1.call-done = bf16[1,1024,2048]{2,1,0:T(8,128)(2,1)} async-done(((bf16[1,256,2048]{2,1,0:T(8,128)(2,1)}), bf16[1,1024,2048]{2,1,0:T(8,128)(2,1)}) %all-gather.39.cloned.1.call-update) | async-done | bytes 4194320 | tf_op jit(solution)/shard_map/all_gather | solution.py:291
  872.8 14.2 fusion.95
  887.0 21.6 fusion.3
  908.6 28.1 %fusion.5 = bf16[2,4,1024,1024]{2,3,1,0:T(8,128)(2,1)} fusion(f32[2,1024,1024,4]{2,1,3,0:T(8,128)} %get-tuple-element.328, f32[2,4,1024,1024]{2,3,1,0:T(8,128)} %get-tuple-element.326, f32[2,4,1024]{2,1,0:T(4,128)S(1)} %get-tuple-element.327, f32[2,4,1024]{2,1,0:T(4,128)S(1)} %bitcast.384), kind=kLoop, calls=%fused_computation.10 | loop fusion | flops 33554432 | bytes 83951616 | tf_op jit(solution)/shard_map/while/body/eval_jaxpr/convert_element_type | solution.py:96
  936.7 9.1 fusion.94
  959.8 7.8 convert_bitcast_fusion.1
  975.6 44.7 %reduce-scatter.31.cloned.1.call-done = bf16[1,256,2048]{2,1,0:T(8,128)(2,1)} async-done(((bf16[1,1024,2048]{2,1,0:T(8,128)(2,1)}), bf16[1,256,2048]{2,1,0:T(8,128)(2,1)}) %reduce-scatter.31.cloned.1.call-update) | async-done | bytes 1048592 | tf_op jit(solution)/shard_map/reduce_scatter | solution.py:109
  1025.4 52.1 %all-gather.33.cloned.1.call-done = bf16[1,1024,2048]{2,1,0:T(8,128)(2,1)} async-done(((bf16[1,256,2048]{2,1,0:T(8,128)(2,1)}), bf16[1,1024,2048]{2,1,0:T(8,128)(2,1)}) %all-gather.33.cloned.1.call-update) | async-done | bytes 4194320 | tf_op jit(solution)/shard_map/all_gather | solution.py:213
  1085.5 13.6 fusion.126
  1099.1 13.1 exponential_reduce_fusion
  1112.2 13.3 fusion.78
  1132.7 14.3 convolution_convert_fusion.1
  1147.0 38.3 %reduce-scatter.25.cloned.1.call-done = bf16[1,256,2048]{2,1,0:T(8,128)(2,1)} async-done(((bf16[1,1024,2048]{2,1,0:T(8,128)(2,1)}), bf16[1,256,2048]{2,1,0:T(8,128)(2,1)}) %reduce-scatter.25.cloned.1.call-update) | async-done | bytes 1048592 | tf_op jit(solution)/shard_map/reduce_scatter | solution.py:109
  1187.7 77.3 %reduce-scatter.23.cloned.1.call-done = bf16[1,256,2048]{2,1,0:T(8,128)(2,1)} async-done(((bf16[4,256,2048]{2,1,0:T(8,128)(2,1)}), bf16[1,256,2048]{2,1,0:T(8,128)(2,1)}) %reduce-scatter.23.cloned.1.call-update) | async-done | bytes 1048592 | tf_op jit(solution)/shard_map/reduce_scatter | solution.py:109
  1278.9 73.0 %all-gather.35.cloned.1.call-done = bf16[4,256,2048]{2,1,0:T(8,128)(2,1)} async-done(((bf16[1,256,2048]{2,1,0:T(8,128)(2,1)}), bf16[4,256,2048]{2,1,0:T(8,128)(2,1)}) %all-gather.35.cloned.1.call-update) | async-done | bytes 4194320 | tf_op jit(solution)/shard_map/all_gather | solution.py:249
  1351.8 23.6 fusion.128
  1375.4 57.7 %all-gather.41.cloned.1.call-done = bf16[4,256,2048]{2,1,0:T(8,128)(2,1)} async-done(((bf16[1,256,2048]{2,1,0:T(8,128)(2,1)}), bf16[4,256,2048]{2,1,0:T(8,128)(2,1)}) %all-gather.41.cloned.1.call-update) | async-done | bytes 4194320 | tf_op jit(solution)/shard_map/all_gather | solution.py:265
  1433.1 21.9 multiply_convert_fusion.1
  1455.0 24.2 fusion.31
  1479.3 75.4 %reduce-scatter.33.cloned.1.call-done = bf16[1,256,2048]{2,1,0:T(8,128)(2,1)} async-done(((bf16[4,256,2048]{2,1,0:T(8,128)(2,1)}), bf16[1,256,2048]{2,1,0:T(8,128)(2,1)}) %reduce-scatter.33.cloned.1.call-update) | async-done | bytes 1048592 | tf_op jit(solution)/shard_map/reduce_scatter | solution.py:109
  1572.7 6.7 fusion.129
  1591.1 21.7 all-gather.43.cloned.1.call-done
  1618.1 14.1 fusion.98
  1632.2 21.6 fusion
  1653.8 28.2 %fusion.2 = bf16[2,4,1024,1024]{2,3,1,0:T(8,128)(2,1)} fusion(f32[2,1024,1024,4]{2,1,3,0:T(8,128)} %get-tuple-element.332, f32[2,4,1024,1024]{2,3,1,0:T(8,128)} %get-tuple-element.330, f32[2,4,1024]{2,1,0:T(4,128)S(1)} %get-tuple-element.331, f32[2,4,1024]{2,1,0:T(4,128)S(1)} %bitcast.388), kind=kLoop, calls=%fused_computation.5 | loop fusion | flops 33554432 | bytes 83951616 | tf_op jit(solution)/shard_map/while/body/eval_jaxpr/convert_element_type | solution.py:96
  1682.1 11.1 fusion.93
  1720.7 16.9 fusion.131
  1737.7 18.6 bitcast_add_fusion.1
  1756.3 16.8 copy.230
  1773.1 27.1 %fusion.10 = f32[2048,4096,1]{1,0,2:T(8,128)} fusion(bf16[4,256,2048]{2,1,0:T(8,128)(2,1)} %all-gather.31.cloned.1.call-done, bf16[4,256,2048]{2,1,0:T(8,128)(2,1)} %get-tuple-element.273, bf16[4,256,2048]{2,1,0:T(8,128)(2,1)} %get-tuple-element.272), kind=kOutput, calls=%fused_computation.34 | convolution fusion | flops 17196646400 | bytes 46137344 | tf_op jit(solution)/shard_map/std,stf->df/dot_general | solution.py:279
  1800.2 32.8 %bitcast_add_fusion = f32[2048,4096]{1,0:T(8,128)} fusion(f32[2048,4096,1]{1,0,2:T(8,128)} %fusion.10, bf16[4,256,2048]{2,1,0:T(8,128)(2,1)} %all-gather.35.cloned.1.call-done, bf16[4,256,2048]{2,1,0:T(8,128)(2,1)} %get-tuple-element.275, bf16[4,256,2048]{2,1,0:T(8,128)(2,1)} %get-tuple-element.274), kind=kOutput, calls=%fused_computation | convolution fusion | flops 17205035008 | bytes 79691776 | tf_op jit(solution)/shard_map/std,stf->df/dot_general | solution.py:279
  1833.0 22.8 copy.270
  1864.0 35.2 %reduce-scatter.39.cloned.1.call-done = f32[1,4,256,4096]{3,2,1,0:T(8,128)} async-done(((f32[2,4,256,4096]{3,2,1,0:T(8,128)}), f32[1,4,256,4096]{3,2,1,0:T(8,128)}) %reduce-scatter.39.cloned.1.call-update) | async-done | bytes 16777232 | tf_op jit(solution)/shard_map/reduce_scatter | solution.py:137
  1899.2 6.9 convert_bitcast_fusion
  1906.2 14.9 convolution_convert_fusion
  1921.2 75.2 %reduce-scatter.37.cloned.1.call-done = f32[1,256,1280]{2,1,0:T(8,128)} async-done(((f32[4,256,1280]{2,1,0:T(8,128)}), f32[1,256,1280]{2,1,0:T(8,128)}) %reduce-scatter.37.cloned.1.call-update) | async-done | bytes 1310736 | tf_op jit(solution)/shard_map/reduce_scatter | solution.py:138
  1996.5 89.8 %reduce-scatter.45.cloned.1.call-done = f32[2048,1,256]{2,0,1:T(8,128)} async-done(((f32[2048,4,256]{2,0,1:T(8,128)}), f32[2048,1,256]{2,0,1:T(8,128)}) %reduce-scatter.45.cloned.1.call-update) | async-done | bytes 2097168
  2086.4 156.6 %reduce-scatter.43.cloned.1.call-done = f32[1,256,4096]{2,1,0:T(8,128)} async-done(((f32[4,256,4096]{2,1,0:T(8,128)}), f32[1,256,4096]{2,1,0:T(8,128)}) %reduce-scatter.43.cloned.1.call-update) | async-done | bytes 4194320
  2248.3 50.8 %reduce-scatter.35.cloned.1.call-done = bf16[1,256,2048]{2,1,0:T(8,128)(2,1)} async-done(((bf16[1,1024,2048]{2,1,0:T(8,128)(2,1)}), bf16[1,256,2048]{2,1,0:T(8,128)(2,1)}) %reduce-scatter.35.cloned.1.call-update) | async-done | bytes 1048592 | tf_op jit(solution)/shard_map/reduce_scatter | solution.py:109
  2301.1 77.7 %reduce-scatter.27.cloned.1.call-done = bf16[1,256,2048]{2,1,0:T(8,128)(2,1)} async-done(((bf16[4,256,2048]{2,1,0:T(8,128)(2,1)}), bf16[1,256,2048]{2,1,0:T(8,128)(2,1)}) %reduce-scatter.27.cloned.1.call-update) | async-done | bytes 1048592 | tf_op jit(solution)/shard_map/reduce_scatter | solution.py:109
  2408.1 8.3 all-to-all-done.1
  2421.5 21.2 collective-permute-start.1
  2442.8 173.1 %psum.7 = f32[2,2048]{1,0:T(2,128)S(1)} all-reduce(f32[2,2048]{1,0:T(2,128)S(1)} %pad_maximum_fusion.29), channel_id=1, replica_groups=mesh['dp'=2,'row'=4,'col'=4] {'dp','row','col'}, use_global_device_ids=true, to_apply=%region_34.35 | all-reduce | flops 4096 | bytes 32768 | tf_op jit(solution)/shard_map/psum | solution.py:346
  2628.6 8.1 fusion.122
  (384 shorter events, 285.1 us)
Async XLA Ops:
  7.2 208.7 %copy-start = (bf16[2048,512]{1,0:T(8,128)(2,1)S(1)}, bf16[2048,512]{1,0:T(8,128)(2,1)}, u32[]{:S(2)}) copy-start(bf16[2048,512]{1,0:T(8,128)(2,1)} %param.20) | copy-start | bytes 6291460
  7.2 153.0 %all-gather.45.cloned.1.call-start = ((), (), s32[]{:S(2)}) async-start(), calls=%async_computation.36 | async-start | bytes 3276800 | tf_op jit(solution)/shard_map/all_gather | solution.py:124
  12.9 2.0 collective-permute-start
  15.7 217.2 %all-gather.47.cloned.1.call-start = ((), (), s32[]{:S(2)}) async-start(), calls=%async_computation.37 | async-start | bytes 7864320 | tf_op jit(solution)/shard_map/all_gather | solution.py:125
  167.7 32.6 %all-to-all-start = ((bf16[2,1,4,256,1,512]{5,3,0,4,1,2:T(8,128)(2,1)}), bf16[2,1,4,256,1,512]{5,3,0,4,1,2:T(8,128)(2,1)}, u32[]{:S(2)}, u32[]{:S(2)}) async-start(bf16[2,1,4,256,1,512]{5,3,0,4,1,2:T(8,128)(2,1)} %copy.182), calls=%async_computation | async-start | bytes 4194304 | tf_op jit(solution)/shard_map/all_to_all | solution.py:147
  172.2 94.8 %all-gather.29.cloned.1.call-start = ((), (), s32[]{:S(2)}) async-start(), calls=%async_computation.17 | async-start | bytes 5242880 | tf_op jit(solution)/shard_map/all_gather | solution.py:213
  215.8 106.0 %all-gather.53.cloned.1.call-start = ((), (), s32[]{:S(2)}) async-start(), calls=%async_computation.40 | async-start | bytes 5242880 | tf_op jit(solution)/shard_map/all_gather | solution.py:124
  217.5 194.2 %all-gather.49.cloned.1.call-start = ((), (), s32[]{:S(2)}) async-start(), calls=%async_computation.38 | async-start | bytes 10485760 | tf_op jit(solution)/shard_map/all_gather | solution.py:124
  220.8 246.9 %reduce-scatter.21.cloned.1.call-start = ((), (), s32[]{:S(2)}) async-start(), calls=%async_computation.18 | async-start | bytes 5242880 | tf_op jit(solution)/shard_map/reduce_scatter | solution.py:109
  232.3 41.3 %copy-start.24 = (f32[1024,32]{0,1:T(8,128)}, f32[1024,32]{0,1:T(8,128)S(1)}, u32[]{:S(2)}) copy-start(f32[1024,32]{0,1:T(8,128)S(1)} %get-tuple-element.318) | copy-start | bytes 393220
  321.2 191.8 %all-gather.55.cloned.1.call-start = ((), (), s32[]{:S(2)}) async-start(), calls=%async_computation.41 | async-start | bytes 12582912 | tf_op jit(solution)/shard_map/all_gather | solution.py:125
  328.1 216.4 %all-gather.51.cloned.1.call-start = ((), (), s32[]{:S(2)}) async-start(), calls=%async_computation.39 | async-start | bytes 25165824 | tf_op jit(solution)/shard_map/all_gather | solution.py:125
  411.7 56.0 %copy-start.4 = (f32[1,256,2048]{2,1,0:T(8,128)S(1)}, f32[1,256,2048]{2,1,0:T(8,128)}, u32[]{:S(2)}) copy-start(f32[1,256,2048]{2,1,0:T(8,128)} %reshape.1131) | copy-start | bytes 6291460
  411.7 194.9 %all-gather.31.cloned.1.call-start = ((), (), s32[]{:S(2)}) async-start(), calls=%async_computation.19 | async-start | bytes 5242880 | tf_op jit(solution)/shard_map/all_gather | solution.py:249
  420.4 392.0 %copy-start.53 = (f32[4,1,512]{2,1,0:T(1,128)}, f32[4,1,512]{2,1,0:T(1,128)S(1)}, u32[]{:S(2)}) copy-start(f32[4,1,512]{2,1,0:T(1,128)S(1)} %all-gather.10) | copy-start | bytes 24580
  469.3 343.0 %copy-start.66 = (f32[256]{0:T(256)}, f32[256]{0:T(256)S(1)}, u32[]{:S(2)}) copy-start(f32[256]{0:T(256)S(1)} %add_rsqrt_fusion.2) | copy-start | bytes 3076
  471.9 215.9 %all-gather.37.cloned.1.call-start = ((), (), s32[]{:S(2)}) async-start(), calls=%async_computation.25 | async-start | bytes 5242880 | tf_op jit(solution)/shard_map/all_gather | solution.py:265
  513.0 296.4 %reduce-scatter.29.cloned.1.call-start = ((), (), s32[]{:S(2)}) async-start(), calls=%async_computation.26 | async-start | bytes 5242880 | tf_op jit(solution)/shard_map/reduce_scatter | solution.py:109
  734.0 75.5 %copy-start.10 = (bf16[1,256,2048]{2,1,0:T(8,128)(2,1)S(1)}, bf16[1,256,2048]{2,1,0:T(8,128)(2,1)}, u32[]{:S(2)}) copy-start(bf16[1,256,2048]{2,1,0:T(8,128)(2,1)} %reduce-scatter.21.cloned.1.call-done) | copy-start | bytes 3145732
  734.0 133.5 %all-gather.39.cloned.1.call-start = ((), (), s32[]{:S(2)}) async-start(), calls=%async_computation.27 | async-start | bytes 5242880 | tf_op jit(solution)/shard_map/all_gather | solution.py:291
  814.3 206.0 %reduce-scatter.31.cloned.1.call-start = ((), (), s32[]{:S(2)}) async-start(), calls=%async_computation.28 | async-start | bytes 5242880 | tf_op jit(solution)/shard_map/reduce_scatter | solution.py:109
  967.6 109.9 %all-gather.33.cloned.1.call-start = ((), (), s32[]{:S(2)}) async-start(), calls=%async_computation.21 | async-start | bytes 5242880 | tf_op jit(solution)/shard_map/all_gather | solution.py:213
  967.6 52.7 %copy-start.57 = (f32[4,1,512]{2,1,0:T(1,128)S(1)}, f32[4,1,512]{2,1,0:T(1,128)}, u32[]{:S(2)}) copy-start(f32[4,1,512]{2,1,0:T(1,128)} %copy-done.56) | copy-start | bytes 24580
  967.7 52.7 %copy-start.73 = (f32[256]{0:T(256)S(1)}, f32[256]{0:T(256)}, u32[]{:S(2)}) copy-start(f32[256]{0:T(256)} %copy-done.72) | copy-start | bytes 3076
  975.6 49.2 %copy-start.62 = (s32[1,1,1024]{2,0,1:T(1,128)S(1)}, s32[1,1,1024]{2,0,1:T(1,128)}, u32[]{:S(2)}) copy-start(s32[1,1,1024]{2,0,1:T(1,128)} %get-tuple-element.309) | copy-start | bytes 12292
  975.6 49.8 %copy-start.70 = (f32[256]{0:T(256)}, f32[256]{0:T(256)S(1)}, u32[]{:S(2)}) copy-start(f32[256]{0:T(256)S(1)} %add_rsqrt_fusion.1) | copy-start | bytes 3076
  1024.7 160.6 %reduce-scatter.25.cloned.1.call-start = ((), (), s32[]{:S(2)}) async-start(), calls=%async_computation.22 | async-start | bytes 5242880 | tf_op jit(solution)/shard_map/reduce_scatter | solution.py:109
  1132.6 132.3 %reduce-scatter.23.cloned.1.call-start = ((), (), s32[]{:S(2)}) async-start(), calls=%async_computation.20 | async-start | bytes 5242880 | tf_op jit(solution)/shard_map/reduce_scatter | solution.py:109
  1146.9 118.0 %copy-start.11 = (bf16[1,256,2048]{2,1,0:T(8,128)(2,1)S(1)}, bf16[1,256,2048]{2,1,0:T(8,128)(2,1)}, u32[]{:S(2)}) copy-start(bf16[1,256,2048]{2,1,0:T(8,128)(2,1)} %reduce-scatter.21.cloned.1.call-done) | copy-start | bytes 3145732
  1146.9 118.0 %copy-start.54 = (f32[4,1,512]{2,1,0:T(1,128)S(1)}, f32[4,1,512]{2,1,0:T(1,128)}, u32[]{:S(2)}) copy-start(f32[4,1,512]{2,1,0:T(1,128)} %copy-done.53) | copy-start | bytes 24580
  1146.9 118.0 %copy-start.67 = (f32[256]{0:T(256)S(1)}, f32[256]{0:T(256)}, u32[]{:S(2)}) copy-start(f32[256]{0:T(256)} %copy-done.66) | copy-start | bytes 3076
  1146.9 118.0 %copy-start.77 = (f32[256]{0:T(256)S(1)}, f32[256]{0:T(256)}, u32[]{:S(2)}) copy-start(f32[256]{0:T(256)} %copy-done.76) | copy-start | bytes 3076
  1147.0 204.9 %all-gather.35.cloned.1.call-start = ((), (), s32[]{:S(2)}) async-start(), calls=%async_computation.23 | async-start | bytes 5242880 | tf_op jit(solution)/shard_map/all_gather | solution.py:249
  1187.7 370.0 %copy-start.68 = (f32[256]{0:T(256)}, f32[256]{0:T(256)S(1)}, u32[]{:S(2)}) copy-start(f32[256]{0:T(256)S(1)} %add_rsqrt_fusion) | copy-start | bytes 3076
  1270.4 162.7 %all-gather.41.cloned.1.call-start = ((), (), s32[]{:S(2)}) async-start(), calls=%async_computation.29 | async-start | bytes 5242880 | tf_op jit(solution)/shard_map/all_gather | solution.py:265
  1277.5 98.0 %copy-start.7 = (f32[1,256,2048]{2,1,0:T(8,128)}, f32[1,256,2048]{2,1,0:T(8,128)S(1)}, u32[]{:S(2)}) copy-start(f32[1,256,2048]{2,1,0:T(8,128)S(1)} %reshape.1134) | copy-start | bytes 6291460
  1278.8 275.9 %reduce-scatter.33.cloned.1.call-start = ((), (), s32[]{:S(2)}) async-start(), calls=%async_computation.30 | async-start | bytes 5242880 | tf_op jit(solution)/shard_map/reduce_scatter | solution.py:109
  1479.2 75.5 %copy-start.5 = (f32[1,256,2048]{2,1,0:T(8,128)S(1)}, f32[1,256,2048]{2,1,0:T(8,128)}, u32[]{:S(2)}) copy-start(f32[1,256,2048]{2,1,0:T(8,128)} %reshape.1132) | copy-start | bytes 6291460
  1479.2 75.5 %copy-start.12 = (bf16[1,256,2048]{2,1,0:T(8,128)(2,1)S(1)}, bf16[1,256,2048]{2,1,0:T(8,128)(2,1)}, u32[]{:S(2)}) copy-start(bf16[1,256,2048]{2,1,0:T(8,128)(2,1)} %reduce-scatter.25.cloned.1.call-done) | copy-start | bytes 3145732
  1479.3 133.6 %all-gather.43.cloned.1.call-start = ((), (), s32[]{:S(2)}) async-start(), calls=%async_computation.31 | async-start | bytes 5242880 | tf_op jit(solution)/shard_map/all_gather | solution.py:291
  1559.6 297.4 %all-reduce.6.cloned.1.call-start = ((), (), s32[]{:S(2)}) async-start(), calls=%async_computation.45 | async-start | bytes 20971520
  1720.7 142.6 %reduce-scatter.41.cloned.1.call-start = ((), (), s32[]{:S(2)}) async-start(), calls=%async_computation.35 | async-start | bytes 25165824 | tf_op jit(solution)/shard_map/reduce_scatter | solution.py:137
  1773.1 126.1 %reduce-scatter.39.cloned.1.call-start = ((), (), s32[]{:S(2)}) async-start(), calls=%async_computation.34 | async-start | bytes 50331648 | tf_op jit(solution)/shard_map/reduce_scatter | solution.py:137
  1855.8 140.6 %reduce-scatter.37.cloned.1.call-start = ((), (), s32[]{:S(2)}) async-start(), calls=%async_computation.33 | async-start | bytes 6553600 | tf_op jit(solution)/shard_map/reduce_scatter | solution.py:138
  1863.2 223.1 %reduce-scatter.45.cloned.1.call-start = ((), (), s32[]{:S(2)}) async-start(), calls=%async_computation.47 | async-start | bytes 10485760
  1863.9 379.1 %reduce-scatter.43.cloned.1.call-start = ((), (), s32[]{:S(2)}) async-start(), calls=%async_computation.46 | async-start | bytes 20971520
  1899.2 399.9 %reduce-scatter.35.cloned.1.call-start = ((), (), s32[]{:S(2)}) async-start(), calls=%async_computation.32 | async-start | bytes 5242880 | tf_op jit(solution)/shard_map/reduce_scatter | solution.py:109
  1906.1 472.6 %reduce-scatter.27.cloned.1.call-start = ((), (), s32[]{:S(2)}) async-start(), calls=%async_computation.24 | async-start | bytes 5242880 | tf_op jit(solution)/shard_map/reduce_scatter | solution.py:109
  1921.1 500.4 %all-gather.57.cloned.1.call-start = ((), (), s32[]{:S(2)}) async-start(), calls=%async_computation.42 | async-start | bytes 3932160 | tf_op jit(solution)/shard_map/all_gather | solution.py:139
  1996.4 632.1 %all-gather.61.cloned.1.call-start = ((), (), s32[]{:S(2)}) async-start(), calls=%async_computation.44 | async-start | bytes 6291456 | tf_op jit(solution)/shard_map/all_gather | solution.py:139
  2086.4 542.2 %all-gather.59.cloned.1.call-start = ((), (), s32[]{:S(2)}) async-start(), calls=%async_computation.43 | async-start | bytes 12582912 | tf_op jit(solution)/shard_map/all_gather | solution.py:139
  2243.0 56.0 %copy-start.6 = (f32[1,256,2048]{2,1,0:T(8,128)S(1)}, f32[1,256,2048]{2,1,0:T(8,128)}, u32[]{:S(2)}) copy-start(f32[1,256,2048]{2,1,0:T(8,128)} %reshape.1132) | copy-start | bytes 6291460
  2243.0 56.0 %copy-start.58 = (f32[4,1,512]{2,1,0:T(1,128)S(1)}, f32[4,1,512]{2,1,0:T(1,128)}, u32[]{:S(2)}) copy-start(f32[4,1,512]{2,1,0:T(1,128)} %copy-done.56) | copy-start | bytes 24580
  2243.0 56.0 %copy-start.71 = (f32[256]{0:T(256)S(1)}, f32[256]{0:T(256)}, u32[]{:S(2)}) copy-start(f32[256]{0:T(256)} %copy-done.70) | copy-start | bytes 3076
  2243.1 135.7 %copy-start.13 = (bf16[1,256,2048]{2,1,0:T(8,128)(2,1)S(1)}, bf16[1,256,2048]{2,1,0:T(8,128)(2,1)}, u32[]{:S(2)}) copy-start(bf16[1,256,2048]{2,1,0:T(8,128)(2,1)} %reduce-scatter.25.cloned.1.call-done) | copy-start | bytes 3145732
  2243.1 135.7 %copy-start.55 = (f32[4,1,512]{2,1,0:T(1,128)S(1)}, f32[4,1,512]{2,1,0:T(1,128)}, u32[]{:S(2)}) copy-start(f32[4,1,512]{2,1,0:T(1,128)} %copy-done.53) | copy-start | bytes 24580
  2243.1 135.7 %copy-start.69 = (f32[256]{0:T(256)S(1)}, f32[256]{0:T(256)}, u32[]{:S(2)}) copy-start(f32[256]{0:T(256)} %copy-done.68) | copy-start | bytes 3076
  2243.1 135.6 %copy-start.75 = (f32[256]{0:T(256)S(1)}, f32[256]{0:T(256)}, u32[]{:S(2)}) copy-start(f32[256]{0:T(256)} %copy-done.74) | copy-start | bytes 3076
  2388.1 28.4 %all-to-all-start.1 = ((bf16[2,1,1,256,4,512]{5,3,2,1,0,4:T(8,128)(2,1)}), bf16[2,1,1,256,4,512]{5,3,2,1,0,4:T(8,128)(2,1)S(1)}, u32[]{:S(2)}, u32[]{:S(2)}) async-start(bf16[2,1,1,256,4,512]{5,3,2,1,0,4:T(8,128)(2,1)} %pad_maximum_fusion.11), calls=%async_computation.5 | async-start | bytes 4194304 | tf_op jit(solution)/shard_map/all_to_all | solution.py:153
  2408.1 34.6 %copy-start.63 = (f32[2048]{0:T(1024)S(1)}, f32[2048]{0:T(1024)}, u32[]{:S(2)}) copy-start(f32[2048]{0:T(1024)} %get-tuple-element.264) | copy-start | bytes 24580
  2408.1 34.6 %copy-start.65 = (f32[2048]{0:T(1024)S(1)}, f32[2048]{0:T(1024)}, u32[]{:S(2)}) copy-start(f32[2048]{0:T(1024)} %get-tuple-element.262) | copy-start | bytes 24580
  2408.1 34.6 %copy-start.64 = (f32[2048]{0:T(1024)S(1)}, f32[2048]{0:T(1024)}, u32[]{:S(2)}) copy-start(f32[2048]{0:T(1024)} %get-tuple-element.268) | copy-start | bytes 24580
  2416.5 201.6 %all-to-all-start.3 = ((f32[2,1,1,256,4,512]{5,3,2,1,0,4:T(8,128)}), f32[2,1,1,256,4,512]{5,3,2,1,0,4:T(8,128)}, u32[]{:S(2)}, u32[]{:S(2)}) async-start(f32[2,1,1,256,4,512]{5,3,2,1,0,4:T(8,128)} %pad_maximum_fusion.6), calls=%async_computation.11 | async-start | bytes 8388608 | tf_op jit(solution)/shard_map/all_to_all | solution.py:153
  2421.5 201.2 %collective-permute-start.1 = (f32[512,1280]{1,0:T(8,128)}, f32[512,1280]{1,0:T(8,128)}, u32[]{:S(2)}, u32[]{:S(2)}) collective-permute-start(f32[512,1280]{1,0:T(8,128)} %bitcast.439), channel_id=1, source_target_pairs={{0,0},{1,4},{2,8},{3,12},{4,1},{5,5},{6,9},{7,13},{8,2},{9,6},{10,... | collective-permute-start | bytes 7864328 | tf_op jit(solution)/shard_map/ppermute | solution.py:142
  (58 other events, 456.4 us)
Sparse Core Ops, SparseCore 0:
  15.8 144.3 all-gather.44
  164.7 13.3 all-gather.46
  216.0 50.9 all-gather.28
  269.3 52.5 all-gather.52
  324.1 87.4 all-gather.48
  415.1 52.5 reduce-scatter.20
  469.8 19.8 all-gather.54
  491.2 31.2 all-gather.50
  524.6 81.9 all-gather.30
  608.6 79.2 all-gather.36
  734.1 75.2 reduce-scatter.28
  814.4 53.0 all-gather.38
  967.7 52.5 reduce-scatter.30
  1024.9 52.5 all-gather.32
  1132.7 52.5 reduce-scatter.24
  1188.1 76.7 reduce-scatter.22
  1270.6 81.2 all-gather.34
  1353.8 79.2 all-gather.40
  1479.4 75.2 reduce-scatter.32
  1559.7 53.0 all-gather.42
  1720.8 43.0 all-reduce.5
  1773.2 25.4 reduce-scatter.40
  1856.0 43.1 reduce-scatter.38
  1901.3 95.0 reduce-scatter.36
  1999.5 86.8 reduce-scatter.44
  2089.3 153.7 reduce-scatter.42
  2246.4 52.5 reduce-scatter.34
  2301.9 76.7 reduce-scatter.26
  2380.3 11.8 all-gather.56
  2393.6 14.8 all-gather.60
  2410.0 21.0 all-gather.58

commit v4 on v3

--- a/solution.py
+++ b/solution.py
@@ -117,26 +117,33 @@
         (a * n_col + b, b * n_col + a) for a in range(n_row) for b in range(n_col)
     ]
 
-    def gather_features(block, axis, axis_name):
+    def gather_half(mine, axis, axis_name):
         count = n_row if axis_name == "row" else n_col
-        half = block.shape[axis] // n_dp
-        mine = lax.dynamic_slice_in_dim(block, lax.axis_index("dp") * half, half, axis=axis)
         gathered = lax.all_gather(mine, axis_name, axis=axis)
         gathered = lax.all_gather(gathered, "dp", axis=axis)
         gathered = jnp.swapaxes(gathered, axis, axis + 1)
-        shape = list(block.shape)
-        shape[axis] = block.shape[axis] * count
+        shape = list(mine.shape)
+        shape[axis] = mine.shape[axis] * count * n_dp
         return gathered.reshape(shape)
 
-    def reduce_features(partial, axis, axis_name):
+    def own_half(block, axis):
+        half = block.shape[axis] // n_dp
+        return lax.dynamic_slice_in_dim(block, lax.axis_index("dp") * half, half, axis=axis)
+
+    def gather_features(block, axis, axis_name):
+        return gather_half(own_half(block, axis), axis, axis_name)
+
+    def reduce_half(partial, axis, axis_name):
         count = n_row if axis_name == "row" else n_col
         half = partial.shape[axis] // (count * n_dp)
         shape = list(partial.shape)
         shape[axis : axis + 1] = [count, n_dp, half]
         split = jnp.swapaxes(partial.reshape(shape), axis, axis + 1)
         split = lax.psum_scatter(split, "dp", scatter_dimension=axis)
-        split = lax.psum_scatter(split, axis_name, scatter_dimension=axis)
-        return lax.all_gather(split, "dp", axis=axis, tiled=True)
+        return lax.psum_scatter(split, axis_name, scatter_dimension=axis)
+
+    def reduce_features(partial, axis, axis_name):
+        return lax.all_gather(reduce_half(partial, axis, axis_name), "dp", axis=axis, tiled=True)
 
     def transpose_grid(block):
         return lax.ppermute(block, ("row", "col"), transpose_pairs)
@@ -180,8 +187,10 @@
         group_count = heads_q // heads_k
         ffn_cols = w_gate.shape[1]
 
-        w_attn = gather_features(
-            transpose_grid(jnp.concatenate([w_query, w_key, w_value, w_out.T], axis=1)), 0, "col"
+        w_attn = gather_half(
+            transpose_grid(own_half(jnp.concatenate([w_query, w_key, w_value, w_out.T], axis=1), 0)),
+            0,
+            "col",
         )
         w_qkv = w_attn[:, :qkv_cols]
         w_out_heads = w_attn[:, qkv_cols:].T
@@ -258,7 +267,9 @@
                 "stf,fd->std", act_low, w_down_all, preferred_element_type=jnp.float32
             )
             ffn_branch = scatter_low(ffn_part, "col", 0)
-            outs_list.append((resid_mid + RESIDUAL_SCALE * ffn_branch).astype(jnp.bfloat16))
+            outs_list.append(
+                to_features((resid_mid + RESIDUAL_SCALE * ffn_branch).astype(jnp.bfloat16)[None])
+            )
 
             grad_rows = cotangent_t[batch_index].astype(jnp.float32)
             grad_ffn = (RESIDUAL_SCALE * grad_rows).astype(jnp.bfloat16)
@@ -330,7 +341,9 @@
             scaled_attn = grad_normed_attn * gain_attn_all
             gain_attn_total = gain_attn_total + jnp.sum(grad_normed_attn * norm_attn, axis=(0, 1))
             inner_attn = jnp.mean(scaled_attn * norm_attn, axis=-1, keepdims=True)
-            inputs_grad.append(grad_mid + inv_attn * (scaled_attn - norm_attn * inner_attn))
+            inputs_grad.append(
+                to_features((grad_mid + inv_attn * (scaled_attn - norm_attn * inner_attn))[None])
+            )
             fresh_attn = jnp.concatenate([fresh_qkv, fresh_out], axis=1)
             if grad_attn_w is None:
                 grad_attn_w = fresh_attn
@@ -342,23 +355,29 @@
 
         total_pair = reduce_features(grad_pair_w, 0, "row")
         total_down = reduce_features(grad_down_w, 1, "row")
-        total_attn = transpose_grid(reduce_features(grad_attn_w, 0, "col"))
-        gain_totals = lax.psum(
-            jnp.stack([gain_attn_total, gain_ffn_total]), ("dp", "row", "col")
+        gain_rows = lax.psum(jnp.stack([gain_attn_total, gain_ffn_total], axis=1), "row")
+        gain_cols = jnp.pad(gain_rows, ((0, 0), (0, 126)))
+        total_attn = lax.all_gather(
+            transpose_grid(
+                reduce_half(jnp.concatenate([grad_attn_w, gain_cols], axis=1), 0, "col")
+            ),
+            "dp",
+            axis=0,
+            tiled=True,
         )
-        gain_totals = lax.dynamic_slice_in_dim(gain_totals, row_index * width_r, width_r, axis=1)
+        attn_cols = qkv_cols + w_out.shape[0]
         return (
-            to_features(jnp.stack(outs_list)),
-            to_features(jnp.stack(inputs_grad)),
+            jnp.concatenate(outs_list),
+            jnp.concatenate(inputs_grad),
             total_attn[:, :query_cols],
             total_attn[:, query_cols:key_end],
             total_attn[:, key_end:qkv_cols],
-            total_attn[:, qkv_cols:].T,
+            total_attn[:, qkv_cols:attn_cols].T,
             total_pair[:, :ffn_cols],
             total_pair[:, ffn_cols:],
             total_down,
-            gain_totals[0],
-            gain_totals[1],
+            total_attn[:, attn_cols],
+            total_attn[:, attn_cols + 1],
         )
 
     return shards

time: 2660 us -> 2490 us (0.936)
  blocking collectives: 245 us -> 87.7 us
    psum x1, blocking collectives: 173 us -> 15.9 us  [shards(): lax.psum(jnp.stack([gain_attn_total, gain_ffn_total], axis=1), 'row')]
    reduce_scatter x8, waiting for transfers between devices: 487 us -> 412 us  [scatter_low(): lax.psum_scatter(partial.astype(jnp.bfloat16), axis_name, scatter_dimensi...]
    all_gather x9, waiting for transfers between devices: 229 us -> 188 us  [the longest x3 187 us: gather_half(): gathered = lax.all_gather(mine, axis_name, axis=axis)]
    unnamed x34 -> x33, waiting for transfers between devices: 248 us -> 288 us
    reduce_scatter x3 -> x4, waiting for transfers between devices: 110 us -> 146 us  [the longest x1 104 us: reduce_half(): return lax.psum_scatter(split, axis_name, scatter_dimension=axis)]
    all_gather x2, waiting for transfers between devices: 74.9 us -> 106 us  [shards(): spread_grad_attn = lax.all_gather(grad_attn, 'row', axis=1, tiled=True)]
    all_to_all x2 -> x4, waiting for transfers between devices: 8.35 us -> 36.7 us  [to_features(): rows = lax.all_to_all(rows, 'row', 3, 2)]
    reshape x3 -> x5, local copies, waits for them, and re-layouts: 54.3 us -> 82.1 us  [the longest x4 67.5 us: reduce_half(): split = jnp.swapaxes(partial.reshape(shape), axis, axis + 1)]
  transfers between devices with their start and end apart: 36 -> 38, of which waited for: 24 -> 25; matrix products, arithmetic and copies ran while one was open for 18% -> 19% of each run, Pallas kernels for 0% -> 0%
where the time goes in v4:
time: 2490 us; the launch traced here: 2480 us
  waiting for transfers between devices  1490 us (60%)
  matrix products  477 us (19%)
  local copies, waits for them, and re-layouts  215 us (9%)
  other arithmetic  165 us (7%)
  blocking collectives  87.7 us (4%)
  starting transfers between devices  26.1 us (1%)
    reduce_scatter x8, waiting for transfers between devices, scatter_low(): lax.psum_scatter(partial.astype(jnp.bfloat16), axis_name, scatter_dimensi...  412 us
    unnamed x33, waiting for transfers between devices  288 us
    all_gather x3, waiting for transfers between devices, gather_half(): gathered = lax.all_gather(mine, axis_name, axis=axis)  187 us
    all_gather x2, waiting for transfers between devices, shards(): spread_ffn = lax.all_gather(normed_ffn, 'col', axis=0, tiled=True)  121 us
    all_gather x2, waiting for transfers between devices, shards(): spread_grad_ffn = lax.all_gather(grad_ffn, 'col', axis=0, tiled=True)  116 us
    all_gather x2, waiting for transfers between devices, shards(): spread_grad_attn = lax.all_gather(grad_attn, 'row', axis=1, tiled=True)  106 us
    reduce_scatter x1, waiting for transfers between devices, reduce_half(): return lax.psum_scatter(split, axis_name, scatter_dimension=axis)  104 us
    all_gather x2, waiting for transfers between devices, shards(): spread_attn = lax.all_gather(normed_attn, 'row', axis=1, tiled=True)  80.9 us
  transfers between devices with their start and end apart: 38, of which 25 were waited for; matrix products, arithmetic and copies ran while one was open for 19% of the time, Pallas kernels for 0%

profile of v4, /device:TPU:0, one launch (start us, length us, event | category | flops | bytes accessed | tf_op | source)
XLA Modules:
  0.0 2480.3 jit_solution(7486226778931867328)
XLA Ops:
  13.3 103.4 %all-gather.46.cloned.1.call-done = bf16[1024,1280]{0,1:T(8,128)(2,1)} async-done(((bf16[256,1280]{0,1:T(8,128)(2,1)}), bf16[1024,1280]{0,1:T(8,128)(2,1)}) %all-gather.46.cloned.1.call-update) | async-done | bytes 2621456 | tf_op jit(solution)/shard_map/all_gather | solution.py:122
  128.7 28.1 %all-gather.8 = f32[4,1,512]{2,1,0:T(1,128)S(1)} all-gather(f32[1,1,512]{2,1,0:T(1,128)S(1)} %bitcast.412), channel_id=1, replica_groups=mesh['dp'=2,'row'=4,'col'=4] {'row'}, dimensions={0}, use_global_device_ids=true | all-gather | bytes 10240 | tf_op jit(solution)/shard_map/all_gather | solution.py:199
  177.3 7.8 all_gather.78
  194.6 28.9 %all-gather.28.cloned.1.call-done = bf16[1,1024,2048]{2,1,0:T(8,128)(2,1)} async-done(((bf16[1,256,2048]{2,1,0:T(8,128)(2,1)}), bf16[1,1024,2048]{2,1,0:T(8,128)(2,1)}) %all-gather.28.cloned.1.call-update) | async-done | bytes 4194320 | tf_op jit(solution)/shard_map/all_gather | solution.py:222
  230.4 13.9 fusion.131
  244.3 13.4 exponential_reduce_fusion.1
  257.7 13.6 fusion.78
  284.6 83.5 %all-gather.50.cloned.1.call-done = bf16[1024,4096]{1,0:T(8,128)(2,1)} async-done(((bf16[256,4096]{1,0:T(8,128)(2,1)}), bf16[1024,4096]{1,0:T(8,128)(2,1)}) %all-gather.50.cloned.1.call-update) | async-done | bytes 8388624 | tf_op jit(solution)/shard_map/all_gather | solution.py:122
  368.8 8.0 all-gather.9
  376.8 47.3 %reduce-scatter.19.cloned.1.call-done = bf16[1,256,2048]{2,1,0:T(8,128)(2,1)} async-done(((bf16[1,1024,2048]{2,1,0:T(8,128)(2,1)}), bf16[1,256,2048]{2,1,0:T(8,128)(2,1)}) %reduce-scatter.19.cloned.1.call-update) | async-done | bytes 1048592 | tf_op jit(solution)/shard_map/reduce_scatter | solution.py:109
  430.2 28.0 %all_to_all.90 = bf16[2,1,4,256,1,512]{5,3,0,4,1,2:T(8,128)(2,1)S(1)} all-to-all(bf16[2,1,4,256,1,512]{5,3,0,4,1,2:T(8,128)(2,1)S(1)} %copy.170), channel_id=1, replica_groups=mesh['dp'=2,'row'=4,'col'=4] {'row'}, dimensions={2} | all-to-all | bytes 4194304 | tf_op jit(solution)/shard_map/all_to_all | solution.py:154
  469.5 16.8 copy.165
  486.3 14.6 reshape.1139
  501.0 14.1 copy.162
  515.1 47.9 %all-gather.30.cloned.1.call-done = bf16[4,256,2048]{2,1,0:T(8,128)(2,1)} async-done(((bf16[1,256,2048]{2,1,0:T(8,128)(2,1)}), bf16[4,256,2048]{2,1,0:T(8,128)(2,1)}) %all-gather.30.cloned.1.call-update) | async-done | bytes 4194320 | tf_op jit(solution)/shard_map/all_gather | solution.py:258
  563.0 23.5 fusion.133
  586.5 57.8 %all-gather.36.cloned.1.call-done = bf16[4,256,2048]{2,1,0:T(8,128)(2,1)} async-done(((bf16[1,256,2048]{2,1,0:T(8,128)(2,1)}), bf16[4,256,2048]{2,1,0:T(8,128)(2,1)}) %all-gather.36.cloned.1.call-update) | async-done | bytes 4194320 | tf_op jit(solution)/shard_map/all_gather | solution.py:276
  644.3 21.9 multiply_convert_fusion.3
  666.1 24.3 fusion.37
  690.5 75.4 %reduce-scatter.27.cloned.1.call-done = bf16[1,256,2048]{2,1,0:T(8,128)(2,1)} async-done(((bf16[4,256,2048]{2,1,0:T(8,128)(2,1)}), bf16[1,256,2048]{2,1,0:T(8,128)(2,1)}) %reduce-scatter.27.cloned.1.call-update) | async-done | bytes 1048592 | tf_op jit(solution)/shard_map/reduce_scatter | solution.py:109
  770.8 53.2 %all-gather.38.cloned.1.call-done = bf16[1,1024,2048]{2,1,0:T(8,128)(2,1)} async-done(((bf16[1,256,2048]{2,1,0:T(8,128)(2,1)}), bf16[1,1024,2048]{2,1,0:T(8,128)(2,1)}) %all-gather.38.cloned.1.call-update) | async-done | bytes 4194320 | tf_op jit(solution)/shard_map/all_gather | solution.py:302
  829.2 14.2 fusion.98
  843.4 21.6 fusion.3
  865.1 28.1 %fusion.5 = bf16[2,4,1024,1024]{2,3,1,0:T(8,128)(2,1)} fusion(f32[2,1024,1024,4]{2,1,3,0:T(8,128)} %get-tuple-element.328, f32[2,4,1024,1024]{2,3,1,0:T(8,128)} %get-tuple-element.326, f32[2,4,1024]{2,1,0:T(4,128)S(1)} %get-tuple-element.327, f32[2,4,1024]{2,1,0:T(4,128)S(1)} %bitcast.354), kind=kLoop, calls=%fused_computation.10 | loop fusion | flops 33554432 | bytes 83951616 | tf_op jit(solution)/shard_map/while/body/eval_jaxpr/convert_element_type | solution.py:96
  893.1 9.1 fusion.97
  925.0 44.4 %reduce-scatter.29.cloned.1.call-done = bf16[1,256,2048]{2,1,0:T(8,128)(2,1)} async-done(((bf16[1,1024,2048]{2,1,0:T(8,128)(2,1)}), bf16[1,256,2048]{2,1,0:T(8,128)(2,1)}) %reduce-scatter.29.cloned.1.call-update) | async-done | bytes 1048592 | tf_op jit(solution)/shard_map/reduce_scatter | solution.py:109
  974.5 52.1 %all-gather.32.cloned.1.call-done = bf16[1,1024,2048]{2,1,0:T(8,128)(2,1)} async-done(((bf16[1,256,2048]{2,1,0:T(8,128)(2,1)}), bf16[1,1024,2048]{2,1,0:T(8,128)(2,1)}) %all-gather.32.cloned.1.call-update) | async-done | bytes 4194320 | tf_op jit(solution)/shard_map/all_gather | solution.py:222
  1034.3 13.7 fusion.132
  1047.9 13.1 exponential_reduce_fusion
  1061.0 13.3 fusion.81
  1081.9 13.8 convolution_convert_fusion.1
  1095.8 38.4 %reduce-scatter.23.cloned.1.call-done = bf16[1,256,2048]{2,1,0:T(8,128)(2,1)} async-done(((bf16[1,1024,2048]{2,1,0:T(8,128)(2,1)}), bf16[1,256,2048]{2,1,0:T(8,128)(2,1)}) %reduce-scatter.23.cloned.1.call-update) | async-done | bytes 1048592 | tf_op jit(solution)/shard_map/reduce_scatter | solution.py:109
  1136.5 77.3 %reduce-scatter.21.cloned.1.call-done = bf16[1,256,2048]{2,1,0:T(8,128)(2,1)} async-done(((bf16[4,256,2048]{2,1,0:T(8,128)(2,1)}), bf16[1,256,2048]{2,1,0:T(8,128)(2,1)}) %reduce-scatter.21.cloned.1.call-update) | async-done | bytes 1048592 | tf_op jit(solution)/shard_map/reduce_scatter | solution.py:109
  1227.8 72.8 %all-gather.34.cloned.1.call-done = bf16[4,256,2048]{2,1,0:T(8,128)(2,1)} async-done(((bf16[1,256,2048]{2,1,0:T(8,128)(2,1)}), bf16[4,256,2048]{2,1,0:T(8,128)(2,1)}) %all-gather.34.cloned.1.call-update) | async-done | bytes 4194320 | tf_op jit(solution)/shard_map/all_gather | solution.py:258
  1300.6 23.5 fusion.134
  1324.1 57.8 %all-gather.40.cloned.1.call-done = bf16[4,256,2048]{2,1,0:T(8,128)(2,1)} async-done(((bf16[1,256,2048]{2,1,0:T(8,128)(2,1)}), bf16[4,256,2048]{2,1,0:T(8,128)(2,1)}) %all-gather.40.cloned.1.call-update) | async-done | bytes 4194320 | tf_op jit(solution)/shard_map/all_gather | solution.py:276
  1381.8 21.9 multiply_convert_fusion.1
  1403.7 24.2 fusion.38
  1428.0 75.4 %reduce-scatter.31.cloned.1.call-done = bf16[1,256,2048]{2,1,0:T(8,128)(2,1)} async-done(((bf16[4,256,2048]{2,1,0:T(8,128)(2,1)}), bf16[1,256,2048]{2,1,0:T(8,128)(2,1)}) %reduce-scatter.31.cloned.1.call-update) | async-done | bytes 1048592 | tf_op jit(solution)/shard_map/reduce_scatter | solution.py:109
  1508.4 53.2 %all-gather.42.cloned.1.call-done = bf16[1,1024,2048]{2,1,0:T(8,128)(2,1)} async-done(((bf16[1,256,2048]{2,1,0:T(8,128)(2,1)}), bf16[1,1024,2048]{2,1,0:T(8,128)(2,1)}) %all-gather.42.cloned.1.call-update) | async-done | bytes 4194320 | tf_op jit(solution)/shard_map/all_gather | solution.py:302
  1566.8 14.1 fusion.101
  1580.8 21.6 fusion
  1602.5 28.2 %fusion.2 = bf16[2,4,1024,1024]{2,3,1,0:T(8,128)(2,1)} fusion(f32[2,1024,1024,4]{2,1,3,0:T(8,128)} %get-tuple-element.332, f32[2,4,1024,1024]{2,3,1,0:T(8,128)} %get-tuple-element.330, f32[2,4,1024]{2,1,0:T(4,128)S(1)} %get-tuple-element.331, f32[2,4,1024]{2,1,0:T(4,128)S(1)} %bitcast.358), kind=kLoop, calls=%fused_computation.5 | loop fusion | flops 33554432 | bytes 83951616 | tf_op jit(solution)/shard_map/while/body/eval_jaxpr/convert_element_type | solution.py:96
  1630.7 11.0 fusion.96
  1653.7 15.6 fusion.135
  1669.3 17.5 bitcast_add_fusion.1
  1686.9 16.7 copy.187
  1719.6 7.0 maximum_add_fusion
  1729.0 15.9 psum.7
  1744.9 10.0 select_maximum_fusion
  1754.9 15.7 reshape.1117
  1770.6 12.2 copy.217
  1783.4 26.7 %fusion.9 = f32[2048,4096,1]{1,0,2:T(8,128)} fusion(bf16[4,256,2048]{2,1,0:T(8,128)(2,1)} %all-gather.30.cloned.1.call-done, bf16[4,256,2048]{2,1,0:T(8,128)(2,1)} %get-tuple-element.273, bf16[4,256,2048]{2,1,0:T(8,128)(2,1)} %get-tuple-element.272), kind=kOutput, calls=%fused_computation.36 | convolution fusion | flops 17196646400 | bytes 46137344 | tf_op jit(solution)/shard_map/std,stf->df/dot_general | solution.py:290
  1810.1 32.9 %bitcast_add_fusion = f32[2048,4096]{1,0:T(8,128)} fusion(f32[2048,4096,1]{1,0,2:T(8,128)} %fusion.9, bf16[4,256,2048]{2,1,0:T(8,128)(2,1)} %all-gather.34.cloned.1.call-done, bf16[4,256,2048]{2,1,0:T(8,128)(2,1)} %get-tuple-element.275, bf16[4,256,2048]{2,1,0:T(8,128)(2,1)} %get-tuple-element.274), kind=kOutput, calls=%fused_computation | convolution fusion | flops 17205035008 | bytes 79691776 | tf_op jit(solution)/shard_map/std,stf->df/dot_general | solution.py:290
  1843.0 22.8 copy.216
  1867.2 41.2 %reduce-scatter.39.cloned.1.call-done = f32[1,4,256,4096]{3,2,1,0:T(8,128)} async-done(((f32[2,4,256,4096]{3,2,1,0:T(8,128)}), f32[1,4,256,4096]{3,2,1,0:T(8,128)}) %reduce-scatter.39.cloned.1.call-update) | async-done | bytes 16777232 | tf_op jit(solution)/shard_map/reduce_scatter | solution.py:142
  1908.6 13.8 convolution_convert_fusion
  1922.5 76.6 %reduce-scatter.45.cloned.1.call-done = f32[2048,1,256]{2,0,1:T(8,128)} async-done(((f32[2048,4,256]{2,0,1:T(8,128)}), f32[2048,1,256]{2,0,1:T(8,128)}) %reduce-scatter.45.cloned.1.call-update) | async-done | bytes 2097168
  1999.1 104.4 %reduce-scatter.37.cloned.1.call-done = f32[1,256,1408]{1,2,0:T(8,128)} async-done(((f32[4,256,1408]{1,2,0:T(8,128)}), f32[1,256,1408]{1,2,0:T(8,128)}) %reduce-scatter.37.cloned.1.call-update) | async-done | bytes 1441808 | tf_op jit(solution)/shard_map/reduce_scatter | solution.py:143
  2106.7 209.7 %reduce-scatter.43.cloned.1.call-done = f32[1,256,4096]{2,1,0:T(8,128)} async-done(((f32[4,256,4096]{2,1,0:T(8,128)}), f32[1,256,4096]{2,1,0:T(8,128)}) %reduce-scatter.43.cloned.1.call-update) | async-done | bytes 4194320
  2342.0 54.1 %reduce-scatter.25.cloned.1.call-done = bf16[1,256,2048]{2,1,0:T(8,128)(2,1)} async-done(((bf16[4,256,2048]{2,1,0:T(8,128)(2,1)}), bf16[1,256,2048]{2,1,0:T(8,128)(2,1)}) %reduce-scatter.25.cloned.1.call-update) | async-done | bytes 1048592 | tf_op jit(solution)/shard_map/reduce_scatter | solution.py:109
  2413.4 8.5 all-to-all-done.2
  2428.3 21.7 all-to-all-done.5
  2462.1 8.1 fusion.128
  (375 shorter events, 265.4 us)
Async XLA Ops:
  7.2 165.2 %copy-start = (bf16[2048,512]{1,0:T(8,128)(2,1)S(1)}, bf16[2048,512]{1,0:T(8,128)(2,1)}, u32[]{:S(2)}) copy-start(bf16[2048,512]{1,0:T(8,128)(2,1)} %param.20) | copy-start | bytes 6291460
  7.2 109.5 %all-gather.46.cloned.1.call-start = ((), (), s32[]{:S(2)}) async-start(), calls=%async_computation.41 | async-start | bytes 3276800 | tf_op jit(solution)/shard_map/all_gather | solution.py:122
  11.7 0.7 collective-permute-start
  13.3 176.1 %all-gather.48.cloned.1.call-start = ((), (), s32[]{:S(2)}) async-start(), calls=%async_computation.42 | async-start | bytes 7864320 | tf_op jit(solution)/shard_map/all_gather | solution.py:123
  124.1 32.6 %all-to-all-start = ((bf16[2,1,4,256,1,512]{5,3,0,4,1,2:T(8,128)(2,1)}), bf16[2,1,4,256,1,512]{5,3,0,4,1,2:T(8,128)(2,1)}, u32[]{:S(2)}, u32[]{:S(2)}) async-start(bf16[2,1,4,256,1,512]{5,3,0,4,1,2:T(8,128)(2,1)} %copy.152), calls=%async_computation | async-start | bytes 4194304 | tf_op jit(solution)/shard_map/all_to_all | solution.py:154
  128.7 94.8 %all-gather.28.cloned.1.call-start = ((), (), s32[]{:S(2)}) async-start(), calls=%async_computation.20 | async-start | bytes 5242880 | tf_op jit(solution)/shard_map/all_gather | solution.py:222
  172.3 106.0 %all-gather.54.cloned.1.call-start = ((), (), s32[]{:S(2)}) async-start(), calls=%async_computation.45 | async-start | bytes 5242880 | tf_op jit(solution)/shard_map/all_gather | solution.py:122
  173.9 194.2 %all-gather.50.cloned.1.call-start = ((), (), s32[]{:S(2)}) async-start(), calls=%async_computation.43 | async-start | bytes 10485760 | tf_op jit(solution)/shard_map/all_gather | solution.py:122
  177.2 246.9 %reduce-scatter.19.cloned.1.call-start = ((), (), s32[]{:S(2)}) async-start(), calls=%async_computation.21 | async-start | bytes 5242880 | tf_op jit(solution)/shard_map/reduce_scatter | solution.py:109
  188.7 41.3 %copy-start.19 = (f32[1024,32]{0,1:T(8,128)}, f32[1024,32]{0,1:T(8,128)S(1)}, u32[]{:S(2)}) copy-start(f32[1024,32]{0,1:T(8,128)S(1)} %get-tuple-element.318) | copy-start | bytes 393220
  229.7 28.0 %copy-start.21 = (bf16[1,1024,128]{1,2,0:T(8,128)(2,1)}, bf16[1,1024,128]{1,2,0:T(8,128)(2,1)S(1)}, u32[]{:S(2)}) copy-start(bf16[1,1024,128]{1,2,0:T(8,128)(2,1)S(1)} %slice.363) | copy-start | bytes 786436
  277.7 191.9 %all-gather.56.cloned.1.call-start = ((), (), s32[]{:S(2)}) async-start(), calls=%async_computation.46 | async-start | bytes 12582912 | tf_op jit(solution)/shard_map/all_gather | solution.py:123
  284.5 216.4 %all-gather.52.cloned.1.call-start = ((), (), s32[]{:S(2)}) async-start(), calls=%async_computation.44 | async-start | bytes 25165824 | tf_op jit(solution)/shard_map/all_gather | solution.py:123
  368.1 56.0 %copy-start.4 = (f32[1,256,2048]{2,1,0:T(8,128)S(1)}, f32[1,256,2048]{2,1,0:T(8,128)}, u32[]{:S(2)}) copy-start(f32[1,256,2048]{2,1,0:T(8,128)} %reshape.1120) | copy-start | bytes 6291460
  368.1 194.9 %all-gather.30.cloned.1.call-start = ((), (), s32[]{:S(2)}) async-start(), calls=%async_computation.22 | async-start | bytes 5242880 | tf_op jit(solution)/shard_map/all_gather | solution.py:258
  376.8 392.0 %copy-start.47 = (f32[4,1,512]{2,1,0:T(1,128)}, f32[4,1,512]{2,1,0:T(1,128)S(1)}, u32[]{:S(2)}) copy-start(f32[4,1,512]{2,1,0:T(1,128)S(1)} %all-gather.9) | copy-start | bytes 24580
  425.7 343.0 %copy-start.65 = (f32[256]{0:T(256)}, f32[256]{0:T(256)S(1)}, u32[]{:S(2)}) copy-start(f32[256]{0:T(256)S(1)} %add_rsqrt_fusion.2) | copy-start | bytes 3076
  428.4 215.9 %all-gather.36.cloned.1.call-start = ((), (), s32[]{:S(2)}) async-start(), calls=%async_computation.28 | async-start | bytes 5242880 | tf_op jit(solution)/shard_map/all_gather | solution.py:276
  469.5 296.4 %reduce-scatter.27.cloned.1.call-start = ((), (), s32[]{:S(2)}) async-start(), calls=%async_computation.29 | async-start | bytes 5242880 | tf_op jit(solution)/shard_map/reduce_scatter | solution.py:109
  690.4 75.5 %copy-start.10 = (bf16[1,256,2048]{2,1,0:T(8,128)(2,1)S(1)}, bf16[1,256,2048]{2,1,0:T(8,128)(2,1)}, u32[]{:S(2)}) copy-start(bf16[1,256,2048]{2,1,0:T(8,128)(2,1)} %reduce-scatter.19.cloned.1.call-done) | copy-start | bytes 3145732
  690.4 133.5 %all-gather.38.cloned.1.call-start = ((), (), s32[]{:S(2)}) async-start(), calls=%async_computation.30 | async-start | bytes 5242880 | tf_op jit(solution)/shard_map/all_gather | solution.py:302
  770.7 198.7 %reduce-scatter.29.cloned.1.call-start = ((), (), s32[]{:S(2)}) async-start(), calls=%async_computation.31 | async-start | bytes 5242880 | tf_op jit(solution)/shard_map/reduce_scatter | solution.py:109
  916.7 109.9 %all-gather.32.cloned.1.call-start = ((), (), s32[]{:S(2)}) async-start(), calls=%async_computation.24 | async-start | bytes 5242880 | tf_op jit(solution)/shard_map/all_gather | solution.py:222
  917.0 52.5 %copy-start.51 = (f32[4,1,512]{2,1,0:T(1,128)S(1)}, f32[4,1,512]{2,1,0:T(1,128)}, u32[]{:S(2)}) copy-start(f32[4,1,512]{2,1,0:T(1,128)} %copy-done.50) | copy-start | bytes 24580
  917.0 52.5 %copy-start.72 = (f32[256]{0:T(256)S(1)}, f32[256]{0:T(256)}, u32[]{:S(2)}) copy-start(f32[256]{0:T(256)} %copy-done.71) | copy-start | bytes 3076
  925.0 48.9 %copy-start.61 = (s32[1,1,1024]{2,0,1:T(1,128)S(1)}, s32[1,1,1024]{2,0,1:T(1,128)}, u32[]{:S(2)}) copy-start(s32[1,1,1024]{2,0,1:T(1,128)} %get-tuple-element.311) | copy-start | bytes 12292
  925.0 49.5 %copy-start.69 = (f32[256]{0:T(256)}, f32[256]{0:T(256)S(1)}, u32[]{:S(2)}) copy-start(f32[256]{0:T(256)S(1)} %add_rsqrt_fusion.1) | copy-start | bytes 3076
  973.9 160.3 %reduce-scatter.23.cloned.1.call-start = ((), (), s32[]{:S(2)}) async-start(), calls=%async_computation.25 | async-start | bytes 5242880 | tf_op jit(solution)/shard_map/reduce_scatter | solution.py:109
  1081.4 132.3 %reduce-scatter.21.cloned.1.call-start = ((), (), s32[]{:S(2)}) async-start(), calls=%async_computation.23 | async-start | bytes 5242880 | tf_op jit(solution)/shard_map/reduce_scatter | solution.py:109
  1095.7 118.0 %copy-start.11 = (bf16[1,256,2048]{2,1,0:T(8,128)(2,1)S(1)}, bf16[1,256,2048]{2,1,0:T(8,128)(2,1)}, u32[]{:S(2)}) copy-start(bf16[1,256,2048]{2,1,0:T(8,128)(2,1)} %reduce-scatter.19.cloned.1.call-done) | copy-start | bytes 3145732
  1095.7 118.0 %copy-start.48 = (f32[4,1,512]{2,1,0:T(1,128)S(1)}, f32[4,1,512]{2,1,0:T(1,128)}, u32[]{:S(2)}) copy-start(f32[4,1,512]{2,1,0:T(1,128)} %copy-done.47) | copy-start | bytes 24580
  1095.7 118.0 %copy-start.66 = (f32[256]{0:T(256)S(1)}, f32[256]{0:T(256)}, u32[]{:S(2)}) copy-start(f32[256]{0:T(256)} %copy-done.65) | copy-start | bytes 3076
  1095.7 118.0 %copy-start.76 = (f32[256]{0:T(256)S(1)}, f32[256]{0:T(256)}, u32[]{:S(2)}) copy-start(f32[256]{0:T(256)} %copy-done.75) | copy-start | bytes 3076
  1095.7 204.9 %all-gather.34.cloned.1.call-start = ((), (), s32[]{:S(2)}) async-start(), calls=%async_computation.26 | async-start | bytes 5242880 | tf_op jit(solution)/shard_map/all_gather | solution.py:258
  1136.5 369.9 %copy-start.67 = (f32[256]{0:T(256)}, f32[256]{0:T(256)S(1)}, u32[]{:S(2)}) copy-start(f32[256]{0:T(256)S(1)} %add_rsqrt_fusion) | copy-start | bytes 3076
  1219.2 162.6 %all-gather.40.cloned.1.call-start = ((), (), s32[]{:S(2)}) async-start(), calls=%async_computation.32 | async-start | bytes 5242880 | tf_op jit(solution)/shard_map/all_gather | solution.py:276
  1226.2 97.9 %copy-start.7 = (f32[1,256,2048]{2,1,0:T(8,128)}, f32[1,256,2048]{2,1,0:T(8,128)S(1)}, u32[]{:S(2)}) copy-start(f32[1,256,2048]{2,1,0:T(8,128)S(1)} %reshape.1123) | copy-start | bytes 6291460
  1227.5 275.9 %reduce-scatter.31.cloned.1.call-start = ((), (), s32[]{:S(2)}) async-start(), calls=%async_computation.33 | async-start | bytes 5242880 | tf_op jit(solution)/shard_map/reduce_scatter | solution.py:109
  1427.9 75.5 %copy-start.5 = (f32[1,256,2048]{2,1,0:T(8,128)S(1)}, f32[1,256,2048]{2,1,0:T(8,128)}, u32[]{:S(2)}) copy-start(f32[1,256,2048]{2,1,0:T(8,128)} %reshape.1121) | copy-start | bytes 6291460
  1428.0 75.5 %copy-start.12 = (bf16[1,256,2048]{2,1,0:T(8,128)(2,1)S(1)}, bf16[1,256,2048]{2,1,0:T(8,128)(2,1)}, u32[]{:S(2)}) copy-start(bf16[1,256,2048]{2,1,0:T(8,128)(2,1)} %reduce-scatter.23.cloned.1.call-done) | copy-start | bytes 3145732
  1428.0 133.6 %all-gather.42.cloned.1.call-start = ((), (), s32[]{:S(2)}) async-start(), calls=%async_computation.34 | async-start | bytes 5242880 | tf_op jit(solution)/shard_map/all_gather | solution.py:302
  1508.3 218.4 %reduce-scatter.33.cloned.1.call-start = ((), (), s32[]{:S(2)}) async-start(), calls=%async_computation.35 | async-start | bytes 5242880 | tf_op jit(solution)/shard_map/reduce_scatter | solution.py:109
  1602.5 28.3 %copy-start.26 = (bf16[1,1024,8,32]{1,3,2,0:T(8,128)(2,1)S(1)}, bf16[1,1024,8,32]{1,3,2,0:T(8,128)(2,1)}, u32[]{:S(2)}) copy-start(bf16[1,1024,8,32]{1,3,2,0:T(8,128)(2,1)} %copy-done.25) | copy-start | bytes 1572868
  1602.5 28.3 %copy-start.28 = (bf16[1,1024,8,32]{1,3,2,0:T(8,128)(2,1)S(1)}, bf16[1,1024,8,32]{1,3,2,0:T(8,128)(2,1)}, u32[]{:S(2)}) copy-start(bf16[1,1024,8,32]{1,3,2,0:T(8,128)(2,1)} %copy-done.27) | copy-start | bytes 1572868
  1653.7 212.2 %reduce-scatter.41.cloned.1.call-start = ((), (), s32[]{:S(2)}) async-start(), calls=%async_computation.40 | async-start | bytes 25165824 | tf_op jit(solution)/shard_map/reduce_scatter | solution.py:142
  1653.7 15.6 copy-start.83
  1703.6 163.0 %reduce-scatter.35.cloned.1.call-start = ((), (), s32[]{:S(2)}) async-start(), calls=%async_computation.36 | async-start | bytes 17301504 | tf_op jit(solution)/shard_map/reduce_scatter | solution.py:142
  1782.9 125.5 %reduce-scatter.39.cloned.1.call-start = ((), (), s32[]{:S(2)}) async-start(), calls=%async_computation.39 | async-start | bytes 50331648 | tf_op jit(solution)/shard_map/reduce_scatter | solution.py:142
  1865.8 133.2 %reduce-scatter.45.cloned.1.call-start = ((), (), s32[]{:S(2)}) async-start(), calls=%async_computation.50 | async-start | bytes 10485760
  1866.6 237.0 %reduce-scatter.37.cloned.1.call-start = ((), (), s32[]{:S(2)}) async-start(), calls=%async_computation.37 | async-start | bytes 7208960 | tf_op jit(solution)/shard_map/reduce_scatter | solution.py:143
  1867.2 449.2 %reduce-scatter.43.cloned.1.call-start = ((), (), s32[]{:S(2)}) async-start(), calls=%async_computation.49 | async-start | bytes 20971520
  1908.4 487.7 %reduce-scatter.25.cloned.1.call-start = ((), (), s32[]{:S(2)}) async-start(), calls=%async_computation.27 | async-start | bytes 5242880 | tf_op jit(solution)/shard_map/reduce_scatter | solution.py:109
  1922.4 531.5 %all-gather.60.cloned.1.call-start = ((), (), s32[]{:S(2)}) async-start(), calls=%async_computation.48 | async-start | bytes 6291456 | tf_op jit(solution)/shard_map/all_gather | solution.py:146
  1999.1 454.9 %all-gather.44.cloned.1.call-start = ((), (), s32[]{:S(2)}) async-start(), calls=%async_computation.38 | async-start | bytes 4325376 | tf_op jit(solution)/shard_map/all_gather | solution.py:360
  2103.5 2.0 collective-permute-start.1
  2106.7 355.4 %all-gather.58.cloned.1.call-start = ((), (), s32[]{:S(2)}) async-start(), calls=%async_computation.47 | async-start | bytes 12582912 | tf_op jit(solution)/shard_map/all_gather | solution.py:146
  2319.5 18.1 all-to-all-start.1
  2327.3 68.8 %copy-start.13 = (bf16[1,256,2048]{2,1,0:T(8,128)(2,1)S(1)}, bf16[1,256,2048]{2,1,0:T(8,128)(2,1)}, u32[]{:S(2)}) copy-start(bf16[1,256,2048]{2,1,0:T(8,128)(2,1)} %reduce-scatter.23.cloned.1.call-done) | copy-start | bytes 3145732
  2327.3 68.8 %copy-start.49 = (f32[4,1,512]{2,1,0:T(1,128)S(1)}, f32[4,1,512]{2,1,0:T(1,128)}, u32[]{:S(2)}) copy-start(f32[4,1,512]{2,1,0:T(1,128)} %copy-done.47) | copy-start | bytes 24580
  2327.3 68.8 %copy-start.68 = (f32[256]{0:T(256)S(1)}, f32[256]{0:T(256)}, u32[]{:S(2)}) copy-start(f32[256]{0:T(256)} %copy-done.67) | copy-start | bytes 3076
  2327.3 68.8 %copy-start.74 = (f32[256]{0:T(256)S(1)}, f32[256]{0:T(256)}, u32[]{:S(2)}) copy-start(f32[256]{0:T(256)} %copy-done.73) | copy-start | bytes 3076
  2337.5 67.3 %all-to-all-start.4 = ((f32[1,1,1,256,4,512]{5,3,2,1,0,4:T(8,128)}), f32[1,1,1,256,4,512]{5,3,2,1,0,4:T(8,128)}, u32[]{:S(2)}, u32[]{:S(2)}) async-start(f32[1,1,1,256,4,512]{5,3,2,1,0,4:T(8,128)} %copy.175), calls=%async_computation.10 | async-start | bytes 4194304 | tf_op jit(solution)/shard_map/all_to_all | solution.py:160
  2404.8 17.1 all-to-all-start.2
  2421.9 28.0 %all-to-all-start.5 = ((f32[1,1,1,256,4,512]{5,3,2,1,0,4:T(8,128)}), f32[1,1,1,256,4,512]{5,3,2,1,0,4:T(8,128)S(1)}, u32[]{:S(2)}, u32[]{:S(2)}) async-start(f32[1,1,1,256,4,512]{5,3,2,1,0,4:T(8,128)} %copy.180), calls=%async_computation.13 | async-start | bytes 4194304 | tf_op jit(solution)/shard_map/all_to_all | solution.py:160
  (59 other events, 330.3 us)
Sparse Core Ops, SparseCore 0:
  13.4 103.2 all-gather.45
  121.2 13.3 all-gather.47
  172.4 50.9 all-gather.27
  225.7 52.5 all-gather.53
  280.6 87.4 all-gather.49
  371.5 52.5 reduce-scatter.18
  426.2 19.8 all-gather.55
  447.6 31.2 all-gather.51
  481.1 81.9 all-gather.29
  565.0 79.2 all-gather.35
  690.5 75.2 reduce-scatter.26
  770.8 53.0 all-gather.37
  916.8 52.5 reduce-scatter.28
  974.0 52.5 all-gather.31
  1081.6 52.5 reduce-scatter.22
  1136.9 76.7 reduce-scatter.20
  1219.3 81.2 all-gather.33
  1302.6 79.2 all-gather.39
  1428.1 75.3 reduce-scatter.30
  1508.4 53.0 all-gather.41
  1653.8 52.5 reduce-scatter.32
  1708.7 25.0 reduce-scatter.40
  1783.0 18.7 reduce-scatter.34
  1866.0 42.3 reduce-scatter.38
  1911.4 87.5 reduce-scatter.44
  2001.2 102.2 reduce-scatter.36
  2106.5 209.9 reduce-scatter.42
  2319.3 76.7 reduce-scatter.24
  2397.7 14.1 all-gather.59
  2413.3 12.8 all-gather.43
  2427.7 21.0 all-gather.57

commit v5 on v4

--- a/solution.py
+++ b/solution.py
@@ -140,7 +140,9 @@
         shape[axis : axis + 1] = [count, n_dp, half]
         split = jnp.swapaxes(partial.reshape(shape), axis, axis + 1)
         split = lax.psum_scatter(split, "dp", scatter_dimension=axis)
-        return lax.psum_scatter(split, axis_name, scatter_dimension=axis)
+        return lax.psum_scatter(
+            split.astype(jnp.bfloat16), axis_name, scatter_dimension=axis
+        ).astype(jnp.float32)
 
     def reduce_features(partial, axis, axis_name):
         return lax.all_gather(reduce_half(partial, axis, axis_name), "dp", axis=axis, tiled=True)
@@ -267,11 +269,13 @@
                 "stf,fd->std", act_low, w_down_all, preferred_element_type=jnp.float32
             )
             ffn_branch = scatter_low(ffn_part, "col", 0)
-            outs_list.append(
-                to_features((resid_mid + RESIDUAL_SCALE * ffn_branch).astype(jnp.bfloat16)[None])
-            )
-
-            grad_rows = cotangent_t[batch_index].astype(jnp.float32)
+            block_out = (resid_mid + RESIDUAL_SCALE * ffn_branch).astype(jnp.bfloat16)
+            block_out, cotangent_here = lax.optimization_barrier(
+                (block_out, cotangent_t[batch_index])
+            )
+            outs_list.append(to_features(block_out[None]))
+
+            grad_rows = cotangent_here.astype(jnp.float32)
             grad_ffn = (RESIDUAL_SCALE * grad_rows).astype(jnp.bfloat16)
             spread_grad_ffn = lax.all_gather(grad_ffn, "col", axis=0, tiled=True)
             fresh_down = jnp.einsum(

time: 2490 us -> 2470 us (level)
  waiting for transfers between devices: 1490 us -> 1440 us
  other arithmetic: 165 us -> 198 us
    unnamed x33, waiting for transfers between devices: 288 us -> 191 us
    reduce_scatter x1, waiting for transfers between devices: 104 us -> 56.3 us  [reduce_half(): lax.psum_scatter(split.astype(jnp.bfloat16), axis_name, scatter_dimension...]
    all_gather x2, waiting for transfers between devices: 116 us -> 163 us  [shards(): spread_grad_ffn = lax.all_gather(grad_ffn, 'col', axis=0, tiled=True)]
    convert_element_type x1 -> x10, other arithmetic: 1.85 us -> 38.7 us  [the longest x3 20 us: reduce_half(): split.astype(jnp.bfloat16)]
    all_gather x2, waiting for transfers between devices: 121 us -> 151 us  [shards(): spread_ffn = lax.all_gather(normed_ffn, 'col', axis=0, tiled=True)]
  transfers between devices with their start and end apart: 38 -> 38, of which waited for: 25 -> 28; matrix products, arithmetic and copies ran while one was open for 19% -> 17% of each run, Pallas kernels for 0% -> 0%
where the time goes in v5:
time: 2470 us; the launch traced here: 2460 us
  waiting for transfers between devices  1440 us (58%)
  matrix products  465 us (19%)
  local copies, waits for them, and re-layouts  230 us (9%)
  other arithmetic  198 us (8%)
  blocking collectives  87.9 us (4%)
    reduce_scatter x8, waiting for transfers between devices, scatter_low(): lax.psum_scatter(partial.astype(jnp.bfloat16), axis_name, scatter_dimensi...  404 us
    unnamed x33, waiting for transfers between devices  191 us
    all_gather x3, waiting for transfers between devices, gather_half(): gathered = lax.all_gather(mine, axis_name, axis=axis)  188 us
    all_gather x2, waiting for transfers between devices, shards(): spread_grad_ffn = lax.all_gather(grad_ffn, 'col', axis=0, tiled=True)  163 us
    all_gather x2, waiting for transfers between devices, shards(): spread_ffn = lax.all_gather(normed_ffn, 'col', axis=0, tiled=True)  151 us
    all_gather x2, waiting for transfers between devices, shards(): spread_grad_attn = lax.all_gather(grad_attn, 'row', axis=1, tiled=True)  106 us
    all_gather x2, waiting for transfers between devices, shards(): spread_attn = lax.all_gather(normed_attn, 'row', axis=1, tiled=True)  80.9 us
    reshape x4, local copies, waits for them, and re-layouts, reduce_half(): split = jnp.swapaxes(partial.reshape(shape), axis, axis + 1)  67.3 us
  transfers between devices with their start and end apart: 38, of which 28 were waited for; matrix products, arithmetic and copies ran while one was open for 17% of the time, Pallas kernels for 0%

profile of v5, /device:TPU:0, one launch (start us, length us, event | category | flops | bytes accessed | tf_op | source)
XLA Modules:
  0.0 2463.1 jit_solution(8247580662542167195)
XLA Ops:
  13.3 103.4 %all-gather.46.cloned.1.call-done = bf16[1024,1280]{0,1:T(8,128)(2,1)} async-done(((bf16[256,1280]{0,1:T(8,128)(2,1)}), bf16[1024,1280]{0,1:T(8,128)(2,1)}) %all-gather.46.cloned.1.call-update) | async-done | bytes 2621456 | tf_op jit(solution)/shard_map/all_gather | solution.py:122
  128.7 28.1 %all-gather.8 = f32[4,1,512]{2,1,0:T(1,128)S(1)} all-gather(f32[1,1,512]{2,1,0:T(1,128)S(1)} %bitcast.414), channel_id=1, replica_groups=mesh['dp'=2,'row'=4,'col'=4] {'row'}, dimensions={0}, use_global_device_ids=true | all-gather | bytes 10240 | tf_op jit(solution)/shard_map/all_gather | solution.py:201
  194.6 28.8 %all-gather.28.cloned.1.call-done = bf16[1,1024,2048]{2,1,0:T(8,128)(2,1)} async-done(((bf16[1,256,2048]{2,1,0:T(8,128)(2,1)}), bf16[1,1024,2048]{2,1,0:T(8,128)(2,1)}) %all-gather.28.cloned.1.call-update) | async-done | bytes 4194320 | tf_op jit(solution)/shard_map/all_gather | solution.py:224
  230.4 13.9 fusion.132
  244.3 13.4 exponential_reduce_fusion.1
  257.7 13.3 fusion.78
  284.6 83.5 %all-gather.50.cloned.1.call-done = bf16[1024,4096]{1,0:T(8,128)(2,1)} async-done(((bf16[256,4096]{1,0:T(8,128)(2,1)}), bf16[1024,4096]{1,0:T(8,128)(2,1)}) %all-gather.50.cloned.1.call-update) | async-done | bytes 8388624 | tf_op jit(solution)/shard_map/all_gather | solution.py:122
  368.8 8.0 all-gather.9
  376.8 47.3 %reduce-scatter.19.cloned.1.call-done = bf16[1,256,2048]{2,1,0:T(8,128)(2,1)} async-done(((bf16[1,1024,2048]{2,1,0:T(8,128)(2,1)}), bf16[1,256,2048]{2,1,0:T(8,128)(2,1)}) %reduce-scatter.19.cloned.1.call-update) | async-done | bytes 1048592 | tf_op jit(solution)/shard_map/reduce_scatter | solution.py:109
  428.4 17.7 all-gather.56.cloned.1.call-done
  446.1 16.8 copy.165
  462.9 14.9 reshape.1097
  478.9 14.2 copy.162
  493.2 69.8 %all-gather.30.cloned.1.call-done = bf16[4,256,2048]{2,1,0:T(8,128)(2,1)} async-done(((bf16[1,256,2048]{2,1,0:T(8,128)(2,1)}), bf16[4,256,2048]{2,1,0:T(8,128)(2,1)}) %all-gather.30.cloned.1.call-update) | async-done | bytes 4194320 | tf_op jit(solution)/shard_map/all_gather | solution.py:260
  563.0 21.5 fusion.134
  595.0 10.4 convolution_convert_fusion.1
  607.3 28.7 %all_to_all.90 = bf16[2,1,4,256,1,512]{5,3,0,4,1,2:T(8,128)(2,1)S(1)} all-to-all(bf16[2,1,4,256,1,512]{5,3,0,4,1,2:T(8,128)(2,1)S(1)} %copy.166), channel_id=1, replica_groups=mesh['dp'=2,'row'=4,'col'=4] {'row'}, dimensions={2} | all-to-all | bytes 4194304 | tf_op jit(solution)/shard_map/all_to_all | solution.py:156
  641.6 39.3 %reduce-scatter.21.cloned.1.call-done = bf16[1,256,2048]{2,1,0:T(8,128)(2,1)} async-done(((bf16[4,256,2048]{2,1,0:T(8,128)(2,1)}), bf16[1,256,2048]{2,1,0:T(8,128)(2,1)}) %reduce-scatter.21.cloned.1.call-update) | async-done | bytes 1048592 | tf_op jit(solution)/shard_map/reduce_scatter | solution.py:109
  684.9 81.4 %all-gather.36.cloned.1.call-done = bf16[4,256,2048]{2,1,0:T(8,128)(2,1)} async-done(((bf16[1,256,2048]{2,1,0:T(8,128)(2,1)}), bf16[4,256,2048]{2,1,0:T(8,128)(2,1)}) %all-gather.36.cloned.1.call-update) | async-done | bytes 4194320 | tf_op jit(solution)/shard_map/all_gather | solution.py:280
  766.2 20.5 multiply_convert_fusion.3
  786.7 23.8 fusion.37
  810.6 75.4 %reduce-scatter.27.cloned.1.call-done = bf16[1,256,2048]{2,1,0:T(8,128)(2,1)} async-done(((bf16[4,256,2048]{2,1,0:T(8,128)(2,1)}), bf16[1,256,2048]{2,1,0:T(8,128)(2,1)}) %reduce-scatter.27.cloned.1.call-update) | async-done | bytes 1048592 | tf_op jit(solution)/shard_map/reduce_scatter | solution.py:109
  891.1 53.2 %all-gather.38.cloned.1.call-done = bf16[1,1024,2048]{2,1,0:T(8,128)(2,1)} async-done(((bf16[1,256,2048]{2,1,0:T(8,128)(2,1)}), bf16[1,1024,2048]{2,1,0:T(8,128)(2,1)}) %all-gather.38.cloned.1.call-update) | async-done | bytes 4194320 | tf_op jit(solution)/shard_map/all_gather | solution.py:306
  949.5 14.5 fusion.98
  964.0 21.6 fusion.3
  985.6 28.1 %fusion.5 = bf16[2,4,1024,1024]{2,3,1,0:T(8,128)(2,1)} fusion(f32[2,1024,1024,4]{2,1,3,0:T(8,128)} %get-tuple-element.331, f32[2,4,1024,1024]{2,3,1,0:T(8,128)} %get-tuple-element.329, f32[2,4,1024]{2,1,0:T(4,128)S(1)} %get-tuple-element.330, f32[2,4,1024]{2,1,0:T(4,128)S(1)} %bitcast.356), kind=kLoop, calls=%fused_computation.10 | loop fusion | flops 33554432 | bytes 83951616 | tf_op jit(solution)/shard_map/while/body/eval_jaxpr/convert_element_type | solution.py:96
  1013.6 9.1 fusion.97
  1045.5 44.5 %reduce-scatter.29.cloned.1.call-done = bf16[1,256,2048]{2,1,0:T(8,128)(2,1)} async-done(((bf16[1,1024,2048]{2,1,0:T(8,128)(2,1)}), bf16[1,256,2048]{2,1,0:T(8,128)(2,1)}) %reduce-scatter.29.cloned.1.call-update) | async-done | bytes 1048592 | tf_op jit(solution)/shard_map/reduce_scatter | solution.py:109
  1095.0 52.1 %all-gather.32.cloned.1.call-done = bf16[1,1024,2048]{2,1,0:T(8,128)(2,1)} async-done(((bf16[1,256,2048]{2,1,0:T(8,128)(2,1)}), bf16[1,1024,2048]{2,1,0:T(8,128)(2,1)}) %all-gather.32.cloned.1.call-update) | async-done | bytes 4194320 | tf_op jit(solution)/shard_map/all_gather | solution.py:224
  1154.7 13.7 fusion.133
  1168.4 13.1 exponential_reduce_fusion
  1181.5 13.3 fusion.81
  1202.4 52.3 %reduce-scatter.23.cloned.1.call-done = bf16[1,256,2048]{2,1,0:T(8,128)(2,1)} async-done(((bf16[1,1024,2048]{2,1,0:T(8,128)(2,1)}), bf16[1,256,2048]{2,1,0:T(8,128)(2,1)}) %reduce-scatter.23.cloned.1.call-update) | async-done | bytes 1048592 | tf_op jit(solution)/shard_map/reduce_scatter | solution.py:109
  1261.7 80.8 %all-gather.34.cloned.1.call-done = bf16[4,256,2048]{2,1,0:T(8,128)(2,1)} async-done(((bf16[1,256,2048]{2,1,0:T(8,128)(2,1)}), bf16[4,256,2048]{2,1,0:T(8,128)(2,1)}) %all-gather.34.cloned.1.call-update) | async-done | bytes 4194320 | tf_op jit(solution)/shard_map/all_gather | solution.py:260
  1342.5 21.5 fusion.135
  1371.9 12.5 convolution_convert_fusion
  1390.3 69.6 %reduce-scatter.25.cloned.1.call-done = bf16[1,256,2048]{2,1,0:T(8,128)(2,1)} async-done(((bf16[4,256,2048]{2,1,0:T(8,128)(2,1)}), bf16[1,256,2048]{2,1,0:T(8,128)(2,1)}) %reduce-scatter.25.cloned.1.call-update) | async-done | bytes 1048592 | tf_op jit(solution)/shard_map/reduce_scatter | solution.py:109
  1464.1 81.2 %all-gather.40.cloned.1.call-done = bf16[4,256,2048]{2,1,0:T(8,128)(2,1)} async-done(((bf16[1,256,2048]{2,1,0:T(8,128)(2,1)}), bf16[4,256,2048]{2,1,0:T(8,128)(2,1)}) %all-gather.40.cloned.1.call-update) | async-done | bytes 4194320 | tf_op jit(solution)/shard_map/all_gather | solution.py:280
  1545.2 20.3 multiply_convert_fusion.1
  1565.6 23.8 fusion.38
  1589.5 75.4 %reduce-scatter.31.cloned.1.call-done = bf16[1,256,2048]{2,1,0:T(8,128)(2,1)} async-done(((bf16[4,256,2048]{2,1,0:T(8,128)(2,1)}), bf16[1,256,2048]{2,1,0:T(8,128)(2,1)}) %reduce-scatter.31.cloned.1.call-update) | async-done | bytes 1048592 | tf_op jit(solution)/shard_map/reduce_scatter | solution.py:109
  1669.9 53.2 %all-gather.42.cloned.1.call-done = bf16[1,1024,2048]{2,1,0:T(8,128)(2,1)} async-done(((bf16[1,256,2048]{2,1,0:T(8,128)(2,1)}), bf16[1,1024,2048]{2,1,0:T(8,128)(2,1)}) %all-gather.42.cloned.1.call-update) | async-done | bytes 4194320 | tf_op jit(solution)/shard_map/all_gather | solution.py:306
  1728.4 14.3 fusion.101
  1742.6 21.6 fusion
  1764.3 28.3 %fusion.2 = bf16[2,4,1024,1024]{2,3,1,0:T(8,128)(2,1)} fusion(f32[2,1024,1024,4]{2,1,3,0:T(8,128)} %get-tuple-element.335, f32[2,4,1024,1024]{2,3,1,0:T(8,128)} %get-tuple-element.333, f32[2,4,1024]{2,1,0:T(4,128)S(1)} %get-tuple-element.334, f32[2,4,1024]{2,1,0:T(4,128)S(1)} %bitcast.360), kind=kLoop, calls=%fused_computation.5 | loop fusion | flops 33554432 | bytes 83951616 | tf_op jit(solution)/shard_map/while/body/eval_jaxpr/convert_element_type | solution.py:96
  1792.6 11.0 fusion.96
  1815.5 16.0 fusion.136
  1831.5 17.5 bitcast_add_fusion.1
  1849.0 16.4 copy.187
  1890.9 15.3 psum.7
  1906.2 10.0 select_maximum_fusion
  1916.2 15.7 reshape.1074
  1931.9 12.3 copy.217
  1944.5 26.7 %fusion.9 = f32[2048,4096,1]{1,0,2:T(8,128)} fusion(bf16[4,256,2048]{2,1,0:T(8,128)(2,1)} %all-gather.30.cloned.1.call-done, bf16[4,256,2048]{2,1,0:T(8,128)(2,1)} %get-tuple-element.281, bf16[4,256,2048]{2,1,0:T(8,128)(2,1)} %get-tuple-element.280), kind=kOutput, calls=%fused_computation.37 | convolution fusion | flops 17196646400 | bytes 46137344 | tf_op jit(solution)/shard_map/std,stf->df/dot_general | solution.py:294
  1971.2 32.8 %bitcast_add_fusion = f32[2048,4096]{1,0:T(8,128)} fusion(f32[2048,4096,1]{1,0,2:T(8,128)} %fusion.9, bf16[4,256,2048]{2,1,0:T(8,128)(2,1)} %all-gather.34.cloned.1.call-done, bf16[4,256,2048]{2,1,0:T(8,128)(2,1)} %get-tuple-element.283, bf16[4,256,2048]{2,1,0:T(8,128)(2,1)} %get-tuple-element.282), kind=kOutput, calls=%fused_computation | convolution fusion | flops 17205035008 | bytes 79691776 | tf_op jit(solution)/shard_map/std,stf->df/dot_general | solution.py:294
  2003.9 22.9 copy.216
  2038.0 31.3 %reduce-scatter.39.cloned.1.call-done = f32[1,4,256,4096]{3,2,1,0:T(8,128)} async-done(((f32[2,4,256,4096]{3,2,1,0:T(8,128)}), f32[1,4,256,4096]{3,2,1,0:T(8,128)}) %reduce-scatter.39.cloned.1.call-update) | async-done | bytes 16777232 | tf_op jit(solution)/shard_map/reduce_scatter | solution.py:142
  2069.2 9.1 convert_bitcast_fusion
  2078.4 48.2 %reduce-scatter.45.cloned.1.call-done = bf16[2048,1,256]{2,0,1:T(8,128)(2,1)} async-done(((bf16[2048,4,256]{2,0,1:T(8,128)(2,1)}), bf16[2048,1,256]{2,0,1:T(8,128)(2,1)}) %reduce-scatter.45.cloned.1.call-update) | async-done | bytes 1048592
  2129.3 56.3 %reduce-scatter.37.cloned.1.call-done = bf16[1,256,1408]{1,2,0:T(8,128)(2,1)} async-done(((bf16[4,256,1408]{1,2,0:T(8,128)(2,1)}), bf16[1,256,1408]{1,2,0:T(8,128)(2,1)}) %reduce-scatter.37.cloned.1.call-update) | async-done | bytes 720912 | tf_op jit(solution)/shard_map/reduce_scatter | solution.py:143
  2188.8 142.5 %reduce-scatter.43.cloned.1.call-done = bf16[1,256,4096]{2,1,0:T(8,128)(2,1)} async-done(((bf16[4,256,4096]{2,1,0:T(8,128)(2,1)}), bf16[1,256,4096]{2,1,0:T(8,128)(2,1)}) %reduce-scatter.43.cloned.1.call-update) | async-done | bytes 2097168
  2367.5 19.5 all-to-all-done.4
  2410.8 21.6 all-to-all-done.5
  2444.6 8.1 fusion.128
  (399 shorter events, 321.7 us)
Async XLA Ops:
  7.2 165.2 %copy-start = (bf16[2048,512]{1,0:T(8,128)(2,1)S(1)}, bf16[2048,512]{1,0:T(8,128)(2,1)}, u32[]{:S(2)}) copy-start(bf16[2048,512]{1,0:T(8,128)(2,1)} %param.20) | copy-start | bytes 6291460
  7.2 109.5 %all-gather.46.cloned.1.call-start = ((), (), s32[]{:S(2)}) async-start(), calls=%async_computation.41 | async-start | bytes 3276800 | tf_op jit(solution)/shard_map/all_gather | solution.py:122
  11.7 0.7 collective-permute-start
  13.3 176.1 %all-gather.48.cloned.1.call-start = ((), (), s32[]{:S(2)}) async-start(), calls=%async_computation.42 | async-start | bytes 7864320 | tf_op jit(solution)/shard_map/all_gather | solution.py:123
  124.1 32.7 %all-to-all-start = ((bf16[2,1,4,256,1,512]{5,3,0,4,1,2:T(8,128)(2,1)}), bf16[2,1,4,256,1,512]{5,3,0,4,1,2:T(8,128)(2,1)}, u32[]{:S(2)}, u32[]{:S(2)}) async-start(bf16[2,1,4,256,1,512]{5,3,0,4,1,2:T(8,128)(2,1)} %copy.152), calls=%async_computation | async-start | bytes 4194304 | tf_op jit(solution)/shard_map/all_to_all | solution.py:156
  128.7 94.8 %all-gather.28.cloned.1.call-start = ((), (), s32[]{:S(2)}) async-start(), calls=%async_computation.20 | async-start | bytes 5242880 | tf_op jit(solution)/shard_map/all_gather | solution.py:224
  172.3 106.0 %all-gather.54.cloned.1.call-start = ((), (), s32[]{:S(2)}) async-start(), calls=%async_computation.45 | async-start | bytes 5242880 | tf_op jit(solution)/shard_map/all_gather | solution.py:122
  173.9 194.2 %all-gather.50.cloned.1.call-start = ((), (), s32[]{:S(2)}) async-start(), calls=%async_computation.43 | async-start | bytes 10485760 | tf_op jit(solution)/shard_map/all_gather | solution.py:122
  177.2 246.9 %reduce-scatter.19.cloned.1.call-start = ((), (), s32[]{:S(2)}) async-start(), calls=%async_computation.21 | async-start | bytes 5242880 | tf_op jit(solution)/shard_map/reduce_scatter | solution.py:109
  188.8 41.2 %copy-start.30 = (f32[1024,32]{0,1:T(8,128)}, f32[1024,32]{0,1:T(8,128)S(1)}, u32[]{:S(2)}) copy-start(f32[1024,32]{0,1:T(8,128)S(1)} %get-tuple-element.321) | copy-start | bytes 393220
  229.7 28.0 %copy-start.32 = (bf16[1,1024,128]{1,2,0:T(8,128)(2,1)}, bf16[1,1024,128]{1,2,0:T(8,128)(2,1)S(1)}, u32[]{:S(2)}) copy-start(bf16[1,1024,128]{1,2,0:T(8,128)(2,1)S(1)} %slice.361) | copy-start | bytes 786436
  230.0 14.3 copy-start.56
  277.5 168.6 %all-gather.56.cloned.1.call-start = ((), (), s32[]{:S(2)}) async-start(), calls=%async_computation.46 | async-start | bytes 12582912 | tf_op jit(solution)/shard_map/all_gather | solution.py:123
  284.5 194.4 %all-gather.52.cloned.1.call-start = ((), (), s32[]{:S(2)}) async-start(), calls=%async_computation.44 | async-start | bytes 25165824 | tf_op jit(solution)/shard_map/all_gather | solution.py:123
  368.1 56.0 %copy-start.4 = (f32[1,256,2048]{2,1,0:T(8,128)S(1)}, f32[1,256,2048]{2,1,0:T(8,128)}, u32[]{:S(2)}) copy-start(f32[1,256,2048]{2,1,0:T(8,128)} %reshape.1077) | copy-start | bytes 6291460
  368.1 194.9 %all-gather.30.cloned.1.call-start = ((), (), s32[]{:S(2)}) async-start(), calls=%async_computation.22 | async-start | bytes 5242880 | tf_op jit(solution)/shard_map/all_gather | solution.py:260
  376.8 1291.0 %copy-start.60 = (f32[4,1,512]{2,1,0:T(1,128)}, f32[4,1,512]{2,1,0:T(1,128)S(1)}, u32[]{:S(2)}) copy-start(f32[4,1,512]{2,1,0:T(1,128)S(1)} %all-gather.9) | copy-start | bytes 24580
  428.4 252.5 %reduce-scatter.21.cloned.1.call-start = ((), (), s32[]{:S(2)}) async-start(), calls=%async_computation.23 | async-start | bytes 5242880 | tf_op jit(solution)/shard_map/reduce_scatter | solution.py:109
  605.4 160.8 %all-gather.36.cloned.1.call-start = ((), (), s32[]{:S(2)}) async-start(), calls=%async_computation.28 | async-start | bytes 5242880 | tf_op jit(solution)/shard_map/all_gather | solution.py:280
  636.0 44.9 %copy-start.8 = (bf16[1,256,2048]{2,1,0:T(8,128)(2,1)S(1)}, bf16[1,256,2048]{2,1,0:T(8,128)(2,1)}, u32[]{:S(2)}) copy-start(bf16[1,256,2048]{2,1,0:T(8,128)(2,1)} %reduce-scatter.19.cloned.1.call-done) | copy-start | bytes 3145732
  684.8 201.2 %reduce-scatter.27.cloned.1.call-start = ((), (), s32[]{:S(2)}) async-start(), calls=%async_computation.29 | async-start | bytes 5242880 | tf_op jit(solution)/shard_map/reduce_scatter | solution.py:109
  810.5 133.7 %all-gather.38.cloned.1.call-start = ((), (), s32[]{:S(2)}) async-start(), calls=%async_computation.30 | async-start | bytes 5242880 | tf_op jit(solution)/shard_map/all_gather | solution.py:306
  891.0 58.5 %copy-start.35 = (f32[1,8,1024]{2,1,0:T(8,128)S(1)}, f32[1,8,1024]{2,1,0:T(8,128)}, u32[]{:S(2)}) copy-start(f32[1,8,1024]{2,1,0:T(8,128)} %copy-done.34) | copy-start | bytes 98308
  891.0 199.0 %reduce-scatter.29.cloned.1.call-start = ((), (), s32[]{:S(2)}) async-start(), calls=%async_computation.31 | async-start | bytes 5242880 | tf_op jit(solution)/shard_map/reduce_scatter | solution.py:109
  949.5 14.5 copy-start.33
  1037.2 109.9 %all-gather.32.cloned.1.call-start = ((), (), s32[]{:S(2)}) async-start(), calls=%async_computation.24 | async-start | bytes 5242880 | tf_op jit(solution)/shard_map/all_gather | solution.py:224
  1037.4 52.5 %copy-start.63 = (f32[4,1,512]{2,1,0:T(1,128)S(1)}, f32[4,1,512]{2,1,0:T(1,128)}, u32[]{:S(2)}) copy-start(f32[4,1,512]{2,1,0:T(1,128)} %copy-done.62) | copy-start | bytes 24580
  1037.5 52.5 %copy-start.80 = (f32[256]{0:T(256)S(1)}, f32[256]{0:T(256)}, u32[]{:S(2)}) copy-start(f32[256]{0:T(256)} %copy-done.79) | copy-start | bytes 3076
  1045.4 49.0 %copy-start.73 = (s32[1,1,1024]{2,0,1:T(1,128)S(1)}, s32[1,1,1024]{2,0,1:T(1,128)}, u32[]{:S(2)}) copy-start(s32[1,1,1024]{2,0,1:T(1,128)} %get-tuple-element.313) | copy-start | bytes 12292
  1045.5 49.6 %copy-start.81 = (f32[256]{0:T(256)}, f32[256]{0:T(256)S(1)}, u32[]{:S(2)}) copy-start(f32[256]{0:T(256)S(1)} %add_rsqrt_fusion.1) | copy-start | bytes 3076
  1094.4 160.3 %reduce-scatter.23.cloned.1.call-start = ((), (), s32[]{:S(2)}) async-start(), calls=%async_computation.25 | async-start | bytes 5242880 | tf_op jit(solution)/shard_map/reduce_scatter | solution.py:109
  1201.9 55.2 %copy-start.9 = (bf16[1,256,2048]{2,1,0:T(8,128)(2,1)S(1)}, bf16[1,256,2048]{2,1,0:T(8,128)(2,1)}, u32[]{:S(2)}) copy-start(bf16[1,256,2048]{2,1,0:T(8,128)(2,1)} %reduce-scatter.19.cloned.1.call-done) | copy-start | bytes 3145732
  1201.9 140.6 %all-gather.34.cloned.1.call-start = ((), (), s32[]{:S(2)}) async-start(), calls=%async_computation.26 | async-start | bytes 5242880 | tf_op jit(solution)/shard_map/all_gather | solution.py:260
  1257.2 410.6 %copy-start.77 = (f32[256]{0:T(256)}, f32[256]{0:T(256)S(1)}, u32[]{:S(2)}) copy-start(f32[256]{0:T(256)S(1)} %add_rsqrt_fusion) | copy-start | bytes 3076
  1261.6 198.2 %reduce-scatter.25.cloned.1.call-start = ((), (), s32[]{:S(2)}) async-start(), calls=%async_computation.27 | async-start | bytes 5242880 | tf_op jit(solution)/shard_map/reduce_scatter | solution.py:109
  1384.4 75.5 %copy-start.6 = (f32[1,256,2048]{2,1,0:T(8,128)S(1)}, f32[1,256,2048]{2,1,0:T(8,128)}, u32[]{:S(2)}) copy-start(f32[1,256,2048]{2,1,0:T(8,128)} %reshape.1078) | copy-start | bytes 6291460
  1384.4 75.5 %copy-start.10 = (bf16[1,256,2048]{2,1,0:T(8,128)(2,1)S(1)}, bf16[1,256,2048]{2,1,0:T(8,128)(2,1)}, u32[]{:S(2)}) copy-start(bf16[1,256,2048]{2,1,0:T(8,128)(2,1)} %reduce-scatter.23.cloned.1.call-done) | copy-start | bytes 3145732
  1384.4 160.8 %all-gather.40.cloned.1.call-start = ((), (), s32[]{:S(2)}) async-start(), calls=%async_computation.32 | async-start | bytes 5242880 | tf_op jit(solution)/shard_map/all_gather | solution.py:280
  1463.8 201.0 %reduce-scatter.31.cloned.1.call-start = ((), (), s32[]{:S(2)}) async-start(), calls=%async_computation.33 | async-start | bytes 5242880 | tf_op jit(solution)/shard_map/reduce_scatter | solution.py:109
  1589.4 133.7 %all-gather.42.cloned.1.call-start = ((), (), s32[]{:S(2)}) async-start(), calls=%async_computation.34 | async-start | bytes 5242880 | tf_op jit(solution)/shard_map/all_gather | solution.py:306
  1667.8 60.6 %copy-start.83 = (f32[256]{0:T(256)}, f32[256]{0:T(256)S(1)}, u32[]{:S(2)}) copy-start(f32[256]{0:T(256)S(1)} %broadcast_multiply_fusion.1) | copy-start | bytes 3076
  1669.9 218.7 %reduce-scatter.33.cloned.1.call-start = ((), (), s32[]{:S(2)}) async-start(), calls=%async_computation.35 | async-start | bytes 5242880 | tf_op jit(solution)/shard_map/reduce_scatter | solution.py:109
  1764.3 28.3 %copy-start.39 = (bf16[1,1024,8,32]{1,3,2,0:T(8,128)(2,1)S(1)}, bf16[1,1024,8,32]{1,3,2,0:T(8,128)(2,1)}, u32[]{:S(2)}) copy-start(bf16[1,1024,8,32]{1,3,2,0:T(8,128)(2,1)} %copy-done.38) | copy-start | bytes 1572868
  1764.3 28.3 %copy-start.41 = (bf16[1,1024,8,32]{1,3,2,0:T(8,128)(2,1)S(1)}, bf16[1,1024,8,32]{1,3,2,0:T(8,128)(2,1)}, u32[]{:S(2)}) copy-start(bf16[1,1024,8,32]{1,3,2,0:T(8,128)(2,1)} %copy-done.40) | copy-start | bytes 1572868
  1815.5 211.4 %reduce-scatter.41.cloned.1.call-start = ((), (), s32[]{:S(2)}) async-start(), calls=%async_computation.40 | async-start | bytes 25165824 | tf_op jit(solution)/shard_map/reduce_scatter | solution.py:142
  1815.5 16.0 copy-start.23
  1865.5 167.3 %reduce-scatter.35.cloned.1.call-start = ((), (), s32[]{:S(2)}) async-start(), calls=%async_computation.36 | async-start | bytes 17301504 | tf_op jit(solution)/shard_map/reduce_scatter | solution.py:142
  1944.2 125.0 %reduce-scatter.39.cloned.1.call-start = ((), (), s32[]{:S(2)}) async-start(), calls=%async_computation.39 | async-start | bytes 50331648 | tf_op jit(solution)/shard_map/reduce_scatter | solution.py:142
  2026.8 99.8 %reduce-scatter.45.cloned.1.call-start = ((), (), s32[]{:S(2)}) async-start(), calls=%async_computation.50 | async-start | bytes 5242880
  2032.7 152.9 %reduce-scatter.37.cloned.1.call-start = ((), (), s32[]{:S(2)}) async-start(), calls=%async_computation.37 | async-start | bytes 3604480 | tf_op jit(solution)/shard_map/reduce_scatter | solution.py:143
  2037.9 293.4 %reduce-scatter.43.cloned.1.call-start = ((), (), s32[]{:S(2)}) async-start(), calls=%async_computation.49 | async-start | bytes 10485760
  2078.3 358.2 %all-gather.60.cloned.1.call-start = ((), (), s32[]{:S(2)}) async-start(), calls=%async_computation.48 | async-start | bytes 6291456 | tf_op jit(solution)/shard_map/all_gather | solution.py:148
  2129.3 307.2 %all-gather.44.cloned.1.call-start = ((), (), s32[]{:S(2)}) async-start(), calls=%async_computation.38 | async-start | bytes 4325376 | tf_op jit(solution)/shard_map/all_gather | solution.py:364
  2186.9 0.8 collective-permute-start.1
  2188.8 146.7 %copy-start.24 = (bf16[1,256,2048]{2,1,0:T(8,128)(2,1)S(1)}, bf16[1,256,2048]{2,1,0:T(8,128)(2,1)}, u32[]{:S(2)}) copy-start(bf16[1,256,2048]{2,1,0:T(8,128)(2,1)} %add_convert_fusion.1) | copy-start | bytes 3145732
  2188.8 255.8 %all-gather.58.cloned.1.call-start = ((), (), s32[]{:S(2)}) async-start(), calls=%async_computation.47 | async-start | bytes 12582912 | tf_op jit(solution)/shard_map/all_gather | solution.py:148
  2339.4 17.5 all-to-all-start.2
  2357.9 29.1 %all-to-all-start.4 = ((f32[1,1,1,256,4,512]{5,3,2,1,0,4:T(8,128)}), f32[1,1,1,256,4,512]{5,3,2,1,0,4:T(8,128)}, u32[]{:S(2)}, u32[]{:S(2)}) async-start(f32[1,1,1,256,4,512]{5,3,2,1,0,4:T(8,128)} %copy.176), calls=%async_computation.10 | async-start | bytes 4194304 | tf_op jit(solution)/shard_map/all_to_all | solution.py:162
  2362.4 28.9 %copy-start.11 = (bf16[1,256,2048]{2,1,0:T(8,128)(2,1)S(1)}, bf16[1,256,2048]{2,1,0:T(8,128)(2,1)}, u32[]{:S(2)}) copy-start(bf16[1,256,2048]{2,1,0:T(8,128)(2,1)} %reduce-scatter.23.cloned.1.call-done) | copy-start | bytes 3145732
  2362.4 28.9 %copy-start.61 = (f32[4,1,512]{2,1,0:T(1,128)S(1)}, f32[4,1,512]{2,1,0:T(1,128)}, u32[]{:S(2)}) copy-start(f32[4,1,512]{2,1,0:T(1,128)} %copy-done.60) | copy-start | bytes 24580
  2362.4 28.9 %copy-start.78 = (f32[256]{0:T(256)S(1)}, f32[256]{0:T(256)}, u32[]{:S(2)}) copy-start(f32[256]{0:T(256)} %copy-done.77) | copy-start | bytes 3076
  2362.4 28.9 %copy-start.84 = (f32[256]{0:T(256)S(1)}, f32[256]{0:T(256)}, u32[]{:S(2)}) copy-start(f32[256]{0:T(256)} %copy-done.83) | copy-start | bytes 3076
  2387.0 17.5 all-to-all-start.3
  2404.5 28.0 %all-to-all-start.5 = ((f32[1,1,1,256,4,512]{5,3,2,1,0,4:T(8,128)}), f32[1,1,1,256,4,512]{5,3,2,1,0,4:T(8,128)S(1)}, u32[]{:S(2)}, u32[]{:S(2)}) async-start(f32[1,1,1,256,4,512]{5,3,2,1,0,4:T(8,128)} %copy.180), calls=%async_computation.13 | async-start | bytes 4194304 | tf_op jit(solution)/shard_map/all_to_all | solution.py:162
  (66 other events, 358.8 us)
Sparse Core Ops, SparseCore 0:
  13.4 103.2 all-gather.45
  121.2 13.3 all-gather.47
  172.4 50.9 all-gather.27
  225.7 52.5 all-gather.53
  280.6 87.4 all-gather.49
  371.5 52.5 reduce-scatter.18
  426.2 19.8 all-gather.55
  447.6 31.2 all-gather.51
  481.1 81.9 all-gather.29
  605.5 75.2 reduce-scatter.20
  685.0 81.2 all-gather.35
  810.7 75.2 reduce-scatter.26
  891.1 53.0 all-gather.37
  1037.3 52.5 reduce-scatter.28
  1094.5 52.5 all-gather.31
  1202.0 52.5 reduce-scatter.22
  1261.8 80.7 all-gather.33
  1384.5 75.2 reduce-scatter.24
  1464.0 81.2 all-gather.39
  1589.5 75.2 reduce-scatter.30
  1670.0 53.0 all-gather.41
  1815.6 52.5 reduce-scatter.32
  1870.5 25.0 reduce-scatter.40
  1944.4 18.6 reduce-scatter.34
  2026.9 42.2 reduce-scatter.38
  2072.6 53.8 reduce-scatter.44
  2129.3 56.3 reduce-scatter.36
  2188.7 142.5 reduce-scatter.42
  2333.5 13.6 all-gather.59
  2348.5 12.8 all-gather.43
  2363.6 21.0 all-gather.57

commit v6 on v5

--- a/solution.py
+++ b/solution.py
@@ -111,6 +111,37 @@
     ).astype(jnp.float32)
 
 
+def run_interleaved(streams):
+    pending = {}
+    finished = {}
+
+    def feed(index, value):
+        try:
+            pending[index] = streams[index].send(value)
+        except StopIteration as stop:
+            finished[index] = stop.value
+
+    for index in range(len(streams)):
+        feed(index, None)
+    previous = None
+    while len(finished) < len(streams):
+        for index in range(len(streams)):
+            if index in finished:
+                continue
+            if previous is not None and previous[0] == index:
+                feed(index, previous[1])
+                previous = None
+                if index in finished:
+                    continue
+            collective, operand = pending[index]
+            if previous is not None:
+                owner, result = previous
+                result, operand = lax.optimization_barrier((result, operand))
+                feed(owner, result)
+            previous = (index, collective(operand))
+    return [finished[index] for index in range(len(streams))]
+
+
 def make_shards(n_dp, n_row, n_col):
     assert n_row == n_col
     transpose_pairs = [
@@ -149,6 +180,18 @@
 
     def transpose_grid(block):
         return lax.ppermute(block, ("row", "col"), transpose_pairs)
+
+    def gather_tokens(rows):
+        return lax.all_gather(rows, "row", axis=1, tiled=True)
+
+    def scatter_tokens(rows):
+        return lax.psum_scatter(rows, "row", scatter_dimension=1, tiled=True)
+
+    def gather_seqs(rows):
+        return lax.all_gather(rows, "col", axis=0, tiled=True)
+
+    def scatter_seqs(rows):
+        return lax.psum_scatter(rows, "col", scatter_dimension=0, tiled=True)
 
     def to_tokens(rows):
         batches, local, seq_len, width = rows.shape
@@ -209,19 +252,12 @@
         hidden_t = to_tokens(hidden_in)
         cotangent_t = to_tokens(cotangent)
 
-        grad_attn_w = None
-        grad_pair_w = None
-        grad_down_w = None
-        gain_attn_total = jnp.zeros(gain_attn_all.shape, jnp.float32)
-        gain_ffn_total = jnp.zeros(gain_ffn_all.shape, jnp.float32)
-        outs_list = []
-        inputs_grad = []
-        for batch_index in range(batches):
+        def micro_batch(batch_index):
             rows_f = hidden_t[batch_index].astype(jnp.float32)
             inv_attn = lax.rsqrt(jnp.mean(rows_f * rows_f, axis=-1, keepdims=True) + EPSILON)
             norm_attn = rows_f * inv_attn
             normed_attn = (norm_attn * gain_attn_all).astype(jnp.bfloat16)
-            spread_attn = lax.all_gather(normed_attn, "row", axis=1, tiled=True)
+            spread_attn = yield (gather_tokens, normed_attn)
             qkv = jnp.einsum(
                 "std,dm->stm", spread_attn, w_qkv, preferred_element_type=jnp.float32
             )
@@ -252,12 +288,13 @@
             attn_part = jnp.einsum(
                 "stm,md->std", mixed, w_out_heads, preferred_element_type=jnp.float32
             )
-            attn_branch = scatter_low(attn_part, "row", 1)
+            attn_branch = yield (scatter_tokens, attn_part.astype(jnp.bfloat16))
+            attn_branch = attn_branch.astype(jnp.float32)
             resid_mid = rows_f + RESIDUAL_SCALE * attn_branch
             inv_ffn = lax.rsqrt(jnp.mean(resid_mid * resid_mid, axis=-1, keepdims=True) + EPSILON)
             norm_ffn = resid_mid * inv_ffn
             normed_ffn = (norm_ffn * gain_ffn_all).astype(jnp.bfloat16)
-            spread_ffn = lax.all_gather(normed_ffn, "col", axis=0, tiled=True)
+            spread_ffn = yield (gather_seqs, normed_ffn)
             pair = jnp.einsum(
                 "std,df->stf", spread_ffn, w_pair, preferred_element_type=jnp.float32
             )
@@ -268,16 +305,14 @@
             ffn_part = jnp.einsum(
                 "stf,fd->std", act_low, w_down_all, preferred_element_type=jnp.float32
             )
-            ffn_branch = scatter_low(ffn_part, "col", 0)
+            ffn_branch = yield (scatter_seqs, ffn_part.astype(jnp.bfloat16))
+            ffn_branch = ffn_branch.astype(jnp.float32)
             block_out = (resid_mid + RESIDUAL_SCALE * ffn_branch).astype(jnp.bfloat16)
-            block_out, cotangent_here = lax.optimization_barrier(
-                (block_out, cotangent_t[batch_index])
-            )
-            outs_list.append(to_features(block_out[None]))
-
-            grad_rows = cotangent_here.astype(jnp.float32)
+            block_features = to_features(block_out[None])
+
+            grad_rows = cotangent_t[batch_index].astype(jnp.float32)
             grad_ffn = (RESIDUAL_SCALE * grad_rows).astype(jnp.bfloat16)
-            spread_grad_ffn = lax.all_gather(grad_ffn, "col", axis=0, tiled=True)
+            spread_grad_ffn = yield (gather_seqs, grad_ffn)
             fresh_down = jnp.einsum(
                 "stf,std->fd", act_low, spread_grad_ffn, preferred_element_type=jnp.float32
             )
@@ -297,13 +332,14 @@
             grad_normed_part = jnp.einsum(
                 "stf,df->std", paired_gradient, w_pair, preferred_element_type=jnp.float32
             )
-            grad_normed_ffn = scatter_low(grad_normed_part, "col", 0)
+            grad_normed_ffn = yield (scatter_seqs, grad_normed_part.astype(jnp.bfloat16))
+            grad_normed_ffn = grad_normed_ffn.astype(jnp.float32)
             scaled_ffn = grad_normed_ffn * gain_ffn_all
-            gain_ffn_total = gain_ffn_total + jnp.sum(grad_normed_ffn * norm_ffn, axis=(0, 1))
+            gain_ffn_part = jnp.sum(grad_normed_ffn * norm_ffn, axis=(0, 1))
             inner_ffn = jnp.mean(scaled_ffn * norm_ffn, axis=-1, keepdims=True)
             grad_mid = grad_rows + inv_ffn * (scaled_ffn - norm_ffn * inner_ffn)
             grad_attn = (RESIDUAL_SCALE * grad_mid).astype(jnp.bfloat16)
-            spread_grad_attn = lax.all_gather(grad_attn, "row", axis=1, tiled=True)
+            spread_grad_attn = yield (gather_tokens, grad_attn)
             fresh_out = jnp.einsum(
                 "std,stm->dm", spread_grad_attn, mixed, preferred_element_type=jnp.float32
             )
@@ -341,21 +377,32 @@
             grad_normed_attn_part = jnp.einsum(
                 "stm,dm->std", grad_qkv, w_qkv, preferred_element_type=jnp.float32
             )
-            grad_normed_attn = scatter_low(grad_normed_attn_part, "row", 1)
+            grad_normed_attn = yield (
+                scatter_tokens, grad_normed_attn_part.astype(jnp.bfloat16)
+            )
+            grad_normed_attn = grad_normed_attn.astype(jnp.float32)
             scaled_attn = grad_normed_attn * gain_attn_all
-            gain_attn_total = gain_attn_total + jnp.sum(grad_normed_attn * norm_attn, axis=(0, 1))
+            gain_attn_part = jnp.sum(grad_normed_attn * norm_attn, axis=(0, 1))
             inner_attn = jnp.mean(scaled_attn * norm_attn, axis=-1, keepdims=True)
-            inputs_grad.append(
-                to_features((grad_mid + inv_attn * (scaled_attn - norm_attn * inner_attn))[None])
+            input_features = to_features(
+                (grad_mid + inv_attn * (scaled_attn - norm_attn * inner_attn))[None]
             )
             fresh_attn = jnp.concatenate([fresh_qkv, fresh_out], axis=1)
-            if grad_attn_w is None:
-                grad_attn_w = fresh_attn
-                grad_pair_w, grad_down_w = fresh_pair, fresh_down
-            else:
-                grad_attn_w = grad_attn_w + fresh_attn
-                grad_pair_w = grad_pair_w + fresh_pair
-                grad_down_w = grad_down_w + fresh_down
+            return (
+                block_features,
+                input_features,
+                fresh_attn,
+                fresh_pair,
+                fresh_down,
+                gain_attn_part,
+                gain_ffn_part,
+            )
+
+        results = run_interleaved([micro_batch(b) for b in range(batches)])
+        sums = [sum(parts[1:], parts[0]) for parts in zip(*[r[2:] for r in results])]
+        grad_attn_w, grad_pair_w, grad_down_w, gain_attn_total, gain_ffn_total = sums
+        outs_list = [r[0] for r in results]
+        inputs_grad = [r[1] for r in results]
 
         total_pair = reduce_features(grad_pair_w, 0, "row")
         total_down = reduce_features(grad_down_w, 1, "row")

time: 2470 us -> 2120 us (0.86)
  waiting for transfers between devices: 1440 us -> 1040 us
  starting transfers between devices: 24.5 us -> 71.2 us
    all_gather x8, waiting for transfers between devices: 500 us -> 304 us  [the longest x4 217 us: gather_seqs(): return lax.all_gather(rows, 'col', axis=0, tiled=True)]
    reduce_scatter x8, waiting for transfers between devices: 404 us -> 224 us  [the longest x4 184 us: scatter_seqs(): return lax.psum_scatter(rows, 'col', scatter_dimension=0, tiled=True)]
    all_gather x3, waiting for transfers between devices: 188 us -> 139 us  [gather_half(): gathered = lax.all_gather(mine, axis_name, axis=axis)]
    all_to_all x1, starting transfers between devices: 4.52 us -> 50.9 us  [to_tokens(): rows = lax.all_to_all(rows, 'row', 2, 3)]
  transfers between devices with their start and end apart: 38 -> 38, of which waited for: 28 -> 25; matrix products, arithmetic and copies ran while one was open for 17% -> 40% of each run, Pallas kernels for 0% -> 0%
where the time goes in v6:
time: 2120 us; the launch traced here: 2110 us
  waiting for transfers between devices  1040 us (49%)
  matrix products  469 us (22%)
  local copies, waits for them, and re-layouts  227 us (11%)
  other arithmetic  197 us (9%)
  blocking collectives  89.2 us (4%)
  starting transfers between devices  71.2 us (3%)
    all_gather x4, waiting for transfers between devices, gather_seqs(): return lax.all_gather(rows, 'col', axis=0, tiled=True)  217 us
    unnamed x33, waiting for transfers between devices  191 us
    reduce_scatter x4, waiting for transfers between devices, scatter_seqs(): return lax.psum_scatter(rows, 'col', scatter_dimension=0, tiled=True)  184 us
    all_gather x3, waiting for transfers between devices, gather_half(): gathered = lax.all_gather(mine, axis_name, axis=axis)  139 us
    all_gather x4, waiting for transfers between devices, gather_tokens(): return lax.all_gather(rows, 'row', axis=1, tiled=True)  86.9 us
    reshape x4, local copies, waits for them, and re-layouts, reduce_half(): split = jnp.swapaxes(partial.reshape(shape), axis, axis + 1)  67.6 us
    dot_general x2, matrix products, micro_batch(): jnp.einsum('std,stf->df', spread_ffn, paired_gradient, preferred_element_...  59.3 us
    convert_element_type x2, other arithmetic, attend_backward(): grad_scores = (attn_probs * (grad_probs - jnp.sum(attn_probs * grad_probs...  58.3 us
  transfers between devices with their start and end apart: 38, of which 25 were waited for; matrix products, arithmetic and copies ran while one was open for 40% of the time, Pallas kernels for 0%

profile of v6, /device:TPU:0, one launch (start us, length us, event | category | flops | bytes accessed | tf_op | source)
XLA Modules:
  0.0 2110.8 jit_solution(7588742813771385908)
XLA Ops:
  16.3 50.9 %all-to-all-start = ((bf16[2,1,4,256,1,512]{5,3,0,4,1,2:T(8,128)(2,1)}), bf16[2,1,4,256,1,512]{5,3,0,4,1,2:T(8,128)(2,1)}, u32[]{:S(2)}, u32[]{:S(2)}) async-start(bf16[2,1,4,256,1,512]{5,3,0,4,1,2:T(8,128)(2,1)} %copy.152), calls=%async_computation | async-start | bytes 4194304 | tf_op jit(solution)/shard_map/all_to_all | solution.py:199
  67.2 27.3 %all-gather.8 = f32[4,1,512]{2,1,0:T(1,128)S(1)} all-gather(f32[1,1,512]{2,1,0:T(1,128)S(1)} %bitcast.416), channel_id=1, replica_groups=mesh['dp'=2,'row'=4,'col'=4] {'row'}, dimensions={0}, use_global_device_ids=true | all-gather | bytes 10240 | tf_op jit(solution)/shard_map/all_gather | solution.py:244
  122.6 9.2 all_gather.81
  136.5 35.4 %all-gather.28.cloned.1.call-done = bf16[1,1024,2048]{2,1,0:T(8,128)(2,1)} async-done(((bf16[1,256,2048]{2,1,0:T(8,128)(2,1)}), bf16[1,1024,2048]{2,1,0:T(8,128)(2,1)}) %all-gather.28.cloned.1.call-update) | async-done | bytes 4194320 | tf_op jit(solution)/shard_map/all_gather | solution.py:185
  172.2 17.1 all-gather.48.cloned.1.call-done
  198.1 13.7 fusion.131
  211.9 13.4 exponential_reduce_fusion.1
  225.3 13.4 fusion.78
  253.4 14.2 fusion.132
  267.6 13.5 exponential_reduce_fusion
  281.1 14.1 fusion.81
  318.1 39.3 %reduce-scatter.21.cloned.1.call-done = bf16[1,256,2048]{2,1,0:T(8,128)(2,1)} async-done(((bf16[1,1024,2048]{2,1,0:T(8,128)(2,1)}), bf16[1,256,2048]{2,1,0:T(8,128)(2,1)}) %reduce-scatter.21.cloned.1.call-update) | async-done | bytes 1048592 | tf_op jit(solution)/shard_map/reduce_scatter | solution.py:188
  357.4 54.9 %all-gather.54.cloned.1.call-done = bf16[2048,1024]{0,1:T(8,128)(2,1)} async-done(((bf16[2048,256]{0,1:T(8,128)(2,1)}), bf16[2048,1024]{0,1:T(8,128)(2,1)}) %all-gather.54.cloned.1.call-update) | async-done | bytes 4194320 | tf_op jit(solution)/shard_map/all_gather | solution.py:153
  418.7 83.7 %all-gather.50.cloned.1.call-done = bf16[1024,4096]{1,0:T(8,128)(2,1)} async-done(((bf16[256,4096]{1,0:T(8,128)(2,1)}), bf16[1024,4096]{1,0:T(8,128)(2,1)}) %all-gather.50.cloned.1.call-update) | async-done | bytes 8388624 | tf_op jit(solution)/shard_map/all_gather | solution.py:153
  506.6 78.6 %all-gather.32.cloned.1.call-done = bf16[4,256,2048]{2,1,0:T(8,128)(2,1)} async-done(((bf16[1,256,2048]{2,1,0:T(8,128)(2,1)}), bf16[4,256,2048]{2,1,0:T(8,128)(2,1)}) %all-gather.32.cloned.1.call-update) | async-done | bytes 4194320 | tf_op jit(solution)/shard_map/all_gather | solution.py:191
  585.3 20.3 all-gather.56.cloned.1.call-done
  605.6 16.4 copy.167
  622.0 15.2 reshape.1153
  638.4 15.5 copy.164
  653.9 20.4 fusion.133
  682.1 10.4 convolution_convert_fusion.1
  692.5 29.9 %all-gather.34.cloned.1.call-done = bf16[4,256,2048]{2,1,0:T(8,128)(2,1)} async-done(((bf16[1,256,2048]{2,1,0:T(8,128)(2,1)}), bf16[4,256,2048]{2,1,0:T(8,128)(2,1)}) %all-gather.34.cloned.1.call-update) | async-done | bytes 4194320 | tf_op jit(solution)/shard_map/all_gather | solution.py:191
  722.6 21.5 %fusion.134 = f32[4,256,4096]{2,1,0:T(8,128)S(1)} fusion(bf16[4,256,2048]{2,1,0:T(8,128)(2,1)} %all-gather.34.cloned.1.call-done, bf16[2048,4096,1]{1,0,2:T(8,128)(2,1)} %bitcast.318), kind=kOutput, calls=%fused_computation.248 | convolution fusion | flops 17179869184 | bytes 37748736 | tf_op jit(solution)/shard_map/std,df->stf/dot_general | solution.py:298
  752.0 12.5 convolution_convert_fusion
  764.6 36.0 %reduce-scatter.23.cloned.1.call-done = bf16[1,256,2048]{2,1,0:T(8,128)(2,1)} async-done(((bf16[4,256,2048]{2,1,0:T(8,128)(2,1)}), bf16[1,256,2048]{2,1,0:T(8,128)(2,1)}) %reduce-scatter.23.cloned.1.call-update) | async-done | bytes 1048592 | tf_op jit(solution)/shard_map/reduce_scatter | solution.py:194
  800.8 28.5 %all_to_all.90 = bf16[2,1,4,256,1,512]{5,3,0,4,1,2:T(8,128)(2,1)S(1)} all-to-all(bf16[2,1,4,256,1,512]{5,3,0,4,1,2:T(8,128)(2,1)S(1)} %copy.169), channel_id=1, replica_groups=mesh['dp'=2,'row'=4,'col'=4] {'row'}, dimensions={2} | all-to-all | bytes 4194304 | tf_op jit(solution)/shard_map/all_to_all | solution.py:199
  837.7 42.9 %reduce-scatter.25.cloned.1.call-done = bf16[1,256,2048]{2,1,0:T(8,128)(2,1)} async-done(((bf16[4,256,2048]{2,1,0:T(8,128)(2,1)}), bf16[1,256,2048]{2,1,0:T(8,128)(2,1)}) %reduce-scatter.25.cloned.1.call-update) | async-done | bytes 1048592 | tf_op jit(solution)/shard_map/reduce_scatter | solution.py:194
  892.0 71.9 %all-gather.36.cloned.1.call-done = bf16[4,256,2048]{2,1,0:T(8,128)(2,1)} async-done(((bf16[1,256,2048]{2,1,0:T(8,128)(2,1)}), bf16[4,256,2048]{2,1,0:T(8,128)(2,1)}) %all-gather.36.cloned.1.call-update) | async-done | bytes 4194320 | tf_op jit(solution)/shard_map/all_gather | solution.py:191
  963.9 20.4 multiply_convert_fusion.3
  984.4 24.0 %fusion.37 = bf16[4,256,2048]{2,1,0:T(8,128)(2,1)} fusion(bf16[2048,4096,1]{1,0,2:T(8,128)(2,1)} %bitcast.319, bf16[4,256,2048]{2,1,0:T(8,128)(2,1)} %get-tuple-element.335, bf16[4,256,2048]{2,1,0:T(8,128)(2,1)} %get-tuple-element.334), kind=kOutput, calls=%fused_computation.70 | convolution fusion | flops 17198743552 | bytes 29360128 | tf_op jit(solution)/shard_map/stf,df->std/dot_general | solution.py:332
  1008.3 36.8 %all-gather.38.cloned.1.call-done = bf16[4,256,2048]{2,1,0:T(8,128)(2,1)} async-done(((bf16[1,256,2048]{2,1,0:T(8,128)(2,1)}), bf16[4,256,2048]{2,1,0:T(8,128)(2,1)}) %all-gather.38.cloned.1.call-update) | async-done | bytes 4194320 | tf_op jit(solution)/shard_map/all_gather | solution.py:191
  1045.4 21.0 multiply_convert_fusion.1
  1066.4 23.8 %fusion.38 = bf16[4,256,2048]{2,1,0:T(8,128)(2,1)} fusion(bf16[2048,4096,1]{1,0,2:T(8,128)(2,1)} %bitcast.320, bf16[4,256,2048]{2,1,0:T(8,128)(2,1)} %get-tuple-element.333, bf16[4,256,2048]{2,1,0:T(8,128)(2,1)} %get-tuple-element.332), kind=kOutput, calls=%fused_computation.71 | convolution fusion | flops 17198743552 | bytes 29360128 | tf_op jit(solution)/shard_map/stf,df->std/dot_general | solution.py:332
  1090.2 32.4 %reduce-scatter.27.cloned.1.call-done = bf16[1,256,2048]{2,1,0:T(8,128)(2,1)} async-done(((bf16[4,256,2048]{2,1,0:T(8,128)(2,1)}), bf16[1,256,2048]{2,1,0:T(8,128)(2,1)}) %reduce-scatter.27.cloned.1.call-update) | async-done | bytes 1048592 | tf_op jit(solution)/shard_map/reduce_scatter | solution.py:194
  1129.5 73.1 %reduce-scatter.29.cloned.1.call-done = bf16[1,256,2048]{2,1,0:T(8,128)(2,1)} async-done(((bf16[4,256,2048]{2,1,0:T(8,128)(2,1)}), bf16[1,256,2048]{2,1,0:T(8,128)(2,1)}) %reduce-scatter.29.cloned.1.call-update) | async-done | bytes 1048592 | tf_op jit(solution)/shard_map/reduce_scatter | solution.py:194
  1207.9 50.3 %all-gather.40.cloned.1.call-done = bf16[1,1024,2048]{2,1,0:T(8,128)(2,1)} async-done(((bf16[1,256,2048]{2,1,0:T(8,128)(2,1)}), bf16[1,1024,2048]{2,1,0:T(8,128)(2,1)}) %all-gather.40.cloned.1.call-update) | async-done | bytes 4194320 | tf_op jit(solution)/shard_map/all_gather | solution.py:185
  1263.5 23.0 %fusion.3 = (f32[2,4,1024]{2,1,0:T(4,128)S(1)}, f32[2,1024,1024,4]{2,1,3,0:T(8,128)}) fusion(f32[2,4,1024,1024]{2,3,1,0:T(8,128)} %get-tuple-element.386, f32[2,4,1024]{2,1,0:T(4,128)S(1)} %bitcast.360, bf16[1024,2,64,1]{0,2,3,1:T(8,128)(2,1)S(1)} %bitcast.354, bf16[1024,2,4,64]{0,3,2,1:T(8,128)(2,1)S(1)} %bitcast.344), kind=kOutput, calls=%fused_computation.8 | convolution fusion | flops 1098899456 | bytes 68485120 | tf_op jit(solution)/shard_map/while/body/eval_jaxpr/qkgd,pkd->kgqp/dot_general | solution.py:85
  1286.5 29.0 %fusion.5 = bf16[2,4,1024,1024]{2,3,1,0:T(8,128)(2,1)} fusion(f32[2,1024,1024,4]{2,1,3,0:T(8,128)} %get-tuple-element.390, f32[2,4,1024,1024]{2,3,1,0:T(8,128)} %get-tuple-element.386, f32[2,4,1024]{2,1,0:T(4,128)S(1)} %get-tuple-element.389, f32[2,4,1024]{2,1,0:T(4,128)S(1)} %bitcast.361), kind=kLoop, calls=%fused_computation.10 | loop fusion | flops 33554432 | bytes 83951616 | tf_op jit(solution)/shard_map/while/body/eval_jaxpr/convert_element_type | solution.py:96
  1315.5 8.7 fusion.97
  1324.3 13.3 fusion.98
  1338.5 8.9 convolution_multiply_fusion.1
  1360.6 22.8 %fusion = (f32[2,4,1024]{2,1,0:T(4,128)S(1)}, f32[2,1024,1024,4]{2,1,3,0:T(8,128)}) fusion(f32[2,4,1024,1024]{2,3,1,0:T(8,128)} %get-tuple-element.388, f32[2,4,1024]{2,1,0:T(4,128)S(1)} %bitcast.356, bf16[1024,2,64,1]{0,2,3,1:T(8,128)(2,1)S(1)} %bitcast.352, bf16[1024,2,4,64]{0,3,2,1:T(8,128)(2,1)S(1)} %bitcast.346), kind=kOutput, calls=%fused_computation.3 | convolution fusion | flops 1098899456 | bytes 68485120 | tf_op jit(solution)/shard_map/while/body/eval_jaxpr/qkgd,pkd->kgqp/dot_general | solution.py:85
  1383.4 29.3 %fusion.2 = bf16[2,4,1024,1024]{2,3,1,0:T(8,128)(2,1)} fusion(f32[2,1024,1024,4]{2,1,3,0:T(8,128)} %get-tuple-element.392, f32[2,4,1024,1024]{2,3,1,0:T(8,128)} %get-tuple-element.388, f32[2,4,1024]{2,1,0:T(4,128)S(1)} %get-tuple-element.391, f32[2,4,1024]{2,1,0:T(4,128)S(1)} %bitcast.357), kind=kLoop, calls=%fused_computation.5 | loop fusion | flops 33554432 | bytes 83951616 | tf_op jit(solution)/shard_map/while/body/eval_jaxpr/convert_element_type | solution.py:96
  1412.7 8.7 fusion.96
  1421.5 13.3 fusion.101
  1435.7 8.9 convolution_multiply_fusion
  1452.1 15.7 fusion.135
  1467.7 17.5 bitcast_add_fusion.1
  1485.2 16.7 copy.187
  1534.7 15.7 psum.7
  1550.4 10.0 select_maximum_fusion
  1560.5 15.8 reshape.1126
  1576.2 12.3 copy.217
  1588.6 26.6 %fusion.9 = f32[2048,4096,1]{1,0,2:T(8,128)} fusion(bf16[4,256,2048]{2,1,0:T(8,128)(2,1)} %all-gather.32.cloned.1.call-done, bf16[4,256,2048]{2,1,0:T(8,128)(2,1)} %get-tuple-element.335, bf16[4,256,2048]{2,1,0:T(8,128)(2,1)} %get-tuple-element.334), kind=kOutput, calls=%fused_computation.37 | convolution fusion | flops 17196646400 | bytes 46137344 | tf_op jit(solution)/shard_map/std,stf->df/dot_general | solution.py:329
  1615.2 32.7 %bitcast_add_fusion = f32[2048,4096]{1,0:T(8,128)} fusion(f32[2048,4096,1]{1,0,2:T(8,128)} %fusion.9, bf16[4,256,2048]{2,1,0:T(8,128)(2,1)} %all-gather.34.cloned.1.call-done, bf16[4,256,2048]{2,1,0:T(8,128)(2,1)} %get-tuple-element.333, bf16[4,256,2048]{2,1,0:T(8,128)(2,1)} %get-tuple-element.332), kind=kOutput, calls=%fused_computation | convolution fusion | flops 17205035008 | bytes 79691776 | tf_op jit(solution)/shard_map/std,stf->df/dot_general | solution.py:329
  1647.9 22.9 %copy.216 = f32[4,2,256,4096]{3,2,0,1:T(8,128)} copy(f32[4,2,256,4096]{3,2,1,0:T(8,128)} %bitcast.314) | data formatting | bytes 67108864 | tf_op jit(solution)/shard_map/reshape | solution.py:172
  1681.9 31.5 %reduce-scatter.39.cloned.1.call-done = f32[1,4,256,4096]{3,2,1,0:T(8,128)} async-done(((f32[2,4,256,4096]{3,2,1,0:T(8,128)}), f32[1,4,256,4096]{3,2,1,0:T(8,128)}) %reduce-scatter.39.cloned.1.call-update) | async-done | bytes 16777232 | tf_op jit(solution)/shard_map/reduce_scatter | solution.py:173
  1713.4 9.0 convert_bitcast_fusion
  1722.5 48.2 %reduce-scatter.45.cloned.1.call-done = bf16[2048,1,256]{2,0,1:T(8,128)(2,1)} async-done(((bf16[2048,4,256]{2,0,1:T(8,128)(2,1)}), bf16[2048,1,256]{2,0,1:T(8,128)(2,1)}) %reduce-scatter.45.cloned.1.call-update) | async-done | bytes 1048592
  1773.5 56.3 %reduce-scatter.37.cloned.1.call-done = bf16[1,256,1408]{1,2,0:T(8,128)(2,1)} async-done(((bf16[4,256,1408]{1,2,0:T(8,128)(2,1)}), bf16[1,256,1408]{1,2,0:T(8,128)(2,1)}) %reduce-scatter.37.cloned.1.call-update) | async-done | bytes 720912 | tf_op jit(solution)/shard_map/reduce_scatter | solution.py:174
  1833.3 142.2 %reduce-scatter.43.cloned.1.call-done = bf16[1,256,4096]{2,1,0:T(8,128)(2,1)} async-done(((bf16[4,256,4096]{2,1,0:T(8,128)(2,1)}), bf16[1,256,4096]{2,1,0:T(8,128)(2,1)}) %reduce-scatter.43.cloned.1.call-update) | async-done | bytes 2097168
  1997.0 9.9 all-to-all-done.3
  2034.0 18.4 all-to-all-done.5
  2058.8 21.6 %all-to-all-done.4 = f32[1,1,1,256,4,512]{5,3,2,1,0,4:T(8,128)S(1)} async-done(((f32[1,1,1,256,4,512]{5,3,2,1,0,4:T(8,128)}), f32[1,1,1,256,4,512]{5,3,2,1,0,4:T(8,128)S(1)}, u32[]{:S(2)}, u32[]{:S(2)}) %all-to-all-start.4) | async-done | bytes 2097184 | tf_op jit(solution)/shard_map/all_to_all | solution.py:205
  (431 shorter events, 303.6 us)
Async XLA Ops:
  7.2 295.1 %copy-start = (bf16[2048,512]{1,0:T(8,128)(2,1)S(1)}, bf16[2048,512]{1,0:T(8,128)(2,1)}, u32[]{:S(2)}) copy-start(bf16[2048,512]{1,0:T(8,128)(2,1)} %param.20) | copy-start | bytes 6291460
  7.2 110.9 %all-gather.46.cloned.1.call-start = ((), (), s32[]{:S(2)}) async-start(), calls=%async_computation.41 | async-start | bytes 3276800 | tf_op jit(solution)/shard_map/all_gather | solution.py:153
  11.7 0.7 collective-permute-start
  13.3 53.9 %copy-start.100 = (f32[512]{0:T(512)S(1)}, f32[512]{0:T(512)}, u32[]{:S(2)}) copy-start(f32[512]{0:T(512)} %param.21) | copy-start | bytes 6148
  16.3 78.2 %all-to-all-start = ((bf16[2,1,4,256,1,512]{5,3,0,4,1,2:T(8,128)(2,1)}), bf16[2,1,4,256,1,512]{5,3,0,4,1,2:T(8,128)(2,1)}, u32[]{:S(2)}, u32[]{:S(2)}) async-start(bf16[2,1,4,256,1,512]{5,3,0,4,1,2:T(8,128)(2,1)} %copy.152), calls=%async_computation | async-start | bytes 4194304 | tf_op jit(solution)/shard_map/all_to_all | solution.py:199
  67.2 104.7 %all-gather.28.cloned.1.call-start = ((), (), s32[]{:S(2)}) async-start(), calls=%async_computation.20 | async-start | bytes 5242880 | tf_op jit(solution)/shard_map/all_gather | solution.py:185
  118.0 71.2 %all-gather.48.cloned.1.call-start = ((), (), s32[]{:S(2)}) async-start(), calls=%async_computation.42 | async-start | bytes 7864320 | tf_op jit(solution)/shard_map/all_gather | solution.py:154
  122.5 122.8 %all-gather.30.cloned.1.call-start = ((), (), s32[]{:S(2)}) async-start(), calls=%async_computation.21 | async-start | bytes 5242880 | tf_op jit(solution)/shard_map/all_gather | solution.py:185
  134.9 62.1 %copy-start.32 = (f32[1024,32]{0,1:T(8,128)}, f32[1024,32]{0,1:T(8,128)S(1)}, u32[]{:S(2)}) copy-start(f32[1024,32]{0,1:T(8,128)S(1)} %get-tuple-element.382) | copy-start | bytes 393220
  134.9 118.1 %copy-start.30 = (f32[1024,32]{0,1:T(8,128)}, f32[1024,32]{0,1:T(8,128)S(1)}, u32[]{:S(2)}) copy-start(f32[1024,32]{0,1:T(8,128)S(1)} %get-tuple-element.377) | copy-start | bytes 393220
  172.0 130.3 %reduce-scatter.19.cloned.1.call-start = ((), (), s32[]{:S(2)}) async-start(), calls=%async_computation.22 | async-start | bytes 5242880 | tf_op jit(solution)/shard_map/reduce_scatter | solution.py:188
  192.3 46.5 %copy-start.23 = (bf16[4,2,256,1280]{3,2,1,0:T(8,128)(2,1)}, bf16[4,2,256,1280]{3,2,1,0:T(8,128)(2,1)S(1)}, u32[]{:S(2)}) copy-start(bf16[4,2,256,1280]{3,2,1,0:T(8,128)(2,1)S(1)} %copy.160) | copy-start | bytes 15728644
  245.4 112.0 %reduce-scatter.21.cloned.1.call-start = ((), (), s32[]{:S(2)}) async-start(), calls=%async_computation.23 | async-start | bytes 5242880 | tf_op jit(solution)/shard_map/reduce_scatter | solution.py:188
  302.2 110.2 %all-gather.54.cloned.1.call-start = ((), (), s32[]{:S(2)}) async-start(), calls=%async_computation.45 | async-start | bytes 5242880 | tf_op jit(solution)/shard_map/all_gather | solution.py:153
  303.9 198.5 %all-gather.50.cloned.1.call-start = ((), (), s32[]{:S(2)}) async-start(), calls=%async_computation.43 | async-start | bytes 10485760 | tf_op jit(solution)/shard_map/all_gather | solution.py:153
  307.2 278.1 %all-gather.32.cloned.1.call-start = ((), (), s32[]{:S(2)}) async-start(), calls=%async_computation.24 | async-start | bytes 5242880 | tf_op jit(solution)/shard_map/all_gather | solution.py:191
  315.7 189.0 %copy-start.61 = (f32[4,1,512]{2,1,0:T(1,128)}, f32[4,1,512]{2,1,0:T(1,128)S(1)}, u32[]{:S(2)}) copy-start(f32[4,1,512]{2,1,0:T(1,128)S(1)} %all-gather.9) | copy-start | bytes 24580
  357.4 248.2 %all-gather.56.cloned.1.call-start = ((), (), s32[]{:S(2)}) async-start(), calls=%async_computation.46 | async-start | bytes 12582912 | tf_op jit(solution)/shard_map/all_gather | solution.py:154
  418.6 219.8 %all-gather.52.cloned.1.call-start = ((), (), s32[]{:S(2)}) async-start(), calls=%async_computation.44 | async-start | bytes 25165824 | tf_op jit(solution)/shard_map/all_gather | solution.py:154
  502.4 220.0 %all-gather.34.cloned.1.call-start = ((), (), s32[]{:S(2)}) async-start(), calls=%async_computation.25 | async-start | bytes 5242880 | tf_op jit(solution)/shard_map/all_gather | solution.py:191
  585.3 215.3 %reduce-scatter.23.cloned.1.call-start = ((), (), s32[]{:S(2)}) async-start(), calls=%async_computation.26 | async-start | bytes 5242880 | tf_op jit(solution)/shard_map/reduce_scatter | solution.py:194
  638.4 43.7 %slice-start = ((s8[8388608]{0:T(1024)(128)(4,1)}), s8[4194304]{0:T(1024)(128)(4,1)S(1)}, s32[]{:S(2)}) async-start(s8[8388608]{0:T(1024)(128)(4,1)} %bitcast.328), calls=%async_computation.51 | async-start | bytes 8388608
  722.4 158.2 %reduce-scatter.25.cloned.1.call-start = ((), (), s32[]{:S(2)}) async-start(), calls=%async_computation.27 | async-start | bytes 5242880 | tf_op jit(solution)/shard_map/reduce_scatter | solution.py:194
  764.5 36.1 %copy-start.50 = (bf16[2,1,1024,512]{3,2,1,0:T(8,128)(2,1)S(1)}, bf16[2,1,1024,512]{3,2,1,0:T(8,128)(2,1)}, u32[]{:S(2)}) copy-start(bf16[2,1,1024,512]{3,2,1,0:T(8,128)(2,1)} %param.23) | copy-start | bytes 6291460
  800.6 163.3 %all-gather.36.cloned.1.call-start = ((), (), s32[]{:S(2)}) async-start(), calls=%async_computation.28 | async-start | bytes 5242880 | tf_op jit(solution)/shard_map/all_gather | solution.py:191
  836.4 49.0 %copy-start.9 = (f32[1,256,2048]{2,1,0:T(8,128)}, f32[1,256,2048]{2,1,0:T(8,128)S(1)}, u32[]{:S(2)}) copy-start(f32[1,256,2048]{2,1,0:T(8,128)S(1)} %reshape.1131) | copy-start | bytes 6291460
  880.6 164.5 %all-gather.38.cloned.1.call-start = ((), (), s32[]{:S(2)}) async-start(), calls=%async_computation.29 | async-start | bytes 5242880 | tf_op jit(solution)/shard_map/all_gather | solution.py:191
  963.9 158.7 %reduce-scatter.27.cloned.1.call-start = ((), (), s32[]{:S(2)}) async-start(), calls=%async_computation.30 | async-start | bytes 5242880 | tf_op jit(solution)/shard_map/reduce_scatter | solution.py:194
  1045.1 157.5 %reduce-scatter.29.cloned.1.call-start = ((), (), s32[]{:S(2)}) async-start(), calls=%async_computation.31 | async-start | bytes 5242880 | tf_op jit(solution)/shard_map/reduce_scatter | solution.py:194
  1090.2 32.5 %copy-start.6 = (f32[1,256,2048]{2,1,0:T(8,128)S(1)}, f32[1,256,2048]{2,1,0:T(8,128)}, u32[]{:S(2)}) copy-start(f32[1,256,2048]{2,1,0:T(8,128)} %reshape.1129) | copy-start | bytes 6291460
  1090.2 32.5 %copy-start.13 = (bf16[1,256,2048]{2,1,0:T(8,128)(2,1)S(1)}, bf16[1,256,2048]{2,1,0:T(8,128)(2,1)}, u32[]{:S(2)}) copy-start(bf16[1,256,2048]{2,1,0:T(8,128)(2,1)} %reduce-scatter.19.cloned.1.call-done) | copy-start | bytes 3145732
  1090.2 32.5 %copy-start.62 = (f32[4,1,512]{2,1,0:T(1,128)S(1)}, f32[4,1,512]{2,1,0:T(1,128)}, u32[]{:S(2)}) copy-start(f32[4,1,512]{2,1,0:T(1,128)} %copy-done.61) | copy-start | bytes 24580
  1090.2 32.5 %copy-start.84 = (f32[256]{0:T(256)S(1)}, f32[256]{0:T(256)}, u32[]{:S(2)}) copy-start(f32[256]{0:T(256)} %copy-done.83) | copy-start | bytes 3076
  1122.6 135.6 %all-gather.40.cloned.1.call-start = ((), (), s32[]{:S(2)}) async-start(), calls=%async_computation.32 | async-start | bytes 5242880 | tf_op jit(solution)/shard_map/all_gather | solution.py:185
  1126.2 76.5 %copy-start.3 = (f32[1,256,2048]{2,1,0:T(8,128)S(1)}, f32[1,256,2048]{2,1,0:T(8,128)}, u32[]{:S(2)}) copy-start(f32[1,256,2048]{2,1,0:T(8,128)} %reshape.1130) | copy-start | bytes 6291460
  1126.2 76.5 %copy-start.87 = (f32[256]{0:T(256)S(1)}, f32[256]{0:T(256)}, u32[]{:S(2)}) copy-start(f32[256]{0:T(256)} %copy-done.86) | copy-start | bytes 3076
  1129.5 76.5 %copy-start.16 = (bf16[1,256,2048]{2,1,0:T(8,128)(2,1)S(1)}, bf16[1,256,2048]{2,1,0:T(8,128)(2,1)}, u32[]{:S(2)}) copy-start(bf16[1,256,2048]{2,1,0:T(8,128)(2,1)} %reduce-scatter.21.cloned.1.call-done) | copy-start | bytes 3145732
  1202.7 152.5 %all-gather.42.cloned.1.call-start = ((), (), s32[]{:S(2)}) async-start(), calls=%async_computation.33 | async-start | bytes 5242880 | tf_op jit(solution)/shard_map/all_gather | solution.py:185
  1206.0 52.2 %copy-start.96 = (f32[256]{0:T(256)}, f32[256]{0:T(256)S(1)}, u32[]{:S(2)}) copy-start(f32[256]{0:T(256)S(1)} %broadcast_multiply_fusion.2) | copy-start | bytes 3076
  1258.2 193.8 %reduce-scatter.31.cloned.1.call-start = ((), (), s32[]{:S(2)}) async-start(), calls=%async_computation.34 | async-start | bytes 5242880 | tf_op jit(solution)/shard_map/reduce_scatter | solution.py:188
  1286.5 29.0 %copy-start.47 = (bf16[1,1024,8,32]{1,3,2,0:T(8,128)(2,1)S(1)}, bf16[1,1024,8,32]{1,3,2,0:T(8,128)(2,1)}, u32[]{:S(2)}) copy-start(bf16[1,1024,8,32]{1,3,2,0:T(8,128)(2,1)} %copy-done.46) | copy-start | bytes 1572868
  1286.5 29.0 %copy-start.49 = (bf16[1,1024,8,32]{1,3,2,0:T(8,128)(2,1)S(1)}, bf16[1,1024,8,32]{1,3,2,0:T(8,128)(2,1)}, u32[]{:S(2)}) copy-start(bf16[1,1024,8,32]{1,3,2,0:T(8,128)(2,1)} %copy-done.48) | copy-start | bytes 1572868
  1355.3 170.3 %reduce-scatter.33.cloned.1.call-start = ((), (), s32[]{:S(2)}) async-start(), calls=%async_computation.35 | async-start | bytes 5242880 | tf_op jit(solution)/shard_map/reduce_scatter | solution.py:188
  1383.4 29.3 %copy-start.43 = (bf16[1,1024,8,32]{1,3,2,0:T(8,128)(2,1)S(1)}, bf16[1,1024,8,32]{1,3,2,0:T(8,128)(2,1)}, u32[]{:S(2)}) copy-start(bf16[1,1024,8,32]{1,3,2,0:T(8,128)(2,1)} %copy-done.42) | copy-start | bytes 1572868
  1383.4 29.3 %copy-start.45 = (bf16[1,1024,8,32]{1,3,2,0:T(8,128)(2,1)S(1)}, bf16[1,1024,8,32]{1,3,2,0:T(8,128)(2,1)}, u32[]{:S(2)}) copy-start(bf16[1,1024,8,32]{1,3,2,0:T(8,128)(2,1)} %copy-done.44) | copy-start | bytes 1572868
  1452.0 218.9 %reduce-scatter.41.cloned.1.call-start = ((), (), s32[]{:S(2)}) async-start(), calls=%async_computation.40 | async-start | bytes 25165824 | tf_op jit(solution)/shard_map/reduce_scatter | solution.py:173
  1501.9 174.9 %reduce-scatter.35.cloned.1.call-start = ((), (), s32[]{:S(2)}) async-start(), calls=%async_computation.36 | async-start | bytes 17301504 | tf_op jit(solution)/shard_map/reduce_scatter | solution.py:173
  1588.6 124.8 %reduce-scatter.39.cloned.1.call-start = ((), (), s32[]{:S(2)}) async-start(), calls=%async_computation.39 | async-start | bytes 50331648 | tf_op jit(solution)/shard_map/reduce_scatter | solution.py:173
  1670.8 99.9 %reduce-scatter.45.cloned.1.call-start = ((), (), s32[]{:S(2)}) async-start(), calls=%async_computation.50 | async-start | bytes 5242880
  1676.7 153.1 %reduce-scatter.37.cloned.1.call-start = ((), (), s32[]{:S(2)}) async-start(), calls=%async_computation.37 | async-start | bytes 3604480 | tf_op jit(solution)/shard_map/reduce_scatter | solution.py:174
  1681.8 293.7 %reduce-scatter.43.cloned.1.call-start = ((), (), s32[]{:S(2)}) async-start(), calls=%async_computation.49 | async-start | bytes 10485760
  1722.5 333.6 %all-gather.60.cloned.1.call-start = ((), (), s32[]{:S(2)}) async-start(), calls=%async_computation.48 | async-start | bytes 6291456 | tf_op jit(solution)/shard_map/all_gather | solution.py:179
  1773.5 311.0 %all-gather.44.cloned.1.call-start = ((), (), s32[]{:S(2)}) async-start(), calls=%async_computation.38 | async-start | bytes 4325376 | tf_op jit(solution)/shard_map/all_gather | solution.py:411
  1831.0 0.8 collective-permute-start.1
  1833.0 146.7 %copy-start.99 = (f32[256]{0:T(256)S(1)}, f32[256]{0:T(256)}, u32[]{:S(2)}) copy-start(f32[256]{0:T(256)} %get-tuple-element.370) | copy-start | bytes 3076
  1833.0 146.7 %copy-start.17 = (bf16[1,256,2048]{2,1,0:T(8,128)(2,1)S(1)}, bf16[1,256,2048]{2,1,0:T(8,128)(2,1)}, u32[]{:S(2)}) copy-start(bf16[1,256,2048]{2,1,0:T(8,128)(2,1)} %reduce-scatter.21.cloned.1.call-done) | copy-start | bytes 3145732
  1833.0 146.7 %copy-start.88 = (f32[256]{0:T(256)S(1)}, f32[256]{0:T(256)}, u32[]{:S(2)}) copy-start(f32[256]{0:T(256)} %copy-done.86) | copy-start | bytes 3076
  1833.0 146.7 %copy-start.93 = (f32[256]{0:T(256)S(1)}, f32[256]{0:T(256)}, u32[]{:S(2)}) copy-start(f32[256]{0:T(256)} %copy-done.91) | copy-start | bytes 3076
  1833.0 146.7 %copy-start.97 = (f32[256]{0:T(256)S(1)}, f32[256]{0:T(256)}, u32[]{:S(2)}) copy-start(f32[256]{0:T(256)} %copy-done.96) | copy-start | bytes 3076
  1833.0 259.5 %all-gather.58.cloned.1.call-start = ((), (), s32[]{:S(2)}) async-start(), calls=%async_computation.47 | async-start | bytes 12582912 | tf_op jit(solution)/shard_map/all_gather | solution.py:179
  1988.5 18.3 all-to-all-start.3
  2006.9 16.6 all-to-all-start.1
  2023.5 28.9 %all-to-all-start.5 = ((f32[1,1,1,256,4,512]{5,3,2,1,0,4:T(8,128)}), f32[1,1,1,256,4,512]{5,3,2,1,0,4:T(8,128)}, u32[]{:S(2)}, u32[]{:S(2)}) async-start(f32[1,1,1,256,4,512]{5,3,2,1,0,4:T(8,128)} %copy.180), calls=%async_computation.13 | async-start | bytes 4194304 | tf_op jit(solution)/shard_map/all_to_all | solution.py:205
  2052.4 28.0 %all-to-all-start.4 = ((f32[1,1,1,256,4,512]{5,3,2,1,0,4:T(8,128)}), f32[1,1,1,256,4,512]{5,3,2,1,0,4:T(8,128)S(1)}, u32[]{:S(2)}, u32[]{:S(2)}) async-start(f32[1,1,1,256,4,512]{5,3,2,1,0,4:T(8,128)} %copy.179), calls=%async_computation.11 | async-start | bytes 4194304 | tf_op jit(solution)/shard_map/all_to_all | solution.py:205
  (83 other events, 632.9 us)
Sparse Core Ops, SparseCore 0:
  13.4 103.2 all-gather.45
  119.1 52.7 all-gather.27
  174.0 15.1 all-gather.47
  191.6 53.7 all-gather.29
  248.7 52.5 reduce-scatter.18
  304.7 52.5 reduce-scatter.20
  359.8 52.5 all-gather.53
  414.8 87.4 all-gather.49
  504.5 80.7 all-gather.31
  587.2 18.3 all-gather.55
  607.1 31.2 all-gather.51
  640.4 81.9 all-gather.33
  725.2 75.2 reduce-scatter.22
  803.3 77.2 reduce-scatter.24
  882.6 81.2 all-gather.35
  965.9 79.2 all-gather.37
  1047.3 75.2 reduce-scatter.26
  1125.3 77.2 reduce-scatter.28
  1205.0 53.0 all-gather.39
  1260.4 52.5 all-gather.41
  1355.3 52.4 reduce-scatter.30
  1452.1 52.5 reduce-scatter.32
  1507.0 25.0 reduce-scatter.40
  1588.7 18.7 reduce-scatter.34
  1671.0 42.4 reduce-scatter.38
  1716.8 53.8 reduce-scatter.44
  1773.5 56.3 reduce-scatter.36
  1832.9 142.5 reduce-scatter.42
  1977.6 13.6 all-gather.59
  1992.7 12.8 all-gather.43
  2007.8 21.0 all-gather.57

commit v7 on v6

--- a/solution.py
+++ b/solution.py
@@ -111,7 +111,7 @@
     ).astype(jnp.float32)
 
 
-def run_interleaved(streams):
+def run_interleaved(streams, first, keep_first):
     pending = {}
     finished = {}
 
@@ -123,7 +123,7 @@
 
     for index in range(len(streams)):
         feed(index, None)
-    previous = None
+    previous = (-1, first)
     while len(finished) < len(streams):
         for index in range(len(streams)):
             if index in finished:
@@ -137,7 +137,10 @@
             if previous is not None:
                 owner, result = previous
                 result, operand = lax.optimization_barrier((result, operand))
-                feed(owner, result)
+                if owner >= 0:
+                    feed(owner, result)
+                else:
+                    keep_first(result)
             previous = (index, collective(operand))
     return [finished[index] for index in range(len(streams))]
 
@@ -237,12 +240,10 @@
             0,
             "col",
         )
-        w_qkv = w_attn[:, :qkv_cols]
-        w_out_heads = w_attn[:, qkv_cols:].T
-        w_pair = gather_features(jnp.concatenate([w_gate, w_up], axis=1), 0, "row")
-        w_down_all = gather_features(w_down, 1, "row")
-        gain_attn_all = lax.all_gather(gain_attn, "row", tiled=True)
-        gain_ffn_all = lax.all_gather(gain_ffn, "row", tiled=True)
+        shared = {}
+        gain_attn_all, gain_ffn_all = lax.all_gather(
+            jnp.stack([gain_attn, gain_ffn]), "row", axis=1, tiled=True
+        )
 
         segments = lax.all_gather(segment_ids, "row", axis=1, tiled=True)
         segments = lax.dynamic_slice_in_dim(segments, col_index * local, local, axis=1)
@@ -258,6 +259,8 @@
             norm_attn = rows_f * inv_attn
             normed_attn = (norm_attn * gain_attn_all).astype(jnp.bfloat16)
             spread_attn = yield (gather_tokens, normed_attn)
+            w_qkv = shared["attn"][:, :qkv_cols]
+            w_out_heads = shared["attn"][:, qkv_cols:].T
             qkv = jnp.einsum(
                 "std,dm->stm", spread_attn, w_qkv, preferred_element_type=jnp.float32
             )
@@ -295,20 +298,22 @@
             norm_ffn = resid_mid * inv_ffn
             normed_ffn = (norm_ffn * gain_ffn_all).astype(jnp.bfloat16)
             spread_ffn = yield (gather_seqs, normed_ffn)
+            w_pair_all = shared["pair"]
             pair = jnp.einsum(
-                "std,df->stf", spread_ffn, w_pair, preferred_element_type=jnp.float32
+                "std,df->stf", spread_ffn, w_pair_all, preferred_element_type=jnp.float32
             )
             gate_rows = pair[..., :ffn_cols]
             up_rows = pair[..., ffn_cols:]
             sigmoid_gate = jax.nn.sigmoid(gate_rows)
             act_low = (gate_rows * sigmoid_gate * up_rows).astype(jnp.bfloat16)
+            w_down_all = shared["down"]
             ffn_part = jnp.einsum(
                 "stf,fd->std", act_low, w_down_all, preferred_element_type=jnp.float32
             )
             ffn_branch = yield (scatter_seqs, ffn_part.astype(jnp.bfloat16))
             ffn_branch = ffn_branch.astype(jnp.float32)
             block_out = (resid_mid + RESIDUAL_SCALE * ffn_branch).astype(jnp.bfloat16)
-            block_features = to_features(block_out[None])
+            block_features = yield (to_features, block_out[None])
 
             grad_rows = cotangent_t[batch_index].astype(jnp.float32)
             grad_ffn = (RESIDUAL_SCALE * grad_rows).astype(jnp.bfloat16)
@@ -330,7 +335,7 @@
                 "std,stf->df", spread_ffn, paired_gradient, preferred_element_type=jnp.float32
             )
             grad_normed_part = jnp.einsum(
-                "stf,df->std", paired_gradient, w_pair, preferred_element_type=jnp.float32
+                "stf,df->std", paired_gradient, w_pair_all, preferred_element_type=jnp.float32
             )
             grad_normed_ffn = yield (scatter_seqs, grad_normed_part.astype(jnp.bfloat16))
             grad_normed_ffn = grad_normed_ffn.astype(jnp.float32)
@@ -384,8 +389,8 @@
             scaled_attn = grad_normed_attn * gain_attn_all
             gain_attn_part = jnp.sum(grad_normed_attn * norm_attn, axis=(0, 1))
             inner_attn = jnp.mean(scaled_attn * norm_attn, axis=-1, keepdims=True)
-            input_features = to_features(
-                (grad_mid + inv_attn * (scaled_attn - norm_attn * inner_attn))[None]
+            input_features = yield (
+                to_features, (grad_mid + inv_attn * (scaled_attn - norm_attn * inner_attn))[None]
             )
             fresh_attn = jnp.concatenate([fresh_qkv, fresh_out], axis=1)
             return (
@@ -398,7 +403,18 @@
                 gain_ffn_part,
             )
 
-        results = run_interleaved([micro_batch(b) for b in range(batches)])
+        def weight_stream():
+            shared["pair"] = yield (
+                lambda rows: gather_features(rows, 0, "row"),
+                jnp.concatenate([w_gate, w_up], axis=1),
+            )
+            shared["down"] = yield (lambda rows: gather_features(rows, 1, "row"), w_down)
+            return None
+
+        streams = [micro_batch(b) for b in range(batches)]
+        streams.insert(1, weight_stream())
+        results = run_interleaved(streams, w_attn, lambda kept: shared.update(attn=kept))
+        results = [r for r in results if r is not None]
         sums = [sum(parts[1:], parts[0]) for parts in zip(*[r[2:] for r in results])]
         grad_attn_w, grad_pair_w, grad_down_w, gain_attn_total, gain_ffn_total = sums
         outs_list = [r[0] for r in results]

time: 2120 us -> 2280 us (1.075)
  waiting for transfers between devices: 1040 us -> 1250 us
  starting transfers between devices: 71.2 us -> 28.6 us
  blocking collectives: 89.2 us -> 50.2 us
    all_gather x3, waiting for transfers between devices: 139 us -> 244 us  [gather_half(): gathered = lax.all_gather(mine, axis_name, axis=axis)]
    reduce_scatter x4, waiting for transfers between devices: 39.3 us -> 102 us  [scatter_tokens(): return lax.psum_scatter(rows, 'row', scatter_dimension=1, tiled=True)]
    all_to_all x1 -> x2, starting transfers between devices: 50.9 us -> 8.14 us  [to_tokens(): rows = lax.all_to_all(rows, 'row', 2, 3)]
    reduce_scatter x4, waiting for transfers between devices: 184 us -> 217 us  [scatter_seqs(): return lax.psum_scatter(rows, 'col', scatter_dimension=0, tiled=True)]
    all_to_all x1 -> x0, blocking collectives: 28.5 us -> none  [to_tokens(): rows = lax.all_to_all(rows, 'row', 2, 3)]
  transfers between devices with their start and end apart: 38 -> 39, of which waited for: 25 -> 25; matrix products, arithmetic and copies ran while one was open for 40% -> 36% of each run, Pallas kernels for 0% -> 0%
where the time goes in v7:
time: 2280 us; the launch traced here: 2270 us
  waiting for transfers between devices  1250 us (55%)
  matrix products  477 us (21%)
  local copies, waits for them, and re-layouts  240 us (11%)
  other arithmetic  207 us (9%)
  blocking collectives  50.2 us (2%)
  starting transfers between devices  28.6 us (1%)
    all_gather x3, waiting for transfers between devices, gather_half(): gathered = lax.all_gather(mine, axis_name, axis=axis)  244 us
    all_gather x4, waiting for transfers between devices, gather_seqs(): return lax.all_gather(rows, 'col', axis=0, tiled=True)  226 us
    reduce_scatter x4, waiting for transfers between devices, scatter_seqs(): return lax.psum_scatter(rows, 'col', scatter_dimension=0, tiled=True)  217 us
    unnamed x33, waiting for transfers between devices  191 us
    reduce_scatter x4, waiting for transfers between devices, scatter_tokens(): return lax.psum_scatter(rows, 'row', scatter_dimension=1, tiled=True)  102 us
    all_gather x4, waiting for transfers between devices, gather_tokens(): return lax.all_gather(rows, 'row', axis=1, tiled=True)  97.9 us
    reshape x4, local copies, waits for them, and re-layouts, reduce_half(): split = jnp.swapaxes(partial.reshape(shape), axis, axis + 1)  67.3 us
    dot_general x2, matrix products, micro_batch(): jnp.einsum('std,stf->df', spread_ffn, paired_gradient, preferred_element_...  59.6 us
  transfers between devices with their start and end apart: 39, of which 25 were waited for; matrix products, arithmetic and copies ran while one was open for 36% of the time, Pallas kernels for 0%

profile of v7, /device:TPU:0, one launch (start us, length us, event | category | flops | bytes accessed | tf_op | source)
XLA Modules:
  0.0 2272.2 jit_solution(6215392003529230530)
XLA Ops:
  13.2 103.4 %all-gather.44.cloned.1.call-done = bf16[1024,1280]{0,1:T(8,128)(2,1)} async-done(((bf16[256,1280]{0,1:T(8,128)(2,1)}), bf16[1024,1280]{0,1:T(8,128)(2,1)}) %all-gather.44.cloned.1.call-update) | async-done | bytes 2621456 | tf_op jit(solution)/shard_map/all_gather | solution.py:156
  126.3 26.5 %all_gather.79 = f32[2,2048]{1,0:T(2,128)S(1)} all-gather(f32[2,512]{1,0:T(2,128)S(1)} %pad_maximum_fusion.30), channel_id=1, replica_groups=mesh['dp'=2,'row'=4,'col'=4] {'row'}, dimensions={1}, use_global_device_ids=true | all-gather | bytes 20480 | tf_op jit(solution)/shard_map/all_gather | solution.py:244
  184.3 47.8 %all-gather.26.cloned.1.call-done = bf16[1,1024,2048]{2,1,0:T(8,128)(2,1)} async-done(((bf16[1,256,2048]{2,1,0:T(8,128)(2,1)}), bf16[1,1024,2048]{2,1,0:T(8,128)(2,1)}) %all-gather.26.cloned.1.call-update) | async-done | bytes 4194320 | tf_op jit(solution)/shard_map/all_gather | solution.py:188
  235.3 87.6 %all-gather.48.cloned.1.call-done = bf16[1024,4096]{1,0:T(8,128)(2,1)} async-done(((bf16[256,4096]{1,0:T(8,128)(2,1)}), bf16[1024,4096]{1,0:T(8,128)(2,1)}) %all-gather.48.cloned.1.call-update) | async-done | bytes 8388624 | tf_op jit(solution)/shard_map/all_gather | solution.py:156
  323.6 8.1 all_gather.86
  336.4 18.0 all-gather.50.cloned.1.call-done
  354.4 14.0 copy.157
  376.5 13.6 fusion.159
  390.2 13.5 exponential_reduce_fusion.1
  403.8 13.4 fusion.103
  424.3 54.2 %reduce-scatter.19.cloned.1.call-done = bf16[1,256,2048]{2,1,0:T(8,128)(2,1)} async-done(((bf16[1,1024,2048]{2,1,0:T(8,128)(2,1)}), bf16[1,256,2048]{2,1,0:T(8,128)(2,1)}) %reduce-scatter.19.cloned.1.call-update) | async-done | bytes 1048592 | tf_op jit(solution)/shard_map/reduce_scatter | solution.py:191
  484.8 52.7 %all-gather.52.cloned.1.call-done = bf16[2048,1024]{0,1:T(8,128)(2,1)} async-done(((bf16[2048,256]{0,1:T(8,128)(2,1)}), bf16[2048,1024]{0,1:T(8,128)(2,1)}) %all-gather.52.cloned.1.call-update) | async-done | bytes 4194320 | tf_op jit(solution)/shard_map/all_gather | solution.py:156
  551.7 15.5 fusion.160
  567.2 13.1 exponential_reduce_fusion
  580.3 13.4 fusion.106
  600.7 16.4 copy.164
  617.1 14.6 reshape.1123
  637.2 47.8 %reduce-scatter.21.cloned.1.call-done = bf16[1,256,2048]{2,1,0:T(8,128)(2,1)} async-done(((bf16[1,1024,2048]{2,1,0:T(8,128)(2,1)}), bf16[1,256,2048]{2,1,0:T(8,128)(2,1)}) %reduce-scatter.21.cloned.1.call-update) | async-done | bytes 1048592 | tf_op jit(solution)/shard_map/reduce_scatter | solution.py:191
  688.8 79.1 %all-gather.30.cloned.1.call-done = bf16[4,256,2048]{2,1,0:T(8,128)(2,1)} async-done(((bf16[1,256,2048]{2,1,0:T(8,128)(2,1)}), bf16[4,256,2048]{2,1,0:T(8,128)(2,1)}) %all-gather.30.cloned.1.call-update) | async-done | bytes 4194320 | tf_op jit(solution)/shard_map/all_gather | solution.py:194
  768.0 21.5 fusion.14
  797.3 12.5 fusion.51
  809.9 39.3 %all-gather.32.cloned.1.call-done = bf16[4,256,2048]{2,1,0:T(8,128)(2,1)} async-done(((bf16[1,256,2048]{2,1,0:T(8,128)(2,1)}), bf16[4,256,2048]{2,1,0:T(8,128)(2,1)}) %all-gather.32.cloned.1.call-update) | async-done | bytes 4194320 | tf_op jit(solution)/shard_map/all_gather | solution.py:194
  849.3 21.7 fusion.12
  878.9 12.5 fusion.54
  891.4 35.9 %reduce-scatter.23.cloned.1.call-done = bf16[1,256,2048]{2,1,0:T(8,128)(2,1)} async-done(((bf16[4,256,2048]{2,1,0:T(8,128)(2,1)}), bf16[1,256,2048]{2,1,0:T(8,128)(2,1)}) %reduce-scatter.23.cloned.1.call-update) | async-done | bytes 1048592 | tf_op jit(solution)/shard_map/reduce_scatter | solution.py:197
  931.0 76.4 %reduce-scatter.25.cloned.1.call-done = bf16[1,256,2048]{2,1,0:T(8,128)(2,1)} async-done(((bf16[4,256,2048]{2,1,0:T(8,128)(2,1)}), bf16[1,256,2048]{2,1,0:T(8,128)(2,1)}) %reduce-scatter.25.cloned.1.call-update) | async-done | bytes 1048592 | tf_op jit(solution)/shard_map/reduce_scatter | solution.py:197
  1019.7 10.6 all-to-all-done.1
  1042.5 16.7 all-to-all-done.3
  1087.7 70.7 %all-gather.34.cloned.1.call-done = bf16[4,256,2048]{2,1,0:T(8,128)(2,1)} async-done(((bf16[1,256,2048]{2,1,0:T(8,128)(2,1)}), bf16[4,256,2048]{2,1,0:T(8,128)(2,1)}) %all-gather.34.cloned.1.call-update) | async-done | bytes 4194320 | tf_op jit(solution)/shard_map/all_gather | solution.py:194
  1158.5 20.4 multiply_convert_fusion.3
  1178.9 23.9 %fusion.57 = bf16[4,256,2048]{2,1,0:T(8,128)(2,1)} fusion(bf16[2048,4096]{1,0:T(8,128)(2,1)} %bitcast.357, bf16[4,256,2048]{2,1,0:T(8,128)(2,1)} %get-tuple-element.363, bf16[4,256,2048]{2,1,0:T(8,128)(2,1)} %get-tuple-element.362), kind=kOutput, calls=%fused_computation.85 | convolution fusion | flops 17198743552 | bytes 29360128 | tf_op jit(solution)/shard_map/stf,df->std/dot_general | solution.py:337
  1202.8 36.9 %all-gather.36.cloned.1.call-done = bf16[4,256,2048]{2,1,0:T(8,128)(2,1)} async-done(((bf16[1,256,2048]{2,1,0:T(8,128)(2,1)}), bf16[4,256,2048]{2,1,0:T(8,128)(2,1)}) %all-gather.36.cloned.1.call-update) | async-done | bytes 4194320 | tf_op jit(solution)/shard_map/all_gather | solution.py:194
  1239.9 21.0 multiply_convert_fusion.1
  1260.9 23.8 %fusion.60 = bf16[4,256,2048]{2,1,0:T(8,128)(2,1)} fusion(bf16[2048,4096]{1,0:T(8,128)(2,1)} %bitcast.358, bf16[4,256,2048]{2,1,0:T(8,128)(2,1)} %get-tuple-element.361, bf16[4,256,2048]{2,1,0:T(8,128)(2,1)} %get-tuple-element.360), kind=kOutput, calls=%fused_computation.86 | convolution fusion | flops 17198743552 | bytes 29360128 | tf_op jit(solution)/shard_map/stf,df->std/dot_general | solution.py:337
  1284.8 32.4 %reduce-scatter.27.cloned.1.call-done = bf16[1,256,2048]{2,1,0:T(8,128)(2,1)} async-done(((bf16[4,256,2048]{2,1,0:T(8,128)(2,1)}), bf16[1,256,2048]{2,1,0:T(8,128)(2,1)}) %reduce-scatter.27.cloned.1.call-update) | async-done | bytes 1048592 | tf_op jit(solution)/shard_map/reduce_scatter | solution.py:197
  1325.2 72.0 %reduce-scatter.29.cloned.1.call-done = bf16[1,256,2048]{2,1,0:T(8,128)(2,1)} async-done(((bf16[4,256,2048]{2,1,0:T(8,128)(2,1)}), bf16[1,256,2048]{2,1,0:T(8,128)(2,1)}) %reduce-scatter.29.cloned.1.call-update) | async-done | bytes 1048592 | tf_op jit(solution)/shard_map/reduce_scatter | solution.py:197
  1402.7 50.0 %all-gather.38.cloned.1.call-done = bf16[1,1024,2048]{2,1,0:T(8,128)(2,1)} async-done(((bf16[1,256,2048]{2,1,0:T(8,128)(2,1)}), bf16[1,1024,2048]{2,1,0:T(8,128)(2,1)}) %all-gather.38.cloned.1.call-update) | async-done | bytes 4194320 | tf_op jit(solution)/shard_map/all_gather | solution.py:188
  1458.1 23.0 %fusion.3 = (f32[2,4,1024]{2,1,0:T(4,128)S(1)}, f32[2,1024,1024,4]{2,1,3,0:T(8,128)}) fusion(f32[2,4,1024,1024]{2,3,1,0:T(8,128)} %get-tuple-element.410, f32[2,4,1024]{2,1,0:T(4,128)S(1)} %bitcast.390, bf16[1024,2,64,1]{0,2,3,1:T(8,128)(2,1)S(1)} %bitcast.386, bf16[1024,2,4,64]{0,3,2,1:T(8,128)(2,1)S(1)} %bitcast.379), kind=kOutput, calls=%fused_computation.8 | convolution fusion | flops 1098899456 | bytes 68485120 | tf_op jit(solution)/shard_map/while/body/eval_jaxpr/qkgd,pkd->kgqp/dot_general | solution.py:85
  1481.1 29.0 %fusion.5 = bf16[2,4,1024,1024]{2,3,1,0:T(8,128)(2,1)} fusion(f32[2,1024,1024,4]{2,1,3,0:T(8,128)} %get-tuple-element.414, f32[2,4,1024,1024]{2,3,1,0:T(8,128)} %get-tuple-element.410, f32[2,4,1024]{2,1,0:T(4,128)S(1)} %get-tuple-element.413, f32[2,4,1024]{2,1,0:T(4,128)S(1)} %bitcast.391), kind=kLoop, calls=%fused_computation.10 | loop fusion | flops 33554432 | bytes 83951616 | tf_op jit(solution)/shard_map/while/body/eval_jaxpr/convert_element_type | solution.py:96
  1510.1 8.7 fusion.122
  1518.8 13.3 fusion.123
  1533.1 8.8 convolution_multiply_fusion.1
  1555.6 22.8 %fusion = (f32[2,4,1024]{2,1,0:T(4,128)S(1)}, f32[2,1024,1024,4]{2,1,3,0:T(8,128)}) fusion(f32[2,4,1024,1024]{2,3,1,0:T(8,128)} %get-tuple-element.412, f32[2,4,1024]{2,1,0:T(4,128)S(1)} %bitcast.394, bf16[1024,2,64,1]{0,2,3,1:T(8,128)(2,1)S(1)} %bitcast.388, bf16[1024,2,4,64]{0,3,2,1:T(8,128)(2,1)S(1)} %bitcast.381), kind=kOutput, calls=%fused_computation.3 | convolution fusion | flops 1098899456 | bytes 68485120 | tf_op jit(solution)/shard_map/while/body/eval_jaxpr/qkgd,pkd->kgqp/dot_general | solution.py:85
  1578.4 29.3 %fusion.2 = bf16[2,4,1024,1024]{2,3,1,0:T(8,128)(2,1)} fusion(f32[2,1024,1024,4]{2,1,3,0:T(8,128)} %get-tuple-element.416, f32[2,4,1024,1024]{2,3,1,0:T(8,128)} %get-tuple-element.412, f32[2,4,1024]{2,1,0:T(4,128)S(1)} %get-tuple-element.415, f32[2,4,1024]{2,1,0:T(4,128)S(1)} %bitcast.395), kind=kLoop, calls=%fused_computation.5 | loop fusion | flops 33554432 | bytes 83951616 | tf_op jit(solution)/shard_map/while/body/eval_jaxpr/convert_element_type | solution.py:96
  1607.8 8.7 fusion.121
  1616.5 13.3 fusion.126
  1630.8 8.9 convolution_multiply_fusion
  1647.1 15.7 fusion.161
  1662.8 17.6 bitcast_add_fusion.1
  1680.4 16.4 copy.185
  1727.3 15.6 psum.7
  1743.0 10.0 select_maximum_fusion
  1753.0 15.7 reshape.1133
  1768.7 12.3 copy.214
  1781.1 26.8 %fusion.24 = f32[2048,4096,1]{1,0,2:T(8,128)} fusion(bf16[4,256,2048]{2,1,0:T(8,128)(2,1)} %all-gather.30.cloned.1.call-done, bf16[4,256,2048]{2,1,0:T(8,128)(2,1)} %get-tuple-element.363, bf16[4,256,2048]{2,1,0:T(8,128)(2,1)} %get-tuple-element.362), kind=kOutput, calls=%fused_computation.52 | convolution fusion | flops 17196646400 | bytes 46137344 | tf_op jit(solution)/shard_map/std,stf->df/dot_general | solution.py:334
  1807.9 32.7 %bitcast_add_fusion = f32[2048,4096]{1,0:T(8,128)} fusion(f32[2048,4096,1]{1,0,2:T(8,128)} %fusion.24, bf16[4,256,2048]{2,1,0:T(8,128)(2,1)} %all-gather.32.cloned.1.call-done, bf16[4,256,2048]{2,1,0:T(8,128)(2,1)} %get-tuple-element.361, bf16[4,256,2048]{2,1,0:T(8,128)(2,1)} %get-tuple-element.360), kind=kOutput, calls=%fused_computation | convolution fusion | flops 17205035008 | bytes 79691776 | tf_op jit(solution)/shard_map/std,stf->df/dot_general | solution.py:334
  1840.6 22.8 %copy.213 = f32[4,2,256,4096]{3,2,0,1:T(8,128)} copy(f32[4,2,256,4096]{3,2,1,0:T(8,128)} %bitcast.350) | data formatting | bytes 67108864 | tf_op jit(solution)/shard_map/reshape | solution.py:175
  1874.5 31.7 %reduce-scatter.39.cloned.1.call-done = f32[1,4,256,4096]{3,2,1,0:T(8,128)} async-done(((f32[2,4,256,4096]{3,2,1,0:T(8,128)}), f32[1,4,256,4096]{3,2,1,0:T(8,128)}) %reduce-scatter.39.cloned.1.call-update) | async-done | bytes 16777232 | tf_op jit(solution)/shard_map/reduce_scatter | solution.py:176
  1906.2 9.1 convert_bitcast_fusion
  1915.3 48.2 %reduce-scatter.45.cloned.1.call-done = bf16[2048,1,256]{2,0,1:T(8,128)(2,1)} async-done(((bf16[2048,4,256]{2,0,1:T(8,128)(2,1)}), bf16[2048,1,256]{2,0,1:T(8,128)(2,1)}) %reduce-scatter.45.cloned.1.call-update) | async-done | bytes 1048592
  1966.3 56.3 %reduce-scatter.37.cloned.1.call-done = bf16[1,256,1408]{1,2,0:T(8,128)(2,1)} async-done(((bf16[4,256,1408]{1,2,0:T(8,128)(2,1)}), bf16[1,256,1408]{1,2,0:T(8,128)(2,1)}) %reduce-scatter.37.cloned.1.call-update) | async-done | bytes 720912 | tf_op jit(solution)/shard_map/reduce_scatter | solution.py:177
  2025.8 142.6 %reduce-scatter.43.cloned.1.call-done = bf16[1,256,4096]{2,1,0:T(8,128)(2,1)} async-done(((bf16[4,256,4096]{2,1,0:T(8,128)(2,1)}), bf16[1,256,4096]{2,1,0:T(8,128)(2,1)}) %reduce-scatter.43.cloned.1.call-update) | async-done | bytes 2097168
  2189.6 20.2 all-to-all-done.4
  2221.3 21.4 all-to-all-done.5
  (406 shorter events, 323.7 us)
Async XLA Ops:
  7.2 109.3 %all-gather.44.cloned.1.call-start = ((), (), s32[]{:S(2)}) async-start(), calls=%async_computation.41 | async-start | bytes 3276800 | tf_op jit(solution)/shard_map/all_gather | solution.py:156
  11.5 0.7 collective-permute-start
  12.3 108.7 %copy-start.43 = (bf16[2,1,1024,512]{3,2,1,0:T(8,128)(2,1)S(1)}, bf16[2,1,1024,512]{3,2,1,0:T(8,128)(2,1)}, u32[]{:S(2)}) copy-start(bf16[2,1,1024,512]{3,2,1,0:T(8,128)(2,1)} %param.12) | copy-start | bytes 6291460
  13.1 161.1 %all-gather.46.cloned.1.call-start = ((), (), s32[]{:S(2)}) async-start(), calls=%async_computation.42 | async-start | bytes 7864320 | tf_op jit(solution)/shard_map/all_gather | solution.py:157
  122.5 30.3 %all-to-all-start = ((bf16[2,1,4,256,1,512]{5,3,0,4,1,2:T(8,128)(2,1)}), bf16[2,1,4,256,1,512]{5,3,0,4,1,2:T(8,128)(2,1)S(1)}, u32[]{:S(2)}, u32[]{:S(2)}) async-start(bf16[2,1,4,256,1,512]{5,3,0,4,1,2:T(8,128)(2,1)} %copy.155), calls=%async_computation | async-start | bytes 4194304 | tf_op jit(solution)/shard_map/all_to_all | solution.py:202
  126.2 105.9 %all-gather.26.cloned.1.call-start = ((), (), s32[]{:S(2)}) async-start(), calls=%async_computation.20 | async-start | bytes 5242880 | tf_op jit(solution)/shard_map/all_gather | solution.py:188
  152.8 18.1 copy-start.66
  152.8 534.0 %copy-start.54 = (f32[1,2048]{1,0:T(1,128)}, f32[1,2048]{1,0:T(1,128)S(1)}, u32[]{:S(2)}) copy-start(f32[1,2048]{1,0:T(1,128)S(1)} %get-tuple-element.394) | copy-start | bytes 24580
  160.2 1240.0 %copy-start = (f32[1,256,2048]{2,1,0:T(8,128)}, f32[1,256,2048]{2,1,0:T(8,128)S(1)}, u32[]{:S(2)}) copy-start(f32[1,256,2048]{2,1,0:T(8,128)S(1)} %reshape.1137) | copy-start | bytes 6291460
  179.5 143.4 %all-gather.48.cloned.1.call-start = ((), (), s32[]{:S(2)}) async-start(), calls=%async_computation.43 | async-start | bytes 10485760 | tf_op jit(solution)/shard_map/all_gather | solution.py:156
  235.2 119.2 %all-gather.50.cloned.1.call-start = ((), (), s32[]{:S(2)}) async-start(), calls=%async_computation.44 | async-start | bytes 25165824 | tf_op jit(solution)/shard_map/all_gather | solution.py:157
  322.9 101.3 %all-gather.28.cloned.1.call-start = ((), (), s32[]{:S(2)}) async-start(), calls=%async_computation.21 | async-start | bytes 5242880 | tf_op jit(solution)/shard_map/all_gather | solution.py:188
  334.8 40.5 %copy-start.25 = (f32[1024,32]{0,1:T(8,128)}, f32[1024,32]{0,1:T(8,128)S(1)}, u32[]{:S(2)}) copy-start(f32[1024,32]{0,1:T(8,128)S(1)} %get-tuple-element.406) | copy-start | bytes 393220
  334.8 216.5 %copy-start.23 = (f32[1024,32]{0,1:T(8,128)}, f32[1024,32]{0,1:T(8,128)S(1)}, u32[]{:S(2)}) copy-start(f32[1024,32]{0,1:T(8,128)S(1)} %get-tuple-element.401) | copy-start | bytes 393220
  368.5 110.0 %reduce-scatter.19.cloned.1.call-start = ((), (), s32[]{:S(2)}) async-start(), calls=%async_computation.22 | async-start | bytes 5242880 | tf_op jit(solution)/shard_map/reduce_scatter | solution.py:191
  375.0 28.8 %copy-start.27 = (bf16[1,1024,128]{1,2,0:T(8,128)(2,1)}, bf16[1,1024,128]{1,2,0:T(8,128)(2,1)S(1)}, u32[]{:S(2)}) copy-start(bf16[1,1024,128]{1,2,0:T(8,128)(2,1)S(1)} %slice.363) | copy-start | bytes 786436
  375.3 14.9 copy-start.58
  375.3 14.9 copy-start.60
  375.7 14.5 copy-start.35
  375.7 14.5 copy-start.37
  424.2 113.2 %all-gather.52.cloned.1.call-start = ((), (), s32[]{:S(2)}) async-start(), calls=%async_computation.45 | async-start | bytes 5242880 | tf_op jit(solution)/shard_map/all_gather | solution.py:156
  484.7 116.0 %all-gather.54.cloned.1.call-start = ((), (), s32[]{:S(2)}) async-start(), calls=%async_computation.46 | async-start | bytes 12582912 | tf_op jit(solution)/shard_map/all_gather | solution.py:157
  543.7 141.3 %reduce-scatter.21.cloned.1.call-start = ((), (), s32[]{:S(2)}) async-start(), calls=%async_computation.23 | async-start | bytes 5242880 | tf_op jit(solution)/shard_map/reduce_scatter | solution.py:191
  551.0 29.3 %copy-start.29 = (bf16[1,1024,128]{1,2,0:T(8,128)(2,1)}, bf16[1,1024,128]{1,2,0:T(8,128)(2,1)S(1)}, u32[]{:S(2)}) copy-start(bf16[1,1024,128]{1,2,0:T(8,128)(2,1)S(1)} %slice.362) | copy-start | bytes 786436
  551.3 15.8 copy-start.62
  551.3 15.8 copy-start.64
  551.6 15.5 copy-start.39
  551.7 15.5 copy-start.41
  631.7 136.2 %all-gather.30.cloned.1.call-start = ((), (), s32[]{:S(2)}) async-start(), calls=%async_computation.24 | async-start | bytes 5242880 | tf_op jit(solution)/shard_map/all_gather | solution.py:194
  685.0 164.2 %all-gather.32.cloned.1.call-start = ((), (), s32[]{:S(2)}) async-start(), calls=%async_computation.25 | async-start | bytes 5242880 | tf_op jit(solution)/shard_map/all_gather | solution.py:194
  768.0 159.4 %reduce-scatter.23.cloned.1.call-start = ((), (), s32[]{:S(2)}) async-start(), calls=%async_computation.26 | async-start | bytes 5242880 | tf_op jit(solution)/shard_map/reduce_scatter | solution.py:197
  849.2 158.2 %reduce-scatter.25.cloned.1.call-start = ((), (), s32[]{:S(2)}) async-start(), calls=%async_computation.27 | async-start | bytes 5242880 | tf_op jit(solution)/shard_map/reduce_scatter | solution.py:197
  1012.4 17.9 all-to-all-start.1
  1030.3 28.9 %all-to-all-start.3 = ((bf16[2,1,4,256,1,512]{5,3,0,4,1,2:T(8,128)(2,1)}), bf16[2,1,4,256,1,512]{5,3,0,4,1,2:T(8,128)(2,1)}, u32[]{:S(2)}, u32[]{:S(2)}) async-start(bf16[2,1,4,256,1,512]{5,3,0,4,1,2:T(8,128)(2,1)} %copy.168), calls=%async_computation.7 | async-start | bytes 4194304 | tf_op jit(solution)/shard_map/all_to_all | solution.py:202
  1059.2 17.4 all-to-all-start.2
  1063.5 95.0 %all-gather.34.cloned.1.call-start = ((), (), s32[]{:S(2)}) async-start(), calls=%async_computation.28 | async-start | bytes 5242880 | tf_op jit(solution)/shard_map/all_gather | solution.py:194
  1076.7 163.0 %all-gather.36.cloned.1.call-start = ((), (), s32[]{:S(2)}) async-start(), calls=%async_computation.29 | async-start | bytes 5242880 | tf_op jit(solution)/shard_map/all_gather | solution.py:194
  1158.5 158.7 %reduce-scatter.27.cloned.1.call-start = ((), (), s32[]{:S(2)}) async-start(), calls=%async_computation.30 | async-start | bytes 5242880 | tf_op jit(solution)/shard_map/reduce_scatter | solution.py:197
  1239.7 157.5 %reduce-scatter.29.cloned.1.call-start = ((), (), s32[]{:S(2)}) async-start(), calls=%async_computation.31 | async-start | bytes 5242880 | tf_op jit(solution)/shard_map/reduce_scatter | solution.py:197
  1284.8 32.5 %copy-start.55 = (f32[1,2048]{1,0:T(1,128)S(1)}, f32[1,2048]{1,0:T(1,128)}, u32[]{:S(2)}) copy-start(f32[1,2048]{1,0:T(1,128)} %copy-done.54) | copy-start | bytes 24580
  1284.8 32.5 %copy-start.76 = (f32[256]{0:T(256)S(1)}, f32[256]{0:T(256)}, u32[]{:S(2)}) copy-start(f32[256]{0:T(256)} %copy-done.75) | copy-start | bytes 3076
  1317.2 135.6 %all-gather.38.cloned.1.call-start = ((), (), s32[]{:S(2)}) async-start(), calls=%async_computation.32 | async-start | bytes 5242880 | tf_op jit(solution)/shard_map/all_gather | solution.py:188
  1321.7 75.5 %copy-start.73 = (f32[256]{0:T(256)S(1)}, f32[256]{0:T(256)}, u32[]{:S(2)}) copy-start(f32[256]{0:T(256)} %copy-done.72) | copy-start | bytes 3076
  1397.2 153.0 %all-gather.40.cloned.1.call-start = ((), (), s32[]{:S(2)}) async-start(), calls=%async_computation.33 | async-start | bytes 5242880 | tf_op jit(solution)/shard_map/all_gather | solution.py:188
  1452.8 194.3 %reduce-scatter.31.cloned.1.call-start = ((), (), s32[]{:S(2)}) async-start(), calls=%async_computation.34 | async-start | bytes 5242880 | tf_op jit(solution)/shard_map/reduce_scatter | solution.py:191
  1481.1 29.0 %copy-start.36 = (bf16[1,1024,8,32]{1,3,2,0:T(8,128)(2,1)S(1)}, bf16[1,1024,8,32]{1,3,2,0:T(8,128)(2,1)}, u32[]{:S(2)}) copy-start(bf16[1,1024,8,32]{1,3,2,0:T(8,128)(2,1)} %copy-done.35) | copy-start | bytes 1572868
  1481.1 29.0 %copy-start.38 = (bf16[1,1024,8,32]{1,3,2,0:T(8,128)(2,1)S(1)}, bf16[1,1024,8,32]{1,3,2,0:T(8,128)(2,1)}, u32[]{:S(2)}) copy-start(bf16[1,1024,8,32]{1,3,2,0:T(8,128)(2,1)} %copy-done.37) | copy-start | bytes 1572868
  1550.3 174.3 %reduce-scatter.33.cloned.1.call-start = ((), (), s32[]{:S(2)}) async-start(), calls=%async_computation.35 | async-start | bytes 5242880 | tf_op jit(solution)/shard_map/reduce_scatter | solution.py:191
  1578.4 29.4 %copy-start.40 = (bf16[1,1024,8,32]{1,3,2,0:T(8,128)(2,1)S(1)}, bf16[1,1024,8,32]{1,3,2,0:T(8,128)(2,1)}, u32[]{:S(2)}) copy-start(bf16[1,1024,8,32]{1,3,2,0:T(8,128)(2,1)} %copy-done.39) | copy-start | bytes 1572868
  1578.4 29.3 %copy-start.42 = (bf16[1,1024,8,32]{1,3,2,0:T(8,128)(2,1)S(1)}, bf16[1,1024,8,32]{1,3,2,0:T(8,128)(2,1)}, u32[]{:S(2)}) copy-start(bf16[1,1024,8,32]{1,3,2,0:T(8,128)(2,1)} %copy-done.41) | copy-start | bytes 1572868
  1616.5 13.5 copy-start.24
  1647.1 216.5 %reduce-scatter.41.cloned.1.call-start = ((), (), s32[]{:S(2)}) async-start(), calls=%async_computation.40 | async-start | bytes 25165824 | tf_op jit(solution)/shard_map/reduce_scatter | solution.py:176
  1647.1 15.7 copy-start.20
  1696.8 172.7 %reduce-scatter.35.cloned.1.call-start = ((), (), s32[]{:S(2)}) async-start(), calls=%async_computation.36 | async-start | bytes 17301504 | tf_op jit(solution)/shard_map/reduce_scatter | solution.py:176
  1781.0 125.2 %reduce-scatter.39.cloned.1.call-start = ((), (), s32[]{:S(2)}) async-start(), calls=%async_computation.39 | async-start | bytes 50331648 | tf_op jit(solution)/shard_map/reduce_scatter | solution.py:176
  1863.5 100.0 %reduce-scatter.45.cloned.1.call-start = ((), (), s32[]{:S(2)}) async-start(), calls=%async_computation.50 | async-start | bytes 5242880
  1869.4 153.2 %reduce-scatter.37.cloned.1.call-start = ((), (), s32[]{:S(2)}) async-start(), calls=%async_computation.37 | async-start | bytes 3604480 | tf_op jit(solution)/shard_map/reduce_scatter | solution.py:177
  1874.4 293.9 %reduce-scatter.43.cloned.1.call-start = ((), (), s32[]{:S(2)}) async-start(), calls=%async_computation.49 | async-start | bytes 10485760
  1915.3 306.0 %all-gather.58.cloned.1.call-start = ((), (), s32[]{:S(2)}) async-start(), calls=%async_computation.48 | async-start | bytes 6291456 | tf_op jit(solution)/shard_map/all_gather | solution.py:182
  1966.2 280.5 %all-gather.42.cloned.1.call-start = ((), (), s32[]{:S(2)}) async-start(), calls=%async_computation.38 | async-start | bytes 4325376 | tf_op jit(solution)/shard_map/all_gather | solution.py:427
  2023.8 0.8 collective-permute-start.1
  2025.7 229.1 %all-gather.56.cloned.1.call-start = ((), (), s32[]{:S(2)}) async-start(), calls=%async_computation.47 | async-start | bytes 12582912 | tf_op jit(solution)/shard_map/all_gather | solution.py:182
  2180.3 29.5 %all-to-all-start.4 = ((f32[1,1,1,256,4,512]{5,3,2,1,0,4:T(8,128)}), f32[1,1,1,256,4,512]{5,3,2,1,0,4:T(8,128)}, u32[]{:S(2)}, u32[]{:S(2)}) async-start(f32[1,1,1,256,4,512]{5,3,2,1,0,4:T(8,128)} %copy.177), calls=%async_computation.12 | async-start | bytes 4194304 | tf_op jit(solution)/shard_map/all_to_all | solution.py:208
  2214.6 28.1 %all-to-all-start.5 = ((f32[1,1,1,256,4,512]{5,3,2,1,0,4:T(8,128)}), f32[1,1,1,256,4,512]{5,3,2,1,0,4:T(8,128)S(1)}, u32[]{:S(2)}, u32[]{:S(2)}) async-start(f32[1,1,1,256,4,512]{5,3,2,1,0,4:T(8,128)} %copy.178), calls=%async_computation.13 | async-start | bytes 4194304 | tf_op jit(solution)/shard_map/all_to_all | solution.py:208
  (69 other events, 331.9 us)
Sparse Core Ops, SparseCore 0:
  13.2 103.2 all-gather.43
  121.0 13.3 all-gather.45
  179.6 52.4 all-gather.25
  235.4 87.4 all-gather.47
  324.3 30.0 all-gather.49
  368.6 53.7 all-gather.27
  425.9 52.5 reduce-scatter.18
  484.9 52.5 all-gather.51
  543.8 19.8 all-gather.53
  631.9 53.0 reduce-scatter.20
  687.1 80.7 all-gather.29
  769.9 79.2 all-gather.31
  852.1 75.2 reduce-scatter.22
  930.1 77.2 reduce-scatter.24
  1076.8 81.5 all-gather.33
  1160.4 79.2 all-gather.35
  1241.8 75.2 reduce-scatter.26
  1319.9 77.2 reduce-scatter.28
  1399.6 53.0 all-gather.37
  1455.0 52.5 all-gather.39
  1550.4 52.4 reduce-scatter.30
  1647.2 52.5 reduce-scatter.32
  1702.1 25.0 reduce-scatter.40
  1781.2 18.7 reduce-scatter.34
  1863.6 42.4 reduce-scatter.38
  1909.6 53.8 reduce-scatter.44
  1966.2 56.3 reduce-scatter.36
  2025.7 142.6 reduce-scatter.42
  2170.5 13.6 all-gather.57
  2185.5 12.8 all-gather.41
  2200.6 21.0 all-gather.55

commit v8 on v6

--- a/solution.py
+++ b/solution.py
@@ -174,6 +174,14 @@
         return lax.psum_scatter(
             split.astype(jnp.bfloat16), axis_name, scatter_dimension=axis
         ).astype(jnp.float32)
+
+    def reduce_half_exchange(partial, axis_name):
+        count = n_row if axis_name == "row" else n_col
+        half = partial.shape[0] // (count * n_dp)
+        split = jnp.swapaxes(partial.reshape((count, n_dp, half) + partial.shape[1:]), 0, 1)
+        split = lax.psum_scatter(split, "dp", scatter_dimension=0)
+        blocks = lax.all_to_all(split.astype(jnp.bfloat16), axis_name, 0, 0)
+        return jnp.sum(blocks.astype(jnp.float32), axis=0)
 
     def reduce_features(partial, axis, axis_name):
         return lax.all_gather(reduce_half(partial, axis, axis_name), "dp", axis=axis, tiled=True)
@@ -241,8 +249,9 @@
         w_out_heads = w_attn[:, qkv_cols:].T
         w_pair = gather_features(jnp.concatenate([w_gate, w_up], axis=1), 0, "row")
         w_down_all = gather_features(w_down, 1, "row")
-        gain_attn_all = lax.all_gather(gain_attn, "row", tiled=True)
-        gain_ffn_all = lax.all_gather(gain_ffn, "row", tiled=True)
+        gain_attn_all, gain_ffn_all = lax.all_gather(
+            jnp.stack([gain_attn, gain_ffn]), "row", axis=1, tiled=True
+        )
 
         segments = lax.all_gather(segment_ids, "row", axis=1, tiled=True)
         segments = lax.dynamic_slice_in_dim(segments, col_index * local, local, axis=1)
@@ -410,7 +419,7 @@
         gain_cols = jnp.pad(gain_rows, ((0, 0), (0, 126)))
         total_attn = lax.all_gather(
             transpose_grid(
-                reduce_half(jnp.concatenate([grad_attn_w, gain_cols], axis=1), 0, "col")
+                reduce_half_exchange(jnp.concatenate([grad_attn_w, gain_cols], axis=1), "col")
             ),
             "dp",
             axis=0,

time: 2120 us -> 2050 us (0.967)
  waiting for transfers between devices: 1040 us -> 963 us
    reduce_scatter x1, waiting for transfers between devices: 56.3 us -> 0.02 us  [reduce_half_exchange(): split = lax.psum_scatter(split, 'dp', scatter_dimension=0)]
    reshape x0 -> x2, local copies, waits for them, and re-layouts: none -> 33.6 us  [reduce_half_exchange(): partial.reshape((count, n_dp, half) + partial.shape[1:])]
    reduce_scatter x3 -> x2, waiting for transfers between devices: 31.6 us -> 0.04 us  [reduce_half(): split = lax.psum_scatter(split, 'dp', scatter_dimension=axis)]
    reshape x4 -> x2, local copies, waits for them, and re-layouts: 67.6 us -> 39.5 us  [reduce_half(): split = jnp.swapaxes(partial.reshape(shape), axis, axis + 1)]
    unnamed x33 -> x32, waiting for transfers between devices: 191 us -> 179 us
  transfers between devices with their start and end apart: 38 -> 38, of which waited for: 25 -> 24; matrix products, arithmetic and copies ran while one was open for 40% -> 42% of each run, Pallas kernels for 0% -> 0%
where the time goes in v8:
time: 2050 us; the launch traced here: 2040 us
  waiting for transfers between devices  963 us (47%)
  matrix products  471 us (23%)
  local copies, waits for them, and re-layouts  233 us (11%)
  other arithmetic  203 us (10%)
  blocking collectives  81 us (4%)
  starting transfers between devices  75.8 us (4%)
    all_gather x4, waiting for transfers between devices, gather_seqs(): return lax.all_gather(rows, 'col', axis=0, tiled=True)  217 us
    reduce_scatter x4, waiting for transfers between devices, scatter_seqs(): return lax.psum_scatter(rows, 'col', scatter_dimension=0, tiled=True)  184 us
    unnamed x32, waiting for transfers between devices  179 us
    all_gather x3, waiting for transfers between devices, gather_half(): gathered = lax.all_gather(mine, axis_name, axis=axis)  139 us
    all_gather x4, waiting for transfers between devices, gather_tokens(): return lax.all_gather(rows, 'row', axis=1, tiled=True)  86 us
    dot_general x2, matrix products, micro_batch(): jnp.einsum('std,stf->df', spread_ffn, paired_gradient, preferred_element_...  61.7 us
    convert_element_type x2, other arithmetic, attend_backward(): grad_scores = (attn_probs * (grad_probs - jnp.sum(attn_probs * grad_probs...  58.3 us
    all_to_all x4, waiting for transfers between devices, to_features(): rows = lax.all_to_all(rows, 'row', 3, 2)  56.9 us
  transfers between devices with their start and end apart: 38, of which 24 were waited for; matrix products, arithmetic and copies ran while one was open for 42% of the time, Pallas kernels for 0%

profile of v8, /device:TPU:0, one launch (start us, length us, event | category | flops | bytes accessed | tf_op | source)
XLA Modules:
  0.0 2042.8 jit_solution(4701881860825137041)
XLA Ops:
  16.3 50.9 %all-to-all-start = ((bf16[2,1,4,256,1,512]{5,3,0,4,1,2:T(8,128)(2,1)}), bf16[2,1,4,256,1,512]{5,3,0,4,1,2:T(8,128)(2,1)}, u32[]{:S(2)}, u32[]{:S(2)}) async-start(bf16[2,1,4,256,1,512]{5,3,0,4,1,2:T(8,128)(2,1)} %copy.149), calls=%async_computation | async-start | bytes 4194304 | tf_op jit(solution)/shard_map/all_to_all | solution.py:207
  67.2 27.4 %all_gather.75 = f32[2,2048]{1,0:T(2,128)S(1)} all-gather(f32[2,512]{1,0:T(2,128)S(1)} %pad_maximum_fusion.29), channel_id=1, replica_groups=mesh['dp'=2,'row'=4,'col'=4] {'row'}, dimensions={1}, use_global_device_ids=true | all-gather | bytes 20480 | tf_op jit(solution)/shard_map/all_gather | solution.py:252
  122.7 9.3 all_gather.78
  136.7 34.6 %all-gather.26.cloned.1.call-done = bf16[1,1024,2048]{2,1,0:T(8,128)(2,1)} async-done(((bf16[1,256,2048]{2,1,0:T(8,128)(2,1)}), bf16[1,1024,2048]{2,1,0:T(8,128)(2,1)}) %all-gather.26.cloned.1.call-update) | async-done | bytes 4194320 | tf_op jit(solution)/shard_map/all_gather | solution.py:193
  171.5 17.1 all-gather.46.cloned.1.call-done
  197.5 13.7 fusion.131
  211.2 13.4 exponential_reduce_fusion.1
  224.7 13.4 fusion.78
  252.7 14.2 fusion.132
  267.0 13.5 exponential_reduce_fusion
  280.5 14.1 fusion.81
  309.2 47.5 %reduce-scatter.20.cloned.1.call-done = bf16[1,256,2048]{2,1,0:T(8,128)(2,1)} async-done(((bf16[1,1024,2048]{2,1,0:T(8,128)(2,1)}), bf16[1,256,2048]{2,1,0:T(8,128)(2,1)}) %reduce-scatter.20.cloned.1.call-update) | async-done | bytes 1048592 | tf_op jit(solution)/shard_map/reduce_scatter | solution.py:196
  356.8 55.0 %all-gather.52.cloned.1.call-done = bf16[2048,1024]{0,1:T(8,128)(2,1)} async-done(((bf16[2048,256]{0,1:T(8,128)(2,1)}), bf16[2048,1024]{0,1:T(8,128)(2,1)}) %all-gather.52.cloned.1.call-update) | async-done | bytes 4194320 | tf_op jit(solution)/shard_map/all_gather | solution.py:153
  418.0 83.7 %all-gather.48.cloned.1.call-done = bf16[1024,4096]{1,0:T(8,128)(2,1)} async-done(((bf16[256,4096]{1,0:T(8,128)(2,1)}), bf16[1024,4096]{1,0:T(8,128)(2,1)}) %all-gather.48.cloned.1.call-update) | async-done | bytes 8388624 | tf_op jit(solution)/shard_map/all_gather | solution.py:153
  505.9 78.6 %all-gather.30.cloned.1.call-done = bf16[4,256,2048]{2,1,0:T(8,128)(2,1)} async-done(((bf16[1,256,2048]{2,1,0:T(8,128)(2,1)}), bf16[4,256,2048]{2,1,0:T(8,128)(2,1)}) %all-gather.30.cloned.1.call-update) | async-done | bytes 4194320 | tf_op jit(solution)/shard_map/all_gather | solution.py:199
  584.7 20.3 all-gather.54.cloned.1.call-done
  604.9 16.4 copy.164
  621.3 15.2 reshape.1153
  637.8 15.5 copy.161
  653.2 20.4 fusion.133
  681.5 10.4 convolution_convert_fusion.1
  691.8 29.9 %all-gather.32.cloned.1.call-done = bf16[4,256,2048]{2,1,0:T(8,128)(2,1)} async-done(((bf16[1,256,2048]{2,1,0:T(8,128)(2,1)}), bf16[4,256,2048]{2,1,0:T(8,128)(2,1)}) %all-gather.32.cloned.1.call-update) | async-done | bytes 4194320 | tf_op jit(solution)/shard_map/all_gather | solution.py:199
  722.0 21.5 %fusion.134 = f32[4,256,4096]{2,1,0:T(8,128)S(1)} fusion(bf16[4,256,2048]{2,1,0:T(8,128)(2,1)} %all-gather.32.cloned.1.call-done, bf16[2048,4096,1]{1,0,2:T(8,128)(2,1)} %bitcast.311), kind=kOutput, calls=%fused_computation.250 | convolution fusion | flops 17179869184 | bytes 37748736 | tf_op jit(solution)/shard_map/std,df->stf/dot_general | solution.py:307
  751.4 12.5 convolution_convert_fusion
  763.9 36.0 %reduce-scatter.22.cloned.1.call-done = bf16[1,256,2048]{2,1,0:T(8,128)(2,1)} async-done(((bf16[4,256,2048]{2,1,0:T(8,128)(2,1)}), bf16[1,256,2048]{2,1,0:T(8,128)(2,1)}) %reduce-scatter.22.cloned.1.call-update) | async-done | bytes 1048592 | tf_op jit(solution)/shard_map/reduce_scatter | solution.py:202
  800.2 28.5 %all_to_all.95 = bf16[2,1,4,256,1,512]{5,3,0,4,1,2:T(8,128)(2,1)S(1)} all-to-all(bf16[2,1,4,256,1,512]{5,3,0,4,1,2:T(8,128)(2,1)S(1)} %copy.166), channel_id=1, replica_groups=mesh['dp'=2,'row'=4,'col'=4] {'row'}, dimensions={2} | all-to-all | bytes 4194304 | tf_op jit(solution)/shard_map/all_to_all | solution.py:207
  837.1 42.9 %reduce-scatter.24.cloned.1.call-done = bf16[1,256,2048]{2,1,0:T(8,128)(2,1)} async-done(((bf16[4,256,2048]{2,1,0:T(8,128)(2,1)}), bf16[1,256,2048]{2,1,0:T(8,128)(2,1)}) %reduce-scatter.24.cloned.1.call-update) | async-done | bytes 1048592 | tf_op jit(solution)/shard_map/reduce_scatter | solution.py:202
  891.3 71.9 %all-gather.34.cloned.1.call-done = bf16[4,256,2048]{2,1,0:T(8,128)(2,1)} async-done(((bf16[1,256,2048]{2,1,0:T(8,128)(2,1)}), bf16[4,256,2048]{2,1,0:T(8,128)(2,1)}) %all-gather.34.cloned.1.call-update) | async-done | bytes 4194320 | tf_op jit(solution)/shard_map/all_gather | solution.py:199
  963.3 20.4 multiply_convert_fusion.3
  983.7 24.0 %fusion.37 = bf16[4,256,2048]{2,1,0:T(8,128)(2,1)} fusion(bf16[2048,4096,1]{1,0,2:T(8,128)(2,1)} %bitcast.312, bf16[4,256,2048]{2,1,0:T(8,128)(2,1)} %get-tuple-element.337, bf16[4,256,2048]{2,1,0:T(8,128)(2,1)} %get-tuple-element.336), kind=kOutput, calls=%fused_computation.70 | convolution fusion | flops 17198743552 | bytes 29360128 | tf_op jit(solution)/shard_map/stf,df->std/dot_general | solution.py:341
  1007.7 36.8 %all-gather.36.cloned.1.call-done = bf16[4,256,2048]{2,1,0:T(8,128)(2,1)} async-done(((bf16[1,256,2048]{2,1,0:T(8,128)(2,1)}), bf16[4,256,2048]{2,1,0:T(8,128)(2,1)}) %all-gather.36.cloned.1.call-update) | async-done | bytes 4194320 | tf_op jit(solution)/shard_map/all_gather | solution.py:199
  1044.7 21.0 %multiply_convert_fusion.1 = (bf16[4,256,2048]{2,1,0:T(8,128)(2,1)}, bf16[4,256,2048]{2,1,0:T(8,128)(2,1)}) fusion(f32[4,256,4096]{2,1,0:T(8,128)} %copy-done.18, bf16[4,256,2048]{2,1,0:T(8,128)(2,1)} %all-gather.36.cloned.1.call-done, bf16[2048,2048,1]{1,0,2:T(8,128)(2,1)} %reshape.1153), kind=kOutput, calls=%fused_computation.28 | convolution fusion | flops 8617197568 | bytes 37748736 | tf_op jit(solution)/shard_map/std,fd->stf/dot_general | solution.py:328
  1065.7 23.8 %fusion.38 = bf16[4,256,2048]{2,1,0:T(8,128)(2,1)} fusion(bf16[2048,4096,1]{1,0,2:T(8,128)(2,1)} %bitcast.313, bf16[4,256,2048]{2,1,0:T(8,128)(2,1)} %get-tuple-element.335, bf16[4,256,2048]{2,1,0:T(8,128)(2,1)} %get-tuple-element.334), kind=kOutput, calls=%fused_computation.71 | convolution fusion | flops 17198743552 | bytes 29360128 | tf_op jit(solution)/shard_map/stf,df->std/dot_general | solution.py:341
  1089.6 32.4 %reduce-scatter.26.cloned.1.call-done = bf16[1,256,2048]{2,1,0:T(8,128)(2,1)} async-done(((bf16[4,256,2048]{2,1,0:T(8,128)(2,1)}), bf16[1,256,2048]{2,1,0:T(8,128)(2,1)}) %reduce-scatter.26.cloned.1.call-update) | async-done | bytes 1048592 | tf_op jit(solution)/shard_map/reduce_scatter | solution.py:202
  1128.8 73.2 %reduce-scatter.28.cloned.1.call-done = bf16[1,256,2048]{2,1,0:T(8,128)(2,1)} async-done(((bf16[4,256,2048]{2,1,0:T(8,128)(2,1)}), bf16[1,256,2048]{2,1,0:T(8,128)(2,1)}) %reduce-scatter.28.cloned.1.call-update) | async-done | bytes 1048592 | tf_op jit(solution)/shard_map/reduce_scatter | solution.py:202
  1207.2 50.3 %all-gather.38.cloned.1.call-done = bf16[1,1024,2048]{2,1,0:T(8,128)(2,1)} async-done(((bf16[1,256,2048]{2,1,0:T(8,128)(2,1)}), bf16[1,1024,2048]{2,1,0:T(8,128)(2,1)}) %all-gather.38.cloned.1.call-update) | async-done | bytes 4194320 | tf_op jit(solution)/shard_map/all_gather | solution.py:193
  1262.9 23.0 %fusion.3 = (f32[2,4,1024]{2,1,0:T(4,128)S(1)}, f32[2,1024,1024,4]{2,1,3,0:T(8,128)}) fusion(f32[2,4,1024,1024]{2,3,1,0:T(8,128)} %get-tuple-element.388, f32[2,4,1024]{2,1,0:T(4,128)S(1)} %bitcast.353, bf16[1024,2,64,1]{0,2,3,1:T(8,128)(2,1)S(1)} %bitcast.347, bf16[1024,2,4,64]{0,3,2,1:T(8,128)(2,1)S(1)} %bitcast.337), kind=kOutput, calls=%fused_computation.8 | convolution fusion | flops 1098899456 | bytes 68485120 | tf_op jit(solution)/shard_map/while/body/eval_jaxpr/qkgd,pkd->kgqp/dot_general | solution.py:85
  1285.9 29.0 %fusion.5 = bf16[2,4,1024,1024]{2,3,1,0:T(8,128)(2,1)} fusion(f32[2,1024,1024,4]{2,1,3,0:T(8,128)} %get-tuple-element.392, f32[2,4,1024,1024]{2,3,1,0:T(8,128)} %get-tuple-element.388, f32[2,4,1024]{2,1,0:T(4,128)S(1)} %get-tuple-element.391, f32[2,4,1024]{2,1,0:T(4,128)S(1)} %bitcast.354), kind=kLoop, calls=%fused_computation.10 | loop fusion | flops 33554432 | bytes 83951616 | tf_op jit(solution)/shard_map/while/body/eval_jaxpr/convert_element_type | solution.py:96
  1314.9 8.7 fusion.97
  1323.6 13.3 fusion.98
  1337.9 8.9 convolution_multiply_fusion.1
  1360.1 22.6 %fusion = (f32[2,4,1024]{2,1,0:T(4,128)S(1)}, f32[2,1024,1024,4]{2,1,3,0:T(8,128)}) fusion(f32[2,4,1024,1024]{2,3,1,0:T(8,128)} %get-tuple-element.390, f32[2,4,1024]{2,1,0:T(4,128)S(1)} %bitcast.349, bf16[1024,2,64,1]{0,2,3,1:T(8,128)(2,1)S(1)} %bitcast.345, bf16[1024,2,4,64]{0,3,2,1:T(8,128)(2,1)S(1)} %bitcast.339), kind=kOutput, calls=%fused_computation.3 | convolution fusion | flops 1098899456 | bytes 68485120 | tf_op jit(solution)/shard_map/while/body/eval_jaxpr/qkgd,pkd->kgqp/dot_general | solution.py:85
  1382.7 29.3 %fusion.2 = bf16[2,4,1024,1024]{2,3,1,0:T(8,128)(2,1)} fusion(f32[2,1024,1024,4]{2,1,3,0:T(8,128)} %get-tuple-element.394, f32[2,4,1024,1024]{2,3,1,0:T(8,128)} %get-tuple-element.390, f32[2,4,1024]{2,1,0:T(4,128)S(1)} %get-tuple-element.393, f32[2,4,1024]{2,1,0:T(4,128)S(1)} %bitcast.350), kind=kLoop, calls=%fused_computation.5 | loop fusion | flops 33554432 | bytes 83951616 | tf_op jit(solution)/shard_map/while/body/eval_jaxpr/convert_element_type | solution.py:96
  1412.1 8.7 fusion.96
  1420.8 13.3 fusion.101
  1435.1 8.9 convolution_multiply_fusion
  1451.4 15.7 fusion.135
  1467.1 17.4 bitcast_add_fusion.1
  1484.5 16.7 copy.184
  1501.2 28.9 %fusion.9 = f32[2048,4096,1]{1,0,2:T(8,128)} fusion(bf16[4,256,2048]{2,1,0:T(8,128)(2,1)} %all-gather.30.cloned.1.call-done, bf16[4,256,2048]{2,1,0:T(8,128)(2,1)} %get-tuple-element.337, bf16[4,256,2048]{2,1,0:T(8,128)(2,1)} %get-tuple-element.336), kind=kOutput, calls=%fused_computation.37 | convolution fusion | flops 17196646400 | bytes 46137344 | tf_op jit(solution)/shard_map/std,stf->df/dot_general | solution.py:338
  1530.1 32.9 %bitcast_add_fusion = f32[2048,4096]{1,0:T(8,128)} fusion(f32[2048,4096,1]{1,0,2:T(8,128)} %fusion.9, bf16[4,256,2048]{2,1,0:T(8,128)(2,1)} %all-gather.32.cloned.1.call-done, bf16[4,256,2048]{2,1,0:T(8,128)(2,1)} %get-tuple-element.335, bf16[4,256,2048]{2,1,0:T(8,128)(2,1)} %get-tuple-element.334), kind=kOutput, calls=%fused_computation | convolution fusion | flops 17205035008 | bytes 79691776 | tf_op jit(solution)/shard_map/std,stf->df/dot_general | solution.py:338
  1562.9 22.9 %copy.210 = f32[4,2,256,4096]{3,2,0,1:T(8,128)} copy(f32[4,2,256,4096]{3,2,1,0:T(8,128)} %bitcast.307) | data formatting | bytes 67108864 | tf_op jit(solution)/shard_map/reshape | solution.py:172
  1611.1 8.9 fusion.52
  1620.1 15.8 psum.7
  1635.9 10.0 select_maximum_fusion
  1645.9 15.8 reshape.1131
  1661.7 17.8 copy.178
  1685.5 13.0 convert_bitcast_fusion
  1707.9 48.9 %reduce-scatter.42.cloned.1.call-done = bf16[2048,1,256]{2,0,1:T(8,128)(2,1)} async-done(((bf16[2048,4,256]{2,0,1:T(8,128)(2,1)}), bf16[2048,1,256]{2,0,1:T(8,128)(2,1)}) %reduce-scatter.42.cloned.1.call-update) | async-done | bytes 1048592
  1759.5 13.8 all-to-all-done.6
  1777.8 130.0 %reduce-scatter.40.cloned.1.call-done = bf16[1,256,4096]{2,1,0:T(8,128)(2,1)} async-done(((bf16[4,256,4096]{2,1,0:T(8,128)(2,1)}), bf16[1,256,4096]{2,1,0:T(8,128)(2,1)}) %reduce-scatter.40.cloned.1.call-update) | async-done | bytes 2097168
  1929.2 9.9 all-to-all-done.3
  1966.2 18.4 all-to-all-done.5
  1991.0 21.6 %all-to-all-done.4 = f32[1,1,1,256,4,512]{5,3,2,1,0,4:T(8,128)S(1)} async-done(((f32[1,1,1,256,4,512]{5,3,2,1,0,4:T(8,128)}), f32[1,1,1,256,4,512]{5,3,2,1,0,4:T(8,128)S(1)}, u32[]{:S(2)}, u32[]{:S(2)}) %all-to-all-start.4) | async-done | bytes 2097184 | tf_op jit(solution)/shard_map/all_to_all | solution.py:213
  (429 shorter events, 293.1 us)
Async XLA Ops:
  7.2 294.5 %copy-start = (bf16[2048,512]{1,0:T(8,128)(2,1)S(1)}, bf16[2048,512]{1,0:T(8,128)(2,1)}, u32[]{:S(2)}) copy-start(bf16[2048,512]{1,0:T(8,128)(2,1)} %param.20) | copy-start | bytes 6291460
  7.2 111.0 %all-gather.44.cloned.1.call-start = ((), (), s32[]{:S(2)}) async-start(), calls=%async_computation.40 | async-start | bytes 3276800 | tf_op jit(solution)/shard_map/all_gather | solution.py:153
  11.7 0.7 collective-permute-start
  13.3 54.0 %copy-start.100 = (f32[512]{0:T(512)S(1)}, f32[512]{0:T(512)}, u32[]{:S(2)}) copy-start(f32[512]{0:T(512)} %param.22) | copy-start | bytes 6148
  13.3 53.9 %copy-start.101 = (f32[512]{0:T(512)S(1)}, f32[512]{0:T(512)}, u32[]{:S(2)}) copy-start(f32[512]{0:T(512)} %param.21) | copy-start | bytes 6148
  16.3 78.3 %all-to-all-start = ((bf16[2,1,4,256,1,512]{5,3,0,4,1,2:T(8,128)(2,1)}), bf16[2,1,4,256,1,512]{5,3,0,4,1,2:T(8,128)(2,1)}, u32[]{:S(2)}, u32[]{:S(2)}) async-start(bf16[2,1,4,256,1,512]{5,3,0,4,1,2:T(8,128)(2,1)} %copy.149), calls=%async_computation | async-start | bytes 4194304 | tf_op jit(solution)/shard_map/all_to_all | solution.py:207
  67.2 104.1 %all-gather.26.cloned.1.call-start = ((), (), s32[]{:S(2)}) async-start(), calls=%async_computation.20 | async-start | bytes 5242880 | tf_op jit(solution)/shard_map/all_gather | solution.py:193
  94.6 409.3 %copy-start.61 = (f32[1,2048]{1,0:T(1,128)}, f32[1,2048]{1,0:T(1,128)S(1)}, u32[]{:S(2)}) copy-start(f32[1,2048]{1,0:T(1,128)S(1)} %get-tuple-element.370) | copy-start | bytes 24580
  118.2 70.5 %all-gather.46.cloned.1.call-start = ((), (), s32[]{:S(2)}) async-start(), calls=%async_computation.41 | async-start | bytes 7864320 | tf_op jit(solution)/shard_map/all_gather | solution.py:154
  122.7 122.1 %all-gather.28.cloned.1.call-start = ((), (), s32[]{:S(2)}) async-start(), calls=%async_computation.21 | async-start | bytes 5242880 | tf_op jit(solution)/shard_map/all_gather | solution.py:193
  135.1 61.2 %copy-start.32 = (f32[1024,32]{0,1:T(8,128)}, f32[1024,32]{0,1:T(8,128)S(1)}, u32[]{:S(2)}) copy-start(f32[1024,32]{0,1:T(8,128)S(1)} %get-tuple-element.384) | copy-start | bytes 393220
  135.1 117.2 %copy-start.30 = (f32[1024,32]{0,1:T(8,128)}, f32[1024,32]{0,1:T(8,128)S(1)}, u32[]{:S(2)}) copy-start(f32[1024,32]{0,1:T(8,128)S(1)} %get-tuple-element.379) | copy-start | bytes 393220
  171.3 130.3 %reduce-scatter.18.cloned.1.call-start = ((), (), s32[]{:S(2)}) async-start(), calls=%async_computation.22 | async-start | bytes 5242880 | tf_op jit(solution)/shard_map/reduce_scatter | solution.py:196
  191.7 46.5 %copy-start.23 = (bf16[4,2,256,1280]{3,2,1,0:T(8,128)(2,1)}, bf16[4,2,256,1280]{3,2,1,0:T(8,128)(2,1)S(1)}, u32[]{:S(2)}) copy-start(bf16[4,2,256,1280]{3,2,1,0:T(8,128)(2,1)S(1)} %copy.157) | copy-start | bytes 15728644
  244.7 112.0 %reduce-scatter.20.cloned.1.call-start = ((), (), s32[]{:S(2)}) async-start(), calls=%async_computation.23 | async-start | bytes 5242880 | tf_op jit(solution)/shard_map/reduce_scatter | solution.py:196
  301.6 110.1 %all-gather.52.cloned.1.call-start = ((), (), s32[]{:S(2)}) async-start(), calls=%async_computation.44 | async-start | bytes 5242880 | tf_op jit(solution)/shard_map/all_gather | solution.py:153
  303.2 198.4 %all-gather.48.cloned.1.call-start = ((), (), s32[]{:S(2)}) async-start(), calls=%async_computation.42 | async-start | bytes 10485760 | tf_op jit(solution)/shard_map/all_gather | solution.py:153
  306.6 278.0 %all-gather.30.cloned.1.call-start = ((), (), s32[]{:S(2)}) async-start(), calls=%async_computation.24 | async-start | bytes 5242880 | tf_op jit(solution)/shard_map/all_gather | solution.py:199
  356.7 248.2 %all-gather.54.cloned.1.call-start = ((), (), s32[]{:S(2)}) async-start(), calls=%async_computation.45 | async-start | bytes 12582912 | tf_op jit(solution)/shard_map/all_gather | solution.py:154
  418.0 219.8 %all-gather.50.cloned.1.call-start = ((), (), s32[]{:S(2)}) async-start(), calls=%async_computation.43 | async-start | bytes 25165824 | tf_op jit(solution)/shard_map/all_gather | solution.py:154
  501.7 220.0 %all-gather.32.cloned.1.call-start = ((), (), s32[]{:S(2)}) async-start(), calls=%async_computation.25 | async-start | bytes 5242880 | tf_op jit(solution)/shard_map/all_gather | solution.py:199
  584.6 215.3 %reduce-scatter.22.cloned.1.call-start = ((), (), s32[]{:S(2)}) async-start(), calls=%async_computation.26 | async-start | bytes 5242880 | tf_op jit(solution)/shard_map/reduce_scatter | solution.py:202
  637.8 43.7 %slice-start = ((s8[8388608]{0:T(1024)(128)(4,1)}), s8[4194304]{0:T(1024)(128)(4,1)S(1)}, s32[]{:S(2)}) async-start(s8[8388608]{0:T(1024)(128)(4,1)} %bitcast.321), calls=%async_computation.50 | async-start | bytes 8388608
  721.7 158.2 %reduce-scatter.24.cloned.1.call-start = ((), (), s32[]{:S(2)}) async-start(), calls=%async_computation.27 | async-start | bytes 5242880 | tf_op jit(solution)/shard_map/reduce_scatter | solution.py:202
  763.9 36.0 %copy-start.50 = (bf16[2,1,1024,512]{3,2,1,0:T(8,128)(2,1)S(1)}, bf16[2,1,1024,512]{3,2,1,0:T(8,128)(2,1)}, u32[]{:S(2)}) copy-start(bf16[2,1,1024,512]{3,2,1,0:T(8,128)(2,1)} %param.23) | copy-start | bytes 6291460
  799.9 163.3 %all-gather.34.cloned.1.call-start = ((), (), s32[]{:S(2)}) async-start(), calls=%async_computation.28 | async-start | bytes 5242880 | tf_op jit(solution)/shard_map/all_gather | solution.py:199
  835.7 49.0 %copy-start.9 = (f32[1,256,2048]{2,1,0:T(8,128)}, f32[1,256,2048]{2,1,0:T(8,128)S(1)}, u32[]{:S(2)}) copy-start(f32[1,256,2048]{2,1,0:T(8,128)S(1)} %reshape.1136) | copy-start | bytes 6291460
  880.0 164.5 %all-gather.36.cloned.1.call-start = ((), (), s32[]{:S(2)}) async-start(), calls=%async_computation.29 | async-start | bytes 5242880 | tf_op jit(solution)/shard_map/all_gather | solution.py:199
  963.2 158.7 %reduce-scatter.26.cloned.1.call-start = ((), (), s32[]{:S(2)}) async-start(), calls=%async_computation.30 | async-start | bytes 5242880 | tf_op jit(solution)/shard_map/reduce_scatter | solution.py:202
  1044.5 157.5 %reduce-scatter.28.cloned.1.call-start = ((), (), s32[]{:S(2)}) async-start(), calls=%async_computation.31 | async-start | bytes 5242880 | tf_op jit(solution)/shard_map/reduce_scatter | solution.py:202
  1089.5 32.5 %copy-start.6 = (f32[1,256,2048]{2,1,0:T(8,128)S(1)}, f32[1,256,2048]{2,1,0:T(8,128)}, u32[]{:S(2)}) copy-start(f32[1,256,2048]{2,1,0:T(8,128)} %reshape.1134) | copy-start | bytes 6291460
  1089.5 32.5 %copy-start.13 = (bf16[1,256,2048]{2,1,0:T(8,128)(2,1)S(1)}, bf16[1,256,2048]{2,1,0:T(8,128)(2,1)}, u32[]{:S(2)}) copy-start(bf16[1,256,2048]{2,1,0:T(8,128)(2,1)} %reduce-scatter.18.cloned.1.call-done) | copy-start | bytes 3145732
  1089.5 32.5 %copy-start.62 = (f32[1,2048]{1,0:T(1,128)S(1)}, f32[1,2048]{1,0:T(1,128)}, u32[]{:S(2)}) copy-start(f32[1,2048]{1,0:T(1,128)} %copy-done.61) | copy-start | bytes 24580
  1089.6 32.5 %copy-start.84 = (f32[256]{0:T(256)S(1)}, f32[256]{0:T(256)}, u32[]{:S(2)}) copy-start(f32[256]{0:T(256)} %copy-done.83) | copy-start | bytes 3076
  1121.9 135.6 %all-gather.38.cloned.1.call-start = ((), (), s32[]{:S(2)}) async-start(), calls=%async_computation.32 | async-start | bytes 5242880 | tf_op jit(solution)/shard_map/all_gather | solution.py:193
  1125.5 76.6 %copy-start.3 = (f32[1,256,2048]{2,1,0:T(8,128)S(1)}, f32[1,256,2048]{2,1,0:T(8,128)}, u32[]{:S(2)}) copy-start(f32[1,256,2048]{2,1,0:T(8,128)} %reshape.1135) | copy-start | bytes 6291460
  1125.5 76.6 %copy-start.87 = (f32[256]{0:T(256)S(1)}, f32[256]{0:T(256)}, u32[]{:S(2)}) copy-start(f32[256]{0:T(256)} %copy-done.86) | copy-start | bytes 3076
  1128.8 76.5 %copy-start.16 = (bf16[1,256,2048]{2,1,0:T(8,128)(2,1)S(1)}, bf16[1,256,2048]{2,1,0:T(8,128)(2,1)}, u32[]{:S(2)}) copy-start(bf16[1,256,2048]{2,1,0:T(8,128)(2,1)} %reduce-scatter.20.cloned.1.call-done) | copy-start | bytes 3145732
  1202.0 152.6 %all-gather.40.cloned.1.call-start = ((), (), s32[]{:S(2)}) async-start(), calls=%async_computation.33 | async-start | bytes 5242880 | tf_op jit(solution)/shard_map/all_gather | solution.py:193
  1205.3 52.2 %copy-start.96 = (f32[256]{0:T(256)}, f32[256]{0:T(256)S(1)}, u32[]{:S(2)}) copy-start(f32[256]{0:T(256)S(1)} %broadcast_multiply_fusion.2) | copy-start | bytes 3076
  1257.6 193.8 %reduce-scatter.30.cloned.1.call-start = ((), (), s32[]{:S(2)}) async-start(), calls=%async_computation.34 | async-start | bytes 5242880 | tf_op jit(solution)/shard_map/reduce_scatter | solution.py:196
  1285.9 29.0 %copy-start.47 = (bf16[1,1024,8,32]{1,3,2,0:T(8,128)(2,1)S(1)}, bf16[1,1024,8,32]{1,3,2,0:T(8,128)(2,1)}, u32[]{:S(2)}) copy-start(bf16[1,1024,8,32]{1,3,2,0:T(8,128)(2,1)} %copy-done.46) | copy-start | bytes 1572868
  1354.6 255.2 %reduce-scatter.32.cloned.1.call-start = ((), (), s32[]{:S(2)}) async-start(), calls=%async_computation.35 | async-start | bytes 5242880 | tf_op jit(solution)/shard_map/reduce_scatter | solution.py:196
  1382.7 29.4 %copy-start.43 = (bf16[1,1024,8,32]{1,3,2,0:T(8,128)(2,1)S(1)}, bf16[1,1024,8,32]{1,3,2,0:T(8,128)(2,1)}, u32[]{:S(2)}) copy-start(bf16[1,1024,8,32]{1,3,2,0:T(8,128)(2,1)} %copy-done.42) | copy-start | bytes 1572868
  1382.7 29.3 %copy-start.45 = (bf16[1,1024,8,32]{1,3,2,0:T(8,128)(2,1)S(1)}, bf16[1,1024,8,32]{1,3,2,0:T(8,128)(2,1)}, u32[]{:S(2)}) copy-start(bf16[1,1024,8,32]{1,3,2,0:T(8,128)(2,1)} %copy-done.44) | copy-start | bytes 1572868
  1451.4 228.2 %reduce-scatter.38.cloned.1.call-start = ((), (), s32[]{:S(2)}) async-start(), calls=%async_computation.39 | async-start | bytes 25165824 | tf_op jit(solution)/shard_map/reduce_scatter | solution.py:173
  1501.2 184.3 %reduce-scatter.36.cloned.1.call-start = ((), (), s32[]{:S(2)}) async-start(), calls=%async_computation.38 | async-start | bytes 50331648 | tf_op jit(solution)/shard_map/reduce_scatter | solution.py:173
  1585.8 112.6 %reduce-scatter.34.cloned.1.call-start = ((), (), s32[]{:S(2)}) async-start(), calls=%async_computation.36 | async-start | bytes 17301504 | tf_op jit(solution)/shard_map/reduce_scatter | solution.py:182
  1679.5 77.3 %reduce-scatter.42.cloned.1.call-start = ((), (), s32[]{:S(2)}) async-start(), calls=%async_computation.49 | async-start | bytes 5242880
  1685.4 222.4 %reduce-scatter.40.cloned.1.call-start = ((), (), s32[]{:S(2)}) async-start(), calls=%async_computation.48 | async-start | bytes 10485760
  1703.0 70.4 %all-to-all-start.6 = ((bf16[4,256,1408]{2,1,0:T(8,128)(2,1)}), bf16[4,256,1408]{2,1,0:T(8,128)(2,1)}, u32[]{:S(2)}, u32[]{:S(2)}) async-start(bf16[4,256,1408]{2,1,0:T(8,128)(2,1)} %convert_bitcast_fusion.6), calls=%async_computation.15 | async-start | bytes 5767168 | tf_op jit(solution)/shard_map/all_to_all | solution.py:183
  1707.9 280.4 %all-gather.58.cloned.1.call-start = ((), (), s32[]{:S(2)}) async-start(), calls=%async_computation.47 | async-start | bytes 6291456 | tf_op jit(solution)/shard_map/all_gather | solution.py:187
  1759.5 257.2 %all-gather.42.cloned.1.call-start = ((), (), s32[]{:S(2)}) async-start(), calls=%async_computation.37 | async-start | bytes 4325376 | tf_op jit(solution)/shard_map/all_gather | solution.py:420
  1775.8 0.8 collective-permute-start.1
  1777.7 134.2 %copy-start.99 = (f32[256]{0:T(256)S(1)}, f32[256]{0:T(256)}, u32[]{:S(2)}) copy-start(f32[256]{0:T(256)} %get-tuple-element.372) | copy-start | bytes 3076
  1777.7 134.2 %copy-start.17 = (bf16[1,256,2048]{2,1,0:T(8,128)(2,1)S(1)}, bf16[1,256,2048]{2,1,0:T(8,128)(2,1)}, u32[]{:S(2)}) copy-start(bf16[1,256,2048]{2,1,0:T(8,128)(2,1)} %reduce-scatter.20.cloned.1.call-done) | copy-start | bytes 3145732
  1777.7 134.2 %copy-start.88 = (f32[256]{0:T(256)S(1)}, f32[256]{0:T(256)}, u32[]{:S(2)}) copy-start(f32[256]{0:T(256)} %copy-done.86) | copy-start | bytes 3076
  1777.7 134.2 %copy-start.93 = (f32[256]{0:T(256)S(1)}, f32[256]{0:T(256)}, u32[]{:S(2)}) copy-start(f32[256]{0:T(256)} %copy-done.91) | copy-start | bytes 3076
  1777.8 134.2 %copy-start.97 = (f32[256]{0:T(256)S(1)}, f32[256]{0:T(256)}, u32[]{:S(2)}) copy-start(f32[256]{0:T(256)} %copy-done.96) | copy-start | bytes 3076
  1777.8 246.7 %all-gather.56.cloned.1.call-start = ((), (), s32[]{:S(2)}) async-start(), calls=%async_computation.46 | async-start | bytes 12582912 | tf_op jit(solution)/shard_map/all_gather | solution.py:187
  1920.8 18.3 all-to-all-start.3
  1939.1 16.6 all-to-all-start.1
  1955.8 28.9 %all-to-all-start.5 = ((f32[1,1,1,256,4,512]{5,3,2,1,0,4:T(8,128)}), f32[1,1,1,256,4,512]{5,3,2,1,0,4:T(8,128)}, u32[]{:S(2)}, u32[]{:S(2)}) async-start(f32[1,1,1,256,4,512]{5,3,2,1,0,4:T(8,128)} %copy.177), calls=%async_computation.13 | async-start | bytes 4194304 | tf_op jit(solution)/shard_map/all_to_all | solution.py:213
  1984.7 28.0 %all-to-all-start.4 = ((f32[1,1,1,256,4,512]{5,3,2,1,0,4:T(8,128)}), f32[1,1,1,256,4,512]{5,3,2,1,0,4:T(8,128)S(1)}, u32[]{:S(2)}, u32[]{:S(2)}) async-start(f32[1,1,1,256,4,512]{5,3,2,1,0,4:T(8,128)} %copy.176), calls=%async_computation.11 | async-start | bytes 4194304 | tf_op jit(solution)/shard_map/all_to_all | solution.py:213
  (83 other events, 653.3 us)
Sparse Core Ops, SparseCore 0:
  13.4 103.2 all-gather.43
  119.1 52.1 all-gather.25
  173.4 15.1 all-gather.45
  190.9 53.7 all-gather.27
  248.1 52.5 reduce-scatter.17
  304.1 52.5 reduce-scatter.19
  359.1 52.5 all-gather.51
  414.2 87.4 all-gather.47
  503.8 80.7 all-gather.29
  586.6 18.3 all-gather.53
  606.5 31.2 all-gather.49
  639.8 81.9 all-gather.31
  724.6 75.2 reduce-scatter.21
  802.6 77.2 reduce-scatter.23
  881.9 81.2 all-gather.33
  965.2 79.2 all-gather.35
  1046.6 75.2 reduce-scatter.25
  1124.6 77.2 reduce-scatter.27
  1204.4 53.0 all-gather.37
  1259.8 52.5 all-gather.39
  1354.7 52.4 reduce-scatter.29
  1451.5 52.5 reduce-scatter.31
  1506.3 25.0 reduce-scatter.37
  1586.0 42.8 reduce-scatter.35
  1679.6 18.7 reduce-scatter.33
  1701.8 54.9 reduce-scatter.41
  1759.7 148.0 reduce-scatter.39
  1909.9 13.6 all-gather.57
  1925.2 12.8 all-gather.41
  1940.1 21.0 all-gather.55

commit v9 on v8

--- a/solution.py
+++ b/solution.py
@@ -413,7 +413,9 @@
         outs_list = [r[0] for r in results]
         inputs_grad = [r[1] for r in results]
 
-        total_pair = reduce_features(grad_pair_w, 0, "row")
+        total_pair = lax.all_gather(
+            reduce_half_exchange(grad_pair_w, "row"), "dp", axis=0, tiled=True
+        )
         total_down = reduce_features(grad_down_w, 1, "row")
         gain_rows = lax.psum(jnp.stack([gain_attn_total, gain_ffn_total], axis=1), "row")
         gain_cols = jnp.pad(gain_rows, ((0, 0), (0, 126)))

time: 2050 us -> 2120 us (1.034)
  blocking collectives: 81 us -> 268 us
  waiting for transfers between devices: 963 us -> 843 us
    unnamed x32 -> x29, waiting for transfers between devices: 179 us -> 1.15 us
    all_to_all x0 -> x1, blocking collectives: none -> 97.7 us  [reduce_half_exchange(): blocks = lax.all_to_all(split.astype(jnp.bfloat16), axis_name, 0, 0)]
    unnamed x0 -> x1, blocking collectives: none -> 88.9 us
    all_to_all x1, waiting for transfers between devices: 13.8 us -> 51.6 us  [reduce_half_exchange(): blocks = lax.all_to_all(split.astype(jnp.bfloat16), axis_name, 0, 0)]
    reshape x2 -> x1, local copies, waits for them, and re-layouts: 39.5 us -> 16.4 us  [reduce_half(): split = jnp.swapaxes(partial.reshape(shape), axis, axis + 1)]
  transfers between devices with their start and end apart: 38 -> 36, of which waited for: 24 -> 22; matrix products, arithmetic and copies ran while one was open for 42% -> 40% of each run, Pallas kernels for 0% -> 0%
where the time goes in v9:
time: 2120 us; the launch traced here: 2100 us
  waiting for transfers between devices  843 us (40%)
  matrix products  469 us (22%)
  blocking collectives  268 us (13%)
  local copies, waits for them, and re-layouts  219 us (10%)
  other arithmetic  190 us (9%)
  starting transfers between devices  89.9 us (4%)
    all_gather x4, waiting for transfers between devices, gather_seqs(): return lax.all_gather(rows, 'col', axis=0, tiled=True)  217 us
    reduce_scatter x4, waiting for transfers between devices, scatter_seqs(): return lax.psum_scatter(rows, 'col', scatter_dimension=0, tiled=True)  184 us
    all_gather x3, waiting for transfers between devices, gather_half(): gathered = lax.all_gather(mine, axis_name, axis=axis)  139 us
    all_to_all x1, blocking collectives, reduce_half_exchange(): blocks = lax.all_to_all(split.astype(jnp.bfloat16), axis_name, 0, 0)  97.7 us
    unnamed x1, blocking collectives  88.9 us
    all_gather x4, waiting for transfers between devices, gather_tokens(): return lax.all_gather(rows, 'row', axis=1, tiled=True)  86.1 us
    all_to_all x4, waiting for transfers between devices, to_features(): rows = lax.all_to_all(rows, 'row', 3, 2)  77.9 us
    dot_general x2, matrix products, micro_batch(): jnp.einsum('std,stf->df', spread_ffn, paired_gradient, preferred_element_...  59.4 us
  transfers between devices with their start and end apart: 36, of which 22 were waited for; matrix products, arithmetic and copies ran while one was open for 40% of the time, Pallas kernels for 0%

profile of v9, /device:TPU:0, one launch (start us, length us, event | category | flops | bytes accessed | tf_op | source)
XLA Modules:
  0.0 2095.7 jit_solution(12226884981690419491)
XLA Ops:
  16.3 50.9 %all-to-all-start = ((bf16[2,1,4,256,1,512]{5,3,0,4,1,2:T(8,128)(2,1)}), bf16[2,1,4,256,1,512]{5,3,0,4,1,2:T(8,128)(2,1)}, u32[]{:S(2)}, u32[]{:S(2)}) async-start(bf16[2,1,4,256,1,512]{5,3,0,4,1,2:T(8,128)(2,1)} %copy.145), calls=%async_computation | async-start | bytes 4194304 | tf_op jit(solution)/shard_map/all_to_all | solution.py:207
  67.2 27.4 %all_gather.75 = f32[2,2048]{1,0:T(2,128)S(1)} all-gather(f32[2,512]{1,0:T(2,128)S(1)} %pad_maximum_fusion.29), channel_id=1, replica_groups=mesh['dp'=2,'row'=4,'col'=4] {'row'}, dimensions={1}, use_global_device_ids=true | all-gather | bytes 20480 | tf_op jit(solution)/shard_map/all_gather | solution.py:252
  122.7 9.3 all_gather.78
  136.7 34.6 %all-gather.25.cloned.1.call-done = bf16[1,1024,2048]{2,1,0:T(8,128)(2,1)} async-done(((bf16[1,256,2048]{2,1,0:T(8,128)(2,1)}), bf16[1,1024,2048]{2,1,0:T(8,128)(2,1)}) %all-gather.25.cloned.1.call-update) | async-done | bytes 4194320 | tf_op jit(solution)/shard_map/all_gather | solution.py:193
  171.6 17.1 all-gather.47.cloned.1.call-done
  197.5 13.7 fusion.132
  211.3 13.4 exponential_reduce_fusion.1
  224.7 13.4 fusion.79
  252.8 14.2 fusion.133
  267.0 13.5 exponential_reduce_fusion
  280.5 14.1 fusion.82
  309.2 47.6 %reduce-scatter.19.cloned.1.call-done = bf16[1,256,2048]{2,1,0:T(8,128)(2,1)} async-done(((bf16[1,1024,2048]{2,1,0:T(8,128)(2,1)}), bf16[1,256,2048]{2,1,0:T(8,128)(2,1)}) %reduce-scatter.19.cloned.1.call-update) | async-done | bytes 1048592 | tf_op jit(solution)/shard_map/reduce_scatter | solution.py:196
  356.8 55.0 %all-gather.53.cloned.1.call-done = bf16[2048,1024]{0,1:T(8,128)(2,1)} async-done(((bf16[2048,256]{0,1:T(8,128)(2,1)}), bf16[2048,1024]{0,1:T(8,128)(2,1)}) %all-gather.53.cloned.1.call-update) | async-done | bytes 4194320 | tf_op jit(solution)/shard_map/all_gather | solution.py:153
  418.0 83.7 %all-gather.49.cloned.1.call-done = bf16[1024,4096]{1,0:T(8,128)(2,1)} async-done(((bf16[256,4096]{1,0:T(8,128)(2,1)}), bf16[1024,4096]{1,0:T(8,128)(2,1)}) %all-gather.49.cloned.1.call-update) | async-done | bytes 8388624 | tf_op jit(solution)/shard_map/all_gather | solution.py:153
  506.0 78.6 %all-gather.29.cloned.1.call-done = bf16[4,256,2048]{2,1,0:T(8,128)(2,1)} async-done(((bf16[1,256,2048]{2,1,0:T(8,128)(2,1)}), bf16[4,256,2048]{2,1,0:T(8,128)(2,1)}) %all-gather.29.cloned.1.call-update) | async-done | bytes 4194320 | tf_op jit(solution)/shard_map/all_gather | solution.py:199
  584.7 20.3 all-gather.55.cloned.1.call-done
  605.0 16.4 copy.160
  621.4 15.2 reshape.1149
  637.8 15.5 copy.157
  653.3 20.4 fusion.134
  681.5 10.4 convolution_convert_fusion.1
  691.9 29.8 %all-gather.31.cloned.1.call-done = bf16[4,256,2048]{2,1,0:T(8,128)(2,1)} async-done(((bf16[1,256,2048]{2,1,0:T(8,128)(2,1)}), bf16[4,256,2048]{2,1,0:T(8,128)(2,1)}) %all-gather.31.cloned.1.call-update) | async-done | bytes 4194320 | tf_op jit(solution)/shard_map/all_gather | solution.py:199
  722.0 21.5 %fusion.135 = f32[4,256,4096]{2,1,0:T(8,128)S(1)} fusion(bf16[4,256,2048]{2,1,0:T(8,128)(2,1)} %all-gather.31.cloned.1.call-done, bf16[2048,4096,1]{1,0,2:T(8,128)(2,1)} %bitcast.315), kind=kOutput, calls=%fused_computation.251 | convolution fusion | flops 17179869184 | bytes 37748736 | tf_op jit(solution)/shard_map/std,df->stf/dot_general | solution.py:307
  751.4 12.5 convolution_convert_fusion
  764.0 35.9 %reduce-scatter.21.cloned.1.call-done = bf16[1,256,2048]{2,1,0:T(8,128)(2,1)} async-done(((bf16[4,256,2048]{2,1,0:T(8,128)(2,1)}), bf16[1,256,2048]{2,1,0:T(8,128)(2,1)}) %reduce-scatter.21.cloned.1.call-update) | async-done | bytes 1048592 | tf_op jit(solution)/shard_map/reduce_scatter | solution.py:202
  800.2 28.5 %all_to_all.100 = bf16[2,1,4,256,1,512]{5,3,0,4,1,2:T(8,128)(2,1)S(1)} all-to-all(bf16[2,1,4,256,1,512]{5,3,0,4,1,2:T(8,128)(2,1)S(1)} %copy.162), channel_id=1, replica_groups=mesh['dp'=2,'row'=4,'col'=4] {'row'}, dimensions={2} | all-to-all | bytes 4194304 | tf_op jit(solution)/shard_map/all_to_all | solution.py:207
  837.1 42.9 %reduce-scatter.23.cloned.1.call-done = bf16[1,256,2048]{2,1,0:T(8,128)(2,1)} async-done(((bf16[4,256,2048]{2,1,0:T(8,128)(2,1)}), bf16[1,256,2048]{2,1,0:T(8,128)(2,1)}) %reduce-scatter.23.cloned.1.call-update) | async-done | bytes 1048592 | tf_op jit(solution)/shard_map/reduce_scatter | solution.py:202
  891.4 71.9 %all-gather.33.cloned.1.call-done = bf16[4,256,2048]{2,1,0:T(8,128)(2,1)} async-done(((bf16[1,256,2048]{2,1,0:T(8,128)(2,1)}), bf16[4,256,2048]{2,1,0:T(8,128)(2,1)}) %all-gather.33.cloned.1.call-update) | async-done | bytes 4194320 | tf_op jit(solution)/shard_map/all_gather | solution.py:199
  963.3 20.4 multiply_convert_fusion.3
  983.7 23.9 %fusion.38 = bf16[4,256,2048]{2,1,0:T(8,128)(2,1)} fusion(bf16[2048,4096,1]{1,0,2:T(8,128)(2,1)} %bitcast.316, bf16[4,256,2048]{2,1,0:T(8,128)(2,1)} %get-tuple-element.337, bf16[4,256,2048]{2,1,0:T(8,128)(2,1)} %get-tuple-element.336), kind=kOutput, calls=%fused_computation.71 | convolution fusion | flops 17198743552 | bytes 29360128 | tf_op jit(solution)/shard_map/stf,df->std/dot_general | solution.py:341
  1007.6 36.9 %all-gather.35.cloned.1.call-done = bf16[4,256,2048]{2,1,0:T(8,128)(2,1)} async-done(((bf16[1,256,2048]{2,1,0:T(8,128)(2,1)}), bf16[4,256,2048]{2,1,0:T(8,128)(2,1)}) %all-gather.35.cloned.1.call-update) | async-done | bytes 4194320 | tf_op jit(solution)/shard_map/all_gather | solution.py:199
  1044.8 21.0 %multiply_convert_fusion.1 = (bf16[4,256,2048]{2,1,0:T(8,128)(2,1)}, bf16[4,256,2048]{2,1,0:T(8,128)(2,1)}) fusion(f32[4,256,4096]{2,1,0:T(8,128)} %copy-done.18, bf16[4,256,2048]{2,1,0:T(8,128)(2,1)} %all-gather.35.cloned.1.call-done, bf16[2048,2048,1]{1,0,2:T(8,128)(2,1)} %reshape.1149), kind=kOutput, calls=%fused_computation.29 | convolution fusion | flops 8617197568 | bytes 37748736 | tf_op jit(solution)/shard_map/std,fd->stf/dot_general | solution.py:328
  1065.8 23.8 %fusion.39 = bf16[4,256,2048]{2,1,0:T(8,128)(2,1)} fusion(bf16[2048,4096,1]{1,0,2:T(8,128)(2,1)} %bitcast.317, bf16[4,256,2048]{2,1,0:T(8,128)(2,1)} %get-tuple-element.335, bf16[4,256,2048]{2,1,0:T(8,128)(2,1)} %get-tuple-element.334), kind=kOutput, calls=%fused_computation.72 | convolution fusion | flops 17198743552 | bytes 29360128 | tf_op jit(solution)/shard_map/stf,df->std/dot_general | solution.py:341
  1089.6 32.4 %reduce-scatter.25.cloned.1.call-done = bf16[1,256,2048]{2,1,0:T(8,128)(2,1)} async-done(((bf16[4,256,2048]{2,1,0:T(8,128)(2,1)}), bf16[1,256,2048]{2,1,0:T(8,128)(2,1)}) %reduce-scatter.25.cloned.1.call-update) | async-done | bytes 1048592 | tf_op jit(solution)/shard_map/reduce_scatter | solution.py:202
  1128.9 73.1 %reduce-scatter.27.cloned.1.call-done = bf16[1,256,2048]{2,1,0:T(8,128)(2,1)} async-done(((bf16[4,256,2048]{2,1,0:T(8,128)(2,1)}), bf16[1,256,2048]{2,1,0:T(8,128)(2,1)}) %reduce-scatter.27.cloned.1.call-update) | async-done | bytes 1048592 | tf_op jit(solution)/shard_map/reduce_scatter | solution.py:202
  1207.3 50.3 %all-gather.37.cloned.1.call-done = bf16[1,1024,2048]{2,1,0:T(8,128)(2,1)} async-done(((bf16[1,256,2048]{2,1,0:T(8,128)(2,1)}), bf16[1,1024,2048]{2,1,0:T(8,128)(2,1)}) %all-gather.37.cloned.1.call-update) | async-done | bytes 4194320 | tf_op jit(solution)/shard_map/all_gather | solution.py:193
  1262.9 23.0 %fusion.3 = (f32[2,4,1024]{2,1,0:T(4,128)S(1)}, f32[2,1024,1024,4]{2,1,3,0:T(8,128)}) fusion(f32[2,4,1024,1024]{2,3,1,0:T(8,128)} %get-tuple-element.388, f32[2,4,1024]{2,1,0:T(4,128)S(1)} %bitcast.356, bf16[1024,2,64,1]{0,2,3,1:T(8,128)(2,1)S(1)} %bitcast.350, bf16[1024,2,4,64]{0,3,2,1:T(8,128)(2,1)S(1)} %bitcast.340), kind=kOutput, calls=%fused_computation.8 | convolution fusion | flops 1098899456 | bytes 68485120 | tf_op jit(solution)/shard_map/while/body/eval_jaxpr/qkgd,pkd->kgqp/dot_general | solution.py:85
  1285.9 29.0 %fusion.5 = bf16[2,4,1024,1024]{2,3,1,0:T(8,128)(2,1)} fusion(f32[2,1024,1024,4]{2,1,3,0:T(8,128)} %get-tuple-element.392, f32[2,4,1024,1024]{2,3,1,0:T(8,128)} %get-tuple-element.388, f32[2,4,1024]{2,1,0:T(4,128)S(1)} %get-tuple-element.391, f32[2,4,1024]{2,1,0:T(4,128)S(1)} %bitcast.357), kind=kLoop, calls=%fused_computation.10 | loop fusion | flops 33554432 | bytes 83951616 | tf_op jit(solution)/shard_map/while/body/eval_jaxpr/convert_element_type | solution.py:96
  1314.9 8.7 fusion.98
  1323.7 13.3 fusion.99
  1337.9 8.9 convolution_multiply_fusion.1
  1360.0 22.8 %fusion = (f32[2,4,1024]{2,1,0:T(4,128)S(1)}, f32[2,1024,1024,4]{2,1,3,0:T(8,128)}) fusion(f32[2,4,1024,1024]{2,3,1,0:T(8,128)} %get-tuple-element.390, f32[2,4,1024]{2,1,0:T(4,128)S(1)} %bitcast.352, bf16[1024,2,64,1]{0,2,3,1:T(8,128)(2,1)S(1)} %bitcast.348, bf16[1024,2,4,64]{0,3,2,1:T(8,128)(2,1)S(1)} %bitcast.342), kind=kOutput, calls=%fused_computation.3 | convolution fusion | flops 1098899456 | bytes 68485120 | tf_op jit(solution)/shard_map/while/body/eval_jaxpr/qkgd,pkd->kgqp/dot_general | solution.py:85
  1382.8 29.3 %fusion.2 = bf16[2,4,1024,1024]{2,3,1,0:T(8,128)(2,1)} fusion(f32[2,1024,1024,4]{2,1,3,0:T(8,128)} %get-tuple-element.394, f32[2,4,1024,1024]{2,3,1,0:T(8,128)} %get-tuple-element.390, f32[2,4,1024]{2,1,0:T(4,128)S(1)} %get-tuple-element.393, f32[2,4,1024]{2,1,0:T(4,128)S(1)} %bitcast.353), kind=kLoop, calls=%fused_computation.5 | loop fusion | flops 33554432 | bytes 83951616 | tf_op jit(solution)/shard_map/while/body/eval_jaxpr/convert_element_type | solution.py:96
  1412.2 8.7 fusion.97
  1420.9 13.3 fusion.102
  1435.2 8.9 convolution_multiply_fusion
  1451.5 15.7 fusion.136
  1467.2 17.6 bitcast_add_fusion.1
  1484.7 16.4 copy.179
  1533.5 15.9 psum.7
  1549.4 10.0 select_maximum_fusion
  1559.4 15.7 reshape.1129
  1575.2 17.8 copy.174
  1594.2 26.7 %fusion.10 = f32[2048,4096,1]{1,0,2:T(8,128)} fusion(bf16[4,256,2048]{2,1,0:T(8,128)(2,1)} %all-gather.29.cloned.1.call-done, bf16[4,256,2048]{2,1,0:T(8,128)(2,1)} %get-tuple-element.337, bf16[4,256,2048]{2,1,0:T(8,128)(2,1)} %get-tuple-element.336), kind=kOutput, calls=%fused_computation.38 | convolution fusion | flops 17196646400 | bytes 46137344 | tf_op jit(solution)/shard_map/std,stf->df/dot_general | solution.py:338
  1620.9 32.7 %bitcast_add_fusion = f32[2048,4096]{1,0:T(8,128)} fusion(f32[2048,4096,1]{1,0,2:T(8,128)} %fusion.10, bf16[4,256,2048]{2,1,0:T(8,128)(2,1)} %all-gather.31.cloned.1.call-done, bf16[4,256,2048]{2,1,0:T(8,128)(2,1)} %get-tuple-element.335, bf16[4,256,2048]{2,1,0:T(8,128)(2,1)} %get-tuple-element.334), kind=kOutput, calls=%fused_computation | convolution fusion | flops 17205035008 | bytes 79691776 | tf_op jit(solution)/shard_map/std,stf->df/dot_general | solution.py:338
  1659.5 88.9 %all-reduce.5 = bf16[2,4,256,4096]{3,2,0,1:T(8,128)(2,1)} all-reduce(f32[2,4,256,4096]{3,2,0,1:T(8,128)} %bitcast.311), channel_id=18, replica_groups=mesh['dp'=2,'row'=4,'col'=4] {'dp'}, use_global_device_ids=true, to_apply=%region_31.32.clone | all-reduce | flops 8388608 | bytes 50331648
  1748.4 8.5 fusion.8
  1756.9 97.7 %all_to_all.101 = bf16[4,256,4096]{2,1,0:T(8,128)(2,1)S(1)} all-to-all(bf16[4,256,4096]{2,1,0:T(8,128)(2,1)} %fusion.8), channel_id=1, replica_groups=mesh['dp'=2,'row'=4,'col'=4] {'row'}, dimensions={0} | all-to-all | bytes 16777216 | tf_op jit(solution)/shard_map/all_to_all | solution.py:183
  1880.6 51.6 %all-to-all-done.6 = bf16[4,256,1408]{2,1,0:T(8,128)(2,1)} async-done(((bf16[4,256,1408]{2,1,0:T(8,128)(2,1)}), bf16[4,256,1408]{2,1,0:T(8,128)(2,1)}, u32[]{:S(2)}, u32[]{:S(2)}) %all-to-all-start.6) | async-done | bytes 2883616 | tf_op jit(solution)/shard_map/all_to_all | solution.py:183
  1939.9 12.5 collective-permute-start.1
  1956.4 24.5 %all-to-all-done.3 = bf16[1,1,1,256,4,512]{5,3,2,1,0,4:T(8,128)(2,1)} async-done(((bf16[1,1,1,256,4,512]{5,3,2,1,0,4:T(8,128)(2,1)}), bf16[1,1,1,256,4,512]{5,3,2,1,0,4:T(8,128)(2,1)}, u32[]{:S(2)}, u32[]{:S(2)}) %all-to-all-start.3) | async-done | bytes 1048608 | tf_op jit(solution)/shard_map/all_to_all | solution.py:213
  1991.8 29.1 %all-to-all-done.1 = bf16[1,1,1,256,4,512]{5,3,2,1,0,4:T(8,128)(2,1)S(1)} async-done(((bf16[1,1,1,256,4,512]{5,3,2,1,0,4:T(8,128)(2,1)}), bf16[1,1,1,256,4,512]{5,3,2,1,0,4:T(8,128)(2,1)S(1)}, u32[]{:S(2)}, u32[]{:S(2)}) %all-to-all-start.1) | async-done | bytes 1048608 | tf_op jit(solution)/shard_map/all_to_all | solution.py:213
  2032.1 17.6 all-to-all-done.5
  2054.6 8.0 fusion.129
  (419 shorter events, 297.1 us)
Async XLA Ops:
  7.2 294.5 %copy-start = (bf16[2048,512]{1,0:T(8,128)(2,1)S(1)}, bf16[2048,512]{1,0:T(8,128)(2,1)}, u32[]{:S(2)}) copy-start(bf16[2048,512]{1,0:T(8,128)(2,1)} %param.20) | copy-start | bytes 6291460
  7.2 111.1 %all-gather.45.cloned.1.call-start = ((), (), s32[]{:S(2)}) async-start(), calls=%async_computation.39 | async-start | bytes 3276800 | tf_op jit(solution)/shard_map/all_gather | solution.py:153
  11.7 0.7 collective-permute-start
  13.3 54.0 %copy-start.96 = (f32[512]{0:T(512)S(1)}, f32[512]{0:T(512)}, u32[]{:S(2)}) copy-start(f32[512]{0:T(512)} %param.22) | copy-start | bytes 6148
  13.3 53.9 %copy-start.97 = (f32[512]{0:T(512)S(1)}, f32[512]{0:T(512)}, u32[]{:S(2)}) copy-start(f32[512]{0:T(512)} %param.21) | copy-start | bytes 6148
  16.3 78.3 %all-to-all-start = ((bf16[2,1,4,256,1,512]{5,3,0,4,1,2:T(8,128)(2,1)}), bf16[2,1,4,256,1,512]{5,3,0,4,1,2:T(8,128)(2,1)}, u32[]{:S(2)}, u32[]{:S(2)}) async-start(bf16[2,1,4,256,1,512]{5,3,0,4,1,2:T(8,128)(2,1)} %copy.145), calls=%async_computation | async-start | bytes 4194304 | tf_op jit(solution)/shard_map/all_to_all | solution.py:207
  67.2 104.1 %all-gather.25.cloned.1.call-start = ((), (), s32[]{:S(2)}) async-start(), calls=%async_computation.19 | async-start | bytes 5242880 | tf_op jit(solution)/shard_map/all_gather | solution.py:193
  94.6 409.4 %copy-start.59 = (f32[1,2048]{1,0:T(1,128)}, f32[1,2048]{1,0:T(1,128)S(1)}, u32[]{:S(2)}) copy-start(f32[1,2048]{1,0:T(1,128)S(1)} %get-tuple-element.370) | copy-start | bytes 24580
  118.2 70.5 %all-gather.47.cloned.1.call-start = ((), (), s32[]{:S(2)}) async-start(), calls=%async_computation.40 | async-start | bytes 7864320 | tf_op jit(solution)/shard_map/all_gather | solution.py:154
  122.7 122.1 %all-gather.27.cloned.1.call-start = ((), (), s32[]{:S(2)}) async-start(), calls=%async_computation.20 | async-start | bytes 5242880 | tf_op jit(solution)/shard_map/all_gather | solution.py:193
  135.1 61.3 %copy-start.31 = (f32[1024,32]{0,1:T(8,128)}, f32[1024,32]{0,1:T(8,128)S(1)}, u32[]{:S(2)}) copy-start(f32[1024,32]{0,1:T(8,128)S(1)} %get-tuple-element.384) | copy-start | bytes 393220
  135.1 117.2 %copy-start.29 = (f32[1024,32]{0,1:T(8,128)}, f32[1024,32]{0,1:T(8,128)S(1)}, u32[]{:S(2)}) copy-start(f32[1024,32]{0,1:T(8,128)S(1)} %get-tuple-element.379) | copy-start | bytes 393220
  171.3 130.2 %reduce-scatter.17.cloned.1.call-start = ((), (), s32[]{:S(2)}) async-start(), calls=%async_computation.21 | async-start | bytes 5242880 | tf_op jit(solution)/shard_map/reduce_scatter | solution.py:196
  191.7 46.5 %copy-start.23 = (bf16[4,2,256,1280]{3,2,1,0:T(8,128)(2,1)}, bf16[4,2,256,1280]{3,2,1,0:T(8,128)(2,1)S(1)}, u32[]{:S(2)}) copy-start(bf16[4,2,256,1280]{3,2,1,0:T(8,128)(2,1)S(1)} %copy.153) | copy-start | bytes 15728644
  196.1 28.6 %copy-start.35 = (bf16[1,1024,128]{1,2,0:T(8,128)(2,1)}, bf16[1,1024,128]{1,2,0:T(8,128)(2,1)S(1)}, u32[]{:S(2)}) copy-start(bf16[1,1024,128]{1,2,0:T(8,128)(2,1)S(1)} %slice.365) | copy-start | bytes 786436
  244.8 112.0 %reduce-scatter.19.cloned.1.call-start = ((), (), s32[]{:S(2)}) async-start(), calls=%async_computation.22 | async-start | bytes 5242880 | tf_op jit(solution)/shard_map/reduce_scatter | solution.py:196
  252.1 28.4 %copy-start.33 = (bf16[1,1024,128]{1,2,0:T(8,128)(2,1)}, bf16[1,1024,128]{1,2,0:T(8,128)(2,1)S(1)}, u32[]{:S(2)}) copy-start(bf16[1,1024,128]{1,2,0:T(8,128)(2,1)S(1)} %slice.364) | copy-start | bytes 786436
  301.6 110.2 %all-gather.53.cloned.1.call-start = ((), (), s32[]{:S(2)}) async-start(), calls=%async_computation.43 | async-start | bytes 5242880 | tf_op jit(solution)/shard_map/all_gather | solution.py:153
  303.2 198.5 %all-gather.49.cloned.1.call-start = ((), (), s32[]{:S(2)}) async-start(), calls=%async_computation.41 | async-start | bytes 10485760 | tf_op jit(solution)/shard_map/all_gather | solution.py:153
  306.5 278.1 %all-gather.29.cloned.1.call-start = ((), (), s32[]{:S(2)}) async-start(), calls=%async_computation.23 | async-start | bytes 5242880 | tf_op jit(solution)/shard_map/all_gather | solution.py:199
  356.8 248.2 %all-gather.55.cloned.1.call-start = ((), (), s32[]{:S(2)}) async-start(), calls=%async_computation.44 | async-start | bytes 12582912 | tf_op jit(solution)/shard_map/all_gather | solution.py:154
  418.0 219.8 %all-gather.51.cloned.1.call-start = ((), (), s32[]{:S(2)}) async-start(), calls=%async_computation.42 | async-start | bytes 25165824 | tf_op jit(solution)/shard_map/all_gather | solution.py:154
  501.7 220.0 %all-gather.31.cloned.1.call-start = ((), (), s32[]{:S(2)}) async-start(), calls=%async_computation.24 | async-start | bytes 5242880 | tf_op jit(solution)/shard_map/all_gather | solution.py:199
  584.7 215.3 %reduce-scatter.21.cloned.1.call-start = ((), (), s32[]{:S(2)}) async-start(), calls=%async_computation.25 | async-start | bytes 5242880 | tf_op jit(solution)/shard_map/reduce_scatter | solution.py:202
  637.8 43.7 %slice-start = ((s8[8388608]{0:T(1024)(128)(4,1)}), s8[4194304]{0:T(1024)(128)(4,1)S(1)}, s32[]{:S(2)}) async-start(s8[8388608]{0:T(1024)(128)(4,1)} %bitcast.324), calls=%async_computation.47 | async-start | bytes 8388608
  653.3 28.2 %slice-start.1 = ((s8[8388608]{0:T(1024)(128)(4,1)}), s8[4194304]{0:T(1024)(128)(4,1)S(1)}, s32[]{:S(2)}) async-start(s8[8388608]{0:T(1024)(128)(4,1)} %bitcast.324), calls=%async_computation.48 | async-start | bytes 8388608
  721.8 158.2 %reduce-scatter.23.cloned.1.call-start = ((), (), s32[]{:S(2)}) async-start(), calls=%async_computation.26 | async-start | bytes 5242880 | tf_op jit(solution)/shard_map/reduce_scatter | solution.py:202
  764.0 36.0 %copy-start.49 = (bf16[2,1,1024,512]{3,2,1,0:T(8,128)(2,1)S(1)}, bf16[2,1,1024,512]{3,2,1,0:T(8,128)(2,1)}, u32[]{:S(2)}) copy-start(bf16[2,1,1024,512]{3,2,1,0:T(8,128)(2,1)} %param.23) | copy-start | bytes 6291460
  800.0 163.3 %all-gather.33.cloned.1.call-start = ((), (), s32[]{:S(2)}) async-start(), calls=%async_computation.27 | async-start | bytes 5242880 | tf_op jit(solution)/shard_map/all_gather | solution.py:199
  835.8 49.0 %copy-start.9 = (f32[1,256,2048]{2,1,0:T(8,128)}, f32[1,256,2048]{2,1,0:T(8,128)S(1)}, u32[]{:S(2)}) copy-start(f32[1,256,2048]{2,1,0:T(8,128)S(1)} %reshape.1134) | copy-start | bytes 6291460
  880.0 164.5 %all-gather.35.cloned.1.call-start = ((), (), s32[]{:S(2)}) async-start(), calls=%async_computation.28 | async-start | bytes 5242880 | tf_op jit(solution)/shard_map/all_gather | solution.py:199
  963.3 158.7 %reduce-scatter.25.cloned.1.call-start = ((), (), s32[]{:S(2)}) async-start(), calls=%async_computation.29 | async-start | bytes 5242880 | tf_op jit(solution)/shard_map/reduce_scatter | solution.py:202
  1044.5 157.5 %reduce-scatter.27.cloned.1.call-start = ((), (), s32[]{:S(2)}) async-start(), calls=%async_computation.30 | async-start | bytes 5242880 | tf_op jit(solution)/shard_map/reduce_scatter | solution.py:202
  1089.6 32.5 %copy-start.6 = (f32[1,256,2048]{2,1,0:T(8,128)S(1)}, f32[1,256,2048]{2,1,0:T(8,128)}, u32[]{:S(2)}) copy-start(f32[1,256,2048]{2,1,0:T(8,128)} %reshape.1132) | copy-start | bytes 6291460
  1089.6 32.5 %copy-start.13 = (bf16[1,256,2048]{2,1,0:T(8,128)(2,1)S(1)}, bf16[1,256,2048]{2,1,0:T(8,128)(2,1)}, u32[]{:S(2)}) copy-start(bf16[1,256,2048]{2,1,0:T(8,128)(2,1)} %reduce-scatter.17.cloned.1.call-done) | copy-start | bytes 3145732
  1089.6 32.5 %copy-start.60 = (f32[1,2048]{1,0:T(1,128)S(1)}, f32[1,2048]{1,0:T(1,128)}, u32[]{:S(2)}) copy-start(f32[1,2048]{1,0:T(1,128)} %copy-done.59) | copy-start | bytes 24580
  1089.6 32.5 %copy-start.82 = (f32[256]{0:T(256)S(1)}, f32[256]{0:T(256)}, u32[]{:S(2)}) copy-start(f32[256]{0:T(256)} %copy-done.81) | copy-start | bytes 3076
  1122.0 135.6 %all-gather.37.cloned.1.call-start = ((), (), s32[]{:S(2)}) async-start(), calls=%async_computation.31 | async-start | bytes 5242880 | tf_op jit(solution)/shard_map/all_gather | solution.py:193
  1125.6 76.5 %copy-start.3 = (f32[1,256,2048]{2,1,0:T(8,128)S(1)}, f32[1,256,2048]{2,1,0:T(8,128)}, u32[]{:S(2)}) copy-start(f32[1,256,2048]{2,1,0:T(8,128)} %reshape.1133) | copy-start | bytes 6291460
  1125.6 76.5 %copy-start.85 = (f32[256]{0:T(256)S(1)}, f32[256]{0:T(256)}, u32[]{:S(2)}) copy-start(f32[256]{0:T(256)} %copy-done.84) | copy-start | bytes 3076
  1128.9 76.5 %copy-start.16 = (bf16[1,256,2048]{2,1,0:T(8,128)(2,1)S(1)}, bf16[1,256,2048]{2,1,0:T(8,128)(2,1)}, u32[]{:S(2)}) copy-start(bf16[1,256,2048]{2,1,0:T(8,128)(2,1)} %reduce-scatter.19.cloned.1.call-done) | copy-start | bytes 3145732
  1202.1 152.6 %all-gather.39.cloned.1.call-start = ((), (), s32[]{:S(2)}) async-start(), calls=%async_computation.32 | async-start | bytes 5242880 | tf_op jit(solution)/shard_map/all_gather | solution.py:193
  1205.4 52.2 %copy-start.93 = (f32[256]{0:T(256)}, f32[256]{0:T(256)S(1)}, u32[]{:S(2)}) copy-start(f32[256]{0:T(256)S(1)} %broadcast_multiply_fusion.2) | copy-start | bytes 3076
  1257.6 193.8 %reduce-scatter.29.cloned.1.call-start = ((), (), s32[]{:S(2)}) async-start(), calls=%async_computation.33 | async-start | bytes 5242880 | tf_op jit(solution)/shard_map/reduce_scatter | solution.py:196
  1285.9 29.0 %copy-start.46 = (bf16[1,1024,8,32]{1,3,2,0:T(8,128)(2,1)S(1)}, bf16[1,1024,8,32]{1,3,2,0:T(8,128)(2,1)}, u32[]{:S(2)}) copy-start(bf16[1,1024,8,32]{1,3,2,0:T(8,128)(2,1)} %copy-done.45) | copy-start | bytes 1572868
  1285.9 29.0 %copy-start.48 = (bf16[1,1024,8,32]{1,3,2,0:T(8,128)(2,1)S(1)}, bf16[1,1024,8,32]{1,3,2,0:T(8,128)(2,1)}, u32[]{:S(2)}) copy-start(bf16[1,1024,8,32]{1,3,2,0:T(8,128)(2,1)} %copy-done.47) | copy-start | bytes 1572868
  1354.7 170.1 %reduce-scatter.31.cloned.1.call-start = ((), (), s32[]{:S(2)}) async-start(), calls=%async_computation.34 | async-start | bytes 5242880 | tf_op jit(solution)/shard_map/reduce_scatter | solution.py:196
  1382.8 29.4 %copy-start.42 = (bf16[1,1024,8,32]{1,3,2,0:T(8,128)(2,1)S(1)}, bf16[1,1024,8,32]{1,3,2,0:T(8,128)(2,1)}, u32[]{:S(2)}) copy-start(bf16[1,1024,8,32]{1,3,2,0:T(8,128)(2,1)} %copy-done.41) | copy-start | bytes 1572868
  1382.8 29.3 %copy-start.44 = (bf16[1,1024,8,32]{1,3,2,0:T(8,128)(2,1)S(1)}, bf16[1,1024,8,32]{1,3,2,0:T(8,128)(2,1)}, u32[]{:S(2)}) copy-start(bf16[1,1024,8,32]{1,3,2,0:T(8,128)(2,1)} %copy-done.43) | copy-start | bytes 1572868
  1451.5 202.2 %reduce-scatter.35.cloned.1.call-start = ((), (), s32[]{:S(2)}) async-start(), calls=%async_computation.38 | async-start | bytes 25165824 | tf_op jit(solution)/shard_map/reduce_scatter | solution.py:173
  1501.1 357.1 %reduce-scatter.33.cloned.1.call-start = ((), (), s32[]{:S(2)}) async-start(), calls=%async_computation.35 | async-start | bytes 17301504 | tf_op jit(solution)/shard_map/reduce_scatter | solution.py:182
  1593.0 274.8 %reduce-scatter.37.cloned.1.call-start = ((), (), s32[]{:S(2)}) async-start(), calls=%async_computation.46 | async-start | bytes 5242880
  1659.4 395.1 %all-gather.43.cloned.1.call-start = ((), (), s32[]{:S(2)}) async-start(), calls=%async_computation.37 | async-start | bytes 12582912 | tf_op jit(solution)/shard_map/all_gather | solution.py:416
  1862.8 69.4 %all-to-all-start.6 = ((bf16[4,256,1408]{2,1,0:T(8,128)(2,1)}), bf16[4,256,1408]{2,1,0:T(8,128)(2,1)}, u32[]{:S(2)}, u32[]{:S(2)}) async-start(bf16[4,256,1408]{2,1,0:T(8,128)(2,1)} %convert_bitcast_fusion.5), calls=%async_computation.15 | async-start | bytes 5767168 | tf_op jit(solution)/shard_map/all_to_all | solution.py:183
  1867.7 194.8 %all-gather.57.cloned.1.call-start = ((), (), s32[]{:S(2)}) async-start(), calls=%async_computation.45 | async-start | bytes 6291456 | tf_op jit(solution)/shard_map/all_gather | solution.py:187
  1879.4 73.1 %copy-start.27 = (bf16[1,256,2048]{2,1,0:T(8,128)(2,1)S(1)}, bf16[1,256,2048]{2,1,0:T(8,128)(2,1)}, u32[]{:S(2)}) copy-start(bf16[1,256,2048]{2,1,0:T(8,128)(2,1)} %get-tuple-element.341) | copy-start | bytes 3145732
  1932.2 48.8 %all-to-all-start.3 = ((bf16[1,1,1,256,4,512]{5,3,2,1,0,4:T(8,128)(2,1)}), bf16[1,1,1,256,4,512]{5,3,2,1,0,4:T(8,128)(2,1)}, u32[]{:S(2)}, u32[]{:S(2)}) async-start(bf16[1,1,1,256,4,512]{5,3,2,1,0,4:T(8,128)(2,1)} %copy.164), calls=%async_computation.7 | async-start | bytes 2097152 | tf_op jit(solution)/shard_map/all_to_all | solution.py:213
  1939.9 45.7 %copy-start.22 = (f32[1,256,2048]{2,1,0:T(8,128)S(1)}, f32[1,256,2048]{2,1,0:T(8,128)}, u32[]{:S(2)}) copy-start(f32[1,256,2048]{2,1,0:T(8,128)} %get-tuple-element.342) | copy-start | bytes 6291460
  1939.9 85.4 %collective-permute-start.1 = (f32[256,1408]{1,0:T(8,128)}, f32[256,1408]{1,0:T(8,128)}, u32[]{:S(2)}, u32[]{:S(2)}) collective-permute-start(f32[256,1408]{1,0:T(8,128)} %convert_reduce_fusion.1), channel_id=1, source_target_pairs={{0,0},{1,4},{2,8},{3,12},{4,1},{5,5},{6,9},{7,13},{8,2},{9,6},{10,... | collective-permute-start | bytes 4325384 | tf_op jit(solution)/shard_map/ppermute | solution.py:190
  1981.0 39.8 %all-to-all-start.1 = ((bf16[1,1,1,256,4,512]{5,3,2,1,0,4:T(8,128)(2,1)}), bf16[1,1,1,256,4,512]{5,3,2,1,0,4:T(8,128)(2,1)S(1)}, u32[]{:S(2)}, u32[]{:S(2)}) async-start(bf16[1,1,1,256,4,512]{5,3,2,1,0,4:T(8,128)(2,1)} %copy.161), calls=%async_computation.4 | async-start | bytes 2097152 | tf_op jit(solution)/shard_map/all_to_all | solution.py:213
  1988.0 38.0 %copy-start.21 = (f32[1,256,2048]{2,1,0:T(8,128)S(1)}, f32[1,256,2048]{2,1,0:T(8,128)}, u32[]{:S(2)}) copy-start(f32[1,256,2048]{2,1,0:T(8,128)} %get-tuple-element.340) | copy-start | bytes 6291460
  2020.8 28.8 %all-to-all-start.5 = ((f32[1,1,1,256,4,512]{5,3,2,1,0,4:T(8,128)}), f32[1,1,1,256,4,512]{5,3,2,1,0,4:T(8,128)}, u32[]{:S(2)}, u32[]{:S(2)}) async-start(f32[1,1,1,256,4,512]{5,3,2,1,0,4:T(8,128)} %copy.173), calls=%async_computation.13 | async-start | bytes 4194304 | tf_op jit(solution)/shard_map/all_to_all | solution.py:213
  2025.3 50.7 %all-gather.41.cloned.1.call-start = ((), (), s32[]{:S(2)}) async-start(), calls=%async_computation.36 | async-start | bytes 4325376 | tf_op jit(solution)/shard_map/all_gather | solution.py:422
  2049.6 22.4 %all-to-all-start.4 = ((f32[1,1,1,256,4,512]{5,3,2,1,0,4:T(8,128)}), f32[1,1,1,256,4,512]{5,3,2,1,0,4:T(8,128)S(1)}, u32[]{:S(2)}, u32[]{:S(2)}) async-start(f32[1,1,1,256,4,512]{5,3,2,1,0,4:T(8,128)} %copy.172), calls=%async_computation.11 | async-start | bytes 4194304 | tf_op jit(solution)/shard_map/all_to_all | solution.py:213
  (78 other events, 508.8 us)
Sparse Core Ops, SparseCore 0:
  13.4 103.2 all-gather.44
  119.1 52.1 all-gather.24
  173.4 15.1 all-gather.46
  191.0 53.7 all-gather.26
  248.1 52.5 reduce-scatter.16
  304.2 52.5 reduce-scatter.18
  359.2 52.5 all-gather.52
  414.2 87.4 all-gather.48
  503.9 80.7 all-gather.28
  586.6 18.3 all-gather.54
  606.5 31.2 all-gather.50
  639.8 81.9 all-gather.30
  724.6 75.2 reduce-scatter.20
  802.7 77.2 reduce-scatter.22
  882.0 81.2 all-gather.32
  965.3 79.2 all-gather.34
  1046.6 75.2 reduce-scatter.24
  1124.7 77.2 reduce-scatter.26
  1204.4 53.0 all-gather.36
  1259.8 52.5 all-gather.38
  1354.8 52.4 reduce-scatter.28
  1451.6 52.5 reduce-scatter.30
  1506.4 25.0 reduce-scatter.34
  1593.1 18.7 reduce-scatter.32
  1659.6 51.6 reduce-scatter.36
  1858.4 19.2 all-gather.42
  1879.1 14.8 all-gather.56
  2027.6 20.9 all-gather.40

commit v10 on v8

--- a/solution.py
+++ b/solution.py
@@ -341,7 +341,10 @@
             grad_normed_part = jnp.einsum(
                 "stf,df->std", paired_gradient, w_pair, preferred_element_type=jnp.float32
             )
-            grad_normed_ffn = yield (scatter_seqs, grad_normed_part.astype(jnp.bfloat16))
+            block_features, scatter_operand = lax.optimization_barrier(
+                (block_features, grad_normed_part.astype(jnp.bfloat16))
+            )
+            grad_normed_ffn = yield (scatter_seqs, scatter_operand)
             grad_normed_ffn = grad_normed_ffn.astype(jnp.float32)
             scaled_ffn = grad_normed_ffn * gain_ffn_all
             gain_ffn_part = jnp.sum(grad_normed_ffn * norm_ffn, axis=(0, 1))
@@ -417,10 +420,11 @@
         total_down = reduce_features(grad_down_w, 1, "row")
         gain_rows = lax.psum(jnp.stack([gain_attn_total, gain_ffn_total], axis=1), "row")
         gain_cols = jnp.pad(gain_rows, ((0, 0), (0, 126)))
+        attn_grads = jnp.concatenate([grad_attn_w, gain_cols], axis=1)
+        early_inputs, attn_grads = lax.optimization_barrier((inputs_grad[:-1], attn_grads))
+        inputs_grad = list(early_inputs) + inputs_grad[-1:]
         total_attn = lax.all_gather(
-            transpose_grid(
-                reduce_half_exchange(jnp.concatenate([grad_attn_w, gain_cols], axis=1), "col")
-            ),
+            transpose_grid(reduce_half_exchange(attn_grads, "col")),
             "dp",
             axis=0,
             tiled=True,

time: 2050 us -> 2030 us (level)
  waiting for transfers between devices: 963 us -> 902 us
    all_to_all x4, waiting for transfers between devices: 56.9 us -> 21.9 us  [to_features(): rows = lax.all_to_all(rows, 'row', 3, 2)]
  transfers between devices with their start and end apart: 38 -> 38, of which waited for: 24 -> 22; matrix products, arithmetic and copies ran while one was open for 42% -> 44% of each run, Pallas kernels for 0% -> 0%
where the time goes in v10:
time: 2030 us; the launch traced here: 2010 us
  waiting for transfers between devices  902 us (44%)
  matrix products  482 us (24%)
  local copies, waits for them, and re-layouts  234 us (12%)
  other arithmetic  213 us (10%)
  blocking collectives  88.5 us (4%)
  starting transfers between devices  78.2 us (4%)
    all_gather x4, waiting for transfers between devices, gather_seqs(): return lax.all_gather(rows, 'col', axis=0, tiled=True)  207 us
    unnamed x32, waiting for transfers between devices  174 us
    reduce_scatter x4, waiting for transfers between devices, scatter_seqs(): return lax.psum_scatter(rows, 'col', scatter_dimension=0, tiled=True)  172 us
    all_gather x3, waiting for transfers between devices, gather_half(): gathered = lax.all_gather(mine, axis_name, axis=axis)  139 us
    all_gather x4, waiting for transfers between devices, gather_tokens(): return lax.all_gather(rows, 'row', axis=1, tiled=True)  85.8 us
    dot_general x2, matrix products, micro_batch(): jnp.einsum('std,stf->df', spread_ffn, paired_gradient, preferred_element_...  61.8 us
    convert_element_type x2, other arithmetic, attend_backward(): grad_scores = (attn_probs * (grad_probs - jnp.sum(attn_probs * grad_probs...  58.3 us
    all_to_all x1, starting transfers between devices, to_tokens(): rows = lax.all_to_all(rows, 'row', 2, 3)  50.9 us
  transfers between devices with their start and end apart: 38, of which 22 were waited for; matrix products, arithmetic and copies ran while one was open for 44% of the time, Pallas kernels for 0%

profile of v10, /device:TPU:0, one launch (start us, length us, event | category | flops | bytes accessed | tf_op | source)
XLA Modules:
  0.0 2014.4 jit_solution(17128116698792287654)
XLA Ops:
  16.3 50.9 %all-to-all-start = ((bf16[2,1,4,256,1,512]{5,3,0,4,1,2:T(8,128)(2,1)}), bf16[2,1,4,256,1,512]{5,3,0,4,1,2:T(8,128)(2,1)}, u32[]{:S(2)}, u32[]{:S(2)}) async-start(bf16[2,1,4,256,1,512]{5,3,0,4,1,2:T(8,128)(2,1)} %copy.149), calls=%async_computation | async-start | bytes 4194304 | tf_op jit(solution)/shard_map/all_to_all | solution.py:207
  67.2 27.4 %all_gather.75 = f32[2,2048]{1,0:T(2,128)S(1)} all-gather(f32[2,512]{1,0:T(2,128)S(1)} %pad_maximum_fusion.29), channel_id=1, replica_groups=mesh['dp'=2,'row'=4,'col'=4] {'row'}, dimensions={1}, use_global_device_ids=true | all-gather | bytes 20480 | tf_op jit(solution)/shard_map/all_gather | solution.py:252
  122.7 9.3 all_gather.78
  136.7 34.6 %all-gather.26.cloned.1.call-done = bf16[1,1024,2048]{2,1,0:T(8,128)(2,1)} async-done(((bf16[1,256,2048]{2,1,0:T(8,128)(2,1)}), bf16[1,1024,2048]{2,1,0:T(8,128)(2,1)}) %all-gather.26.cloned.1.call-update) | async-done | bytes 4194320 | tf_op jit(solution)/shard_map/all_gather | solution.py:193
  171.5 17.1 all-gather.46.cloned.1.call-done
  197.5 13.7 fusion.131
  211.2 13.4 exponential_reduce_fusion.1
  224.7 13.4 fusion.78
  252.7 14.2 fusion.132
  267.0 13.5 exponential_reduce_fusion
  280.5 14.1 fusion.81
  309.2 47.5 %reduce-scatter.20.cloned.1.call-done = bf16[1,256,2048]{2,1,0:T(8,128)(2,1)} async-done(((bf16[1,1024,2048]{2,1,0:T(8,128)(2,1)}), bf16[1,256,2048]{2,1,0:T(8,128)(2,1)}) %reduce-scatter.20.cloned.1.call-update) | async-done | bytes 1048592 | tf_op jit(solution)/shard_map/reduce_scatter | solution.py:196
  356.8 55.0 %all-gather.52.cloned.1.call-done = bf16[2048,1024]{0,1:T(8,128)(2,1)} async-done(((bf16[2048,256]{0,1:T(8,128)(2,1)}), bf16[2048,1024]{0,1:T(8,128)(2,1)}) %all-gather.52.cloned.1.call-update) | async-done | bytes 4194320 | tf_op jit(solution)/shard_map/all_gather | solution.py:153
  418.0 83.7 %all-gather.48.cloned.1.call-done = bf16[1024,4096]{1,0:T(8,128)(2,1)} async-done(((bf16[256,4096]{1,0:T(8,128)(2,1)}), bf16[1024,4096]{1,0:T(8,128)(2,1)}) %all-gather.48.cloned.1.call-update) | async-done | bytes 8388624 | tf_op jit(solution)/shard_map/all_gather | solution.py:153
  506.0 78.6 %all-gather.30.cloned.1.call-done = bf16[4,256,2048]{2,1,0:T(8,128)(2,1)} async-done(((bf16[1,256,2048]{2,1,0:T(8,128)(2,1)}), bf16[4,256,2048]{2,1,0:T(8,128)(2,1)}) %all-gather.30.cloned.1.call-update) | async-done | bytes 4194320 | tf_op jit(solution)/shard_map/all_gather | solution.py:199
  584.7 20.3 %all-gather.54.cloned.1.call-done = bf16[2048,8,256]{2,0,1:T(8,128)(2,1)} async-done(((bf16[2048,4,256]{2,0,1:T(8,128)(2,1)}), bf16[2048,8,256]{2,0,1:T(8,128)(2,1)}) %all-gather.54.cloned.1.call-update) | async-done | bytes 8388624 | tf_op jit(solution)/shard_map/all_gather | solution.py:154
  604.9 16.4 copy.164
  621.3 15.2 reshape.1153
  637.8 15.5 copy.161
  653.3 20.4 %fusion.133 = f32[4,256,4096]{2,1,0:T(8,128)S(1)} fusion(bf16[4,256,2048]{2,1,0:T(8,128)(2,1)S(1)} %copy-done.105, bf16[2048,4096,1]{1,0,2:T(8,128)(2,1)} %bitcast.310), kind=kOutput, calls=%fused_computation.249 | convolution fusion | flops 17179869184 | bytes 37748736 | tf_op jit(solution)/shard_map/std,df->stf/dot_general | solution.py:307
  681.5 10.4 convolution_convert_fusion.1
  691.8 29.9 %all-gather.32.cloned.1.call-done = bf16[4,256,2048]{2,1,0:T(8,128)(2,1)} async-done(((bf16[1,256,2048]{2,1,0:T(8,128)(2,1)}), bf16[4,256,2048]{2,1,0:T(8,128)(2,1)}) %all-gather.32.cloned.1.call-update) | async-done | bytes 4194320 | tf_op jit(solution)/shard_map/all_gather | solution.py:199
  722.0 21.5 %fusion.134 = f32[4,256,4096]{2,1,0:T(8,128)S(1)} fusion(bf16[4,256,2048]{2,1,0:T(8,128)(2,1)} %all-gather.32.cloned.1.call-done, bf16[2048,4096,1]{1,0,2:T(8,128)(2,1)} %bitcast.311), kind=kOutput, calls=%fused_computation.250 | convolution fusion | flops 17179869184 | bytes 37748736 | tf_op jit(solution)/shard_map/std,df->stf/dot_general | solution.py:307
  751.4 12.5 convolution_convert_fusion
  763.9 36.0 %reduce-scatter.22.cloned.1.call-done = bf16[1,256,2048]{2,1,0:T(8,128)(2,1)} async-done(((bf16[4,256,2048]{2,1,0:T(8,128)(2,1)}), bf16[1,256,2048]{2,1,0:T(8,128)(2,1)}) %reduce-scatter.22.cloned.1.call-update) | async-done | bytes 1048592 | tf_op jit(solution)/shard_map/reduce_scatter | solution.py:202
  800.2 28.5 %all_to_all.95 = bf16[2,1,4,256,1,512]{5,3,0,4,1,2:T(8,128)(2,1)S(1)} all-to-all(bf16[2,1,4,256,1,512]{5,3,0,4,1,2:T(8,128)(2,1)S(1)} %copy.166), channel_id=1, replica_groups=mesh['dp'=2,'row'=4,'col'=4] {'row'}, dimensions={2} | all-to-all | bytes 4194304 | tf_op jit(solution)/shard_map/all_to_all | solution.py:207
  837.1 42.9 %reduce-scatter.24.cloned.1.call-done = bf16[1,256,2048]{2,1,0:T(8,128)(2,1)} async-done(((bf16[4,256,2048]{2,1,0:T(8,128)(2,1)}), bf16[1,256,2048]{2,1,0:T(8,128)(2,1)}) %reduce-scatter.24.cloned.1.call-update) | async-done | bytes 1048592 | tf_op jit(solution)/shard_map/reduce_scatter | solution.py:202
  891.5 71.7 %all-gather.34.cloned.1.call-done = bf16[4,256,2048]{2,1,0:T(8,128)(2,1)} async-done(((bf16[1,256,2048]{2,1,0:T(8,128)(2,1)}), bf16[4,256,2048]{2,1,0:T(8,128)(2,1)}) %all-gather.34.cloned.1.call-update) | async-done | bytes 4194320 | tf_op jit(solution)/shard_map/all_gather | solution.py:199
  973.3 20.5 %multiply_convert_fusion.3 = (bf16[4,256,2048]{2,1,0:T(8,128)(2,1)}, bf16[4,256,2048]{2,1,0:T(8,128)(2,1)}) fusion(f32[4,256,4096]{2,1,0:T(8,128)} %copy-done.19, bf16[4,256,2048]{2,1,0:T(8,128)(2,1)} %all-gather.34.cloned.1.call-done, bf16[2048,2048,1]{1,0,2:T(8,128)(2,1)} %reshape.1153), kind=kOutput, calls=%fused_computation.30 | convolution fusion | flops 8617197568 | bytes 37748736 | tf_op jit(solution)/shard_map/std,fd->stf/dot_general | solution.py:328
  993.8 23.9 %fusion.37 = bf16[4,256,2048]{2,1,0:T(8,128)(2,1)} fusion(bf16[2048,4096,1]{1,0,2:T(8,128)(2,1)} %bitcast.312, bf16[4,256,2048]{2,1,0:T(8,128)(2,1)} %get-tuple-element.349, bf16[4,256,2048]{2,1,0:T(8,128)(2,1)} %get-tuple-element.348), kind=kOutput, calls=%fused_computation.70 | convolution fusion | flops 17198743552 | bytes 29360128 | tf_op jit(solution)/shard_map/stf,df->std/dot_general | solution.py:341
  1017.7 26.8 %all-gather.36.cloned.1.call-done = bf16[4,256,2048]{2,1,0:T(8,128)(2,1)} async-done(((bf16[1,256,2048]{2,1,0:T(8,128)(2,1)}), bf16[4,256,2048]{2,1,0:T(8,128)(2,1)}) %all-gather.36.cloned.1.call-update) | async-done | bytes 4194320 | tf_op jit(solution)/shard_map/all_gather | solution.py:199
  1056.8 20.4 %multiply_convert_fusion.1 = (bf16[4,256,2048]{2,1,0:T(8,128)(2,1)}, bf16[4,256,2048]{2,1,0:T(8,128)(2,1)}) fusion(f32[4,256,4096]{2,1,0:T(8,128)} %copy-done.18, bf16[4,256,2048]{2,1,0:T(8,128)(2,1)} %all-gather.36.cloned.1.call-done, bf16[2048,2048,1]{1,0,2:T(8,128)(2,1)} %reshape.1153), kind=kOutput, calls=%fused_computation.28 | convolution fusion | flops 8617197568 | bytes 37748736 | tf_op jit(solution)/shard_map/std,fd->stf/dot_general | solution.py:328
  1077.2 23.9 %fusion.38 = bf16[4,256,2048]{2,1,0:T(8,128)(2,1)} fusion(bf16[2048,4096,1]{1,0,2:T(8,128)(2,1)} %bitcast.313, bf16[4,256,2048]{2,1,0:T(8,128)(2,1)} %get-tuple-element.347, bf16[4,256,2048]{2,1,0:T(8,128)(2,1)} %get-tuple-element.346), kind=kOutput, calls=%fused_computation.71 | convolution fusion | flops 17198743552 | bytes 29360128 | tf_op jit(solution)/shard_map/stf,df->std/dot_general | solution.py:341
  1101.1 20.8 %reduce-scatter.26.cloned.1.call-done = bf16[1,256,2048]{2,1,0:T(8,128)(2,1)} async-done(((bf16[4,256,2048]{2,1,0:T(8,128)(2,1)}), bf16[1,256,2048]{2,1,0:T(8,128)(2,1)}) %reduce-scatter.26.cloned.1.call-update) | async-done | bytes 1048592 | tf_op jit(solution)/shard_map/reduce_scatter | solution.py:202
  1130.0 72.0 %reduce-scatter.28.cloned.1.call-done = bf16[1,256,2048]{2,1,0:T(8,128)(2,1)} async-done(((bf16[4,256,2048]{2,1,0:T(8,128)(2,1)}), bf16[1,256,2048]{2,1,0:T(8,128)(2,1)}) %reduce-scatter.28.cloned.1.call-update) | async-done | bytes 1048592 | tf_op jit(solution)/shard_map/reduce_scatter | solution.py:202
  1207.5 50.0 %all-gather.38.cloned.1.call-done = bf16[1,1024,2048]{2,1,0:T(8,128)(2,1)} async-done(((bf16[1,256,2048]{2,1,0:T(8,128)(2,1)}), bf16[1,1024,2048]{2,1,0:T(8,128)(2,1)}) %all-gather.38.cloned.1.call-update) | async-done | bytes 4194320 | tf_op jit(solution)/shard_map/all_gather | solution.py:193
  1262.9 23.0 %fusion.3 = (f32[2,4,1024]{2,1,0:T(4,128)S(1)}, f32[2,1024,1024,4]{2,1,3,0:T(8,128)}) fusion(f32[2,4,1024,1024]{2,3,1,0:T(8,128)} %get-tuple-element.395, f32[2,4,1024]{2,1,0:T(4,128)S(1)} %bitcast.352, bf16[1024,2,64,1]{0,2,3,1:T(8,128)(2,1)S(1)} %bitcast.346, bf16[1024,2,4,64]{0,3,2,1:T(8,128)(2,1)S(1)} %bitcast.337), kind=kOutput, calls=%fused_computation.8 | convolution fusion | flops 1098899456 | bytes 68485120 | tf_op jit(solution)/shard_map/while/body/eval_jaxpr/qkgd,pkd->kgqp/dot_general | solution.py:85
  1285.9 29.0 %fusion.5 = bf16[2,4,1024,1024]{2,3,1,0:T(8,128)(2,1)} fusion(f32[2,1024,1024,4]{2,1,3,0:T(8,128)} %get-tuple-element.399, f32[2,4,1024,1024]{2,3,1,0:T(8,128)} %get-tuple-element.395, f32[2,4,1024]{2,1,0:T(4,128)S(1)} %get-tuple-element.398, f32[2,4,1024]{2,1,0:T(4,128)S(1)} %bitcast.353), kind=kLoop, calls=%fused_computation.10 | loop fusion | flops 33554432 | bytes 83951616 | tf_op jit(solution)/shard_map/while/body/eval_jaxpr/convert_element_type | solution.py:96
  1314.9 8.7 fusion.97
  1323.6 13.3 fusion.98
  1337.9 8.9 convolution_multiply_fusion.1
  1359.9 22.8 %fusion = (f32[2,4,1024]{2,1,0:T(4,128)S(1)}, f32[2,1024,1024,4]{2,1,3,0:T(8,128)}) fusion(f32[2,4,1024,1024]{2,3,1,0:T(8,128)} %get-tuple-element.397, f32[2,4,1024]{2,1,0:T(4,128)S(1)} %bitcast.348, bf16[1024,2,64,1]{0,2,3,1:T(8,128)(2,1)S(1)} %bitcast.344, bf16[1024,2,4,64]{0,3,2,1:T(8,128)(2,1)S(1)} %bitcast.339), kind=kOutput, calls=%fused_computation.3 | convolution fusion | flops 1098899456 | bytes 68485120 | tf_op jit(solution)/shard_map/while/body/eval_jaxpr/qkgd,pkd->kgqp/dot_general | solution.py:85
  1382.7 29.3 %fusion.2 = bf16[2,4,1024,1024]{2,3,1,0:T(8,128)(2,1)} fusion(f32[2,1024,1024,4]{2,1,3,0:T(8,128)} %get-tuple-element.401, f32[2,4,1024,1024]{2,3,1,0:T(8,128)} %get-tuple-element.397, f32[2,4,1024]{2,1,0:T(4,128)S(1)} %get-tuple-element.400, f32[2,4,1024]{2,1,0:T(4,128)S(1)} %bitcast.349), kind=kLoop, calls=%fused_computation.5 | loop fusion | flops 33554432 | bytes 83951616 | tf_op jit(solution)/shard_map/while/body/eval_jaxpr/convert_element_type | solution.py:96
  1412.0 8.7 fusion.96
  1420.8 13.3 fusion.101
  1435.0 8.9 convolution_multiply_fusion
  1451.8 15.6 fusion.135
  1467.4 17.5 bitcast_add_fusion.1
  1485.0 16.5 copy.184
  1501.6 28.9 %fusion.9 = f32[2048,4096,1]{1,0,2:T(8,128)} fusion(bf16[4,256,2048]{2,1,0:T(8,128)(2,1)} %all-gather.30.cloned.1.call-done, bf16[4,256,2048]{2,1,0:T(8,128)(2,1)} %get-tuple-element.349, bf16[4,256,2048]{2,1,0:T(8,128)(2,1)} %get-tuple-element.348), kind=kOutput, calls=%fused_computation.37 | convolution fusion | flops 17196646400 | bytes 46137344 | tf_op jit(solution)/shard_map/std,stf->df/dot_general | solution.py:338
  1530.4 32.9 %bitcast_add_fusion = f32[2048,4096]{1,0:T(8,128)} fusion(f32[2048,4096,1]{1,0,2:T(8,128)} %fusion.9, bf16[4,256,2048]{2,1,0:T(8,128)(2,1)} %all-gather.32.cloned.1.call-done, bf16[4,256,2048]{2,1,0:T(8,128)(2,1)} %get-tuple-element.347, bf16[4,256,2048]{2,1,0:T(8,128)(2,1)} %get-tuple-element.346), kind=kOutput, calls=%fused_computation | convolution fusion | flops 17205035008 | bytes 79691776 | tf_op jit(solution)/shard_map/std,stf->df/dot_general | solution.py:338
  1563.3 22.9 %copy.210 = f32[4,2,256,4096]{3,2,0,1:T(8,128)} copy(f32[4,2,256,4096]{3,2,1,0:T(8,128)} %bitcast.307) | data formatting | bytes 67108864 | tf_op jit(solution)/shard_map/reshape | solution.py:172
  1615.1 7.9 fusion.62
  1635.3 11.3 maximum_add_fusion
  1646.6 23.3 %psum.7 = f32[2048,2]{0,1:T(2,128)S(1)} all-reduce(f32[2048,2]{0,1:T(2,128)S(1)} %pad_maximum_fusion.28), channel_id=1, replica_groups=mesh['dp'=2,'row'=4,'col'=4] {'row'}, use_global_device_ids=true, to_apply=%region_27.28 | all-reduce | flops 4096 | bytes 32768 | tf_op jit(solution)/shard_map/psum | solution.py:421
  1669.9 10.0 select_maximum_fusion
  1679.9 15.8 reshape.1131
  1695.7 17.8 copy.178
  1719.5 13.0 convert_bitcast_fusion
  1744.1 46.0 %reduce-scatter.42.cloned.1.call-done = bf16[2048,1,256]{2,0,1:T(8,128)(2,1)} async-done(((bf16[2048,4,256]{2,0,1:T(8,128)(2,1)}), bf16[2048,1,256]{2,0,1:T(8,128)(2,1)}) %reduce-scatter.42.cloned.1.call-update) | async-done | bytes 1048592
  1792.9 15.9 all-to-all-done.6
  1813.3 127.9 %reduce-scatter.40.cloned.1.call-done = bf16[1,256,4096]{2,1,0:T(8,128)(2,1)} async-done(((bf16[4,256,4096]{2,1,0:T(8,128)(2,1)}), bf16[1,256,4096]{2,1,0:T(8,128)(2,1)}) %reduce-scatter.40.cloned.1.call-update) | async-done | bytes 2097168
  1961.6 21.9 %all-to-all-done.5 = f32[1,1,1,256,4,512]{5,3,2,1,0,4:T(8,128)S(1)} async-done(((f32[1,1,1,256,4,512]{5,3,2,1,0,4:T(8,128)}), f32[1,1,1,256,4,512]{5,3,2,1,0,4:T(8,128)S(1)}, u32[]{:S(2)}, u32[]{:S(2)}) %all-to-all-start.5) | async-done | bytes 2097184 | tf_op jit(solution)/shard_map/all_to_all | solution.py:213
  1996.1 8.1 fusion.128
  (431 shorter events, 293.3 us)
Async XLA Ops:
  7.2 294.5 %copy-start = (bf16[2048,512]{1,0:T(8,128)(2,1)S(1)}, bf16[2048,512]{1,0:T(8,128)(2,1)}, u32[]{:S(2)}) copy-start(bf16[2048,512]{1,0:T(8,128)(2,1)} %param.20) | copy-start | bytes 6291460
  7.2 111.0 %all-gather.44.cloned.1.call-start = ((), (), s32[]{:S(2)}) async-start(), calls=%async_computation.40 | async-start | bytes 3276800 | tf_op jit(solution)/shard_map/all_gather | solution.py:153
  11.7 0.7 collective-permute-start
  13.3 54.0 %copy-start.100 = (f32[512]{0:T(512)S(1)}, f32[512]{0:T(512)}, u32[]{:S(2)}) copy-start(f32[512]{0:T(512)} %param.22) | copy-start | bytes 6148
  13.3 53.9 %copy-start.101 = (f32[512]{0:T(512)S(1)}, f32[512]{0:T(512)}, u32[]{:S(2)}) copy-start(f32[512]{0:T(512)} %param.21) | copy-start | bytes 6148
  16.3 78.3 %all-to-all-start = ((bf16[2,1,4,256,1,512]{5,3,0,4,1,2:T(8,128)(2,1)}), bf16[2,1,4,256,1,512]{5,3,0,4,1,2:T(8,128)(2,1)}, u32[]{:S(2)}, u32[]{:S(2)}) async-start(bf16[2,1,4,256,1,512]{5,3,0,4,1,2:T(8,128)(2,1)} %copy.149), calls=%async_computation | async-start | bytes 4194304 | tf_op jit(solution)/shard_map/all_to_all | solution.py:207
  67.2 104.1 %all-gather.26.cloned.1.call-start = ((), (), s32[]{:S(2)}) async-start(), calls=%async_computation.20 | async-start | bytes 5242880 | tf_op jit(solution)/shard_map/all_gather | solution.py:193
  94.6 409.3 %copy-start.61 = (f32[1,2048]{1,0:T(1,128)}, f32[1,2048]{1,0:T(1,128)S(1)}, u32[]{:S(2)}) copy-start(f32[1,2048]{1,0:T(1,128)S(1)} %get-tuple-element.378) | copy-start | bytes 24580
  118.2 70.5 %all-gather.46.cloned.1.call-start = ((), (), s32[]{:S(2)}) async-start(), calls=%async_computation.41 | async-start | bytes 7864320 | tf_op jit(solution)/shard_map/all_gather | solution.py:154
  122.7 122.1 %all-gather.28.cloned.1.call-start = ((), (), s32[]{:S(2)}) async-start(), calls=%async_computation.21 | async-start | bytes 5242880 | tf_op jit(solution)/shard_map/all_gather | solution.py:193
  135.1 61.2 %copy-start.30 = (f32[1024,32]{0,1:T(8,128)}, f32[1024,32]{0,1:T(8,128)S(1)}, u32[]{:S(2)}) copy-start(f32[1024,32]{0,1:T(8,128)S(1)} %get-tuple-element.391) | copy-start | bytes 393220
  135.1 117.2 %copy-start.28 = (f32[1024,32]{0,1:T(8,128)}, f32[1024,32]{0,1:T(8,128)S(1)}, u32[]{:S(2)}) copy-start(f32[1024,32]{0,1:T(8,128)S(1)} %get-tuple-element.386) | copy-start | bytes 393220
  171.3 130.3 %reduce-scatter.18.cloned.1.call-start = ((), (), s32[]{:S(2)}) async-start(), calls=%async_computation.22 | async-start | bytes 5242880 | tf_op jit(solution)/shard_map/reduce_scatter | solution.py:196
  191.6 46.5 %copy-start.22 = (bf16[4,2,256,1280]{3,2,1,0:T(8,128)(2,1)}, bf16[4,2,256,1280]{3,2,1,0:T(8,128)(2,1)S(1)}, u32[]{:S(2)}) copy-start(bf16[4,2,256,1280]{3,2,1,0:T(8,128)(2,1)S(1)} %copy.157) | copy-start | bytes 15728644
  196.1 28.6 %copy-start.34 = (bf16[1,1024,128]{1,2,0:T(8,128)(2,1)}, bf16[1,1024,128]{1,2,0:T(8,128)(2,1)S(1)}, u32[]{:S(2)}) copy-start(bf16[1,1024,128]{1,2,0:T(8,128)(2,1)S(1)} %slice.365) | copy-start | bytes 786436
  244.7 112.0 %reduce-scatter.20.cloned.1.call-start = ((), (), s32[]{:S(2)}) async-start(), calls=%async_computation.23 | async-start | bytes 5242880 | tf_op jit(solution)/shard_map/reduce_scatter | solution.py:196
  252.1 28.4 %copy-start.32 = (bf16[1,1024,128]{1,2,0:T(8,128)(2,1)}, bf16[1,1024,128]{1,2,0:T(8,128)(2,1)S(1)}, u32[]{:S(2)}) copy-start(bf16[1,1024,128]{1,2,0:T(8,128)(2,1)S(1)} %slice.364) | copy-start | bytes 786436
  301.6 110.2 %all-gather.52.cloned.1.call-start = ((), (), s32[]{:S(2)}) async-start(), calls=%async_computation.44 | async-start | bytes 5242880 | tf_op jit(solution)/shard_map/all_gather | solution.py:153
  303.2 198.5 %all-gather.48.cloned.1.call-start = ((), (), s32[]{:S(2)}) async-start(), calls=%async_computation.42 | async-start | bytes 10485760 | tf_op jit(solution)/shard_map/all_gather | solution.py:153
  306.5 278.1 %all-gather.30.cloned.1.call-start = ((), (), s32[]{:S(2)}) async-start(), calls=%async_computation.24 | async-start | bytes 5242880 | tf_op jit(solution)/shard_map/all_gather | solution.py:199
  356.8 248.2 %all-gather.54.cloned.1.call-start = ((), (), s32[]{:S(2)}) async-start(), calls=%async_computation.45 | async-start | bytes 12582912 | tf_op jit(solution)/shard_map/all_gather | solution.py:154
  418.0 219.8 %all-gather.50.cloned.1.call-start = ((), (), s32[]{:S(2)}) async-start(), calls=%async_computation.43 | async-start | bytes 25165824 | tf_op jit(solution)/shard_map/all_gather | solution.py:154
  501.7 220.0 %all-gather.32.cloned.1.call-start = ((), (), s32[]{:S(2)}) async-start(), calls=%async_computation.25 | async-start | bytes 5242880 | tf_op jit(solution)/shard_map/all_gather | solution.py:199
  584.6 215.3 %reduce-scatter.22.cloned.1.call-start = ((), (), s32[]{:S(2)}) async-start(), calls=%async_computation.26 | async-start | bytes 5242880 | tf_op jit(solution)/shard_map/reduce_scatter | solution.py:202
  637.8 43.7 %slice-start = ((s8[8388608]{0:T(1024)(128)(4,1)}), s8[4194304]{0:T(1024)(128)(4,1)S(1)}, s32[]{:S(2)}) async-start(s8[8388608]{0:T(1024)(128)(4,1)} %bitcast.320), calls=%async_computation.50 | async-start | bytes 8388608
  653.3 28.2 %slice-start.1 = ((s8[8388608]{0:T(1024)(128)(4,1)}), s8[4194304]{0:T(1024)(128)(4,1)S(1)}, s32[]{:S(2)}) async-start(s8[8388608]{0:T(1024)(128)(4,1)} %bitcast.320), calls=%async_computation.51 | async-start | bytes 8388608
  721.7 158.2 %reduce-scatter.24.cloned.1.call-start = ((), (), s32[]{:S(2)}) async-start(), calls=%async_computation.27 | async-start | bytes 5242880 | tf_op jit(solution)/shard_map/reduce_scatter | solution.py:202
  763.9 36.0 %copy-start.48 = (bf16[2,1,1024,512]{3,2,1,0:T(8,128)(2,1)S(1)}, bf16[2,1,1024,512]{3,2,1,0:T(8,128)(2,1)}, u32[]{:S(2)}) copy-start(bf16[2,1,1024,512]{3,2,1,0:T(8,128)(2,1)} %param.23) | copy-start | bytes 6291460
  799.9 163.3 %all-gather.34.cloned.1.call-start = ((), (), s32[]{:S(2)}) async-start(), calls=%async_computation.28 | async-start | bytes 5242880 | tf_op jit(solution)/shard_map/all_gather | solution.py:199
  835.8 44.7 %copy-start.17 = (f32[1,256,2048]{2,1,0:T(8,128)}, f32[1,256,2048]{2,1,0:T(8,128)S(1)}, u32[]{:S(2)}) copy-start(f32[1,256,2048]{2,1,0:T(8,128)S(1)} %reshape.1136) | copy-start | bytes 6291460
  880.0 164.5 %all-gather.36.cloned.1.call-start = ((), (), s32[]{:S(2)}) async-start(), calls=%async_computation.29 | async-start | bytes 5242880 | tf_op jit(solution)/shard_map/all_gather | solution.py:199
  884.8 78.5 %copy-start.6 = (f32[1,256,2048]{2,1,0:T(8,128)S(1)}, f32[1,256,2048]{2,1,0:T(8,128)}, u32[]{:S(2)}) copy-start(f32[1,256,2048]{2,1,0:T(8,128)} %reshape.1134) | copy-start | bytes 6291460
  884.8 78.5 %copy-start.13 = (bf16[1,256,2048]{2,1,0:T(8,128)(2,1)S(1)}, bf16[1,256,2048]{2,1,0:T(8,128)(2,1)}, u32[]{:S(2)}) copy-start(bf16[1,256,2048]{2,1,0:T(8,128)(2,1)} %reduce-scatter.18.cloned.1.call-done) | copy-start | bytes 3145732
  969.0 48.7 %all-to-all-start.1 = ((bf16[1,1,1,256,4,512]{5,3,2,1,0,4:T(8,128)(2,1)}), bf16[1,1,1,256,4,512]{5,3,2,1,0,4:T(8,128)(2,1)}, u32[]{:S(2)}, u32[]{:S(2)}) async-start(bf16[1,1,1,256,4,512]{5,3,2,1,0,4:T(8,128)(2,1)} %copy.165), calls=%async_computation.4 | async-start | bytes 2097152 | tf_op jit(solution)/shard_map/all_to_all | solution.py:213
  973.2 148.7 %reduce-scatter.26.cloned.1.call-start = ((), (), s32[]{:S(2)}) async-start(), calls=%async_computation.30 | async-start | bytes 5242880 | tf_op jit(solution)/shard_map/reduce_scatter | solution.py:202
  1017.7 26.8 %copy-start.10 = (bf16[1,256,2048]{2,1,0:T(8,128)(2,1)S(1)}, bf16[1,256,2048]{2,1,0:T(8,128)(2,1)}, u32[]{:S(2)}) copy-start(bf16[1,256,2048]{2,1,0:T(8,128)(2,1)} %reduce-scatter.20.cloned.1.call-done) | copy-start | bytes 3145732
  1052.3 48.8 %all-to-all-start.3 = ((bf16[1,1,1,256,4,512]{5,3,2,1,0,4:T(8,128)(2,1)}), bf16[1,1,1,256,4,512]{5,3,2,1,0,4:T(8,128)(2,1)}, u32[]{:S(2)}, u32[]{:S(2)}) async-start(bf16[1,1,1,256,4,512]{5,3,2,1,0,4:T(8,128)(2,1)} %copy.169), calls=%async_computation.7 | async-start | bytes 2097152 | tf_op jit(solution)/shard_map/all_to_all | solution.py:213
  1056.6 145.4 %reduce-scatter.28.cloned.1.call-start = ((), (), s32[]{:S(2)}) async-start(), calls=%async_computation.31 | async-start | bytes 5242880 | tf_op jit(solution)/shard_map/reduce_scatter | solution.py:202
  1122.0 135.6 %all-gather.38.cloned.1.call-start = ((), (), s32[]{:S(2)}) async-start(), calls=%async_computation.32 | async-start | bytes 5242880 | tf_op jit(solution)/shard_map/all_gather | solution.py:193
  1126.4 75.6 %copy-start.84 = (f32[256]{0:T(256)S(1)}, f32[256]{0:T(256)}, u32[]{:S(2)}) copy-start(f32[256]{0:T(256)} %copy-done.83) | copy-start | bytes 3076
  1202.0 152.5 %all-gather.40.cloned.1.call-start = ((), (), s32[]{:S(2)}) async-start(), calls=%async_computation.33 | async-start | bytes 5242880 | tf_op jit(solution)/shard_map/all_gather | solution.py:193
  1257.6 194.2 %reduce-scatter.30.cloned.1.call-start = ((), (), s32[]{:S(2)}) async-start(), calls=%async_computation.34 | async-start | bytes 5242880 | tf_op jit(solution)/shard_map/reduce_scatter | solution.py:196
  1285.9 29.0 %copy-start.45 = (bf16[1,1024,8,32]{1,3,2,0:T(8,128)(2,1)S(1)}, bf16[1,1024,8,32]{1,3,2,0:T(8,128)(2,1)}, u32[]{:S(2)}) copy-start(bf16[1,1024,8,32]{1,3,2,0:T(8,128)(2,1)} %copy-done.44) | copy-start | bytes 1572868
  1285.9 29.0 %copy-start.47 = (bf16[1,1024,8,32]{1,3,2,0:T(8,128)(2,1)S(1)}, bf16[1,1024,8,32]{1,3,2,0:T(8,128)(2,1)}, u32[]{:S(2)}) copy-start(bf16[1,1024,8,32]{1,3,2,0:T(8,128)(2,1)} %copy-done.46) | copy-start | bytes 1572868
  1354.6 259.2 %reduce-scatter.32.cloned.1.call-start = ((), (), s32[]{:S(2)}) async-start(), calls=%async_computation.35 | async-start | bytes 5242880 | tf_op jit(solution)/shard_map/reduce_scatter | solution.py:196
  1382.7 29.3 %copy-start.41 = (bf16[1,1024,8,32]{1,3,2,0:T(8,128)(2,1)S(1)}, bf16[1,1024,8,32]{1,3,2,0:T(8,128)(2,1)}, u32[]{:S(2)}) copy-start(bf16[1,1024,8,32]{1,3,2,0:T(8,128)(2,1)} %copy-done.40) | copy-start | bytes 1572868
  1382.7 29.3 %copy-start.43 = (bf16[1,1024,8,32]{1,3,2,0:T(8,128)(2,1)S(1)}, bf16[1,1024,8,32]{1,3,2,0:T(8,128)(2,1)}, u32[]{:S(2)}) copy-start(bf16[1,1024,8,32]{1,3,2,0:T(8,128)(2,1)} %copy-done.42) | copy-start | bytes 1572868
  1451.7 261.8 %reduce-scatter.38.cloned.1.call-start = ((), (), s32[]{:S(2)}) async-start(), calls=%async_computation.39 | async-start | bytes 25165824 | tf_op jit(solution)/shard_map/reduce_scatter | solution.py:173
  1501.5 218.0 %reduce-scatter.36.cloned.1.call-start = ((), (), s32[]{:S(2)}) async-start(), calls=%async_computation.38 | async-start | bytes 50331648 | tf_op jit(solution)/shard_map/reduce_scatter | solution.py:173
  1630.7 49.2 %all-to-all-start.4 = ((f32[1,1,1,256,4,512]{5,3,2,1,0,4:T(8,128)}), f32[1,1,1,256,4,512]{5,3,2,1,0,4:T(8,128)}, u32[]{:S(2)}, u32[]{:S(2)}) async-start(f32[1,1,1,256,4,512]{5,3,2,1,0,4:T(8,128)} %copy.176), calls=%async_computation.11 | async-start | bytes 4194304 | tf_op jit(solution)/shard_map/all_to_all | solution.py:213
  1635.2 97.5 %reduce-scatter.34.cloned.1.call-start = ((), (), s32[]{:S(2)}) async-start(), calls=%async_computation.36 | async-start | bytes 17301504 | tf_op jit(solution)/shard_map/reduce_scatter | solution.py:182
  1713.5 76.6 %reduce-scatter.42.cloned.1.call-start = ((), (), s32[]{:S(2)}) async-start(), calls=%async_computation.49 | async-start | bytes 5242880
  1719.4 221.8 %reduce-scatter.40.cloned.1.call-start = ((), (), s32[]{:S(2)}) async-start(), calls=%async_computation.48 | async-start | bytes 10485760
  1737.2 71.6 %all-to-all-start.6 = ((bf16[4,256,1408]{2,1,0:T(8,128)(2,1)}), bf16[4,256,1408]{2,1,0:T(8,128)(2,1)}, u32[]{:S(2)}, u32[]{:S(2)}) async-start(bf16[4,256,1408]{2,1,0:T(8,128)(2,1)} %convert_bitcast_fusion.6), calls=%async_computation.15 | async-start | bytes 5767168 | tf_op jit(solution)/shard_map/all_to_all | solution.py:183
  1744.1 217.5 %all-gather.58.cloned.1.call-start = ((), (), s32[]{:S(2)}) async-start(), calls=%async_computation.47 | async-start | bytes 6291456 | tf_op jit(solution)/shard_map/all_gather | solution.py:187
  1792.9 195.1 %all-gather.42.cloned.1.call-start = ((), (), s32[]{:S(2)}) async-start(), calls=%async_computation.37 | async-start | bytes 4325376 | tf_op jit(solution)/shard_map/all_gather | solution.py:426
  1811.3 0.8 collective-permute-start.1
  1813.2 132.1 %copy-start.99 = (f32[256]{0:T(256)S(1)}, f32[256]{0:T(256)}, u32[]{:S(2)}) copy-start(f32[256]{0:T(256)} %get-tuple-element.339) | copy-start | bytes 3076
  1813.2 132.1 %copy-start.11 = (bf16[1,256,2048]{2,1,0:T(8,128)(2,1)S(1)}, bf16[1,256,2048]{2,1,0:T(8,128)(2,1)}, u32[]{:S(2)}) copy-start(bf16[1,256,2048]{2,1,0:T(8,128)(2,1)} %reduce-scatter.20.cloned.1.call-done) | copy-start | bytes 3145732
  1813.2 132.1 %copy-start.85 = (f32[256]{0:T(256)S(1)}, f32[256]{0:T(256)}, u32[]{:S(2)}) copy-start(f32[256]{0:T(256)} %copy-done.83) | copy-start | bytes 3076
  1813.2 132.1 %copy-start.91 = (f32[256]{0:T(256)S(1)}, f32[256]{0:T(256)}, u32[]{:S(2)}) copy-start(f32[256]{0:T(256)} %copy-done.89) | copy-start | bytes 3076
  1813.2 132.1 %copy-start.95 = (f32[256]{0:T(256)S(1)}, f32[256]{0:T(256)}, u32[]{:S(2)}) copy-start(f32[256]{0:T(256)} %copy-done.94) | copy-start | bytes 3076
  1813.3 182.9 %all-gather.56.cloned.1.call-start = ((), (), s32[]{:S(2)}) async-start(), calls=%async_computation.46 | async-start | bytes 12582912 | tf_op jit(solution)/shard_map/all_gather | solution.py:187
  1954.9 28.6 %all-to-all-start.5 = ((f32[1,1,1,256,4,512]{5,3,2,1,0,4:T(8,128)}), f32[1,1,1,256,4,512]{5,3,2,1,0,4:T(8,128)S(1)}, u32[]{:S(2)}, u32[]{:S(2)}) async-start(f32[1,1,1,256,4,512]{5,3,2,1,0,4:T(8,128)} %copy.177), calls=%async_computation.13 | async-start | bytes 4194304 | tf_op jit(solution)/shard_map/all_to_all | solution.py:213
  (83 other events, 601.2 us)
Sparse Core Ops, SparseCore 0:
  13.4 103.2 all-gather.43
  119.1 52.1 all-gather.25
  173.4 15.1 all-gather.45
  190.9 53.7 all-gather.27
  248.1 52.5 reduce-scatter.17
  304.1 52.5 reduce-scatter.19
  359.2 52.5 all-gather.51
  414.2 87.4 all-gather.47
  503.8 80.7 all-gather.29
  586.6 18.3 all-gather.53
  606.5 31.2 all-gather.49
  639.8 81.9 all-gather.31
  724.6 75.2 reduce-scatter.21
  802.6 77.2 reduce-scatter.23
  881.9 81.2 all-gather.33
  965.2 79.2 all-gather.35
  1046.6 75.2 reduce-scatter.25
  1124.7 77.2 reduce-scatter.27
  1204.4 53.0 all-gather.37
  1259.8 52.5 all-gather.39
  1354.7 52.4 reduce-scatter.29
  1451.9 52.5 reduce-scatter.31
  1506.7 25.0 reduce-scatter.37
  1586.3 42.9 reduce-scatter.35
  1713.6 19.0 reduce-scatter.33
  1736.1 54.0 reduce-scatter.41
  1793.1 148.0 reduce-scatter.39
  1943.3 13.6 all-gather.57
  1958.6 12.8 all-gather.41
  1973.5 21.0 all-gather.55

commit v11 on v10

--- a/solution.py
+++ b/solution.py
@@ -183,8 +183,17 @@
         blocks = lax.all_to_all(split.astype(jnp.bfloat16), axis_name, 0, 0)
         return jnp.sum(blocks.astype(jnp.float32), axis=0)
 
+    def gather_dp(block, axis):
+        if n_dp != 2:
+            return lax.all_gather(block, "dp", axis=axis, tiled=True)
+        other = lax.ppermute(block, "dp", [(0, 1), (1, 0)])
+        first_core = lax.axis_index("dp") == 0
+        return jnp.concatenate(
+            [jnp.where(first_core, block, other), jnp.where(first_core, other, block)], axis=axis
+        )
+
     def reduce_features(partial, axis, axis_name):
-        return lax.all_gather(reduce_half(partial, axis, axis_name), "dp", axis=axis, tiled=True)
+        return gather_dp(reduce_half(partial, axis, axis_name), axis)
 
     def transpose_grid(block):
         return lax.ppermute(block, ("row", "col"), transpose_pairs)
@@ -423,12 +432,7 @@
         attn_grads = jnp.concatenate([grad_attn_w, gain_cols], axis=1)
         early_inputs, attn_grads = lax.optimization_barrier((inputs_grad[:-1], attn_grads))
         inputs_grad = list(early_inputs) + inputs_grad[-1:]
-        total_attn = lax.all_gather(
-            transpose_grid(reduce_half_exchange(attn_grads, "col")),
-            "dp",
-            axis=0,
-            tiled=True,
-        )
+        total_attn = gather_dp(transpose_grid(reduce_half_exchange(attn_grads, "col")), 0)
         attn_cols = qkv_cols + w_out.shape[0]
         return (
             jnp.concatenate(outs_list),

time: 2030 us -> 2030 us (level); the launches traced: 2010 us -> 1990 us
  waiting for transfers between devices: 902 us -> 870 us
    unnamed x32 -> x29, waiting for transfers between devices: 174 us -> 135 us
    all_to_all x4, waiting for transfers between devices: 21.9 us -> 45.5 us  [to_features(): rows = lax.all_to_all(rows, 'row', 3, 2)]
  transfers between devices with their start and end apart: 38 -> 38, of which waited for: 22 -> 21; matrix products, arithmetic and copies ran while one was open for 44% -> 45% of each run, Pallas kernels for 0% -> 0%
where the time goes in v11:
time: 2030 us; the launch traced here: 1990 us
  waiting for transfers between devices  870 us (43%)
  matrix products  482 us (24%)
  other arithmetic  228 us (11%)
  local copies, waits for them, and re-layouts  217 us (11%)
  blocking collectives  88.7 us (4%)
  starting transfers between devices  88.5 us (4%)
    all_gather x4, waiting for transfers between devices, gather_seqs(): return lax.all_gather(rows, 'col', axis=0, tiled=True)  207 us
    reduce_scatter x4, waiting for transfers between devices, scatter_seqs(): return lax.psum_scatter(rows, 'col', scatter_dimension=0, tiled=True)  172 us
    all_gather x3, waiting for transfers between devices, gather_half(): gathered = lax.all_gather(mine, axis_name, axis=axis)  139 us
    unnamed x29, waiting for transfers between devices  135 us
    all_gather x4, waiting for transfers between devices, gather_tokens(): return lax.all_gather(rows, 'row', axis=1, tiled=True)  85.7 us
    dot_general x2, matrix products, micro_batch(): jnp.einsum('std,stf->df', spread_ffn, paired_gradient, preferred_element_...  61.8 us
    convert_element_type x2, other arithmetic, attend_backward(): grad_scores = (attn_probs * (grad_probs - jnp.sum(attn_probs * grad_probs...  58.3 us
    all_to_all x1, starting transfers between devices, to_tokens(): rows = lax.all_to_all(rows, 'row', 2, 3)  50.9 us
  transfers between devices with their start and end apart: 38, of which 21 were waited for; matrix products, arithmetic and copies ran while one was open for 45% of the time, Pallas kernels for 0%

profile of v11, /device:TPU:0, one launch (start us, length us, event | category | flops | bytes accessed | tf_op | source)
XLA Modules:
  0.0 1990.2 jit_solution(3769570430804619909)
XLA Ops:
  16.3 50.9 %all-to-all-start = ((bf16[2,1,4,256,1,512]{5,3,0,4,1,2:T(8,128)(2,1)}), bf16[2,1,4,256,1,512]{5,3,0,4,1,2:T(8,128)(2,1)}, u32[]{:S(2)}, u32[]{:S(2)}) async-start(bf16[2,1,4,256,1,512]{5,3,0,4,1,2:T(8,128)(2,1)} %copy.149), calls=%async_computation | async-start | bytes 4194304 | tf_op jit(solution)/shard_map/all_to_all | solution.py:216
  67.2 27.4 %all_gather.66 = f32[2,2048]{1,0:T(2,128)S(1)} all-gather(f32[2,512]{1,0:T(2,128)S(1)} %pad_maximum_fusion.32), channel_id=1, replica_groups=mesh['dp'=2,'row'=4,'col'=4] {'row'}, dimensions={1}, use_global_device_ids=true | all-gather | bytes 20480 | tf_op jit(solution)/shard_map/all_gather | solution.py:261
  122.7 9.3 all_gather.69
  136.7 34.6 %all-gather.21.cloned.1.call-done = bf16[1,1024,2048]{2,1,0:T(8,128)(2,1)} async-done(((bf16[1,256,2048]{2,1,0:T(8,128)(2,1)}), bf16[1,1024,2048]{2,1,0:T(8,128)(2,1)}) %all-gather.21.cloned.1.call-update) | async-done | bytes 4194320 | tf_op jit(solution)/shard_map/all_gather | solution.py:202
  171.5 17.1 all-gather.39.cloned.1.call-done
  197.5 13.7 fusion.138
  211.2 13.4 exponential_reduce_fusion.1
  224.7 13.4 fusion.79
  252.7 14.2 fusion.139
  267.0 13.5 exponential_reduce_fusion
  280.5 14.1 fusion.82
  309.2 47.5 %reduce-scatter.20.cloned.1.call-done = bf16[1,256,2048]{2,1,0:T(8,128)(2,1)} async-done(((bf16[1,1024,2048]{2,1,0:T(8,128)(2,1)}), bf16[1,256,2048]{2,1,0:T(8,128)(2,1)}) %reduce-scatter.20.cloned.1.call-update) | async-done | bytes 1048592 | tf_op jit(solution)/shard_map/reduce_scatter | solution.py:205
  356.8 55.0 %all-gather.45.cloned.1.call-done = bf16[2048,1024]{0,1:T(8,128)(2,1)} async-done(((bf16[2048,256]{0,1:T(8,128)(2,1)}), bf16[2048,1024]{0,1:T(8,128)(2,1)}) %all-gather.45.cloned.1.call-update) | async-done | bytes 4194320 | tf_op jit(solution)/shard_map/all_gather | solution.py:153
  418.0 83.7 %all-gather.41.cloned.1.call-done = bf16[1024,4096]{1,0:T(8,128)(2,1)} async-done(((bf16[256,4096]{1,0:T(8,128)(2,1)}), bf16[1024,4096]{1,0:T(8,128)(2,1)}) %all-gather.41.cloned.1.call-update) | async-done | bytes 8388624 | tf_op jit(solution)/shard_map/all_gather | solution.py:153
  505.9 78.6 %all-gather.25.cloned.1.call-done = bf16[4,256,2048]{2,1,0:T(8,128)(2,1)} async-done(((bf16[1,256,2048]{2,1,0:T(8,128)(2,1)}), bf16[4,256,2048]{2,1,0:T(8,128)(2,1)}) %all-gather.25.cloned.1.call-update) | async-done | bytes 4194320 | tf_op jit(solution)/shard_map/all_gather | solution.py:208
  584.6 20.3 %all-gather.47.cloned.1.call-done = bf16[2048,8,256]{2,0,1:T(8,128)(2,1)} async-done(((bf16[2048,4,256]{2,0,1:T(8,128)(2,1)}), bf16[2048,8,256]{2,0,1:T(8,128)(2,1)}) %all-gather.47.cloned.1.call-update) | async-done | bytes 8388624 | tf_op jit(solution)/shard_map/all_gather | solution.py:154
  604.9 16.4 copy.164
  621.3 15.2 reshape.1151
  637.7 15.5 copy.161
  653.2 20.4 %fusion.140 = f32[4,256,4096]{2,1,0:T(8,128)S(1)} fusion(bf16[4,256,2048]{2,1,0:T(8,128)(2,1)S(1)} %copy-done.106, bf16[2048,4096,1]{1,0,2:T(8,128)(2,1)} %bitcast.318), kind=kOutput, calls=%fused_computation.276 | convolution fusion | flops 17179869184 | bytes 37748736 | tf_op jit(solution)/shard_map/std,df->stf/dot_general | solution.py:316
  681.4 10.4 convolution_convert_fusion.1
  691.8 29.9 %all-gather.27.cloned.1.call-done = bf16[4,256,2048]{2,1,0:T(8,128)(2,1)} async-done(((bf16[1,256,2048]{2,1,0:T(8,128)(2,1)}), bf16[4,256,2048]{2,1,0:T(8,128)(2,1)}) %all-gather.27.cloned.1.call-update) | async-done | bytes 4194320 | tf_op jit(solution)/shard_map/all_gather | solution.py:208
  722.0 21.5 %fusion.141 = f32[4,256,4096]{2,1,0:T(8,128)S(1)} fusion(bf16[4,256,2048]{2,1,0:T(8,128)(2,1)} %all-gather.27.cloned.1.call-done, bf16[2048,4096,1]{1,0,2:T(8,128)(2,1)} %bitcast.319), kind=kOutput, calls=%fused_computation.277 | convolution fusion | flops 17179869184 | bytes 37748736 | tf_op jit(solution)/shard_map/std,df->stf/dot_general | solution.py:316
  751.4 12.5 convolution_convert_fusion
  763.9 36.0 %reduce-scatter.22.cloned.1.call-done = bf16[1,256,2048]{2,1,0:T(8,128)(2,1)} async-done(((bf16[4,256,2048]{2,1,0:T(8,128)(2,1)}), bf16[1,256,2048]{2,1,0:T(8,128)(2,1)}) %reduce-scatter.22.cloned.1.call-update) | async-done | bytes 1048592 | tf_op jit(solution)/shard_map/reduce_scatter | solution.py:211
  800.2 28.5 %all_to_all.95 = bf16[2,1,4,256,1,512]{5,3,0,4,1,2:T(8,128)(2,1)S(1)} all-to-all(bf16[2,1,4,256,1,512]{5,3,0,4,1,2:T(8,128)(2,1)S(1)} %copy.166), channel_id=1, replica_groups=mesh['dp'=2,'row'=4,'col'=4] {'row'}, dimensions={2} | all-to-all | bytes 4194304 | tf_op jit(solution)/shard_map/all_to_all | solution.py:216
  837.0 42.9 %reduce-scatter.24.cloned.1.call-done = bf16[1,256,2048]{2,1,0:T(8,128)(2,1)} async-done(((bf16[4,256,2048]{2,1,0:T(8,128)(2,1)}), bf16[1,256,2048]{2,1,0:T(8,128)(2,1)}) %reduce-scatter.24.cloned.1.call-update) | async-done | bytes 1048592 | tf_op jit(solution)/shard_map/reduce_scatter | solution.py:211
  891.5 71.7 %all-gather.29.cloned.1.call-done = bf16[4,256,2048]{2,1,0:T(8,128)(2,1)} async-done(((bf16[1,256,2048]{2,1,0:T(8,128)(2,1)}), bf16[4,256,2048]{2,1,0:T(8,128)(2,1)}) %all-gather.29.cloned.1.call-update) | async-done | bytes 4194320 | tf_op jit(solution)/shard_map/all_gather | solution.py:208
  973.3 20.5 %multiply_convert_fusion.3 = (bf16[4,256,2048]{2,1,0:T(8,128)(2,1)}, bf16[4,256,2048]{2,1,0:T(8,128)(2,1)}) fusion(f32[4,256,4096]{2,1,0:T(8,128)} %copy-done.20, bf16[4,256,2048]{2,1,0:T(8,128)(2,1)} %all-gather.29.cloned.1.call-done, bf16[2048,2048,1]{1,0,2:T(8,128)(2,1)} %reshape.1151), kind=kOutput, calls=%fused_computation.32 | convolution fusion | flops 8617197568 | bytes 37748736 | tf_op jit(solution)/shard_map/std,fd->stf/dot_general | solution.py:337
  993.7 23.9 %fusion.38 = bf16[4,256,2048]{2,1,0:T(8,128)(2,1)} fusion(bf16[2048,4096,1]{1,0,2:T(8,128)(2,1)} %bitcast.320, bf16[4,256,2048]{2,1,0:T(8,128)(2,1)} %get-tuple-element.349, bf16[4,256,2048]{2,1,0:T(8,128)(2,1)} %get-tuple-element.348), kind=kOutput, calls=%fused_computation.85 | convolution fusion | flops 17198743552 | bytes 29360128 | tf_op jit(solution)/shard_map/stf,df->std/dot_general | solution.py:350
  1017.7 26.8 %all-gather.31.cloned.1.call-done = bf16[4,256,2048]{2,1,0:T(8,128)(2,1)} async-done(((bf16[1,256,2048]{2,1,0:T(8,128)(2,1)}), bf16[4,256,2048]{2,1,0:T(8,128)(2,1)}) %all-gather.31.cloned.1.call-update) | async-done | bytes 4194320 | tf_op jit(solution)/shard_map/all_gather | solution.py:208
  1056.7 20.4 %multiply_convert_fusion.1 = (bf16[4,256,2048]{2,1,0:T(8,128)(2,1)}, bf16[4,256,2048]{2,1,0:T(8,128)(2,1)}) fusion(f32[4,256,4096]{2,1,0:T(8,128)} %copy-done.19, bf16[4,256,2048]{2,1,0:T(8,128)(2,1)} %all-gather.31.cloned.1.call-done, bf16[2048,2048,1]{1,0,2:T(8,128)(2,1)} %reshape.1151), kind=kOutput, calls=%fused_computation.30 | convolution fusion | flops 8617197568 | bytes 37748736 | tf_op jit(solution)/shard_map/std,fd->stf/dot_general | solution.py:337
  1077.2 23.9 %fusion.39 = bf16[4,256,2048]{2,1,0:T(8,128)(2,1)} fusion(bf16[2048,4096,1]{1,0,2:T(8,128)(2,1)} %bitcast.321, bf16[4,256,2048]{2,1,0:T(8,128)(2,1)} %get-tuple-element.347, bf16[4,256,2048]{2,1,0:T(8,128)(2,1)} %get-tuple-element.346), kind=kOutput, calls=%fused_computation.86 | convolution fusion | flops 17198743552 | bytes 29360128 | tf_op jit(solution)/shard_map/stf,df->std/dot_general | solution.py:350
  1101.0 20.9 %reduce-scatter.26.cloned.1.call-done = bf16[1,256,2048]{2,1,0:T(8,128)(2,1)} async-done(((bf16[4,256,2048]{2,1,0:T(8,128)(2,1)}), bf16[1,256,2048]{2,1,0:T(8,128)(2,1)}) %reduce-scatter.26.cloned.1.call-update) | async-done | bytes 1048592 | tf_op jit(solution)/shard_map/reduce_scatter | solution.py:211
  1130.0 72.0 %reduce-scatter.28.cloned.1.call-done = bf16[1,256,2048]{2,1,0:T(8,128)(2,1)} async-done(((bf16[4,256,2048]{2,1,0:T(8,128)(2,1)}), bf16[1,256,2048]{2,1,0:T(8,128)(2,1)}) %reduce-scatter.28.cloned.1.call-update) | async-done | bytes 1048592 | tf_op jit(solution)/shard_map/reduce_scatter | solution.py:211
  1207.5 50.0 %all-gather.33.cloned.1.call-done = bf16[1,1024,2048]{2,1,0:T(8,128)(2,1)} async-done(((bf16[1,256,2048]{2,1,0:T(8,128)(2,1)}), bf16[1,1024,2048]{2,1,0:T(8,128)(2,1)}) %all-gather.33.cloned.1.call-update) | async-done | bytes 4194320 | tf_op jit(solution)/shard_map/all_gather | solution.py:202
  1262.9 23.0 %fusion.3 = (f32[2,4,1024]{2,1,0:T(4,128)S(1)}, f32[2,1024,1024,4]{2,1,3,0:T(8,128)}) fusion(f32[2,4,1024,1024]{2,3,1,0:T(8,128)} %get-tuple-element.401, f32[2,4,1024]{2,1,0:T(4,128)S(1)} %bitcast.358, bf16[1024,2,64,1]{0,2,3,1:T(8,128)(2,1)S(1)} %bitcast.352, bf16[1024,2,4,64]{0,3,2,1:T(8,128)(2,1)S(1)} %bitcast.344), kind=kOutput, calls=%fused_computation.8 | convolution fusion | flops 1098899456 | bytes 68485120 | tf_op jit(solution)/shard_map/while/body/eval_jaxpr/qkgd,pkd->kgqp/dot_general | solution.py:85
  1285.9 29.0 %fusion.5 = bf16[2,4,1024,1024]{2,3,1,0:T(8,128)(2,1)} fusion(f32[2,1024,1024,4]{2,1,3,0:T(8,128)} %get-tuple-element.405, f32[2,4,1024,1024]{2,3,1,0:T(8,128)} %get-tuple-element.401, f32[2,4,1024]{2,1,0:T(4,128)S(1)} %get-tuple-element.404, f32[2,4,1024]{2,1,0:T(4,128)S(1)} %bitcast.359), kind=kLoop, calls=%fused_computation.10 | loop fusion | flops 33554432 | bytes 83951616 | tf_op jit(solution)/shard_map/while/body/eval_jaxpr/convert_element_type | solution.py:96
  1314.8 8.7 fusion.98
  1323.6 13.3 fusion.99
  1337.8 8.9 convolution_multiply_fusion.1
  1347.2 7.3 convert_bitcast_fusion.3
  1359.9 22.8 %fusion = (f32[2,4,1024]{2,1,0:T(4,128)S(1)}, f32[2,1024,1024,4]{2,1,3,0:T(8,128)}) fusion(f32[2,4,1024,1024]{2,3,1,0:T(8,128)} %get-tuple-element.403, f32[2,4,1024]{2,1,0:T(4,128)S(1)} %bitcast.354, bf16[1024,2,64,1]{0,2,3,1:T(8,128)(2,1)S(1)} %bitcast.350, bf16[1024,2,4,64]{0,3,2,1:T(8,128)(2,1)S(1)} %bitcast.346), kind=kOutput, calls=%fused_computation.3 | convolution fusion | flops 1098899456 | bytes 68485120 | tf_op jit(solution)/shard_map/while/body/eval_jaxpr/qkgd,pkd->kgqp/dot_general | solution.py:85
  1382.7 29.3 %fusion.2 = bf16[2,4,1024,1024]{2,3,1,0:T(8,128)(2,1)} fusion(f32[2,1024,1024,4]{2,1,3,0:T(8,128)} %get-tuple-element.407, f32[2,4,1024,1024]{2,3,1,0:T(8,128)} %get-tuple-element.403, f32[2,4,1024]{2,1,0:T(4,128)S(1)} %get-tuple-element.406, f32[2,4,1024]{2,1,0:T(4,128)S(1)} %bitcast.355), kind=kLoop, calls=%fused_computation.5 | loop fusion | flops 33554432 | bytes 83951616 | tf_op jit(solution)/shard_map/while/body/eval_jaxpr/convert_element_type | solution.py:96
  1412.0 8.7 fusion.97
  1420.8 13.3 fusion.102
  1435.0 8.9 convolution_multiply_fusion
  1451.8 15.7 fusion.142
  1467.4 17.6 bitcast_add_fusion.1
  1485.0 16.4 copy.184
  1501.4 28.9 %fusion.9 = f32[2048,4096,1]{1,0,2:T(8,128)} fusion(bf16[4,256,2048]{2,1,0:T(8,128)(2,1)} %all-gather.25.cloned.1.call-done, bf16[4,256,2048]{2,1,0:T(8,128)(2,1)} %get-tuple-element.349, bf16[4,256,2048]{2,1,0:T(8,128)(2,1)} %get-tuple-element.348), kind=kOutput, calls=%fused_computation.39 | convolution fusion | flops 17196646400 | bytes 46137344 | tf_op jit(solution)/shard_map/std,stf->df/dot_general | solution.py:347
  1530.3 32.9 %bitcast_add_fusion = f32[2048,4096]{1,0:T(8,128)} fusion(f32[2048,4096,1]{1,0,2:T(8,128)} %fusion.9, bf16[4,256,2048]{2,1,0:T(8,128)(2,1)} %all-gather.27.cloned.1.call-done, bf16[4,256,2048]{2,1,0:T(8,128)(2,1)} %get-tuple-element.347, bf16[4,256,2048]{2,1,0:T(8,128)(2,1)} %get-tuple-element.346), kind=kOutput, calls=%fused_computation | convolution fusion | flops 17205035008 | bytes 79691776 | tf_op jit(solution)/shard_map/std,stf->df/dot_general | solution.py:347
  1563.2 22.9 %copy.210 = f32[4,2,256,4096]{3,2,0,1:T(8,128)} copy(f32[4,2,256,4096]{3,2,1,0:T(8,128)} %bitcast.315) | data formatting | bytes 67108864 | tf_op jit(solution)/shard_map/reshape | solution.py:172
  1615.0 7.3 fusion.63
  1634.8 11.3 maximum_add_fusion
  1646.1 23.5 %psum.7 = f32[2048,2]{0,1:T(2,128)S(1)} all-reduce(f32[2048,2]{0,1:T(2,128)S(1)} %pad_maximum_fusion.31), channel_id=1, replica_groups=mesh['dp'=2,'row'=4,'col'=4] {'row'}, use_global_device_ids=true, to_apply=%region_27.28 | all-reduce | flops 4096 | bytes 32768 | tf_op jit(solution)/shard_map/psum | solution.py:430
  1669.6 10.0 select_maximum_fusion
  1679.6 15.8 reshape.1131
  1695.4 17.8 copy.178
  1719.2 12.9 convert_bitcast_fusion
  1741.8 47.8 %reduce-scatter.42.cloned.1.call-done = bf16[2048,1,256]{2,0,1:T(8,128)(2,1)} async-done(((bf16[2048,4,256]{2,0,1:T(8,128)(2,1)}), bf16[2048,1,256]{2,0,1:T(8,128)(2,1)}) %reduce-scatter.42.cloned.1.call-update) | async-done | bytes 1048592
  1792.3 86.5 %reduce-scatter.40.cloned.1.call-done = bf16[1,256,4096]{2,1,0:T(8,128)(2,1)} async-done(((bf16[4,256,4096]{2,1,0:T(8,128)(2,1)}), bf16[1,256,4096]{2,1,0:T(8,128)(2,1)}) %reduce-scatter.40.cloned.1.call-update) | async-done | bytes 2097168
  1886.6 12.4 collective-permute-start.1
  1918.3 45.5 %all-to-all-done.5 = f32[1,1,1,256,4,512]{5,3,2,1,0,4:T(8,128)S(1)} async-done(((f32[1,1,1,256,4,512]{5,3,2,1,0,4:T(8,128)}), f32[1,1,1,256,4,512]{5,3,2,1,0,4:T(8,128)S(1)}, u32[]{:S(2)}, u32[]{:S(2)}) %all-to-all-start.5) | async-done | bytes 2097184 | tf_op jit(solution)/shard_map/all_to_all | solution.py:222
  (433 shorter events, 289.9 us)
Async XLA Ops:
  7.2 294.5 %copy-start = (bf16[2048,512]{1,0:T(8,128)(2,1)S(1)}, bf16[2048,512]{1,0:T(8,128)(2,1)}, u32[]{:S(2)}) copy-start(bf16[2048,512]{1,0:T(8,128)(2,1)} %param.20) | copy-start | bytes 6291460
  7.2 111.0 %all-gather.37.cloned.1.call-start = ((), (), s32[]{:S(2)}) async-start(), calls=%async_computation.39 | async-start | bytes 3276800 | tf_op jit(solution)/shard_map/all_gather | solution.py:153
  11.7 0.7 collective-permute-start
  13.3 54.0 %copy-start.101 = (f32[512]{0:T(512)S(1)}, f32[512]{0:T(512)}, u32[]{:S(2)}) copy-start(f32[512]{0:T(512)} %param.22) | copy-start | bytes 6148
  13.3 53.9 %copy-start.102 = (f32[512]{0:T(512)S(1)}, f32[512]{0:T(512)}, u32[]{:S(2)}) copy-start(f32[512]{0:T(512)} %param.21) | copy-start | bytes 6148
  16.3 78.3 %all-to-all-start = ((bf16[2,1,4,256,1,512]{5,3,0,4,1,2:T(8,128)(2,1)}), bf16[2,1,4,256,1,512]{5,3,0,4,1,2:T(8,128)(2,1)}, u32[]{:S(2)}, u32[]{:S(2)}) async-start(bf16[2,1,4,256,1,512]{5,3,0,4,1,2:T(8,128)(2,1)} %copy.149), calls=%async_computation | async-start | bytes 4194304 | tf_op jit(solution)/shard_map/all_to_all | solution.py:216
  67.2 104.1 %all-gather.21.cloned.1.call-start = ((), (), s32[]{:S(2)}) async-start(), calls=%async_computation.20 | async-start | bytes 5242880 | tf_op jit(solution)/shard_map/all_gather | solution.py:202
  94.7 409.3 %copy-start.64 = (f32[1,2048]{1,0:T(1,128)}, f32[1,2048]{1,0:T(1,128)S(1)}, u32[]{:S(2)}) copy-start(f32[1,2048]{1,0:T(1,128)S(1)} %get-tuple-element.384) | copy-start | bytes 24580
  118.2 70.5 %all-gather.39.cloned.1.call-start = ((), (), s32[]{:S(2)}) async-start(), calls=%async_computation.40 | async-start | bytes 7864320 | tf_op jit(solution)/shard_map/all_gather | solution.py:154
  122.7 122.0 %all-gather.23.cloned.1.call-start = ((), (), s32[]{:S(2)}) async-start(), calls=%async_computation.21 | async-start | bytes 5242880 | tf_op jit(solution)/shard_map/all_gather | solution.py:202
  135.2 61.2 %copy-start.34 = (f32[1024,32]{0,1:T(8,128)}, f32[1024,32]{0,1:T(8,128)S(1)}, u32[]{:S(2)}) copy-start(f32[1024,32]{0,1:T(8,128)S(1)} %get-tuple-element.397) | copy-start | bytes 393220
  135.2 117.2 %copy-start.32 = (f32[1024,32]{0,1:T(8,128)}, f32[1024,32]{0,1:T(8,128)S(1)}, u32[]{:S(2)}) copy-start(f32[1024,32]{0,1:T(8,128)S(1)} %get-tuple-element.392) | copy-start | bytes 393220
  171.3 130.3 %reduce-scatter.18.cloned.1.call-start = ((), (), s32[]{:S(2)}) async-start(), calls=%async_computation.22 | async-start | bytes 5242880 | tf_op jit(solution)/shard_map/reduce_scatter | solution.py:205
  191.6 46.5 %copy-start.25 = (bf16[4,2,256,1280]{3,2,1,0:T(8,128)(2,1)}, bf16[4,2,256,1280]{3,2,1,0:T(8,128)(2,1)S(1)}, u32[]{:S(2)}) copy-start(bf16[4,2,256,1280]{3,2,1,0:T(8,128)(2,1)S(1)} %copy.157) | copy-start | bytes 15728644
  196.1 28.6 %copy-start.38 = (bf16[1,1024,128]{1,2,0:T(8,128)(2,1)}, bf16[1,1024,128]{1,2,0:T(8,128)(2,1)S(1)}, u32[]{:S(2)}) copy-start(bf16[1,1024,128]{1,2,0:T(8,128)(2,1)S(1)} %slice.408) | copy-start | bytes 786436
  244.7 112.0 %reduce-scatter.20.cloned.1.call-start = ((), (), s32[]{:S(2)}) async-start(), calls=%async_computation.23 | async-start | bytes 5242880 | tf_op jit(solution)/shard_map/reduce_scatter | solution.py:205
  252.1 28.4 %copy-start.36 = (bf16[1,1024,128]{1,2,0:T(8,128)(2,1)}, bf16[1,1024,128]{1,2,0:T(8,128)(2,1)S(1)}, u32[]{:S(2)}) copy-start(bf16[1,1024,128]{1,2,0:T(8,128)(2,1)S(1)} %slice.407) | copy-start | bytes 786436
  301.6 110.1 %all-gather.45.cloned.1.call-start = ((), (), s32[]{:S(2)}) async-start(), calls=%async_computation.43 | async-start | bytes 5242880 | tf_op jit(solution)/shard_map/all_gather | solution.py:153
  303.2 198.5 %all-gather.41.cloned.1.call-start = ((), (), s32[]{:S(2)}) async-start(), calls=%async_computation.41 | async-start | bytes 10485760 | tf_op jit(solution)/shard_map/all_gather | solution.py:153
  306.5 278.1 %all-gather.25.cloned.1.call-start = ((), (), s32[]{:S(2)}) async-start(), calls=%async_computation.24 | async-start | bytes 5242880 | tf_op jit(solution)/shard_map/all_gather | solution.py:208
  356.7 248.2 %all-gather.47.cloned.1.call-start = ((), (), s32[]{:S(2)}) async-start(), calls=%async_computation.44 | async-start | bytes 12582912 | tf_op jit(solution)/shard_map/all_gather | solution.py:154
  417.9 219.8 %all-gather.43.cloned.1.call-start = ((), (), s32[]{:S(2)}) async-start(), calls=%async_computation.42 | async-start | bytes 25165824 | tf_op jit(solution)/shard_map/all_gather | solution.py:154
  501.7 220.0 %all-gather.27.cloned.1.call-start = ((), (), s32[]{:S(2)}) async-start(), calls=%async_computation.25 | async-start | bytes 5242880 | tf_op jit(solution)/shard_map/all_gather | solution.py:208
  584.6 215.3 %reduce-scatter.22.cloned.1.call-start = ((), (), s32[]{:S(2)}) async-start(), calls=%async_computation.26 | async-start | bytes 5242880 | tf_op jit(solution)/shard_map/reduce_scatter | solution.py:211
  637.7 43.7 %slice-start = ((s8[8388608]{0:T(1024)(128)(4,1)}), s8[4194304]{0:T(1024)(128)(4,1)S(1)}, s32[]{:S(2)}) async-start(s8[8388608]{0:T(1024)(128)(4,1)} %bitcast.328), calls=%async_computation.47 | async-start | bytes 8388608
  653.2 28.2 %slice-start.1 = ((s8[8388608]{0:T(1024)(128)(4,1)}), s8[4194304]{0:T(1024)(128)(4,1)S(1)}, s32[]{:S(2)}) async-start(s8[8388608]{0:T(1024)(128)(4,1)} %bitcast.328), calls=%async_computation.48 | async-start | bytes 8388608
  721.7 158.2 %reduce-scatter.24.cloned.1.call-start = ((), (), s32[]{:S(2)}) async-start(), calls=%async_computation.27 | async-start | bytes 5242880 | tf_op jit(solution)/shard_map/reduce_scatter | solution.py:211
  763.9 36.0 %copy-start.52 = (bf16[2,1,1024,512]{3,2,1,0:T(8,128)(2,1)S(1)}, bf16[2,1,1024,512]{3,2,1,0:T(8,128)(2,1)}, u32[]{:S(2)}) copy-start(bf16[2,1,1024,512]{3,2,1,0:T(8,128)(2,1)} %param.23) | copy-start | bytes 6291460
  799.9 163.3 %all-gather.29.cloned.1.call-start = ((), (), s32[]{:S(2)}) async-start(), calls=%async_computation.28 | async-start | bytes 5242880 | tf_op jit(solution)/shard_map/all_gather | solution.py:208
  835.7 44.8 %copy-start.18 = (f32[1,256,2048]{2,1,0:T(8,128)}, f32[1,256,2048]{2,1,0:T(8,128)S(1)}, u32[]{:S(2)}) copy-start(f32[1,256,2048]{2,1,0:T(8,128)S(1)} %reshape.1136) | copy-start | bytes 6291460
  879.9 164.5 %all-gather.31.cloned.1.call-start = ((), (), s32[]{:S(2)}) async-start(), calls=%async_computation.29 | async-start | bytes 5242880 | tf_op jit(solution)/shard_map/all_gather | solution.py:208
  884.7 78.5 %copy-start.6 = (f32[1,256,2048]{2,1,0:T(8,128)S(1)}, f32[1,256,2048]{2,1,0:T(8,128)}, u32[]{:S(2)}) copy-start(f32[1,256,2048]{2,1,0:T(8,128)} %reshape.1134) | copy-start | bytes 6291460
  884.7 78.5 %copy-start.13 = (bf16[1,256,2048]{2,1,0:T(8,128)(2,1)S(1)}, bf16[1,256,2048]{2,1,0:T(8,128)(2,1)}, u32[]{:S(2)}) copy-start(bf16[1,256,2048]{2,1,0:T(8,128)(2,1)} %reduce-scatter.18.cloned.1.call-done) | copy-start | bytes 3145732
  968.9 48.7 %all-to-all-start.1 = ((bf16[1,1,1,256,4,512]{5,3,2,1,0,4:T(8,128)(2,1)}), bf16[1,1,1,256,4,512]{5,3,2,1,0,4:T(8,128)(2,1)}, u32[]{:S(2)}, u32[]{:S(2)}) async-start(bf16[1,1,1,256,4,512]{5,3,2,1,0,4:T(8,128)(2,1)} %copy.165), calls=%async_computation.4 | async-start | bytes 2097152 | tf_op jit(solution)/shard_map/all_to_all | solution.py:222
  973.2 148.7 %reduce-scatter.26.cloned.1.call-start = ((), (), s32[]{:S(2)}) async-start(), calls=%async_computation.30 | async-start | bytes 5242880 | tf_op jit(solution)/shard_map/reduce_scatter | solution.py:211
  1017.7 26.8 %copy-start.3 = (f32[1,256,2048]{2,1,0:T(8,128)S(1)}, f32[1,256,2048]{2,1,0:T(8,128)}, u32[]{:S(2)}) copy-start(f32[1,256,2048]{2,1,0:T(8,128)} %reshape.1135) | copy-start | bytes 6291460
  1017.7 26.8 %copy-start.10 = (bf16[1,256,2048]{2,1,0:T(8,128)(2,1)S(1)}, bf16[1,256,2048]{2,1,0:T(8,128)(2,1)}, u32[]{:S(2)}) copy-start(bf16[1,256,2048]{2,1,0:T(8,128)(2,1)} %reduce-scatter.20.cloned.1.call-done) | copy-start | bytes 3145732
  1052.2 48.8 %all-to-all-start.3 = ((bf16[1,1,1,256,4,512]{5,3,2,1,0,4:T(8,128)(2,1)}), bf16[1,1,1,256,4,512]{5,3,2,1,0,4:T(8,128)(2,1)}, u32[]{:S(2)}, u32[]{:S(2)}) async-start(bf16[1,1,1,256,4,512]{5,3,2,1,0,4:T(8,128)(2,1)} %copy.169), calls=%async_computation.7 | async-start | bytes 2097152 | tf_op jit(solution)/shard_map/all_to_all | solution.py:222
  1056.5 145.5 %reduce-scatter.28.cloned.1.call-start = ((), (), s32[]{:S(2)}) async-start(), calls=%async_computation.31 | async-start | bytes 5242880 | tf_op jit(solution)/shard_map/reduce_scatter | solution.py:211
  1101.0 20.9 %copy-start.90 = (f32[256]{0:T(256)S(1)}, f32[256]{0:T(256)}, u32[]{:S(2)}) copy-start(f32[256]{0:T(256)} %copy-done.89) | copy-start | bytes 3076
  1121.9 135.6 %all-gather.33.cloned.1.call-start = ((), (), s32[]{:S(2)}) async-start(), calls=%async_computation.32 | async-start | bytes 5242880 | tf_op jit(solution)/shard_map/all_gather | solution.py:202
  1126.5 75.5 %copy-start.87 = (f32[256]{0:T(256)S(1)}, f32[256]{0:T(256)}, u32[]{:S(2)}) copy-start(f32[256]{0:T(256)} %copy-done.86) | copy-start | bytes 3076
  1202.0 152.5 %all-gather.35.cloned.1.call-start = ((), (), s32[]{:S(2)}) async-start(), calls=%async_computation.33 | async-start | bytes 5242880 | tf_op jit(solution)/shard_map/all_gather | solution.py:202
  1257.5 194.2 %reduce-scatter.30.cloned.1.call-start = ((), (), s32[]{:S(2)}) async-start(), calls=%async_computation.34 | async-start | bytes 5242880 | tf_op jit(solution)/shard_map/reduce_scatter | solution.py:205
  1285.9 29.0 %copy-start.49 = (bf16[1,1024,8,32]{1,3,2,0:T(8,128)(2,1)S(1)}, bf16[1,1024,8,32]{1,3,2,0:T(8,128)(2,1)}, u32[]{:S(2)}) copy-start(bf16[1,1024,8,32]{1,3,2,0:T(8,128)(2,1)} %copy-done.48) | copy-start | bytes 1572868
  1285.9 29.0 %copy-start.51 = (bf16[1,1024,8,32]{1,3,2,0:T(8,128)(2,1)S(1)}, bf16[1,1024,8,32]{1,3,2,0:T(8,128)(2,1)}, u32[]{:S(2)}) copy-start(bf16[1,1024,8,32]{1,3,2,0:T(8,128)(2,1)} %copy-done.50) | copy-start | bytes 1572868
  1354.6 259.1 %reduce-scatter.32.cloned.1.call-start = ((), (), s32[]{:S(2)}) async-start(), calls=%async_computation.35 | async-start | bytes 5242880 | tf_op jit(solution)/shard_map/reduce_scatter | solution.py:205
  1382.7 29.3 %copy-start.45 = (bf16[1,1024,8,32]{1,3,2,0:T(8,128)(2,1)S(1)}, bf16[1,1024,8,32]{1,3,2,0:T(8,128)(2,1)}, u32[]{:S(2)}) copy-start(bf16[1,1024,8,32]{1,3,2,0:T(8,128)(2,1)} %copy-done.44) | copy-start | bytes 1572868
  1382.7 29.3 %copy-start.47 = (bf16[1,1024,8,32]{1,3,2,0:T(8,128)(2,1)S(1)}, bf16[1,1024,8,32]{1,3,2,0:T(8,128)(2,1)}, u32[]{:S(2)}) copy-start(bf16[1,1024,8,32]{1,3,2,0:T(8,128)(2,1)} %copy-done.46) | copy-start | bytes 1572868
  1451.7 261.5 %reduce-scatter.38.cloned.1.call-start = ((), (), s32[]{:S(2)}) async-start(), calls=%async_computation.38 | async-start | bytes 25165824 | tf_op jit(solution)/shard_map/reduce_scatter | solution.py:173
  1501.4 217.8 %reduce-scatter.36.cloned.1.call-start = ((), (), s32[]{:S(2)}) async-start(), calls=%async_computation.37 | async-start | bytes 50331648 | tf_op jit(solution)/shard_map/reduce_scatter | solution.py:173
  1630.2 49.4 %all-to-all-start.4 = ((f32[1,1,1,256,4,512]{5,3,2,1,0,4:T(8,128)}), f32[1,1,1,256,4,512]{5,3,2,1,0,4:T(8,128)}, u32[]{:S(2)}, u32[]{:S(2)}) async-start(f32[1,1,1,256,4,512]{5,3,2,1,0,4:T(8,128)} %copy.176), calls=%async_computation.11 | async-start | bytes 4194304 | tf_op jit(solution)/shard_map/all_to_all | solution.py:222
  1634.7 97.6 %reduce-scatter.34.cloned.1.call-start = ((), (), s32[]{:S(2)}) async-start(), calls=%async_computation.36 | async-start | bytes 17301504 | tf_op jit(solution)/shard_map/reduce_scatter | solution.py:182
  1713.2 76.4 %reduce-scatter.42.cloned.1.call-start = ((), (), s32[]{:S(2)}) async-start(), calls=%async_computation.46 | async-start | bytes 5242880
  1719.1 159.8 %reduce-scatter.40.cloned.1.call-start = ((), (), s32[]{:S(2)}) async-start(), calls=%async_computation.45 | async-start | bytes 10485760
  1736.8 146.2 %all-to-all-start.6 = ((bf16[4,256,1408]{2,1,0:T(8,128)(2,1)}), bf16[4,256,1408]{2,1,0:T(8,128)(2,1)}, u32[]{:S(2)}, u32[]{:S(2)}) async-start(bf16[4,256,1408]{2,1,0:T(8,128)(2,1)} %convert_bitcast_fusion.6), calls=%async_computation.15 | async-start | bytes 5767168 | tf_op jit(solution)/shard_map/all_to_all | solution.py:183
  1792.3 106.7 %copy-start.11 = (bf16[1,256,2048]{2,1,0:T(8,128)(2,1)S(1)}, bf16[1,256,2048]{2,1,0:T(8,128)(2,1)}, u32[]{:S(2)}) copy-start(bf16[1,256,2048]{2,1,0:T(8,128)(2,1)} %reduce-scatter.20.cloned.1.call-done) | copy-start | bytes 3145732
  1792.3 106.7 %copy-start.88 = (f32[256]{0:T(256)S(1)}, f32[256]{0:T(256)}, u32[]{:S(2)}) copy-start(f32[256]{0:T(256)} %copy-done.86) | copy-start | bytes 3076
  1792.3 106.7 %copy-start.97 = (f32[256]{0:T(256)S(1)}, f32[256]{0:T(256)}, u32[]{:S(2)}) copy-start(f32[256]{0:T(256)} %copy-done.96) | copy-start | bytes 3076
  1792.3 121.5 %collective-permute-start.4 = (f32[2048,256]{1,0:T(8,128)}, f32[2048,256]{1,0:T(8,128)}, u32[]{:S(2)}, u32[]{:S(2)}) collective-permute-start(f32[2048,256]{1,0:T(8,128)} %bitcast_convert_fusion.1), channel_id=1, source_target_pairs={{0,16},{16,0},{1,17},{17,1},{2,18},{18,2},{3,19},{19,3},{4,20},{20... | collective-permute-start | bytes 6291464 | tf_op jit(solution)/shard_map/ppermute | solution.py:189
  1883.0 92.7 %collective-permute-start.3 = (f32[256,4096]{1,0:T(8,128)}, f32[256,4096]{1,0:T(8,128)}, u32[]{:S(2)}, u32[]{:S(2)}) collective-permute-start(f32[256,4096]{1,0:T(8,128)} %bitcast_convert_fusion), channel_id=1, source_target_pairs={{0,16},{16,0},{1,17},{17,1},{2,18},{18,2},{3,19},{19,3},{4,20},{20... | collective-permute-start | bytes 12582920 | tf_op jit(solution)/shard_map/ppermute | solution.py:189
  1886.6 23.6 %collective-permute-start.1 = (f32[256,1408]{1,0:T(8,128)}, f32[256,1408]{1,0:T(8,128)}, u32[]{:S(2)}, u32[]{:S(2)}) collective-permute-start(f32[256,1408]{1,0:T(8,128)} %convert_reduce_fusion), channel_id=1, source_target_pairs={{0,0},{1,4},{2,8},{3,12},{4,1},{5,5},{6,9},{7,13},{8,2},{9,6},{10,... | collective-permute-start | bytes 4325384 | tf_op jit(solution)/shard_map/ppermute | solution.py:199
  1906.5 57.3 %all-to-all-start.5 = ((f32[1,1,1,256,4,512]{5,3,2,1,0,4:T(8,128)}), f32[1,1,1,256,4,512]{5,3,2,1,0,4:T(8,128)S(1)}, u32[]{:S(2)}, u32[]{:S(2)}) async-start(f32[1,1,1,256,4,512]{5,3,2,1,0,4:T(8,128)} %copy.177), calls=%async_computation.13 | async-start | bytes 4194304 | tf_op jit(solution)/shard_map/all_to_all | solution.py:222
  1910.3 57.6 %collective-permute-start.2 = (f32[256,1408]{1,0:T(8,128)}, f32[256,1408]{1,0:T(8,128)}, u32[]{:S(2)}, u32[]{:S(2)}) collective-permute-start(f32[256,1408]{1,0:T(8,128)} %collective-permute-done.1), channel_id=1, source_target_pairs={{0,16},{16,0},{1,17},{17,1},{2,18},{18,2},{3,19},{19,3},{4,20},{20... | collective-permute-start | bytes 4325384 | tf_op jit(solution)/shard_map/ppermute | solution.py:189
  (84 other events, 603.3 us)
Sparse Core Ops, SparseCore 0:
  13.4 103.2 all-gather.36
  119.1 52.1 all-gather.20
  173.4 15.1 all-gather.38
  190.9 53.7 all-gather.22
  248.1 52.5 reduce-scatter.17
  304.1 52.5 reduce-scatter.19
  359.1 52.5 all-gather.44
  414.1 87.4 all-gather.40
  503.8 80.7 all-gather.24
  586.5 18.3 all-gather.46
  606.5 31.2 all-gather.42
  639.7 81.9 all-gather.26
  724.5 75.2 reduce-scatter.21
  802.6 77.2 reduce-scatter.23
  881.9 81.2 all-gather.28
  965.2 79.2 all-gather.30
  1046.6 75.2 reduce-scatter.25
  1124.6 77.2 reduce-scatter.27
  1204.4 53.0 all-gather.32
  1259.8 52.5 all-gather.34
  1354.7 52.4 reduce-scatter.29
  1451.9 52.5 reduce-scatter.31
  1506.7 25.0 reduce-scatter.37
  1586.2 43.0 reduce-scatter.35
  1713.3 18.9 reduce-scatter.33
  1735.7 53.8 reduce-scatter.41
  1792.5 86.3 reduce-scatter.39

commit v12 on v10

--- a/solution.py
+++ b/solution.py
@@ -258,8 +258,9 @@
         places = positions(segments)
         token_place = jnp.broadcast_to(jnp.arange(seq_len), (local, seq_len))
 
-        hidden_t = to_tokens(hidden_in)
-        cotangent_t = to_tokens(cotangent)
+        hidden_t, cotangent_t = to_tokens(jnp.concatenate([hidden_in, cotangent], axis=1)).reshape(
+            (batches, 2, local, chunk, width_r * n_row)
+        ).transpose(1, 0, 2, 3, 4)
 
         def micro_batch(batch_index):
             rows_f = hidden_t[batch_index].astype(jnp.float32)

time: 2030 us -> 2020 us (level)
  waiting for transfers between devices: 902 us -> 945 us
  starting transfers between devices: 78.2 us -> 35.9 us
    all_to_all x1, starting transfers between devices: 50.9 us -> 10 us  [to_tokens(): rows = lax.all_to_all(rows, 'row', 2, 3)]
    reduce_scatter x4, waiting for transfers between devices: 172 us -> 212 us  [scatter_seqs(): return lax.psum_scatter(rows, 'col', scatter_dimension=0, tiled=True)]
    all_gather x1, blocking collectives: 27.4 us -> 66.9 us  [shards(): lax.all_gather(jnp.stack([gain_attn, gain_ffn]), 'row', axis=1, tiled=True)]
    all_to_all x1 -> x0, blocking collectives: 28.5 us -> none  [to_tokens(): rows = lax.all_to_all(rows, 'row', 2, 3)]
    convert_element_type x8 -> x0, local copies, waits for them, and re-layouts: 27.7 us -> none  [the longest x4 14.3 us: micro_batch(): rows_f = hidden_t[batch_index].astype(jnp.float32)]
  transfers between devices with their start and end apart: 38 -> 38, of which waited for: 22 -> 23; matrix products, arithmetic and copies ran while one was open for 44% -> 43% of each run, Pallas kernels for 0% -> 0%
where the time goes in v12:
time: 2020 us; the launch traced here: 2010 us
  waiting for transfers between devices  945 us (47%)
  matrix products  482 us (24%)
  local copies, waits for them, and re-layouts  220 us (11%)
  other arithmetic  211 us (10%)
  blocking collectives  98.6 us (5%)
  starting transfers between devices  35.9 us (2%)
    reduce_scatter x4, waiting for transfers between devices, scatter_seqs(): return lax.psum_scatter(rows, 'col', scatter_dimension=0, tiled=True)  212 us
    all_gather x4, waiting for transfers between devices, gather_seqs(): return lax.all_gather(rows, 'col', axis=0, tiled=True)  210 us
    unnamed x32, waiting for transfers between devices  175 us
    all_gather x3, waiting for transfers between devices, gather_half(): gathered = lax.all_gather(mine, axis_name, axis=axis)  139 us
    all_gather x4, waiting for transfers between devices, gather_tokens(): return lax.all_gather(rows, 'row', axis=1, tiled=True)  85.7 us
    all_gather x1, blocking collectives, shards(): lax.all_gather(jnp.stack([gain_attn, gain_ffn]), 'row', axis=1, tiled=True)  66.9 us
    dot_general x2, matrix products, micro_batch(): jnp.einsum('std,stf->df', spread_ffn, paired_gradient, preferred_element_...  61.8 us
    convert_element_type x2, other arithmetic, attend_backward(): grad_scores = (attn_probs * (grad_probs - jnp.sum(attn_probs * grad_probs...  58.3 us
  transfers between devices with their start and end apart: 38, of which 23 were waited for; matrix products, arithmetic and copies ran while one was open for 43% of the time, Pallas kernels for 0%

profile of v12, /device:TPU:0, one launch (start us, length us, event | category | flops | bytes accessed | tf_op | source)
XLA Modules:
  0.0 2009.5 jit_solution(10078457554873847648)
XLA Ops:
  17.4 10.0 all-to-all-start
  28.4 66.9 %all_gather.75 = f32[2,2048]{1,0:T(2,128)S(1)} all-gather(f32[2,512]{1,0:T(2,128)S(1)} %pad_maximum_fusion.30), channel_id=1, replica_groups=mesh['dp'=2,'row'=4,'col'=4] {'row'}, dimensions={1}, use_global_device_ids=true | all-gather | bytes 20480 | tf_op jit(solution)/shard_map/all_gather | solution.py:252
  95.3 7.4 copy.144
  102.8 7.7 reshape_reshape_squeeze.3
  121.3 8.3 all_gather.78
  134.3 35.8 %all-gather.26.cloned.1.call-done = bf16[1,1024,2048]{2,1,0:T(8,128)(2,1)} async-done(((bf16[1,256,2048]{2,1,0:T(8,128)(2,1)}), bf16[1,1024,2048]{2,1,0:T(8,128)(2,1)}) %all-gather.26.cloned.1.call-update) | async-done | bytes 4194320 | tf_op jit(solution)/shard_map/all_gather | solution.py:193
  170.4 17.1 all-gather.46.cloned.1.call-done
  196.3 13.7 fusion.141
  210.0 13.4 exponential_reduce_fusion.1
  223.5 13.4 fusion.88
  251.5 14.2 fusion.142
  265.8 13.5 exponential_reduce_fusion
  279.3 14.1 fusion.91
  309.9 45.7 %reduce-scatter.20.cloned.1.call-done = bf16[1,256,2048]{2,1,0:T(8,128)(2,1)} async-done(((bf16[1,1024,2048]{2,1,0:T(8,128)(2,1)}), bf16[1,256,2048]{2,1,0:T(8,128)(2,1)}) %reduce-scatter.20.cloned.1.call-update) | async-done | bytes 1048592 | tf_op jit(solution)/shard_map/reduce_scatter | solution.py:196
  355.7 54.9 %all-gather.52.cloned.1.call-done = bf16[2048,1024]{0,1:T(8,128)(2,1)} async-done(((bf16[2048,256]{0,1:T(8,128)(2,1)}), bf16[2048,1024]{0,1:T(8,128)(2,1)}) %all-gather.52.cloned.1.call-update) | async-done | bytes 4194320 | tf_op jit(solution)/shard_map/all_gather | solution.py:153
  416.9 83.7 %all-gather.48.cloned.1.call-done = bf16[1024,4096]{1,0:T(8,128)(2,1)} async-done(((bf16[256,4096]{1,0:T(8,128)(2,1)}), bf16[1024,4096]{1,0:T(8,128)(2,1)}) %all-gather.48.cloned.1.call-update) | async-done | bytes 8388624 | tf_op jit(solution)/shard_map/all_gather | solution.py:153
  507.7 75.7 %all-gather.30.cloned.1.call-done = bf16[4,256,2048]{2,1,0:T(8,128)(2,1)} async-done(((bf16[1,256,2048]{2,1,0:T(8,128)(2,1)}), bf16[4,256,2048]{2,1,0:T(8,128)(2,1)}) %all-gather.30.cloned.1.call-update) | async-done | bytes 4194320 | tf_op jit(solution)/shard_map/all_gather | solution.py:199
  583.5 20.3 %all-gather.54.cloned.1.call-done = bf16[2048,8,256]{2,0,1:T(8,128)(2,1)} async-done(((bf16[2048,4,256]{2,0,1:T(8,128)(2,1)}), bf16[2048,8,256]{2,0,1:T(8,128)(2,1)}) %all-gather.54.cloned.1.call-update) | async-done | bytes 8388624 | tf_op jit(solution)/shard_map/all_gather | solution.py:154
  603.8 16.4 copy.157
  620.2 15.2 reshape.1164
  636.6 15.5 copy.154
  652.1 20.4 %fusion.143 = f32[4,256,4096]{2,1,0:T(8,128)S(1)} fusion(bf16[4,256,2048]{2,1,0:T(8,128)(2,1)S(1)} %copy-done.98, bf16[2048,4096,1]{1,0,2:T(8,128)(2,1)} %bitcast.395), kind=kOutput, calls=%fused_computation.260 | convolution fusion | flops 17179869184 | bytes 37748736 | tf_op jit(solution)/shard_map/std,df->stf/dot_general | solution.py:308
  680.4 10.4 convolution_convert_fusion.1
  690.8 29.8 %all-gather.32.cloned.1.call-done = bf16[4,256,2048]{2,1,0:T(8,128)(2,1)} async-done(((bf16[1,256,2048]{2,1,0:T(8,128)(2,1)}), bf16[4,256,2048]{2,1,0:T(8,128)(2,1)}) %all-gather.32.cloned.1.call-update) | async-done | bytes 4194320 | tf_op jit(solution)/shard_map/all_gather | solution.py:199
  720.8 21.5 %fusion.144 = f32[4,256,4096]{2,1,0:T(8,128)S(1)} fusion(bf16[4,256,2048]{2,1,0:T(8,128)(2,1)} %all-gather.32.cloned.1.call-done, bf16[2048,4096,1]{1,0,2:T(8,128)(2,1)} %bitcast.396), kind=kOutput, calls=%fused_computation.261 | convolution fusion | flops 17179869184 | bytes 37748736 | tf_op jit(solution)/shard_map/std,df->stf/dot_general | solution.py:308
  750.2 12.5 convolution_convert_fusion
  762.7 36.0 %reduce-scatter.22.cloned.1.call-done = bf16[1,256,2048]{2,1,0:T(8,128)(2,1)} async-done(((bf16[4,256,2048]{2,1,0:T(8,128)(2,1)}), bf16[1,256,2048]{2,1,0:T(8,128)(2,1)}) %reduce-scatter.22.cloned.1.call-update) | async-done | bytes 1048592 | tf_op jit(solution)/shard_map/reduce_scatter | solution.py:202
  798.8 80.0 %reduce-scatter.24.cloned.1.call-done = bf16[1,256,2048]{2,1,0:T(8,128)(2,1)} async-done(((bf16[4,256,2048]{2,1,0:T(8,128)(2,1)}), bf16[1,256,2048]{2,1,0:T(8,128)(2,1)}) %reduce-scatter.24.cloned.1.call-update) | async-done | bytes 1048592 | tf_op jit(solution)/shard_map/reduce_scatter | solution.py:202
  884.6 77.5 %all-gather.34.cloned.1.call-done = bf16[4,256,2048]{2,1,0:T(8,128)(2,1)} async-done(((bf16[1,256,2048]{2,1,0:T(8,128)(2,1)}), bf16[4,256,2048]{2,1,0:T(8,128)(2,1)}) %all-gather.34.cloned.1.call-update) | async-done | bytes 4194320 | tf_op jit(solution)/shard_map/all_gather | solution.py:199
  971.8 20.5 %multiply_convert_fusion.3 = (bf16[4,256,2048]{2,1,0:T(8,128)(2,1)}, bf16[4,256,2048]{2,1,0:T(8,128)(2,1)}) fusion(f32[4,256,4096]{2,1,0:T(8,128)} %copy-done.8, bf16[4,256,2048]{2,1,0:T(8,128)(2,1)} %all-gather.34.cloned.1.call-done, bf16[2048,2048,1]{1,0,2:T(8,128)(2,1)} %reshape.1164), kind=kOutput, calls=%fused_computation.30 | convolution fusion | flops 8617197568 | bytes 37748736 | tf_op jit(solution)/shard_map/std,fd->stf/dot_general | solution.py:329
  992.3 23.9 %fusion.37 = bf16[4,256,2048]{2,1,0:T(8,128)(2,1)} fusion(bf16[2048,4096,1]{1,0,2:T(8,128)(2,1)} %bitcast.397, bf16[4,256,2048]{2,1,0:T(8,128)(2,1)} %get-tuple-element.351, bf16[4,256,2048]{2,1,0:T(8,128)(2,1)} %get-tuple-element.350), kind=kOutput, calls=%fused_computation.71 | convolution fusion | flops 17198743552 | bytes 29360128 | tf_op jit(solution)/shard_map/stf,df->std/dot_general | solution.py:342
  1016.3 27.1 %all-gather.36.cloned.1.call-done = bf16[4,256,2048]{2,1,0:T(8,128)(2,1)} async-done(((bf16[1,256,2048]{2,1,0:T(8,128)(2,1)}), bf16[4,256,2048]{2,1,0:T(8,128)(2,1)}) %all-gather.36.cloned.1.call-update) | async-done | bytes 4194320 | tf_op jit(solution)/shard_map/all_gather | solution.py:199
  1051.1 20.3 %multiply_convert_fusion.1 = (bf16[4,256,2048]{2,1,0:T(8,128)(2,1)}, bf16[4,256,2048]{2,1,0:T(8,128)(2,1)}) fusion(f32[4,256,4096]{2,1,0:T(8,128)} %copy-done.7, bf16[4,256,2048]{2,1,0:T(8,128)(2,1)} %all-gather.36.cloned.1.call-done, bf16[2048,2048,1]{1,0,2:T(8,128)(2,1)} %reshape.1164), kind=kOutput, calls=%fused_computation.28 | convolution fusion | flops 8617197568 | bytes 37748736 | tf_op jit(solution)/shard_map/std,fd->stf/dot_general | solution.py:329
  1071.5 23.8 %fusion.38 = bf16[4,256,2048]{2,1,0:T(8,128)(2,1)} fusion(bf16[2048,4096,1]{1,0,2:T(8,128)(2,1)} %bitcast.398, bf16[4,256,2048]{2,1,0:T(8,128)(2,1)} %get-tuple-element.349, bf16[4,256,2048]{2,1,0:T(8,128)(2,1)} %get-tuple-element.348), kind=kOutput, calls=%fused_computation.72 | convolution fusion | flops 17198743552 | bytes 29360128 | tf_op jit(solution)/shard_map/stf,df->std/dot_general | solution.py:342
  1096.3 24.5 %reduce-scatter.26.cloned.1.call-done = bf16[1,256,2048]{2,1,0:T(8,128)(2,1)} async-done(((bf16[4,256,2048]{2,1,0:T(8,128)(2,1)}), bf16[1,256,2048]{2,1,0:T(8,128)(2,1)}) %reduce-scatter.26.cloned.1.call-update) | async-done | bytes 1048592 | tf_op jit(solution)/shard_map/reduce_scatter | solution.py:202
  1129.0 71.9 %reduce-scatter.28.cloned.1.call-done = bf16[1,256,2048]{2,1,0:T(8,128)(2,1)} async-done(((bf16[4,256,2048]{2,1,0:T(8,128)(2,1)}), bf16[1,256,2048]{2,1,0:T(8,128)(2,1)}) %reduce-scatter.28.cloned.1.call-update) | async-done | bytes 1048592 | tf_op jit(solution)/shard_map/reduce_scatter | solution.py:202
  1207.7 48.6 %all-gather.38.cloned.1.call-done = bf16[1,1024,2048]{2,1,0:T(8,128)(2,1)} async-done(((bf16[1,256,2048]{2,1,0:T(8,128)(2,1)}), bf16[1,1024,2048]{2,1,0:T(8,128)(2,1)}) %all-gather.38.cloned.1.call-update) | async-done | bytes 4194320 | tf_op jit(solution)/shard_map/all_gather | solution.py:193
  1261.8 23.0 %fusion.3 = (f32[2,4,1024]{2,1,0:T(4,128)S(1)}, f32[2,1024,1024,4]{2,1,3,0:T(8,128)}) fusion(f32[2,4,1024,1024]{2,3,1,0:T(8,128)} %get-tuple-element.397, f32[2,4,1024]{2,1,0:T(4,128)S(1)} %bitcast.438, bf16[1024,2,64,1]{0,2,3,1:T(8,128)(2,1)S(1)} %bitcast.432, bf16[1024,2,4,64]{0,3,2,1:T(8,128)(2,1)S(1)} %bitcast.422), kind=kOutput, calls=%fused_computation.8 | convolution fusion | flops 1098899456 | bytes 68485120 | tf_op jit(solution)/shard_map/while/body/eval_jaxpr/qkgd,pkd->kgqp/dot_general | solution.py:85
  1284.8 29.0 %fusion.5 = bf16[2,4,1024,1024]{2,3,1,0:T(8,128)(2,1)} fusion(f32[2,1024,1024,4]{2,1,3,0:T(8,128)} %get-tuple-element.401, f32[2,4,1024,1024]{2,3,1,0:T(8,128)} %get-tuple-element.397, f32[2,4,1024]{2,1,0:T(4,128)S(1)} %get-tuple-element.400, f32[2,4,1024]{2,1,0:T(4,128)S(1)} %bitcast.439), kind=kLoop, calls=%fused_computation.10 | loop fusion | flops 33554432 | bytes 83951616 | tf_op jit(solution)/shard_map/while/body/eval_jaxpr/convert_element_type | solution.py:96
  1313.7 8.7 fusion.107
  1322.5 13.3 fusion.108
  1336.7 8.9 convolution_multiply_fusion.1
  1358.8 22.8 %fusion = (f32[2,4,1024]{2,1,0:T(4,128)S(1)}, f32[2,1024,1024,4]{2,1,3,0:T(8,128)}) fusion(f32[2,4,1024,1024]{2,3,1,0:T(8,128)} %get-tuple-element.399, f32[2,4,1024]{2,1,0:T(4,128)S(1)} %bitcast.434, bf16[1024,2,64,1]{0,2,3,1:T(8,128)(2,1)S(1)} %bitcast.430, bf16[1024,2,4,64]{0,3,2,1:T(8,128)(2,1)S(1)} %bitcast.424), kind=kOutput, calls=%fused_computation.3 | convolution fusion | flops 1098899456 | bytes 68485120 | tf_op jit(solution)/shard_map/while/body/eval_jaxpr/qkgd,pkd->kgqp/dot_general | solution.py:85
  1381.6 29.3 %fusion.2 = bf16[2,4,1024,1024]{2,3,1,0:T(8,128)(2,1)} fusion(f32[2,1024,1024,4]{2,1,3,0:T(8,128)} %get-tuple-element.403, f32[2,4,1024,1024]{2,3,1,0:T(8,128)} %get-tuple-element.399, f32[2,4,1024]{2,1,0:T(4,128)S(1)} %get-tuple-element.402, f32[2,4,1024]{2,1,0:T(4,128)S(1)} %bitcast.435), kind=kLoop, calls=%fused_computation.5 | loop fusion | flops 33554432 | bytes 83951616 | tf_op jit(solution)/shard_map/while/body/eval_jaxpr/convert_element_type | solution.py:96
  1411.0 8.7 fusion.106
  1419.7 13.3 fusion.111
  1433.9 8.9 convolution_multiply_fusion
  1450.7 15.7 fusion.145
  1466.4 17.6 bitcast_add_fusion.1
  1483.9 16.4 copy.174
  1500.4 28.9 %fusion.9 = f32[2048,4096,1]{1,0,2:T(8,128)} fusion(bf16[4,256,2048]{2,1,0:T(8,128)(2,1)} %all-gather.30.cloned.1.call-done, bf16[4,256,2048]{2,1,0:T(8,128)(2,1)} %get-tuple-element.351, bf16[4,256,2048]{2,1,0:T(8,128)(2,1)} %get-tuple-element.350), kind=kOutput, calls=%fused_computation.37 | convolution fusion | flops 17196646400 | bytes 46137344 | tf_op jit(solution)/shard_map/std,stf->df/dot_general | solution.py:339
  1529.3 32.9 %bitcast_add_fusion = f32[2048,4096]{1,0:T(8,128)} fusion(f32[2048,4096,1]{1,0,2:T(8,128)} %fusion.9, bf16[4,256,2048]{2,1,0:T(8,128)(2,1)} %all-gather.32.cloned.1.call-done, bf16[4,256,2048]{2,1,0:T(8,128)(2,1)} %get-tuple-element.349, bf16[4,256,2048]{2,1,0:T(8,128)(2,1)} %get-tuple-element.348), kind=kOutput, calls=%fused_computation | convolution fusion | flops 17205035008 | bytes 79691776 | tf_op jit(solution)/shard_map/std,stf->df/dot_general | solution.py:339
  1562.2 22.8 %copy.200 = f32[4,2,256,4096]{3,2,0,1:T(8,128)} copy(f32[4,2,256,4096]{3,2,1,0:T(8,128)} %bitcast.392) | data formatting | bytes 67108864 | tf_op jit(solution)/shard_map/reshape | solution.py:172
  1628.6 11.3 maximum_add_fusion
  1640.0 23.5 %psum.7 = f32[2048,2]{0,1:T(2,128)S(1)} all-reduce(f32[2048,2]{0,1:T(2,128)S(1)} %pad_maximum_fusion.29), channel_id=1, replica_groups=mesh['dp'=2,'row'=4,'col'=4] {'row'}, use_global_device_ids=true, to_apply=%region_27.28 | all-reduce | flops 4096 | bytes 32768 | tf_op jit(solution)/shard_map/psum | solution.py:422
  1663.5 10.0 select_maximum_fusion
  1673.4 16.6 reshape.1142
  1690.0 17.8 copy.168
  1713.8 13.0 convert_bitcast_fusion
  1737.5 46.8 %reduce-scatter.42.cloned.1.call-done = bf16[2048,1,256]{2,0,1:T(8,128)(2,1)} async-done(((bf16[2048,4,256]{2,0,1:T(8,128)(2,1)}), bf16[2048,1,256]{2,0,1:T(8,128)(2,1)}) %reduce-scatter.42.cloned.1.call-update) | async-done | bytes 1048592
  1787.1 15.9 all-to-all-done.5
  1807.5 127.9 %reduce-scatter.40.cloned.1.call-done = bf16[1,256,4096]{2,1,0:T(8,128)(2,1)} async-done(((bf16[4,256,4096]{2,1,0:T(8,128)(2,1)}), bf16[1,256,4096]{2,1,0:T(8,128)(2,1)}) %reduce-scatter.40.cloned.1.call-update) | async-done | bytes 2097168
  1956.1 22.3 %all-to-all-done.4 = f32[1,1,1,256,4,512]{5,3,2,1,0,4:T(8,128)} async-done(((f32[1,1,1,256,4,512]{5,3,2,1,0,4:T(8,128)}), f32[1,1,1,256,4,512]{5,3,2,1,0,4:T(8,128)}, u32[]{:S(2)}, u32[]{:S(2)}) %all-to-all-start.4) | async-done | bytes 2097184 | tf_op jit(solution)/shard_map/all_to_all | solution.py:213
  1991.3 8.1 fusion.138
  (405 shorter events, 268.4 us)
Async XLA Ops:
  7.2 293.3 %copy-start = (bf16[2048,512]{1,0:T(8,128)(2,1)S(1)}, bf16[2048,512]{1,0:T(8,128)(2,1)}, u32[]{:S(2)}) copy-start(bf16[2048,512]{1,0:T(8,128)(2,1)} %param.20) | copy-start | bytes 6291460
  11.6 15.8 collective-permute-start
  17.4 77.9 %all-to-all-start = ((bf16[2,2,4,256,1,512]{5,3,0,1,4,2:T(8,128)(2,1)}), bf16[2,2,4,256,1,512]{5,3,0,1,4,2:T(8,128)(2,1)}, u32[]{:S(2)}, u32[]{:S(2)}) async-start(bf16[2,2,4,256,1,512]{5,3,0,1,4,2:T(8,128)(2,1)} %copy.143), calls=%async_computation | async-start | bytes 8388608 | tf_op jit(solution)/shard_map/all_to_all | solution.py:207
  27.5 89.4 %all-gather.44.cloned.1.call-start = ((), (), s32[]{:S(2)}) async-start(), calls=%async_computation.39 | async-start | bytes 3276800 | tf_op jit(solution)/shard_map/all_gather | solution.py:153
  28.3 141.8 %all-gather.26.cloned.1.call-start = ((), (), s32[]{:S(2)}) async-start(), calls=%async_computation.19 | async-start | bytes 5242880 | tf_op jit(solution)/shard_map/all_gather | solution.py:193
  95.3 17.3 copy-start.74
  95.3 408.2 %copy-start.56 = (f32[1,2048]{1,0:T(1,128)}, f32[1,2048]{1,0:T(1,128)S(1)}, u32[]{:S(2)}) copy-start(f32[1,2048]{1,0:T(1,128)S(1)} %get-tuple-element.383) | copy-start | bytes 24580
  116.0 71.4 %all-gather.46.cloned.1.call-start = ((), (), s32[]{:S(2)}) async-start(), calls=%async_computation.40 | async-start | bytes 7864320 | tf_op jit(solution)/shard_map/all_gather | solution.py:154
  121.2 122.3 %all-gather.28.cloned.1.call-start = ((), (), s32[]{:S(2)}) async-start(), calls=%async_computation.20 | async-start | bytes 5242880 | tf_op jit(solution)/shard_map/all_gather | solution.py:193
  132.7 62.5 %copy-start.26 = (f32[1024,32]{0,1:T(8,128)}, f32[1024,32]{0,1:T(8,128)S(1)}, u32[]{:S(2)}) copy-start(f32[1024,32]{0,1:T(8,128)S(1)} %get-tuple-element.393) | copy-start | bytes 393220
  132.7 118.5 %copy-start.24 = (f32[1024,32]{0,1:T(8,128)}, f32[1024,32]{0,1:T(8,128)S(1)}, u32[]{:S(2)}) copy-start(f32[1024,32]{0,1:T(8,128)S(1)} %get-tuple-element.388) | copy-start | bytes 393220
  170.1 130.3 %reduce-scatter.18.cloned.1.call-start = ((), (), s32[]{:S(2)}) async-start(), calls=%async_computation.21 | async-start | bytes 5242880 | tf_op jit(solution)/shard_map/reduce_scatter | solution.py:196
  190.5 46.5 %copy-start.15 = (bf16[4,2,256,1280]{3,2,1,0:T(8,128)(2,1)}, bf16[4,2,256,1280]{3,2,1,0:T(8,128)(2,1)S(1)}, u32[]{:S(2)}) copy-start(bf16[4,2,256,1280]{3,2,1,0:T(8,128)(2,1)S(1)} %copy.150) | copy-start | bytes 15728644
  194.9 28.6 %copy-start.30 = (bf16[1,1024,128]{1,2,0:T(8,128)(2,1)}, bf16[1,1024,128]{1,2,0:T(8,128)(2,1)S(1)}, u32[]{:S(2)}) copy-start(bf16[1,1024,128]{1,2,0:T(8,128)(2,1)S(1)} %slice.433) | copy-start | bytes 786436
  243.5 112.0 %reduce-scatter.20.cloned.1.call-start = ((), (), s32[]{:S(2)}) async-start(), calls=%async_computation.22 | async-start | bytes 5242880 | tf_op jit(solution)/shard_map/reduce_scatter | solution.py:196
  250.9 28.4 %copy-start.28 = (bf16[1,1024,128]{1,2,0:T(8,128)(2,1)}, bf16[1,1024,128]{1,2,0:T(8,128)(2,1)S(1)}, u32[]{:S(2)}) copy-start(bf16[1,1024,128]{1,2,0:T(8,128)(2,1)S(1)} %slice.432) | copy-start | bytes 786436
  300.4 110.2 %all-gather.52.cloned.1.call-start = ((), (), s32[]{:S(2)}) async-start(), calls=%async_computation.43 | async-start | bytes 5242880 | tf_op jit(solution)/shard_map/all_gather | solution.py:153
  302.0 198.5 %all-gather.48.cloned.1.call-start = ((), (), s32[]{:S(2)}) async-start(), calls=%async_computation.41 | async-start | bytes 10485760 | tf_op jit(solution)/shard_map/all_gather | solution.py:153
  305.2 278.2 %all-gather.30.cloned.1.call-start = ((), (), s32[]{:S(2)}) async-start(), calls=%async_computation.23 | async-start | bytes 5242880 | tf_op jit(solution)/shard_map/all_gather | solution.py:199
  307.2 109.6 %copy-start.78 = (f32[256]{0:T(256)}, f32[256]{0:T(256)S(1)}, u32[]{:S(2)}) copy-start(f32[256]{0:T(256)S(1)} %add_rsqrt_fusion.1) | copy-start | bytes 3076
  355.6 248.2 %all-gather.54.cloned.1.call-start = ((), (), s32[]{:S(2)}) async-start(), calls=%async_computation.44 | async-start | bytes 12582912 | tf_op jit(solution)/shard_map/all_gather | solution.py:154
  416.8 219.8 %all-gather.50.cloned.1.call-start = ((), (), s32[]{:S(2)}) async-start(), calls=%async_computation.42 | async-start | bytes 25165824 | tf_op jit(solution)/shard_map/all_gather | solution.py:154
  500.6 220.0 %all-gather.32.cloned.1.call-start = ((), (), s32[]{:S(2)}) async-start(), calls=%async_computation.24 | async-start | bytes 5242880 | tf_op jit(solution)/shard_map/all_gather | solution.py:199
  583.5 215.3 %reduce-scatter.22.cloned.1.call-start = ((), (), s32[]{:S(2)}) async-start(), calls=%async_computation.25 | async-start | bytes 5242880 | tf_op jit(solution)/shard_map/reduce_scatter | solution.py:202
  636.6 43.8 %slice-start = ((s8[8388608]{0:T(1024)(128)(4,1)}), s8[4194304]{0:T(1024)(128)(4,1)S(1)}, s32[]{:S(2)}) async-start(s8[8388608]{0:T(1024)(128)(4,1)} %bitcast.405), calls=%async_computation.49 | async-start | bytes 8388608
  652.1 28.3 %slice-start.1 = ((s8[8388608]{0:T(1024)(128)(4,1)}), s8[4194304]{0:T(1024)(128)(4,1)S(1)}, s32[]{:S(2)}) async-start(s8[8388608]{0:T(1024)(128)(4,1)} %bitcast.405), calls=%async_computation.50 | async-start | bytes 8388608
  720.6 158.2 %reduce-scatter.24.cloned.1.call-start = ((), (), s32[]{:S(2)}) async-start(), calls=%async_computation.26 | async-start | bytes 5242880 | tf_op jit(solution)/shard_map/reduce_scatter | solution.py:202
  798.8 163.3 %all-gather.34.cloned.1.call-start = ((), (), s32[]{:S(2)}) async-start(), calls=%async_computation.27 | async-start | bytes 5242880 | tf_op jit(solution)/shard_map/all_gather | solution.py:199
  878.8 164.5 %all-gather.36.cloned.1.call-start = ((), (), s32[]{:S(2)}) async-start(), calls=%async_computation.28 | async-start | bytes 5242880 | tf_op jit(solution)/shard_map/all_gather | solution.py:199
  967.1 49.1 %all-to-all-start.1 = ((bf16[1,1,1,256,4,512]{5,3,2,1,0,4:T(8,128)(2,1)}), bf16[1,1,1,256,4,512]{5,3,2,1,0,4:T(8,128)(2,1)}, u32[]{:S(2)}, u32[]{:S(2)}) async-start(bf16[1,1,1,256,4,512]{5,3,2,1,0,4:T(8,128)(2,1)} %copy.158), calls=%async_computation.4 | async-start | bytes 2097152 | tf_op jit(solution)/shard_map/all_to_all | solution.py:213
  971.4 149.4 %reduce-scatter.26.cloned.1.call-start = ((), (), s32[]{:S(2)}) async-start(), calls=%async_computation.29 | async-start | bytes 5242880 | tf_op jit(solution)/shard_map/reduce_scatter | solution.py:202
  1047.3 48.0 %all-to-all-start.2 = ((bf16[1,1,1,256,4,512]{5,3,2,1,0,4:T(8,128)(2,1)}), bf16[1,1,1,256,4,512]{5,3,2,1,0,4:T(8,128)(2,1)S(1)}, u32[]{:S(2)}, u32[]{:S(2)}) async-start(bf16[1,1,1,256,4,512]{5,3,2,1,0,4:T(8,128)(2,1)} %copy.159), calls=%async_computation.6 | async-start | bytes 2097152 | tf_op jit(solution)/shard_map/all_to_all | solution.py:213
  1051.0 149.9 %reduce-scatter.28.cloned.1.call-start = ((), (), s32[]{:S(2)}) async-start(), calls=%async_computation.30 | async-start | bytes 5242880 | tf_op jit(solution)/shard_map/reduce_scatter | solution.py:202
  1095.3 25.6 %copy-start.57 = (f32[1,2048]{1,0:T(1,128)S(1)}, f32[1,2048]{1,0:T(1,128)}, u32[]{:S(2)}) copy-start(f32[1,2048]{1,0:T(1,128)} %copy-done.56) | copy-start | bytes 24580
  1095.3 25.6 %copy-start.79 = (f32[256]{0:T(256)S(1)}, f32[256]{0:T(256)}, u32[]{:S(2)}) copy-start(f32[256]{0:T(256)} %copy-done.78) | copy-start | bytes 3076
  1120.8 80.1 %copy-start.82 = (f32[256]{0:T(256)S(1)}, f32[256]{0:T(256)}, u32[]{:S(2)}) copy-start(f32[256]{0:T(256)} %copy-done.81) | copy-start | bytes 3076
  1120.8 135.5 %all-gather.38.cloned.1.call-start = ((), (), s32[]{:S(2)}) async-start(), calls=%async_computation.31 | async-start | bytes 5242880 | tf_op jit(solution)/shard_map/all_gather | solution.py:193
  1200.9 152.6 %all-gather.40.cloned.1.call-start = ((), (), s32[]{:S(2)}) async-start(), calls=%async_computation.32 | async-start | bytes 5242880 | tf_op jit(solution)/shard_map/all_gather | solution.py:193
  1204.1 57.6 %copy-start.88 = (f32[256]{0:T(256)}, f32[256]{0:T(256)S(1)}, u32[]{:S(2)}) copy-start(f32[256]{0:T(256)S(1)} %broadcast_multiply_fusion.2) | copy-start | bytes 3076
  1256.4 194.2 %reduce-scatter.30.cloned.1.call-start = ((), (), s32[]{:S(2)}) async-start(), calls=%async_computation.33 | async-start | bytes 5242880 | tf_op jit(solution)/shard_map/reduce_scatter | solution.py:196
  1284.8 29.0 %copy-start.41 = (bf16[1,1024,8,32]{1,3,2,0:T(8,128)(2,1)S(1)}, bf16[1,1024,8,32]{1,3,2,0:T(8,128)(2,1)}, u32[]{:S(2)}) copy-start(bf16[1,1024,8,32]{1,3,2,0:T(8,128)(2,1)} %copy-done.40) | copy-start | bytes 1572868
  1284.8 29.0 %copy-start.43 = (bf16[1,1024,8,32]{1,3,2,0:T(8,128)(2,1)S(1)}, bf16[1,1024,8,32]{1,3,2,0:T(8,128)(2,1)}, u32[]{:S(2)}) copy-start(bf16[1,1024,8,32]{1,3,2,0:T(8,128)(2,1)} %copy-done.42) | copy-start | bytes 1572868
  1353.5 258.3 %reduce-scatter.32.cloned.1.call-start = ((), (), s32[]{:S(2)}) async-start(), calls=%async_computation.34 | async-start | bytes 5242880 | tf_op jit(solution)/shard_map/reduce_scatter | solution.py:196
  1381.6 29.3 %copy-start.37 = (bf16[1,1024,8,32]{1,3,2,0:T(8,128)(2,1)S(1)}, bf16[1,1024,8,32]{1,3,2,0:T(8,128)(2,1)}, u32[]{:S(2)}) copy-start(bf16[1,1024,8,32]{1,3,2,0:T(8,128)(2,1)} %copy-done.36) | copy-start | bytes 1572868
  1381.6 29.3 %copy-start.39 = (bf16[1,1024,8,32]{1,3,2,0:T(8,128)(2,1)S(1)}, bf16[1,1024,8,32]{1,3,2,0:T(8,128)(2,1)}, u32[]{:S(2)}) copy-start(bf16[1,1024,8,32]{1,3,2,0:T(8,128)(2,1)} %copy-done.38) | copy-start | bytes 1572868
  1450.7 257.3 %reduce-scatter.38.cloned.1.call-start = ((), (), s32[]{:S(2)}) async-start(), calls=%async_computation.38 | async-start | bytes 25165824 | tf_op jit(solution)/shard_map/reduce_scatter | solution.py:173
  1500.4 213.4 %reduce-scatter.36.cloned.1.call-start = ((), (), s32[]{:S(2)}) async-start(), calls=%async_computation.37 | async-start | bytes 50331648 | tf_op jit(solution)/shard_map/reduce_scatter | solution.py:173
  1624.9 48.5 %all-to-all-start.3 = ((f32[1,1,1,256,4,512]{5,3,2,1,0,4:T(8,128)}), f32[1,1,1,256,4,512]{5,3,2,1,0,4:T(8,128)S(1)}, u32[]{:S(2)}, u32[]{:S(2)}) async-start(f32[1,1,1,256,4,512]{5,3,2,1,0,4:T(8,128)} %copy.166), calls=%async_computation.10 | async-start | bytes 4194304 | tf_op jit(solution)/shard_map/all_to_all | solution.py:213
  1628.6 98.4 %reduce-scatter.34.cloned.1.call-start = ((), (), s32[]{:S(2)}) async-start(), calls=%async_computation.35 | async-start | bytes 17301504 | tf_op jit(solution)/shard_map/reduce_scatter | solution.py:182
  1673.4 16.6 copy-start.13
  1707.8 76.5 %reduce-scatter.42.cloned.1.call-start = ((), (), s32[]{:S(2)}) async-start(), calls=%async_computation.48 | async-start | bytes 5242880
  1713.7 221.6 %reduce-scatter.40.cloned.1.call-start = ((), (), s32[]{:S(2)}) async-start(), calls=%async_computation.47 | async-start | bytes 10485760
  1731.5 71.5 %all-to-all-start.5 = ((bf16[4,256,1408]{2,1,0:T(8,128)(2,1)}), bf16[4,256,1408]{2,1,0:T(8,128)(2,1)}, u32[]{:S(2)}, u32[]{:S(2)}) async-start(bf16[4,256,1408]{2,1,0:T(8,128)(2,1)} %convert_bitcast_fusion.6), calls=%async_computation.14 | async-start | bytes 5767168 | tf_op jit(solution)/shard_map/all_to_all | solution.py:183
  1737.5 218.6 %all-gather.58.cloned.1.call-start = ((), (), s32[]{:S(2)}) async-start(), calls=%async_computation.46 | async-start | bytes 6291456 | tf_op jit(solution)/shard_map/all_gather | solution.py:187
  1787.1 195.8 %all-gather.42.cloned.1.call-start = ((), (), s32[]{:S(2)}) async-start(), calls=%async_computation.36 | async-start | bytes 4325376 | tf_op jit(solution)/shard_map/all_gather | solution.py:427
  1805.5 0.8 collective-permute-start.1
  1807.4 132.1 %copy-start.6 = (bf16[1,256,2048]{2,1,0:T(8,128)(2,1)S(1)}, bf16[1,256,2048]{2,1,0:T(8,128)(2,1)}, u32[]{:S(2)}) copy-start(bf16[1,256,2048]{2,1,0:T(8,128)(2,1)} %reduce-scatter.20.cloned.1.call-done) | copy-start | bytes 3145732
  1807.4 132.1 %copy-start.10 = (bf16[1,256,2048]{2,1,0:T(8,128)(2,1)S(1)}, bf16[1,256,2048]{2,1,0:T(8,128)(2,1)}, u32[]{:S(2)}) copy-start(bf16[1,256,2048]{2,1,0:T(8,128)(2,1)} %reduce-scatter.28.cloned.1.call-done) | copy-start | bytes 3145732
  1807.4 132.1 %copy-start.19 = (bf16[1,256,2048]{2,1,0:T(8,128)(2,1)S(1)}, bf16[1,256,2048]{2,1,0:T(8,128)(2,1)}, u32[]{:S(2)}) copy-start(bf16[1,256,2048]{2,1,0:T(8,128)(2,1)} %reduce-scatter.32.cloned.1.call-done) | copy-start | bytes 3145732
  1807.4 132.1 %copy-start.83 = (f32[256]{0:T(256)S(1)}, f32[256]{0:T(256)}, u32[]{:S(2)}) copy-start(f32[256]{0:T(256)} %copy-done.81) | copy-start | bytes 3076
  1807.4 132.1 %copy-start.89 = (f32[256]{0:T(256)S(1)}, f32[256]{0:T(256)}, u32[]{:S(2)}) copy-start(f32[256]{0:T(256)} %copy-done.88) | copy-start | bytes 3076
  1807.5 183.8 %all-gather.56.cloned.1.call-start = ((), (), s32[]{:S(2)}) async-start(), calls=%async_computation.45 | async-start | bytes 12582912 | tf_op jit(solution)/shard_map/all_gather | solution.py:187
  1948.8 29.6 %copy-start.14 = (f32[1,1,1,256,4,512]{5,3,2,1,0,4:T(8,128)S(1)}, f32[1,1,1,256,4,512]{5,3,2,1,0,4:T(8,128)}, u32[]{:S(2)}) copy-start(f32[1,1,1,256,4,512]{5,3,2,1,0,4:T(8,128)} %copy-done.13) | copy-start | bytes 6291460
  1948.8 29.6 %all-to-all-start.4 = ((f32[1,1,1,256,4,512]{5,3,2,1,0,4:T(8,128)}), f32[1,1,1,256,4,512]{5,3,2,1,0,4:T(8,128)}, u32[]{:S(2)}, u32[]{:S(2)}) async-start(f32[1,1,1,256,4,512]{5,3,2,1,0,4:T(8,128)} %copy.167), calls=%async_computation.12 | async-start | bytes 4194304 | tf_op jit(solution)/shard_map/all_to_all | solution.py:213
  (76 other events, 521.4 us)
Sparse Core Ops, SparseCore 0:
  30.4 86.3 all-gather.43
  119.2 50.8 all-gather.25
  172.2 15.1 all-gather.45
  189.7 53.7 all-gather.27
  246.9 52.5 reduce-scatter.17
  302.9 52.5 reduce-scatter.19
  358.0 52.5 all-gather.51
  413.0 87.4 all-gather.47
  502.7 80.7 all-gather.29
  585.4 18.3 all-gather.53
  605.3 31.2 all-gather.49
  638.6 81.9 all-gather.31
  723.4 75.2 reduce-scatter.21
  801.5 77.2 reduce-scatter.23
  880.8 81.2 all-gather.33
  964.1 79.2 all-gather.35
  1045.5 75.2 reduce-scatter.25
  1123.5 77.2 reduce-scatter.27
  1203.3 53.0 all-gather.37
  1258.6 52.5 all-gather.39
  1353.6 52.4 reduce-scatter.29
  1450.8 52.5 reduce-scatter.31
  1505.7 25.0 reduce-scatter.37
  1585.2 43.0 reduce-scatter.35
  1708.0 18.9 reduce-scatter.33
  1730.4 53.8 reduce-scatter.41
  1787.2 148.0 reduce-scatter.39
  1936.9 13.6 all-gather.57
  1952.7 12.8 all-gather.41
  1967.6 21.0 all-gather.55
